TPU v7x, 32 devices: a whole 2x2x4 slice. The times are simulated.
32 devices in a mesh: tile: 2 (over y), dom: 4 (over x, core), view: 4 (over z).
Axes of the slice: x: 2, y: 2, z: 4, core: 2. Of those that a mesh axis runs over, the one named last changes fastest.
Arguments:
- estimate: float32 [128, 32, 256], P(('tile', 'dom')), parts along dimension 0, may hold values from 0.25 to 4
- observed: float32 [4, 128, 32, 256], P('view', ('tile', 'dom')), parts along dimension 1, may hold values from 0.5 to 8
- psf: float32 [4, 4, 3, 9], P('view'), may hold values from 0.02 to 1
- src_map: int32 [4, 16], replicated, may hold values from 0 to 15, as said below
- depth_band: int32 [4, 64], P('view'), may hold values from 0 to 3, as said below
Outputs:
- new_estimate: float32 [128, 32, 256], P(('tile', 'dom')), parts along dimension 0
There are 2 independent parts, one for each index of `tile`. A program takes and returns all parts, laid end to end along the dimension named above; an argument that names none is the same for every part. Nothing has to cross between parts.
Inputs may be any that keep to these rules, and one draw needn't show every extreme that they name: For each view src_map is a permutation of the 16 joined blocks, and the 4 camera blocks f * 4 to f * 4 + 3 show blocks of 4 different depth slabs, one of each. For each view depth_band never falls along depth; it is 0 at the first plane and 3 at the last.
All inputs are finite; a program needn't handle non-finite values.
Results may differ from a plain program's by a relative error of at most 0.0001.
Values sent between devices are 32-bit elements; how exact they have to be, the bound alone decides.
No kernel may reach another device: no remote copies, remote signals or barrier semaphores. Data moves between devices by JAX's collectives and lax.ppermute only.
A program may use at most 64 MiB of HBM per device.

v0:
```python
import jax
import jax.numpy as jnp
from jax import lax
from jax.sharding import PartitionSpec as P

RADIUS = 4


precise = lax.Precision.HIGHEST


def extended_2(shard, sides, width):
    for axis, dim in sides:
        size, length = (lax.axis_size(axis), shard.shape[dim])
        up = [(i, (i + 1) % size) for i in range(size - 1)]
        down = [(j, i) for i, j in up]
        last = lax.slice_in_dim(shard, length - width, length, axis=dim)
        initial = lax.slice_in_dim(shard, 0, width, axis=dim)
        before = lax.ppermute(last, axis, up)
        after = lax.ppermute(initial, axis, down)
        shard = jnp.concatenate([before, shard, after], axis=dim)
    return shard


def taps_along(field, taps, axis, flipped):
    tap_count = taps.shape[1]
    reach = (tap_count - 1) // 2
    length = field.shape[axis]
    widths = [(0, 0), (0, 0), (0, 0)]
    widths[axis] = (reach, reach)
    padded = jnp.pad(field, widths)
    total = jnp.zeros(field.shape, jnp.float32)
    for offset in range(tap_count):
        start = 2 * reach - offset if flipped else offset
        piece = lax.slice_in_dim(padded, start, start + length, axis=axis)
        total = total + taps[:, offset][:, None, None] * piece
    return total


def lateral_fwd(field, x_taps, y_taps):
    inner = taps_along(field, x_taps, 2, False)
    return taps_along(inner, y_taps, 1, False)


def lateral_back(field, x_taps, y_taps):
    inner = taps_along(field, y_taps, 1, True)
    return taps_along(inner, x_taps, 2, True)


def body(estimate, observed, psf, src_map, depth_band):
    plane_count, row_count, lane_count = estimate.shape
    block_count = lax.axis_size("dom")
    block_rows = row_count // block_count
    dom_index = lax.axis_index("dom")
    view_index = lax.axis_index("view")
    view_count = lax.axis_size("view")
    plane_start = dom_index * plane_count
    slot_ids = jnp.arange(block_count, dtype=jnp.int32)
    my_map = lax.dynamic_index_in_dim(src_map, view_index, 0, keepdims=False)
    grid_map = my_map.reshape(block_count, block_count)
    source_dev = grid_map // block_count
    source_slot = grid_map % block_count
    send_slot = jnp.sum(jnp.where(source_dev == dom_index, source_slot, 0), axis=1)
    blocks = estimate.reshape(plane_count, block_count, block_rows, lane_count)
    outgoing = jnp.take(blocks, send_slot, axis=1)
    arrived = lax.all_to_all(outgoing, "dom", split_axis=1, concat_axis=1, tiled=True)
    my_sources = lax.dynamic_index_in_dim(source_dev, dom_index, 0, keepdims=False)
    camera = jnp.take(arrived, my_sources, axis=1).reshape(plane_count, row_count, lane_count)
    kernels = psf[0]
    band_all = depth_band[0]
    total_planes = band_all.shape[0]
    reach = (kernels.shape[2] - 1) // 2
    ext_count = plane_count + 2 * reach
    ext_index = jnp.clip(
        plane_start - reach + jnp.arange(ext_count, dtype=jnp.int32), 0, total_planes - 1
    )
    band_ext = jnp.take(band_all, ext_index)
    band_own = lax.dynamic_slice_in_dim(band_all, plane_start, plane_count)
    x_own = jnp.take(kernels[:, 2], band_own, axis=0)
    y_own = jnp.take(kernels[:, 1], band_own, axis=0)
    lateral = lateral_fwd(camera, x_own, y_own)
    extended = extended_2(lateral, (("dom", 0),), RADIUS)
    z_pos = jnp.arange(plane_count, dtype=jnp.int32)[:, None]
    s_pos = jnp.arange(ext_count, dtype=jnp.int32)[None, :]
    fwd_tap = s_pos - z_pos
    fwd_valid = (fwd_tap >= 0) & (fwd_tap <= 2 * reach)
    taps_own = jnp.take(kernels[:, 0], band_own, axis=0)
    row_sel = jnp.broadcast_to(z_pos, (plane_count, ext_count))
    depth_fwd = jnp.where(fwd_valid, taps_own[row_sel, jnp.clip(fwd_tap, 0, 2 * reach)], 0.0)
    blurred = jnp.einsum("zs,syx->zyx", depth_fwd, extended, precision=precise)
    ratio_field = observed[0] / blurred
    ratio_ext = extended_2(ratio_field, (("dom", 0),), RADIUS)
    back_tap = z_pos - s_pos + 2 * reach
    back_valid = (back_tap >= 0) & (back_tap <= 2 * reach)
    taps_ext = jnp.take(kernels[:, 0], band_ext, axis=0)
    col_sel = jnp.broadcast_to(s_pos, (plane_count, ext_count))
    depth_back = jnp.where(back_valid, taps_ext[col_sel, jnp.clip(back_tap, 0, 2 * reach)], 0.0)
    zback = jnp.einsum("zs,syx->zyx", depth_back, ratio_ext, precision=precise)
    back = lateral_back(zback, x_own, y_own)
    dest_slot = jnp.sum(
        jnp.where(my_sources[None, :] == slot_ids[:, None], slot_ids[None, :], 0), axis=1
    )
    inverse_slot = jnp.sum(
        jnp.where(send_slot[None, :] == slot_ids[:, None], slot_ids[None, :], 0), axis=1
    )
    back_blocks = back.reshape(plane_count, block_count, block_rows, lane_count)
    returning = jnp.take(back_blocks, dest_slot, axis=1)
    returned = lax.all_to_all(returning, "dom", split_axis=1, concat_axis=1, tiled=True)
    log_corr = jnp.log(jnp.take(returned, inverse_slot, axis=1))
    log_total = lax.psum(log_corr, "view")
    updated = blocks * jnp.exp(log_total / view_count)
    return updated.reshape(plane_count, row_count, lane_count)


def solution(mesh):
    in_specs = (
        P(("tile", "dom"), None, None),
        P("view", ("tile", "dom"), None, None),
        P("view", None, None, None),
        P(),
        P("view", None),
    )
    out_specs = P(("tile", "dom"), None, None)
    return jax.shard_map(body, mesh=mesh, in_specs=in_specs, out_specs=out_specs, check_vma=False)
```

profile of v0, /device:TPU:0, one launch (start us, length us, event | category | flops | bytes accessed | tf_op | source)
XLA Modules:
  0.0 108.7 jit_solution(233660518752022189)
XLA Ops:
  6.5 0.7 copy-done
  7.2 0.1 reshape.184
  7.3 0.1 fusion.101
  7.5 0.1 select_reduce_fusion.1
  7.6 1.6 %gather_fusion.7 = f32[4,16,8,256]{3,2,1,0:T(8,128)S(1)} fusion(f32[16,4,8,256]{3,2,1,0:T(8,128)} %bitcast.51, s32[1024]{0:T(1024)S(1)} %pad_clamp_fusion.3), kind=kCustom, calls=%fused_computation.1.clone | custom fusion | bytes 1048592 | tf_op jit(solution)/shard_map/jit(_take)/gather | solution.py:65
  9.2 0.9 select_bitcast_fusion.2
  10.2 4.2 %all-to-all-start = ((f32[16,4,8,256]{3,2,0,1:T(8,128)}), f32[16,4,8,256]{3,2,0,1:T(8,128)S(1)}, u32[]{:S(2)}, u32[]{:S(2)}) async-start(f32[16,4,8,256]{3,2,0,1:T(8,128)} %select_bitcast_fusion.2), calls=%async_computation | async-start | bytes 1048576 | tf_op jit(solution)/shard_map/all_to_all | solution.py:66
  14.4 0.6 copy-done.1
  15.1 0.7 gather_fusion
  15.8 0.1 compare_and_fusion.4
  15.9 0.6 copy-done.3
  16.5 0.6 gather_fusion.6
  17.1 0.6 gather_fusion.4
  17.7 0.6 gather_fusion.5
  18.2 0.1 broadcast_select_fusion.1
  18.3 0.6 gather_fusion.1
  18.9 0.5 slice_reduce_fusion.16
  19.4 0.1 broadcast_select_fusion
  19.4 3.8 %all-to-all-done = f32[16,4,8,256]{3,2,0,1:T(8,128)S(1)} async-done(((f32[16,4,8,256]{3,2,0,1:T(8,128)}), f32[16,4,8,256]{3,2,0,1:T(8,128)S(1)}, u32[]{:S(2)}, u32[]{:S(2)}) %all-to-all-start) | async-done | bytes 524320 | tf_op jit(solution)/shard_map/all_to_all | solution.py:66
  23.3 0.6 gather_fusion.8
  23.9 0.1 select_bitcast_fusion.1
  24.0 0.2 copy.22
  24.1 1.2 %fusion.51 = f32[16,32,256]{2,0,1:T(8,128)S(1)} fusion(f32[16,32,256]{2,0,1:T(8,128)S(1)} %bitcast.53, f32[16]{0:T(128)S(1)} %get-tuple-element.52, f32[16]{0:T(128)S(1)} %get-tuple-element.51, f32[16]{0:T(128)S(1)} %get-tuple-element.50, f32[16]{0:T(128)S(1)} %get-tuple-element.49, f32[16]{0:T(128)S(1)} %get-tuple-element.48, f32[16]{0:T(128)S(1)} %get-tuple-element.47, ...), kind=kLoop, calls=%fused_computation.95 | loop fusion | flops 2228224 | bytes 1049152 | tf_op jit(solution)/shard_map/add | solution.py:36
  25.3 0.4 fusion.19
  25.7 1.3 %collective-permute-start = (f32[4,32,256]{2,0,1:T(4,128)S(1)}, f32[4,32,256]{2,0,1:T(4,128)S(1)}, u32[]{:S(2)}, u32[]{:S(2)}) collective-permute-start(f32[4,32,256]{2,0,1:T(4,128)S(1)} %get-tuple-element.33), channel_id=1, source_target_pairs={{0,4},{4,8},{8,12},{1,5},{5,9},{9,13},{2,6},{6,10},{10,14},{3,7},{... | collective-permute-start | bytes 393224 | tf_op jit(solution)/shard_map/ppermute | solution.py:19
  27.0 1.3 %collective-permute-start.1 = (f32[4,32,256]{2,0,1:T(4,128)S(1)}, f32[4,32,256]{2,0,1:T(4,128)S(1)}, u32[]{:S(2)}, u32[]{:S(2)}) collective-permute-start(f32[4,32,256]{2,0,1:T(4,128)S(1)} %get-tuple-element.34), channel_id=1, source_target_pairs={{4,0},{8,4},{12,8},{5,1},{9,5},{13,9},{6,2},{10,6},{14,10},{7,3},{... | collective-permute-start | bytes 393224 | tf_op jit(solution)/shard_map/ppermute | solution.py:20
  28.4 0.1 reshape.266
  28.4 2.9 %gather_fusion.3 = f32[384]{0:T(512)S(1)} fusion(f32[16,9]{1,0:T(8,128)S(1)} %get-tuple-element.38, s32[384]{0:T(512)S(1)} %reshape.266), kind=kCustom, calls=%fused_computation.10 | custom fusion | bytes 6144 | tf_op jit(solution)/shard_map/gather | solution.py:89
  31.3 0.1 reshape.269
  31.5 0.9 convolution_divide_fusion
  32.4 4.9 %collective-permute-start.2 = (f32[4,32,256]{2,0,1:T(4,128)S(1)}, f32[4,32,256]{2,0,1:T(4,128)S(1)}, u32[]{:S(2)}, u32[]{:S(2)}) collective-permute-start(f32[4,32,256]{2,0,1:T(4,128)S(1)} %get-tuple-element.31), channel_id=1, source_target_pairs={{0,4},{4,8},{8,12},{1,5},{5,9},{9,13},{2,6},{6,10},{10,14},{3,7},{... | collective-permute-start | bytes 393224 | tf_op jit(solution)/shard_map/ppermute | solution.py:19
  37.3 1.3 %collective-permute-start.3 = (f32[4,32,256]{2,0,1:T(4,128)S(1)}, f32[4,32,256]{2,0,1:T(4,128)S(1)}, u32[]{:S(2)}, u32[]{:S(2)}) collective-permute-start(f32[4,32,256]{2,0,1:T(4,128)S(1)} %get-tuple-element.32), channel_id=1, source_target_pairs={{4,0},{8,4},{12,8},{5,1},{9,5},{13,9},{6,2},{10,6},{14,10},{7,3},{... | collective-permute-start | bytes 393224 | tf_op jit(solution)/shard_map/ppermute | solution.py:20
  38.6 0.1 reshape.260
  38.7 2.9 %gather_fusion.2 = f32[384]{0:T(512)S(1)} fusion(f32[24,9]{1,0:T(8,128)S(1)} %broadcast_select_fusion, s32[384]{0:T(512)S(1)} %reshape.260), kind=kCustom, calls=%fused_computation.9 | custom fusion | bytes 6144 | tf_op jit(solution)/shard_map/gather | solution.py:97
  41.6 0.1 reshape.263
  41.7 0.1 select_reduce_fusion
  41.8 0.7 fusion.5
  42.5 0.3 fusion.35
  42.9 1.2 %fusion.67 = f32[16,32,256]{2,0,1:T(8,128)S(1)} fusion(f32[16,32,256]{2,0,1:T(8,128)S(1)} %fusion.35, f32[16]{0:T(128)S(1)} %get-tuple-element.52, f32[16]{0:T(128)S(1)} %get-tuple-element.51, f32[16]{0:T(128)S(1)} %get-tuple-element.50, f32[16]{0:T(128)S(1)} %get-tuple-element.49, f32[16]{0:T(128)S(1)} %get-tuple-element.48, f32[16]{0:T(128)S(1)} %get-tuple-element.47, ...), kind=kLoop, calls=%fused_computation.111 | loop fusion | flops 2228224 | bytes 1049152 | tf_op jit(solution)/shard_map/add | solution.py:36
  44.0 0.3 copy.23
  44.3 0.6 gather_fusion.9
  44.9 0.9 select_bitcast_fusion
  45.8 4.0 %all-to-all-start.1 = ((f32[16,4,8,256]{3,2,0,1:T(8,128)}), f32[16,4,8,256]{3,2,0,1:T(8,128)S(1)}, u32[]{:S(2)}, u32[]{:S(2)}) async-start(f32[16,4,8,256]{3,2,0,1:T(8,128)} %select_bitcast_fusion), calls=%async_computation.1 | async-start | bytes 1048576 | tf_op jit(solution)/shard_map/all_to_all | solution.py:108
  49.9 8.8 %all-to-all-done.1 = f32[16,4,8,256]{3,2,0,1:T(8,128)S(1)} async-done(((f32[16,4,8,256]{3,2,0,1:T(8,128)}), f32[16,4,8,256]{3,2,0,1:T(8,128)S(1)}, u32[]{:S(2)}, u32[]{:S(2)}) %all-to-all-start.1) | async-done | bytes 524320 | tf_op jit(solution)/shard_map/all_to_all | solution.py:108
  58.7 0.6 gather_fusion.10
  59.3 0.9 bitcast_log_fusion
  60.3 39.7 %all-reduce.6.cloned.1.call-done = f32[16,4,8,256]{3,2,1,0:T(8,128)} async-done(((f32[16,4,8,256]{3,2,1,0:T(8,128)}), f32[16,4,8,256]{3,2,1,0:T(8,128)}) %all-reduce.6.cloned.1.call-update) | async-done | bytes 524304 | tf_op jit(solution)/shard_map/psum | solution.py:110
  100.0 1.9 %multiply_bitcast_fusion = f32[16,32,256]{2,1,0:T(8,128)} fusion(f32[16,4,8,256]{3,2,1,0:T(8,128)} %all-reduce.6.cloned.1.call-done, f32[16,32,256]{2,1,0:T(8,128)S(1)} %copy-done.2), kind=kLoop, calls=%fused_computation.124 | loop fusion | flops 262144 | bytes 1572864 | tf_op jit(solution)/shard_map/reshape | solution.py:112
  (37 shorter events, 0.4 us)
Async XLA Ops:
  6.5 0.7 copy-start
  10.2 13.1 %all-to-all-start = ((f32[16,4,8,256]{3,2,0,1:T(8,128)}), f32[16,4,8,256]{3,2,0,1:T(8,128)S(1)}, u32[]{:S(2)}, u32[]{:S(2)}) async-start(f32[16,4,8,256]{3,2,0,1:T(8,128)} %select_bitcast_fusion.2), calls=%async_computation | async-start | bytes 1048576 | tf_op jit(solution)/shard_map/all_to_all | solution.py:66
  14.4 0.7 copy-start.1
  15.8 0.7 copy-start.3
  25.7 5.7 %collective-permute-start = (f32[4,32,256]{2,0,1:T(4,128)S(1)}, f32[4,32,256]{2,0,1:T(4,128)S(1)}, u32[]{:S(2)}, u32[]{:S(2)}) collective-permute-start(f32[4,32,256]{2,0,1:T(4,128)S(1)} %get-tuple-element.33), channel_id=1, source_target_pairs={{0,4},{4,8},{8,12},{1,5},{5,9},{9,13},{2,6},{6,10},{10,14},{3,7},{... | collective-permute-start | bytes 393224 | tf_op jit(solution)/shard_map/ppermute | solution.py:19
  27.0 4.4 %collective-permute-start.1 = (f32[4,32,256]{2,0,1:T(4,128)S(1)}, f32[4,32,256]{2,0,1:T(4,128)S(1)}, u32[]{:S(2)}, u32[]{:S(2)}) collective-permute-start(f32[4,32,256]{2,0,1:T(4,128)S(1)} %get-tuple-element.34), channel_id=1, source_target_pairs={{4,0},{8,4},{12,8},{5,1},{9,5},{13,9},{6,2},{10,6},{14,10},{7,3},{... | collective-permute-start | bytes 393224 | tf_op jit(solution)/shard_map/ppermute | solution.py:20
  28.4 3.0 %copy-start.4 = (f32[1,16,32,256]{3,2,1,0:T(8,128)S(1)}, f32[1,16,32,256]{3,2,1,0:T(8,128)}, u32[]{:S(2)}) copy-start(f32[1,16,32,256]{3,2,1,0:T(8,128)} %param.10) | copy-start | bytes 1572868
  32.4 9.4 %collective-permute-start.2 = (f32[4,32,256]{2,0,1:T(4,128)S(1)}, f32[4,32,256]{2,0,1:T(4,128)S(1)}, u32[]{:S(2)}, u32[]{:S(2)}) collective-permute-start(f32[4,32,256]{2,0,1:T(4,128)S(1)} %get-tuple-element.31), channel_id=1, source_target_pairs={{0,4},{4,8},{8,12},{1,5},{5,9},{9,13},{2,6},{6,10},{10,14},{3,7},{... | collective-permute-start | bytes 393224 | tf_op jit(solution)/shard_map/ppermute | solution.py:19
  37.3 4.5 %collective-permute-start.3 = (f32[4,32,256]{2,0,1:T(4,128)S(1)}, f32[4,32,256]{2,0,1:T(4,128)S(1)}, u32[]{:S(2)}, u32[]{:S(2)}) collective-permute-start(f32[4,32,256]{2,0,1:T(4,128)S(1)} %get-tuple-element.32), channel_id=1, source_target_pairs={{4,0},{8,4},{12,8},{5,1},{9,5},{13,9},{6,2},{10,6},{14,10},{7,3},{... | collective-permute-start | bytes 393224 | tf_op jit(solution)/shard_map/ppermute | solution.py:20
  45.8 12.8 %all-to-all-start.1 = ((f32[16,4,8,256]{3,2,0,1:T(8,128)}), f32[16,4,8,256]{3,2,0,1:T(8,128)S(1)}, u32[]{:S(2)}, u32[]{:S(2)}) async-start(f32[16,4,8,256]{3,2,0,1:T(8,128)} %select_bitcast_fusion), calls=%async_computation.1 | async-start | bytes 1048576 | tf_op jit(solution)/shard_map/all_to_all | solution.py:108
  49.9 50.1 %all-reduce.6.cloned.1.call-start = ((), (), s32[]{:S(2)}) async-start(), calls=%async_computation.2 | async-start | bytes 1048576 | tf_op jit(solution)/shard_map/psum | solution.py:110
  60.3 39.7 %copy-start.2 = (f32[16,32,256]{2,1,0:T(8,128)S(1)}, f32[16,32,256]{2,1,0:T(8,128)}, u32[]{:S(2)}) copy-start(f32[16,32,256]{2,1,0:T(8,128)} %param.9) | copy-start | bytes 1572868
Sparse Core Ops, SparseCore 0:
  60.4 39.5 all-reduce.5
where the time goes:
time: 109 us
  waiting for transfers between devices  52.3 us (48%)
  starting transfers between devices  17 us (16%)
  local copies, waits for them, and re-layouts  15.6 us (14%)
  between operations  13.7 us (13%)
  other arithmetic  8.56 us (8%)
  matrix products  1.56 us (1%)
    psum x1, waiting for transfers between devices, body(): log_total = lax.psum(log_corr, 'view')  39.7 us
    all_to_all x1, waiting for transfers between devices, body(): lax.all_to_all(returning, 'dom', split_axis=1, concat_axis=1, tiled=True)  8.78 us
    ppermute x2, starting transfers between devices, extended_2(): before = lax.ppermute(last, axis, up)  6.17 us
    all_to_all x1, starting transfers between devices, body(): lax.all_to_all(outgoing, 'dom', split_axis=1, concat_axis=1, tiled=True)  4.24 us
    all_to_all x1, starting transfers between devices, body(): lax.all_to_all(returning, 'dom', split_axis=1, concat_axis=1, tiled=True)  4.03 us
    all_to_all x1, waiting for transfers between devices, body(): lax.all_to_all(outgoing, 'dom', split_axis=1, concat_axis=1, tiled=True)  3.78 us
    add x4, other arithmetic, taps_along(): total = total + taps[:, offset][:, None, None] * piece  3.03 us
    gather x2, local copies, waits for them, and re-layouts, body(): taps_ext[col_sel, jnp.clip(back_tap, 0, 2 * reach)]  2.96 us
  transfers between devices with their start and end apart: 7, of which 3 were waited for; matrix products, arithmetic and copies ran while one was open for 9% of the time, Pallas kernels for 0%

commit v1 on v0

--- a/solution.py
+++ b/solution.py
@@ -20,6 +20,34 @@
         after = lax.ppermute(initial, axis, down)
         shard = jnp.concatenate([before, shard, after], axis=dim)
     return shard
+
+
+def line_sum(value, axis, chunks):
+    size = lax.axis_size(axis)
+    if size == 1:
+        return value
+    if size % 2:
+        return lax.psum(value, axis)
+    me = lax.axis_index(axis)
+    half = size // 2
+    pieces = jnp.split(value, chunks, axis=0)
+    outs = []
+    for acc in pieces:
+        for r in range(1, half):
+            perm = [(r - 1, r), (size - r, size - r - 1)]
+            got = lax.ppermute(acc, axis, perm)
+            take = (me == r) | (me == size - 1 - r)
+            acc = jnp.where(take, got + acc, acc)
+        got = lax.ppermute(acc, axis, [(half - 1, half), (half, half - 1)])
+        take = (me == half - 1) | (me == half)
+        acc = jnp.where(take, acc + got, acc)
+        for r in range(1, half):
+            perm = [(half - r, half - r - 1), (half - 1 + r, half + r)]
+            got = lax.ppermute(acc, axis, perm)
+            take = (me == half - r - 1) | (me == half + r)
+            acc = jnp.where(take, got, acc)
+        outs.append(acc)
+    return jnp.concatenate(outs, axis=0)
 
 
 def taps_along(field, taps, axis, flipped):
@@ -107,7 +135,7 @@
     returning = jnp.take(back_blocks, dest_slot, axis=1)
     returned = lax.all_to_all(returning, "dom", split_axis=1, concat_axis=1, tiled=True)
     log_corr = jnp.log(jnp.take(returned, inverse_slot, axis=1))
-    log_total = lax.psum(log_corr, "view")
+    log_total = line_sum(log_corr, "view", 4)
     updated = blocks * jnp.exp(log_total / view_count)
     return updated.reshape(plane_count, row_count, lane_count)
 

time: 109 us -> 95.2 us (0.87); the launches traced: 109 us -> 93.3 us
  waiting for transfers between devices: 52.3 us -> 32.6 us
  starting transfers between devices: 17 us -> 36 us
  between operations: 13.7 us -> 0.59 us
  other arithmetic: 8.56 us -> 7.11 us
    psum x1 -> x0, waiting for transfers between devices: 39.7 us -> none  [body(): log_total = lax.psum(log_corr, 'view')]
    ppermute x0 -> x12, waiting for transfers between devices: none -> 20.1 us  [the longest x8 20.1 us: line_sum(): got = lax.ppermute(acc, axis, perm)]
    ppermute x0 -> x12, starting transfers between devices: none -> 19 us  [the longest x8 16.3 us: line_sum(): got = lax.ppermute(acc, axis, perm)]
    reshape x1 -> x0, other arithmetic: 1.93 us -> none  [body(): return updated.reshape(plane_count, row_count, lane_count)]
  transfers between devices with their start and end apart: 7 -> 18, of which waited for: 3 -> 10; matrix products, arithmetic and copies ran while one was open for 9% -> 11% of each run, Pallas kernels for 0% -> 0%
where the time goes in v1:
time: 95.2 us; the launch traced here: 93.3 us
  starting transfers between devices  36 us (38%)
  waiting for transfers between devices  32.6 us (34%)
  local copies, waits for them, and re-layouts  15.5 us (16%)
  other arithmetic  7.11 us (7%)
  matrix products  1.54 us (2%)
    ppermute x8, waiting for transfers between devices, line_sum(): got = lax.ppermute(acc, axis, perm)  20.1 us
    ppermute x8, starting transfers between devices, line_sum(): got = lax.ppermute(acc, axis, perm)  16.3 us
    all_to_all x1, waiting for transfers between devices, body(): lax.all_to_all(returning, 'dom', split_axis=1, concat_axis=1, tiled=True)  8.79 us
    ppermute x2, starting transfers between devices, extended_2(): before = lax.ppermute(last, axis, up)  6.17 us
    all_to_all x1, starting transfers between devices, body(): lax.all_to_all(outgoing, 'dom', split_axis=1, concat_axis=1, tiled=True)  4.24 us
    all_to_all x1, starting transfers between devices, body(): lax.all_to_all(returning, 'dom', split_axis=1, concat_axis=1, tiled=True)  4.03 us
    all_to_all x1, waiting for transfers between devices, body(): lax.all_to_all(outgoing, 'dom', split_axis=1, concat_axis=1, tiled=True)  3.71 us
    add x4, other arithmetic, taps_along(): total = total + taps[:, offset][:, None, None] * piece  3.03 us
  transfers between devices with their start and end apart: 18, of which 10 were waited for; matrix products, arithmetic and copies ran while one was open for 11% of the time, Pallas kernels for 0%

profile of v1, /device:TPU:0, one launch (start us, length us, event | category | flops | bytes accessed | tf_op | source)
XLA Modules:
  0.0 93.3 jit_solution(7224869519911240463)
XLA Ops:
  0.0 0.7 copy-done
  1.1 1.6 %gather_fusion.7 = f32[4,16,8,256]{3,2,1,0:T(8,128)S(1)} fusion(f32[16,4,8,256]{3,2,1,0:T(8,128)} %bitcast.84, s32[1024]{0:T(1024)S(1)} %pad_clamp_fusion.3), kind=kCustom, calls=%fused_computation.1.clone | custom fusion | bytes 1048592 | tf_op jit(solution)/shard_map/jit(_take)/gather | solution.py:93
  2.7 0.9 select_bitcast_fusion.2
  3.6 4.2 %all-to-all-start = ((f32[16,4,8,256]{3,2,0,1:T(8,128)}), f32[16,4,8,256]{3,2,0,1:T(8,128)S(1)}, u32[]{:S(2)}, u32[]{:S(2)}) async-start(f32[16,4,8,256]{3,2,0,1:T(8,128)} %select_bitcast_fusion.2), calls=%async_computation | async-start | bytes 1048576 | tf_op jit(solution)/shard_map/all_to_all | solution.py:94
  7.9 0.6 copy-done.1
  8.5 0.7 gather_fusion
  9.4 0.7 copy-done.3
  10.6 0.6 gather_fusion.4
  11.2 0.6 gather_fusion.6
  11.8 0.6 gather_fusion.1
  13.0 3.7 %all-to-all-done = f32[16,4,8,256]{3,2,0,1:T(8,128)S(1)} async-done(((f32[16,4,8,256]{3,2,0,1:T(8,128)}), f32[16,4,8,256]{3,2,0,1:T(8,128)S(1)}, u32[]{:S(2)}, u32[]{:S(2)}) %all-to-all-start) | async-done | bytes 524320 | tf_op jit(solution)/shard_map/all_to_all | solution.py:94
  16.7 0.6 gather_fusion.8
  17.6 1.2 %fusion.51 = f32[16,32,256]{2,0,1:T(8,128)S(1)} fusion(f32[16,32,256]{2,0,1:T(8,128)S(1)} %bitcast.85, f32[16]{0:T(128)S(1)} %get-tuple-element.59, f32[16]{0:T(128)S(1)} %get-tuple-element.58, f32[16]{0:T(128)S(1)} %get-tuple-element.57, f32[16]{0:T(128)S(1)} %get-tuple-element.56, f32[16]{0:T(128)S(1)} %get-tuple-element.55, f32[16]{0:T(128)S(1)} %get-tuple-element.54, ...), kind=kLoop, calls=%fused_computation.95 | loop fusion | flops 2228224 | bytes 1049152 | tf_op jit(solution)/shard_map/add | solution.py:64
  19.2 1.3 %collective-permute-start = (f32[4,32,256]{2,0,1:T(4,128)S(1)}, f32[4,32,256]{2,0,1:T(4,128)S(1)}, u32[]{:S(2)}, u32[]{:S(2)}) collective-permute-start(f32[4,32,256]{2,0,1:T(4,128)S(1)} %get-tuple-element.40), channel_id=1, source_target_pairs={{0,4},{4,8},{8,12},{1,5},{5,9},{9,13},{2,6},{6,10},{10,14},{3,7},{... | collective-permute-start | bytes 393224 | tf_op jit(solution)/shard_map/ppermute | solution.py:19
  20.5 1.3 %collective-permute-start.1 = (f32[4,32,256]{2,0,1:T(4,128)S(1)}, f32[4,32,256]{2,0,1:T(4,128)S(1)}, u32[]{:S(2)}, u32[]{:S(2)}) collective-permute-start(f32[4,32,256]{2,0,1:T(4,128)S(1)} %get-tuple-element.41), channel_id=1, source_target_pairs={{4,0},{8,4},{12,8},{5,1},{9,5},{13,9},{6,2},{10,6},{14,10},{7,3},{... | collective-permute-start | bytes 393224 | tf_op jit(solution)/shard_map/ppermute | solution.py:20
  21.9 2.9 %gather_fusion.3 = f32[384]{0:T(512)S(1)} fusion(f32[16,9]{1,0:T(8,128)S(1)} %get-tuple-element.45, s32[384]{0:T(512)S(1)} %reshape.267), kind=kCustom, calls=%fused_computation.10 | custom fusion | bytes 6144 | tf_op jit(solution)/shard_map/gather | solution.py:117
  24.9 0.9 convolution_divide_fusion
  25.9 4.9 %collective-permute-start.2 = (f32[4,32,256]{2,0,1:T(4,128)S(1)}, f32[4,32,256]{2,0,1:T(4,128)S(1)}, u32[]{:S(2)}, u32[]{:S(2)}) collective-permute-start(f32[4,32,256]{2,0,1:T(4,128)S(1)} %get-tuple-element.38), channel_id=1, source_target_pairs={{0,4},{4,8},{8,12},{1,5},{5,9},{9,13},{2,6},{6,10},{10,14},{3,7},{... | collective-permute-start | bytes 393224 | tf_op jit(solution)/shard_map/ppermute | solution.py:19
  30.8 1.3 %collective-permute-start.3 = (f32[4,32,256]{2,0,1:T(4,128)S(1)}, f32[4,32,256]{2,0,1:T(4,128)S(1)}, u32[]{:S(2)}, u32[]{:S(2)}) collective-permute-start(f32[4,32,256]{2,0,1:T(4,128)S(1)} %get-tuple-element.39), channel_id=1, source_target_pairs={{4,0},{8,4},{12,8},{5,1},{9,5},{13,9},{6,2},{10,6},{14,10},{7,3},{... | collective-permute-start | bytes 393224 | tf_op jit(solution)/shard_map/ppermute | solution.py:20
  32.2 2.9 %gather_fusion.2 = f32[384]{0:T(512)S(1)} fusion(f32[24,9]{1,0:T(8,128)S(1)} %broadcast_select_fusion.4, s32[384]{0:T(512)S(1)} %reshape.261), kind=kCustom, calls=%fused_computation.9 | custom fusion | bytes 6144 | tf_op jit(solution)/shard_map/gather | solution.py:125
  35.3 0.6 fusion.5
  36.3 1.2 %fusion.67 = f32[16,32,256]{2,0,1:T(8,128)S(1)} fusion(f32[16,32,256]{2,0,1:T(8,128)S(1)} %fusion.35, f32[16]{0:T(128)S(1)} %get-tuple-element.59, f32[16]{0:T(128)S(1)} %get-tuple-element.58, f32[16]{0:T(128)S(1)} %get-tuple-element.57, f32[16]{0:T(128)S(1)} %get-tuple-element.56, f32[16]{0:T(128)S(1)} %get-tuple-element.55, f32[16]{0:T(128)S(1)} %get-tuple-element.54, ...), kind=kLoop, calls=%fused_computation.111 | loop fusion | flops 2228224 | bytes 1049152 | tf_op jit(solution)/shard_map/add | solution.py:64
  37.5 0.6 gather_fusion.9
  38.1 0.9 select_bitcast_fusion
  39.0 4.0 %all-to-all-start.1 = ((f32[16,4,8,256]{3,0,2,1:T(8,128)}), f32[16,4,8,256]{3,0,2,1:T(8,128)S(1)}, u32[]{:S(2)}, u32[]{:S(2)}) async-start(f32[16,4,8,256]{3,0,2,1:T(8,128)} %select_bitcast_fusion), calls=%async_computation.1 | async-start | bytes 1048576 | tf_op jit(solution)/shard_map/all_to_all | solution.py:136
  43.0 8.8 %all-to-all-done.1 = f32[16,4,8,256]{3,0,2,1:T(8,128)S(1)} async-done(((f32[16,4,8,256]{3,0,2,1:T(8,128)}), f32[16,4,8,256]{3,0,2,1:T(8,128)S(1)}, u32[]{:S(2)}, u32[]{:S(2)}) %all-to-all-start.1) | async-done | bytes 524320 | tf_op jit(solution)/shard_map/all_to_all | solution.py:136
  51.8 0.6 gather_fusion.10
  52.6 4.2 %collective-permute-start.4 = (f32[4,4,8,256]{3,0,2,1:T(4,128)S(1)}, f32[4,4,8,256]{3,0,2,1:T(4,128)S(1)}, u32[]{:S(2)}, u32[]{:S(2)}) collective-permute-start(f32[4,4,8,256]{3,0,2,1:T(4,128)S(1)} %split.16), channel_id=1, source_target_pairs={{0,1},{3,2},{4,5},{7,6},{8,9},{11,10},{12,13},{15,14},{16,17},{19,... | collective-permute-start | bytes 393224 | tf_op jit(solution)/shard_map/ppermute | solution.py:38
  56.8 2.5 %collective-permute-done.4 = f32[4,4,8,256]{3,0,2,1:T(4,128)S(1)} collective-permute-done((f32[4,4,8,256]{3,0,2,1:T(4,128)S(1)}, f32[4,4,8,256]{3,0,2,1:T(4,128)S(1)}, u32[]{:S(2)}, u32[]{:S(2)}) %collective-permute-start.4) | collective-permute-done | bytes 131104 | tf_op jit(solution)/shard_map/ppermute | solution.py:38
  59.4 4.4 %collective-permute-start.13 = (f32[4,4,8,256]{3,0,2,1:T(4,128)S(1)}, f32[4,4,8,256]{3,0,2,1:T(4,128)S(1)}, u32[]{:S(2)}, u32[]{:S(2)}) collective-permute-start(f32[4,4,8,256]{3,0,2,1:T(4,128)S(1)} %get-tuple-element.32), channel_id=1, source_target_pairs={{0,1},{3,2},{4,5},{7,6},{8,9},{11,10},{12,13},{15,14},{16,17},{19,... | collective-permute-start | bytes 393224 | tf_op jit(solution)/shard_map/ppermute | solution.py:38
  63.8 1.3 %collective-permute-start.10 = (f32[4,4,8,256]{3,0,2,1:T(4,128)S(1)}, f32[4,4,8,256]{3,0,2,1:T(4,128)S(1)}, u32[]{:S(2)}, u32[]{:S(2)}) collective-permute-start(f32[4,4,8,256]{3,0,2,1:T(4,128)S(1)} %get-tuple-element.33), channel_id=1, source_target_pairs={{0,1},{3,2},{4,5},{7,6},{8,9},{11,10},{12,13},{15,14},{16,17},{19,... | collective-permute-start | bytes 393224 | tf_op jit(solution)/shard_map/ppermute | solution.py:38
  65.1 1.3 %collective-permute-start.7 = (f32[4,4,8,256]{3,0,2,1:T(4,128)S(1)}, f32[4,4,8,256]{3,0,2,1:T(4,128)S(1)}, u32[]{:S(2)}, u32[]{:S(2)}) collective-permute-start(f32[4,4,8,256]{3,0,2,1:T(4,128)S(1)} %get-tuple-element.34), channel_id=1, source_target_pairs={{0,1},{3,2},{4,5},{7,6},{8,9},{11,10},{12,13},{15,14},{16,17},{19,... | collective-permute-start | bytes 393224 | tf_op jit(solution)/shard_map/ppermute | solution.py:38
  66.4 0.7 collective-permute-start.5
  67.1 0.6 collective-permute-done.13
  67.6 1.5 %collective-permute-done.10 = f32[4,4,8,256]{3,0,2,1:T(4,128)S(1)} collective-permute-done((f32[4,4,8,256]{3,0,2,1:T(4,128)S(1)}, f32[4,4,8,256]{3,0,2,1:T(4,128)S(1)}, u32[]{:S(2)}, u32[]{:S(2)}) %collective-permute-start.10) | collective-permute-done | bytes 131104 | tf_op jit(solution)/shard_map/ppermute | solution.py:38
  69.1 1.4 %collective-permute-done.7 = f32[4,4,8,256]{3,0,2,1:T(4,128)S(1)} collective-permute-done((f32[4,4,8,256]{3,0,2,1:T(4,128)S(1)}, f32[4,4,8,256]{3,0,2,1:T(4,128)S(1)}, u32[]{:S(2)}, u32[]{:S(2)}) %collective-permute-start.7) | collective-permute-done | bytes 131104 | tf_op jit(solution)/shard_map/ppermute | solution.py:38
  70.6 0.7 collective-permute-start.8
  71.3 0.7 collective-permute-start.11
  72.0 0.7 collective-permute-start.14
  72.7 1.3 %collective-permute-start.6 = (f32[4,4,8,256]{3,0,2,1:T(4,128)S(1)}, f32[4,4,8,256]{3,0,2,1:T(4,128)S(1)}, u32[]{:S(2)}, u32[]{:S(2)}) collective-permute-start(f32[4,4,8,256]{3,0,2,1:T(4,128)S(1)} %bitcast.95), channel_id=1, source_target_pairs={{1,0},{2,3},{5,4},{6,7},{9,8},{10,11},{13,12},{14,15},{17,16},{18,... | collective-permute-start | bytes 393224 | tf_op jit(solution)/shard_map/ppermute | solution.py:46
  74.0 1.3 %collective-permute-start.9 = (f32[4,4,8,256]{3,0,2,1:T(4,128)S(1)}, f32[4,4,8,256]{3,0,2,1:T(4,128)S(1)}, u32[]{:S(2)}, u32[]{:S(2)}) collective-permute-start(f32[4,4,8,256]{3,0,2,1:T(4,128)S(1)} %bitcast.96), channel_id=1, source_target_pairs={{1,0},{2,3},{5,4},{6,7},{9,8},{10,11},{13,12},{14,15},{17,16},{18,... | collective-permute-start | bytes 393224 | tf_op jit(solution)/shard_map/ppermute | solution.py:46
  75.4 1.3 %collective-permute-start.12 = (f32[4,4,8,256]{3,0,2,1:T(4,128)S(1)}, f32[4,4,8,256]{3,0,2,1:T(4,128)S(1)}, u32[]{:S(2)}, u32[]{:S(2)}) collective-permute-start(f32[4,4,8,256]{3,0,2,1:T(4,128)S(1)} %bitcast.97), channel_id=1, source_target_pairs={{1,0},{2,3},{5,4},{6,7},{9,8},{10,11},{13,12},{14,15},{17,16},{18,... | collective-permute-start | bytes 393224 | tf_op jit(solution)/shard_map/ppermute | solution.py:46
  76.7 1.3 %collective-permute-start.15 = (f32[4,4,8,256]{3,0,2,1:T(4,128)S(1)}, f32[4,4,8,256]{3,0,2,1:T(4,128)S(1)}, u32[]{:S(2)}, u32[]{:S(2)}) collective-permute-start(f32[4,4,8,256]{3,0,2,1:T(4,128)S(1)} %bitcast.98), channel_id=1, source_target_pairs={{1,0},{2,3},{5,4},{6,7},{9,8},{10,11},{13,12},{14,15},{17,16},{18,... | collective-permute-start | bytes 393224 | tf_op jit(solution)/shard_map/ppermute | solution.py:46
  78.0 10.1 %collective-permute-done.6 = f32[4,4,8,256]{3,0,2,1:T(4,128)S(1)} collective-permute-done((f32[4,4,8,256]{3,0,2,1:T(4,128)S(1)}, f32[4,4,8,256]{3,0,2,1:T(4,128)S(1)}, u32[]{:S(2)}, u32[]{:S(2)}) %collective-permute-start.6) | collective-permute-done | bytes 131104 | tf_op jit(solution)/shard_map/ppermute | solution.py:46
  88.2 1.4 %collective-permute-done.9 = f32[4,4,8,256]{3,0,2,1:T(4,128)S(1)} collective-permute-done((f32[4,4,8,256]{3,0,2,1:T(4,128)S(1)}, f32[4,4,8,256]{3,0,2,1:T(4,128)S(1)}, u32[]{:S(2)}, u32[]{:S(2)}) %collective-permute-start.9) | collective-permute-done | bytes 131104 | tf_op jit(solution)/shard_map/ppermute | solution.py:46
  89.6 1.3 %collective-permute-done.12 = f32[4,4,8,256]{3,0,2,1:T(4,128)S(1)} collective-permute-done((f32[4,4,8,256]{3,0,2,1:T(4,128)S(1)}, f32[4,4,8,256]{3,0,2,1:T(4,128)S(1)}, u32[]{:S(2)}, u32[]{:S(2)}) %collective-permute-start.12) | collective-permute-done | bytes 131104 | tf_op jit(solution)/shard_map/ppermute | solution.py:46
  91.0 1.3 %collective-permute-done.15 = f32[4,4,8,256]{3,0,2,1:T(4,128)S(1)} collective-permute-done((f32[4,4,8,256]{3,0,2,1:T(4,128)S(1)}, f32[4,4,8,256]{3,0,2,1:T(4,128)S(1)}, u32[]{:S(2)}, u32[]{:S(2)}) %collective-permute-start.15) | collective-permute-done | bytes 131104 | tf_op jit(solution)/shard_map/ppermute | solution.py:46
  92.4 0.9 fusion.76
  (71 shorter events, 4.0 us)
Async XLA Ops:
  0.0 0.7 copy-start
  3.6 13.1 %all-to-all-start = ((f32[16,4,8,256]{3,2,0,1:T(8,128)}), f32[16,4,8,256]{3,2,0,1:T(8,128)S(1)}, u32[]{:S(2)}, u32[]{:S(2)}) async-start(f32[16,4,8,256]{3,2,0,1:T(8,128)} %select_bitcast_fusion.2), calls=%async_computation | async-start | bytes 1048576 | tf_op jit(solution)/shard_map/all_to_all | solution.py:94
  7.9 0.7 copy-start.1
  9.4 0.7 copy-start.3
  19.2 5.7 %collective-permute-start = (f32[4,32,256]{2,0,1:T(4,128)S(1)}, f32[4,32,256]{2,0,1:T(4,128)S(1)}, u32[]{:S(2)}, u32[]{:S(2)}) collective-permute-start(f32[4,32,256]{2,0,1:T(4,128)S(1)} %get-tuple-element.40), channel_id=1, source_target_pairs={{0,4},{4,8},{8,12},{1,5},{5,9},{9,13},{2,6},{6,10},{10,14},{3,7},{... | collective-permute-start | bytes 393224 | tf_op jit(solution)/shard_map/ppermute | solution.py:19
  20.5 4.4 %collective-permute-start.1 = (f32[4,32,256]{2,0,1:T(4,128)S(1)}, f32[4,32,256]{2,0,1:T(4,128)S(1)}, u32[]{:S(2)}, u32[]{:S(2)}) collective-permute-start(f32[4,32,256]{2,0,1:T(4,128)S(1)} %get-tuple-element.41), channel_id=1, source_target_pairs={{4,0},{8,4},{12,8},{5,1},{9,5},{13,9},{6,2},{10,6},{14,10},{7,3},{... | collective-permute-start | bytes 393224 | tf_op jit(solution)/shard_map/ppermute | solution.py:20
  21.9 3.0 %copy-start.4 = (f32[1,16,32,256]{3,2,1,0:T(8,128)S(1)}, f32[1,16,32,256]{3,2,1,0:T(8,128)}, u32[]{:S(2)}) copy-start(f32[1,16,32,256]{3,2,1,0:T(8,128)} %param.10) | copy-start | bytes 1572868
  25.9 9.4 %collective-permute-start.2 = (f32[4,32,256]{2,0,1:T(4,128)S(1)}, f32[4,32,256]{2,0,1:T(4,128)S(1)}, u32[]{:S(2)}, u32[]{:S(2)}) collective-permute-start(f32[4,32,256]{2,0,1:T(4,128)S(1)} %get-tuple-element.38), channel_id=1, source_target_pairs={{0,4},{4,8},{8,12},{1,5},{5,9},{9,13},{2,6},{6,10},{10,14},{3,7},{... | collective-permute-start | bytes 393224 | tf_op jit(solution)/shard_map/ppermute | solution.py:19
  30.8 4.5 %collective-permute-start.3 = (f32[4,32,256]{2,0,1:T(4,128)S(1)}, f32[4,32,256]{2,0,1:T(4,128)S(1)}, u32[]{:S(2)}, u32[]{:S(2)}) collective-permute-start(f32[4,32,256]{2,0,1:T(4,128)S(1)} %get-tuple-element.39), channel_id=1, source_target_pairs={{4,0},{8,4},{12,8},{5,1},{9,5},{13,9},{6,2},{10,6},{14,10},{7,3},{... | collective-permute-start | bytes 393224 | tf_op jit(solution)/shard_map/ppermute | solution.py:20
  39.0 12.8 %all-to-all-start.1 = ((f32[16,4,8,256]{3,0,2,1:T(8,128)}), f32[16,4,8,256]{3,0,2,1:T(8,128)S(1)}, u32[]{:S(2)}, u32[]{:S(2)}) async-start(f32[16,4,8,256]{3,0,2,1:T(8,128)} %select_bitcast_fusion), calls=%async_computation.1 | async-start | bytes 1048576 | tf_op jit(solution)/shard_map/all_to_all | solution.py:136
  52.6 6.7 %collective-permute-start.4 = (f32[4,4,8,256]{3,0,2,1:T(4,128)S(1)}, f32[4,4,8,256]{3,0,2,1:T(4,128)S(1)}, u32[]{:S(2)}, u32[]{:S(2)}) collective-permute-start(f32[4,4,8,256]{3,0,2,1:T(4,128)S(1)} %split.16), channel_id=1, source_target_pairs={{0,1},{3,2},{4,5},{7,6},{8,9},{11,10},{12,13},{15,14},{16,17},{19,... | collective-permute-start | bytes 393224 | tf_op jit(solution)/shard_map/ppermute | solution.py:38
  59.4 8.2 %collective-permute-start.13 = (f32[4,4,8,256]{3,0,2,1:T(4,128)S(1)}, f32[4,4,8,256]{3,0,2,1:T(4,128)S(1)}, u32[]{:S(2)}, u32[]{:S(2)}) collective-permute-start(f32[4,4,8,256]{3,0,2,1:T(4,128)S(1)} %get-tuple-element.32), channel_id=1, source_target_pairs={{0,1},{3,2},{4,5},{7,6},{8,9},{11,10},{12,13},{15,14},{16,17},{19,... | collective-permute-start | bytes 393224 | tf_op jit(solution)/shard_map/ppermute | solution.py:38
  63.8 5.3 %collective-permute-start.10 = (f32[4,4,8,256]{3,0,2,1:T(4,128)S(1)}, f32[4,4,8,256]{3,0,2,1:T(4,128)S(1)}, u32[]{:S(2)}, u32[]{:S(2)}) collective-permute-start(f32[4,4,8,256]{3,0,2,1:T(4,128)S(1)} %get-tuple-element.33), channel_id=1, source_target_pairs={{0,1},{3,2},{4,5},{7,6},{8,9},{11,10},{12,13},{15,14},{16,17},{19,... | collective-permute-start | bytes 393224 | tf_op jit(solution)/shard_map/ppermute | solution.py:38
  65.1 5.4 %collective-permute-start.7 = (f32[4,4,8,256]{3,0,2,1:T(4,128)S(1)}, f32[4,4,8,256]{3,0,2,1:T(4,128)S(1)}, u32[]{:S(2)}, u32[]{:S(2)}) collective-permute-start(f32[4,4,8,256]{3,0,2,1:T(4,128)S(1)} %get-tuple-element.34), channel_id=1, source_target_pairs={{0,1},{3,2},{4,5},{7,6},{8,9},{11,10},{12,13},{15,14},{16,17},{19,... | collective-permute-start | bytes 393224 | tf_op jit(solution)/shard_map/ppermute | solution.py:38
  66.4 6.3 %collective-permute-start.5 = (f32[4,4,8,256]{3,0,2,1:T(4,128)S(1)}, f32[4,4,8,256]{3,0,2,1:T(4,128)S(1)}, u32[]{:S(2)}, u32[]{:S(2)}) collective-permute-start(f32[4,4,8,256]{3,0,2,1:T(4,128)S(1)} %get-tuple-element.31), channel_id=1, source_target_pairs={{1,2},{2,1},{5,6},{6,5},{9,10},{10,9},{13,14},{14,13},{17,18},{18,... | collective-permute-start | bytes 393224 | tf_op jit(solution)/shard_map/ppermute | solution.py:41
  70.6 3.4 %collective-permute-start.8 = (f32[4,4,8,256]{3,0,2,1:T(4,128)S(1)}, f32[4,4,8,256]{3,0,2,1:T(4,128)S(1)}, u32[]{:S(2)}, u32[]{:S(2)}) collective-permute-start(f32[4,4,8,256]{3,0,2,1:T(4,128)S(1)} %get-tuple-element.35), channel_id=1, source_target_pairs={{1,2},{2,1},{5,6},{6,5},{9,10},{10,9},{13,14},{14,13},{17,18},{18,... | collective-permute-start | bytes 393224 | tf_op jit(solution)/shard_map/ppermute | solution.py:41
  71.3 4.0 %collective-permute-start.11 = (f32[4,4,8,256]{3,0,2,1:T(4,128)S(1)}, f32[4,4,8,256]{3,0,2,1:T(4,128)S(1)}, u32[]{:S(2)}, u32[]{:S(2)}) collective-permute-start(f32[4,4,8,256]{3,0,2,1:T(4,128)S(1)} %get-tuple-element.36), channel_id=1, source_target_pairs={{1,2},{2,1},{5,6},{6,5},{9,10},{10,9},{13,14},{14,13},{17,18},{18,... | collective-permute-start | bytes 393224 | tf_op jit(solution)/shard_map/ppermute | solution.py:41
  72.0 4.7 %collective-permute-start.14 = (f32[4,4,8,256]{3,0,2,1:T(4,128)S(1)}, f32[4,4,8,256]{3,0,2,1:T(4,128)S(1)}, u32[]{:S(2)}, u32[]{:S(2)}) collective-permute-start(f32[4,4,8,256]{3,0,2,1:T(4,128)S(1)} %get-tuple-element.37), channel_id=1, source_target_pairs={{1,2},{2,1},{5,6},{6,5},{9,10},{10,9},{13,14},{14,13},{17,18},{18,... | collective-permute-start | bytes 393224 | tf_op jit(solution)/shard_map/ppermute | solution.py:41
  72.7 15.4 %collective-permute-start.6 = (f32[4,4,8,256]{3,0,2,1:T(4,128)S(1)}, f32[4,4,8,256]{3,0,2,1:T(4,128)S(1)}, u32[]{:S(2)}, u32[]{:S(2)}) collective-permute-start(f32[4,4,8,256]{3,0,2,1:T(4,128)S(1)} %bitcast.95), channel_id=1, source_target_pairs={{1,0},{2,3},{5,4},{6,7},{9,8},{10,11},{13,12},{14,15},{17,16},{18,... | collective-permute-start | bytes 393224 | tf_op jit(solution)/shard_map/ppermute | solution.py:46
  74.0 15.5 %collective-permute-start.9 = (f32[4,4,8,256]{3,0,2,1:T(4,128)S(1)}, f32[4,4,8,256]{3,0,2,1:T(4,128)S(1)}, u32[]{:S(2)}, u32[]{:S(2)}) collective-permute-start(f32[4,4,8,256]{3,0,2,1:T(4,128)S(1)} %bitcast.96), channel_id=1, source_target_pairs={{1,0},{2,3},{5,4},{6,7},{9,8},{10,11},{13,12},{14,15},{17,16},{18,... | collective-permute-start | bytes 393224 | tf_op jit(solution)/shard_map/ppermute | solution.py:46
  75.4 15.6 %collective-permute-start.12 = (f32[4,4,8,256]{3,0,2,1:T(4,128)S(1)}, f32[4,4,8,256]{3,0,2,1:T(4,128)S(1)}, u32[]{:S(2)}, u32[]{:S(2)}) collective-permute-start(f32[4,4,8,256]{3,0,2,1:T(4,128)S(1)} %bitcast.97), channel_id=1, source_target_pairs={{1,0},{2,3},{5,4},{6,7},{9,8},{10,11},{13,12},{14,15},{17,16},{18,... | collective-permute-start | bytes 393224 | tf_op jit(solution)/shard_map/ppermute | solution.py:46
  76.7 15.7 %collective-permute-start.15 = (f32[4,4,8,256]{3,0,2,1:T(4,128)S(1)}, f32[4,4,8,256]{3,0,2,1:T(4,128)S(1)}, u32[]{:S(2)}, u32[]{:S(2)}) collective-permute-start(f32[4,4,8,256]{3,0,2,1:T(4,128)S(1)} %bitcast.98), channel_id=1, source_target_pairs={{1,0},{2,3},{5,4},{6,7},{9,8},{10,11},{13,12},{14,15},{17,16},{18,... | collective-permute-start | bytes 393224 | tf_op jit(solution)/shard_map/ppermute | solution.py:46
  91.0 1.4 %copy-start.2 = (f32[16,32,256]{2,1,0:T(8,128)S(1)}, f32[16,32,256]{2,1,0:T(8,128)}, u32[]{:S(2)}) copy-start(f32[16,32,256]{2,1,0:T(8,128)} %param.9) | copy-start | bytes 1572868

commit v2 on v0

--- a/solution.py
+++ b/solution.py
@@ -20,6 +20,46 @@
         after = lax.ppermute(initial, axis, down)
         shard = jnp.concatenate([before, shard, after], axis=dim)
     return shard
+
+
+def line_sum(value, axis, chunks):
+    size = lax.axis_size(axis)
+    if size == 1:
+        return value
+    if size % 2:
+        return lax.psum(value, axis)
+    me = lax.axis_index(axis)
+    half = size // 2
+    acc = jnp.stack(jnp.split(value, chunks, axis=0))
+    rightward = [(i, i + 1) for i in range(size - 1)]
+    leftward = [(i + 1, i) for i in range(size - 1)]
+    left_side = me < half
+
+    def pick(k):
+        return lax.dynamic_index_in_dim(acc, jnp.clip(k, 0, chunks - 1), 0, keepdims=False)
+
+    def put(buf, k, new):
+        valid = (k >= 0) & (k < chunks)
+        kc = jnp.clip(k, 0, chunks - 1)
+        old = lax.dynamic_index_in_dim(buf, kc, 0, keepdims=False)
+        return lax.dynamic_update_index_in_dim(buf, jnp.where(valid, new, old), kc, 0)
+
+    for s in range(chunks + size - 2):
+        k_right = s - me
+        k_left = s - (size - 1 - me)
+        from_left = lax.ppermute(pick(k_right), axis, rightward)
+        from_right = lax.ppermute(pick(k_left), axis, leftward)
+        k_in_left = k_right + 1
+        k_in_right = k_left + 1
+        old_l = pick(k_in_left)
+        new_l = jnp.where(left_side | (me == half), old_l + from_left, from_left)
+        new_l = jnp.where(me >= 1, new_l, old_l)
+        acc = put(acc, k_in_left, new_l)
+        old_r = pick(k_in_right)
+        new_r = jnp.where((~left_side) | (me == half - 1), old_r + from_right, from_right)
+        new_r = jnp.where(me <= size - 2, new_r, old_r)
+        acc = put(acc, k_in_right, new_r)
+    return jnp.concatenate(list(acc), axis=0)
 
 
 def taps_along(field, taps, axis, flipped):
@@ -107,7 +147,7 @@
     returning = jnp.take(back_blocks, dest_slot, axis=1)
     returned = lax.all_to_all(returning, "dom", split_axis=1, concat_axis=1, tiled=True)
     log_corr = jnp.log(jnp.take(returned, inverse_slot, axis=1))
-    log_total = lax.psum(log_corr, "view")
+    log_total = line_sum(log_corr, "view", 4)
     updated = blocks * jnp.exp(log_total / view_count)
     return updated.reshape(plane_count, row_count, lane_count)
 

time: 109 us -> 141 us (1.29)
  starting transfers between devices: 17 us -> 49.5 us
  between operations: 13.7 us -> 0.74 us
  waiting for transfers between devices: 52.3 us -> 64.1 us
    ppermute x0 -> x12, waiting for transfers between devices: none -> 51.6 us  [the longest x6 36.6 us: line_sum(): from_right = lax.ppermute(pick(k_left), axis, leftward)]
    psum x1 -> x0, waiting for transfers between devices: 39.7 us -> none  [body(): log_total = lax.psum(log_corr, 'view')]
    ppermute x0 -> x12, starting transfers between devices: none -> 31.7 us  [the longest x6 23.9 us: line_sum(): from_left = lax.ppermute(pick(k_right), axis, rightward)]
    all_to_all x1, waiting for transfers between devices: 3.78 us -> 0.54 us  [body(): lax.all_to_all(outgoing, 'dom', split_axis=1, concat_axis=1, tiled=True)]
    ppermute x2, waiting for transfers between devices: 0.01 us -> 3.23 us  [extended_2(): after = lax.ppermute(initial, axis, down)]
    reshape x1 -> x0, other arithmetic: 1.93 us -> none  [body(): return updated.reshape(plane_count, row_count, lane_count)]
  transfers between devices with their start and end apart: 7 -> 18, of which waited for: 3 -> 15; matrix products, arithmetic and copies ran while one was open for 9% -> 7% of each run, Pallas kernels for 0% -> 0%
where the time goes in v2:
time: 141 us; the launch traced here: 140 us
  waiting for transfers between devices  64.1 us (45%)
  starting transfers between devices  49.5 us (35%)
  local copies, waits for them, and re-layouts  16.6 us (12%)
  other arithmetic  7.62 us (5%)
  matrix products  1.54 us (1%)
    ppermute x6, waiting for transfers between devices, line_sum(): from_right = lax.ppermute(pick(k_left), axis, leftward)  36.6 us
    ppermute x6, starting transfers between devices, line_sum(): from_left = lax.ppermute(pick(k_right), axis, rightward)  23.9 us
    ppermute x6, waiting for transfers between devices, line_sum(): from_left = lax.ppermute(pick(k_right), axis, rightward)  14.9 us
    all_to_all x1, waiting for transfers between devices, body(): lax.all_to_all(returning, 'dom', split_axis=1, concat_axis=1, tiled=True)  8.79 us
    ppermute x6, starting transfers between devices, line_sum(): from_right = lax.ppermute(pick(k_left), axis, leftward)  7.75 us
    ppermute x2, starting transfers between devices, extended_2(): before = lax.ppermute(last, axis, up)  7.48 us
    all_to_all x1, starting transfers between devices, body(): lax.all_to_all(outgoing, 'dom', split_axis=1, concat_axis=1, tiled=True)  4.24 us
    all_to_all x1, starting transfers between devices, body(): lax.all_to_all(returning, 'dom', split_axis=1, concat_axis=1, tiled=True)  3.52 us
  transfers between devices with their start and end apart: 18, of which 15 were waited for; matrix products, arithmetic and copies ran while one was open for 7% of the time, Pallas kernels for 0%

profile of v2, /device:TPU:0, one launch (start us, length us, event | category | flops | bytes accessed | tf_op | source)
XLA Modules:
  0.0 140.2 jit_solution(9072743424089500350)
XLA Ops:
  0.0 0.7 copy-done
  1.0 1.6 %gather_fusion.7 = f32[4,16,8,256]{3,2,1,0:T(8,128)S(1)} fusion(f32[16,4,8,256]{3,2,1,0:T(8,128)} %bitcast.164, s32[1024]{0:T(1024)S(1)} %pad_clamp_fusion.3), kind=kCustom, calls=%fused_computation.1.clone | custom fusion | bytes 1048592 | tf_op jit(solution)/shard_map/jit(_take)/gather | solution.py:105
  2.6 0.9 select_bitcast_fusion.2
  3.5 4.2 %all-to-all-start = ((f32[16,4,8,256]{3,2,0,1:T(8,128)}), f32[16,4,8,256]{3,2,0,1:T(8,128)S(1)}, u32[]{:S(2)}, u32[]{:S(2)}) async-start(f32[16,4,8,256]{3,2,0,1:T(8,128)} %select_bitcast_fusion.2), calls=%async_computation | async-start | bytes 1048576 | tf_op jit(solution)/shard_map/all_to_all | solution.py:106
  7.8 0.6 copy-done.1
  8.4 0.7 gather_fusion
  9.4 0.6 copy-done.3
  11.9 2.9 %gather_fusion.3 = f32[384]{0:T(512)S(1)} fusion(f32[16,9]{1,0:T(8,128)S(1)} %get-tuple-element.70, s32[384]{0:T(512)S(1)} %reshape.271), kind=kCustom, calls=%fused_computation.10 | custom fusion | bytes 6144 | tf_op jit(solution)/shard_map/gather | solution.py:129
  17.5 1.2 fusion.51
  19.1 2.0 %collective-permute-start = (f32[4,32,256]{2,0,1:T(4,128)S(1)}, f32[4,32,256]{2,0,1:T(4,128)S(1)}, u32[]{:S(2)}, u32[]{:S(2)}) collective-permute-start(f32[4,32,256]{2,0,1:T(4,128)S(1)} %get-tuple-element.65), channel_id=1, source_target_pairs={{0,4},{4,8},{8,12},{1,5},{5,9},{9,13},{2,6},{6,10},{10,14},{3,7},{... | collective-permute-start | bytes 393224 | tf_op jit(solution)/shard_map/ppermute | solution.py:19
  21.1 1.3 collective-permute-start.1
  22.4 3.2 %collective-permute-done.1 = f32[4,32,256]{2,0,1:T(4,128)S(1)} collective-permute-done((f32[4,32,256]{2,0,1:T(4,128)S(1)}, f32[4,32,256]{2,0,1:T(4,128)S(1)}, u32[]{:S(2)}, u32[]{:S(2)}) %collective-permute-start.1) | collective-permute-done | bytes 131104 | tf_op jit(solution)/shard_map/ppermute | solution.py:20
  25.7 0.9 convolution_divide_fusion
  26.6 5.5 %collective-permute-start.2 = (f32[4,32,256]{2,0,1:T(4,128)S(1)}, f32[4,32,256]{2,0,1:T(4,128)S(1)}, u32[]{:S(2)}, u32[]{:S(2)}) collective-permute-start(f32[4,32,256]{2,0,1:T(4,128)S(1)} %get-tuple-element.63), channel_id=1, source_target_pairs={{0,4},{4,8},{8,12},{1,5},{5,9},{9,13},{2,6},{6,10},{10,14},{3,7},{... | collective-permute-start | bytes 393224 | tf_op jit(solution)/shard_map/ppermute | solution.py:19
  32.1 1.3 collective-permute-start.3
  33.5 2.9 %gather_fusion.2 = f32[384]{0:T(512)S(1)} fusion(f32[24,9]{1,0:T(8,128)S(1)} %broadcast_select_fusion, s32[384]{0:T(512)S(1)} %reshape.265), kind=kCustom, calls=%fused_computation.9 | custom fusion | bytes 6144 | tf_op jit(solution)/shard_map/gather | solution.py:137
  36.6 0.6 fusion.5
  37.6 1.2 fusion.67
  38.8 0.6 gather_fusion.9
  39.4 0.9 select_bitcast_fusion
  40.3 3.5 %all-to-all-start.1 = ((f32[16,4,8,256]{3,0,2,1:T(8,128)}), f32[16,4,8,256]{3,0,2,1:T(8,128)S(1)}, u32[]{:S(2)}, u32[]{:S(2)}) async-start(f32[16,4,8,256]{3,0,2,1:T(8,128)} %select_bitcast_fusion), calls=%async_computation.1 | async-start | bytes 1048576 | tf_op jit(solution)/shard_map/all_to_all | solution.py:148
  43.8 8.8 %all-to-all-done.1 = f32[16,4,8,256]{3,0,2,1:T(8,128)S(1)} async-done(((f32[16,4,8,256]{3,0,2,1:T(8,128)}), f32[16,4,8,256]{3,0,2,1:T(8,128)S(1)}, u32[]{:S(2)}, u32[]{:S(2)}) %all-to-all-start.1) | async-done | bytes 524320 | tf_op jit(solution)/shard_map/all_to_all | solution.py:148
  53.6 4.0 %collective-permute-start.4 = (f32[4,4,8,256]{3,0,2,1:T(4,128)S(1)}, f32[4,4,8,256]{3,0,2,1:T(4,128)S(1)}, u32[]{:S(2)}, u32[]{:S(2)}) collective-permute-start(f32[4,4,8,256]{3,0,2,1:T(4,128)S(1)} %get-tuple-element.58), channel_id=1, source_target_pairs={{0,1},{1,2},{2,3},{4,5},{5,6},{6,7},{8,9},{9,10},{10,11},{12,13},{... | collective-permute-start | bytes 393224 | tf_op jit(solution)/shard_map/ppermute | solution.py:50
  57.7 2.5 %collective-permute-done.4 = f32[4,4,8,256]{3,0,2,1:T(4,128)S(1)} collective-permute-done((f32[4,4,8,256]{3,0,2,1:T(4,128)S(1)}, f32[4,4,8,256]{3,0,2,1:T(4,128)S(1)}, u32[]{:S(2)}, u32[]{:S(2)}) %collective-permute-start.4) | collective-permute-done | bytes 131104 | tf_op jit(solution)/shard_map/ppermute | solution.py:50
  60.2 1.3 collective-permute-start.5
  61.6 5.9 %collective-permute-done.5 = f32[4,4,8,256]{3,0,2,1:T(4,128)S(1)} collective-permute-done((f32[4,4,8,256]{3,0,2,1:T(4,128)S(1)}, f32[4,4,8,256]{3,0,2,1:T(4,128)S(1)}, u32[]{:S(2)}, u32[]{:S(2)}) %collective-permute-start.5) | collective-permute-done | bytes 131104 | tf_op jit(solution)/shard_map/ppermute | solution.py:51
  67.6 3.9 %collective-permute-start.6 = (f32[4,4,8,256]{3,0,2,1:T(4,128)S(1)}, f32[4,4,8,256]{3,0,2,1:T(4,128)S(1)}, u32[]{:S(2)}, u32[]{:S(2)}) collective-permute-start(f32[4,4,8,256]{3,0,2,1:T(4,128)S(1)} %get-tuple-element.54), channel_id=1, source_target_pairs={{0,1},{1,2},{2,3},{4,5},{5,6},{6,7},{8,9},{9,10},{10,11},{12,13},{... | collective-permute-start | bytes 393224 | tf_op jit(solution)/shard_map/ppermute | solution.py:50
  71.5 2.5 %collective-permute-done.6 = f32[4,4,8,256]{3,0,2,1:T(4,128)S(1)} collective-permute-done((f32[4,4,8,256]{3,0,2,1:T(4,128)S(1)}, f32[4,4,8,256]{3,0,2,1:T(4,128)S(1)}, u32[]{:S(2)}, u32[]{:S(2)}) %collective-permute-start.6) | collective-permute-done | bytes 131104 | tf_op jit(solution)/shard_map/ppermute | solution.py:50
  74.1 1.3 collective-permute-start.7
  75.4 6.0 %collective-permute-done.7 = f32[4,4,8,256]{3,0,2,1:T(4,128)S(1)} collective-permute-done((f32[4,4,8,256]{3,0,2,1:T(4,128)S(1)}, f32[4,4,8,256]{3,0,2,1:T(4,128)S(1)}, u32[]{:S(2)}, u32[]{:S(2)}) %collective-permute-start.7) | collective-permute-done | bytes 131104 | tf_op jit(solution)/shard_map/ppermute | solution.py:51
  81.5 3.9 %collective-permute-start.8 = (f32[4,4,8,256]{3,0,2,1:T(4,128)S(1)}, f32[4,4,8,256]{3,0,2,1:T(4,128)S(1)}, u32[]{:S(2)}, u32[]{:S(2)}) collective-permute-start(f32[4,4,8,256]{3,0,2,1:T(4,128)S(1)} %get-tuple-element.50), channel_id=1, source_target_pairs={{0,1},{1,2},{2,3},{4,5},{5,6},{6,7},{8,9},{9,10},{10,11},{12,13},{... | collective-permute-start | bytes 393224 | tf_op jit(solution)/shard_map/ppermute | solution.py:50
  85.4 2.5 %collective-permute-done.8 = f32[4,4,8,256]{3,0,2,1:T(4,128)S(1)} collective-permute-done((f32[4,4,8,256]{3,0,2,1:T(4,128)S(1)}, f32[4,4,8,256]{3,0,2,1:T(4,128)S(1)}, u32[]{:S(2)}, u32[]{:S(2)}) %collective-permute-start.8) | collective-permute-done | bytes 131104 | tf_op jit(solution)/shard_map/ppermute | solution.py:50
  88.0 1.3 collective-permute-start.9
  89.3 6.0 %collective-permute-done.9 = f32[4,4,8,256]{3,0,2,1:T(4,128)S(1)} collective-permute-done((f32[4,4,8,256]{3,0,2,1:T(4,128)S(1)}, f32[4,4,8,256]{3,0,2,1:T(4,128)S(1)}, u32[]{:S(2)}, u32[]{:S(2)}) %collective-permute-start.9) | collective-permute-done | bytes 131104 | tf_op jit(solution)/shard_map/ppermute | solution.py:51
  95.4 3.9 %collective-permute-start.10 = (f32[4,4,8,256]{3,0,2,1:T(4,128)S(1)}, f32[4,4,8,256]{3,0,2,1:T(4,128)S(1)}, u32[]{:S(2)}, u32[]{:S(2)}) collective-permute-start(f32[4,4,8,256]{3,0,2,1:T(4,128)S(1)} %get-tuple-element.46), channel_id=1, source_target_pairs={{0,1},{1,2},{2,3},{4,5},{5,6},{6,7},{8,9},{9,10},{10,11},{12,13},{... | collective-permute-start | bytes 393224 | tf_op jit(solution)/shard_map/ppermute | solution.py:50
  99.3 2.5 %collective-permute-done.10 = f32[4,4,8,256]{3,0,2,1:T(4,128)S(1)} collective-permute-done((f32[4,4,8,256]{3,0,2,1:T(4,128)S(1)}, f32[4,4,8,256]{3,0,2,1:T(4,128)S(1)}, u32[]{:S(2)}, u32[]{:S(2)}) %collective-permute-start.10) | collective-permute-done | bytes 131104 | tf_op jit(solution)/shard_map/ppermute | solution.py:50
  101.9 1.3 collective-permute-start.11
  103.2 6.0 %collective-permute-done.11 = f32[4,4,8,256]{3,0,2,1:T(4,128)S(1)} collective-permute-done((f32[4,4,8,256]{3,0,2,1:T(4,128)S(1)}, f32[4,4,8,256]{3,0,2,1:T(4,128)S(1)}, u32[]{:S(2)}, u32[]{:S(2)}) %collective-permute-start.11) | collective-permute-done | bytes 131104 | tf_op jit(solution)/shard_map/ppermute | solution.py:51
  109.3 3.9 %collective-permute-start.12 = (f32[4,4,8,256]{3,0,2,1:T(4,128)S(1)}, f32[4,4,8,256]{3,0,2,1:T(4,128)S(1)}, u32[]{:S(2)}, u32[]{:S(2)}) collective-permute-start(f32[4,4,8,256]{3,0,2,1:T(4,128)S(1)} %get-tuple-element.42), channel_id=1, source_target_pairs={{0,1},{1,2},{2,3},{4,5},{5,6},{6,7},{8,9},{9,10},{10,11},{12,13},{... | collective-permute-start | bytes 393224 | tf_op jit(solution)/shard_map/ppermute | solution.py:50
  113.2 2.5 %collective-permute-done.12 = f32[4,4,8,256]{3,0,2,1:T(4,128)S(1)} collective-permute-done((f32[4,4,8,256]{3,0,2,1:T(4,128)S(1)}, f32[4,4,8,256]{3,0,2,1:T(4,128)S(1)}, u32[]{:S(2)}, u32[]{:S(2)}) %collective-permute-start.12) | collective-permute-done | bytes 131104 | tf_op jit(solution)/shard_map/ppermute | solution.py:50
  115.8 1.3 collective-permute-start.13
  117.1 6.9 %collective-permute-done.13 = f32[4,4,8,256]{3,0,2,1:T(4,128)S(1)} collective-permute-done((f32[4,4,8,256]{3,0,2,1:T(4,128)S(1)}, f32[4,4,8,256]{3,0,2,1:T(4,128)S(1)}, u32[]{:S(2)}, u32[]{:S(2)}) %collective-permute-start.13) | collective-permute-done | bytes 131104 | tf_op jit(solution)/shard_map/ppermute | solution.py:51
  124.1 4.2 %collective-permute-start.14 = (f32[4,4,8,256]{3,0,2,1:T(4,128)S(1)}, f32[4,4,8,256]{3,0,2,1:T(4,128)S(1)}, u32[]{:S(2)}, u32[]{:S(2)}) collective-permute-start(f32[4,4,8,256]{3,0,2,1:T(4,128)S(1)} %get-tuple-element.38), channel_id=1, source_target_pairs={{0,1},{1,2},{2,3},{4,5},{5,6},{6,7},{8,9},{9,10},{10,11},{12,13},{... | collective-permute-start | bytes 393224 | tf_op jit(solution)/shard_map/ppermute | solution.py:50
  128.3 2.5 %collective-permute-done.14 = f32[4,4,8,256]{3,0,2,1:T(4,128)S(1)} collective-permute-done((f32[4,4,8,256]{3,0,2,1:T(4,128)S(1)}, f32[4,4,8,256]{3,0,2,1:T(4,128)S(1)}, u32[]{:S(2)}, u32[]{:S(2)}) %collective-permute-start.14) | collective-permute-done | bytes 131104 | tf_op jit(solution)/shard_map/ppermute | solution.py:50
  130.8 1.3 collective-permute-start.15
  132.2 6.0 %collective-permute-done.15 = f32[4,4,8,256]{3,0,2,1:T(4,128)S(1)} collective-permute-done((f32[4,4,8,256]{3,0,2,1:T(4,128)S(1)}, f32[4,4,8,256]{3,0,2,1:T(4,128)S(1)}, u32[]{:S(2)}, u32[]{:S(2)}) %collective-permute-start.15) | collective-permute-done | bytes 131104 | tf_op jit(solution)/shard_map/ppermute | solution.py:51
  138.4 0.9 copy-done.2
  139.3 0.9 fusion.76
  (88 shorter events, 8.3 us)
Async XLA Ops:
  0.0 0.7 copy-start
  3.5 13.1 %all-to-all-start = ((f32[16,4,8,256]{3,2,0,1:T(8,128)}), f32[16,4,8,256]{3,2,0,1:T(8,128)S(1)}, u32[]{:S(2)}, u32[]{:S(2)}) async-start(f32[16,4,8,256]{3,2,0,1:T(8,128)} %select_bitcast_fusion.2), calls=%async_computation | async-start | bytes 1048576 | tf_op jit(solution)/shard_map/all_to_all | solution.py:106
  7.8 0.7 copy-start.1
  9.3 0.7 copy-start.3
  19.0 6.7 %copy-start.4 = (f32[1,16,32,256]{3,2,1,0:T(8,128)S(1)}, f32[1,16,32,256]{3,2,1,0:T(8,128)}, u32[]{:S(2)}) copy-start(f32[1,16,32,256]{3,2,1,0:T(8,128)} %param.10) | copy-start | bytes 1572868
  19.1 3.4 %collective-permute-start = (f32[4,32,256]{2,0,1:T(4,128)S(1)}, f32[4,32,256]{2,0,1:T(4,128)S(1)}, u32[]{:S(2)}, u32[]{:S(2)}) collective-permute-start(f32[4,32,256]{2,0,1:T(4,128)S(1)} %get-tuple-element.65), channel_id=1, source_target_pairs={{0,4},{4,8},{8,12},{1,5},{5,9},{9,13},{2,6},{6,10},{10,14},{3,7},{... | collective-permute-start | bytes 393224 | tf_op jit(solution)/shard_map/ppermute | solution.py:19
  21.1 4.6 %collective-permute-start.1 = (f32[4,32,256]{2,0,1:T(4,128)S(1)}, f32[4,32,256]{2,0,1:T(4,128)S(1)}, u32[]{:S(2)}, u32[]{:S(2)}) collective-permute-start(f32[4,32,256]{2,0,1:T(4,128)S(1)} %get-tuple-element.66), channel_id=1, source_target_pairs={{4,0},{8,4},{12,8},{5,1},{9,5},{13,9},{6,2},{10,6},{14,10},{7,3},{... | collective-permute-start | bytes 393224 | tf_op jit(solution)/shard_map/ppermute | solution.py:20
  26.6 10.0 %collective-permute-start.2 = (f32[4,32,256]{2,0,1:T(4,128)S(1)}, f32[4,32,256]{2,0,1:T(4,128)S(1)}, u32[]{:S(2)}, u32[]{:S(2)}) collective-permute-start(f32[4,32,256]{2,0,1:T(4,128)S(1)} %get-tuple-element.63), channel_id=1, source_target_pairs={{0,4},{4,8},{8,12},{1,5},{5,9},{9,13},{2,6},{6,10},{10,14},{3,7},{... | collective-permute-start | bytes 393224 | tf_op jit(solution)/shard_map/ppermute | solution.py:19
  32.1 4.5 %collective-permute-start.3 = (f32[4,32,256]{2,0,1:T(4,128)S(1)}, f32[4,32,256]{2,0,1:T(4,128)S(1)}, u32[]{:S(2)}, u32[]{:S(2)}) collective-permute-start(f32[4,32,256]{2,0,1:T(4,128)S(1)} %get-tuple-element.64), channel_id=1, source_target_pairs={{4,0},{8,4},{12,8},{5,1},{9,5},{13,9},{6,2},{10,6},{14,10},{7,3},{... | collective-permute-start | bytes 393224 | tf_op jit(solution)/shard_map/ppermute | solution.py:20
  40.3 12.3 %all-to-all-start.1 = ((f32[16,4,8,256]{3,0,2,1:T(8,128)}), f32[16,4,8,256]{3,0,2,1:T(8,128)S(1)}, u32[]{:S(2)}, u32[]{:S(2)}) async-start(f32[16,4,8,256]{3,0,2,1:T(8,128)} %select_bitcast_fusion), calls=%async_computation.1 | async-start | bytes 1048576 | tf_op jit(solution)/shard_map/all_to_all | solution.py:148
  53.6 6.5 %collective-permute-start.4 = (f32[4,4,8,256]{3,0,2,1:T(4,128)S(1)}, f32[4,4,8,256]{3,0,2,1:T(4,128)S(1)}, u32[]{:S(2)}, u32[]{:S(2)}) collective-permute-start(f32[4,4,8,256]{3,0,2,1:T(4,128)S(1)} %get-tuple-element.58), channel_id=1, source_target_pairs={{0,1},{1,2},{2,3},{4,5},{5,6},{6,7},{8,9},{9,10},{10,11},{12,13},{... | collective-permute-start | bytes 393224 | tf_op jit(solution)/shard_map/ppermute | solution.py:50
  60.2 7.3 %collective-permute-start.5 = (f32[4,4,8,256]{3,0,2,1:T(4,128)S(1)}, f32[4,4,8,256]{3,0,2,1:T(4,128)S(1)}, u32[]{:S(2)}, u32[]{:S(2)}) collective-permute-start(f32[4,4,8,256]{3,0,2,1:T(4,128)S(1)} %get-tuple-element.55), channel_id=1, source_target_pairs={{1,0},{2,1},{3,2},{5,4},{6,5},{7,6},{9,8},{10,9},{11,10},{13,12},{... | collective-permute-start | bytes 393224 | tf_op jit(solution)/shard_map/ppermute | solution.py:51
  67.6 6.4 %collective-permute-start.6 = (f32[4,4,8,256]{3,0,2,1:T(4,128)S(1)}, f32[4,4,8,256]{3,0,2,1:T(4,128)S(1)}, u32[]{:S(2)}, u32[]{:S(2)}) collective-permute-start(f32[4,4,8,256]{3,0,2,1:T(4,128)S(1)} %get-tuple-element.54), channel_id=1, source_target_pairs={{0,1},{1,2},{2,3},{4,5},{5,6},{6,7},{8,9},{9,10},{10,11},{12,13},{... | collective-permute-start | bytes 393224 | tf_op jit(solution)/shard_map/ppermute | solution.py:50
  74.1 7.3 %collective-permute-start.7 = (f32[4,4,8,256]{3,0,2,1:T(4,128)S(1)}, f32[4,4,8,256]{3,0,2,1:T(4,128)S(1)}, u32[]{:S(2)}, u32[]{:S(2)}) collective-permute-start(f32[4,4,8,256]{3,0,2,1:T(4,128)S(1)} %get-tuple-element.51), channel_id=1, source_target_pairs={{1,0},{2,1},{3,2},{5,4},{6,5},{7,6},{9,8},{10,9},{11,10},{13,12},{... | collective-permute-start | bytes 393224 | tf_op jit(solution)/shard_map/ppermute | solution.py:51
  81.5 6.4 %collective-permute-start.8 = (f32[4,4,8,256]{3,0,2,1:T(4,128)S(1)}, f32[4,4,8,256]{3,0,2,1:T(4,128)S(1)}, u32[]{:S(2)}, u32[]{:S(2)}) collective-permute-start(f32[4,4,8,256]{3,0,2,1:T(4,128)S(1)} %get-tuple-element.50), channel_id=1, source_target_pairs={{0,1},{1,2},{2,3},{4,5},{5,6},{6,7},{8,9},{9,10},{10,11},{12,13},{... | collective-permute-start | bytes 393224 | tf_op jit(solution)/shard_map/ppermute | solution.py:50
  88.0 7.3 %collective-permute-start.9 = (f32[4,4,8,256]{3,0,2,1:T(4,128)S(1)}, f32[4,4,8,256]{3,0,2,1:T(4,128)S(1)}, u32[]{:S(2)}, u32[]{:S(2)}) collective-permute-start(f32[4,4,8,256]{3,0,2,1:T(4,128)S(1)} %get-tuple-element.47), channel_id=1, source_target_pairs={{1,0},{2,1},{3,2},{5,4},{6,5},{7,6},{9,8},{10,9},{11,10},{13,12},{... | collective-permute-start | bytes 393224 | tf_op jit(solution)/shard_map/ppermute | solution.py:51
  95.4 6.4 %collective-permute-start.10 = (f32[4,4,8,256]{3,0,2,1:T(4,128)S(1)}, f32[4,4,8,256]{3,0,2,1:T(4,128)S(1)}, u32[]{:S(2)}, u32[]{:S(2)}) collective-permute-start(f32[4,4,8,256]{3,0,2,1:T(4,128)S(1)} %get-tuple-element.46), channel_id=1, source_target_pairs={{0,1},{1,2},{2,3},{4,5},{5,6},{6,7},{8,9},{9,10},{10,11},{12,13},{... | collective-permute-start | bytes 393224 | tf_op jit(solution)/shard_map/ppermute | solution.py:50
  101.9 7.3 %collective-permute-start.11 = (f32[4,4,8,256]{3,0,2,1:T(4,128)S(1)}, f32[4,4,8,256]{3,0,2,1:T(4,128)S(1)}, u32[]{:S(2)}, u32[]{:S(2)}) collective-permute-start(f32[4,4,8,256]{3,0,2,1:T(4,128)S(1)} %get-tuple-element.43), channel_id=1, source_target_pairs={{1,0},{2,1},{3,2},{5,4},{6,5},{7,6},{9,8},{10,9},{11,10},{13,12},{... | collective-permute-start | bytes 393224 | tf_op jit(solution)/shard_map/ppermute | solution.py:51
  109.3 6.4 %collective-permute-start.12 = (f32[4,4,8,256]{3,0,2,1:T(4,128)S(1)}, f32[4,4,8,256]{3,0,2,1:T(4,128)S(1)}, u32[]{:S(2)}, u32[]{:S(2)}) collective-permute-start(f32[4,4,8,256]{3,0,2,1:T(4,128)S(1)} %get-tuple-element.42), channel_id=1, source_target_pairs={{0,1},{1,2},{2,3},{4,5},{5,6},{6,7},{8,9},{9,10},{10,11},{12,13},{... | collective-permute-start | bytes 393224 | tf_op jit(solution)/shard_map/ppermute | solution.py:50
  115.8 8.2 %collective-permute-start.13 = (f32[4,4,8,256]{3,0,2,1:T(4,128)S(1)}, f32[4,4,8,256]{3,0,2,1:T(4,128)S(1)}, u32[]{:S(2)}, u32[]{:S(2)}) collective-permute-start(f32[4,4,8,256]{3,0,2,1:T(4,128)S(1)} %get-tuple-element.39), channel_id=1, source_target_pairs={{1,0},{2,1},{3,2},{5,4},{6,5},{7,6},{9,8},{10,9},{11,10},{13,12},{... | collective-permute-start | bytes 393224 | tf_op jit(solution)/shard_map/ppermute | solution.py:51
  124.1 6.7 %collective-permute-start.14 = (f32[4,4,8,256]{3,0,2,1:T(4,128)S(1)}, f32[4,4,8,256]{3,0,2,1:T(4,128)S(1)}, u32[]{:S(2)}, u32[]{:S(2)}) collective-permute-start(f32[4,4,8,256]{3,0,2,1:T(4,128)S(1)} %get-tuple-element.38), channel_id=1, source_target_pairs={{0,1},{1,2},{2,3},{4,5},{5,6},{6,7},{8,9},{9,10},{10,11},{12,13},{... | collective-permute-start | bytes 393224 | tf_op jit(solution)/shard_map/ppermute | solution.py:50
  130.8 7.3 %collective-permute-start.15 = (f32[4,4,8,256]{3,0,2,1:T(4,128)S(1)}, f32[4,4,8,256]{3,0,2,1:T(4,128)S(1)}, u32[]{:S(2)}, u32[]{:S(2)}) collective-permute-start(f32[4,4,8,256]{3,0,2,1:T(4,128)S(1)} %get-tuple-element.35), channel_id=1, source_target_pairs={{1,0},{2,1},{3,2},{5,4},{6,5},{7,6},{9,8},{10,9},{11,10},{13,12},{... | collective-permute-start | bytes 393224 | tf_op jit(solution)/shard_map/ppermute | solution.py:51
  138.2 1.0 copy-start.2

commit v3 on v0

--- a/solution.py
+++ b/solution.py
@@ -100,16 +100,30 @@
     dest_slot = jnp.sum(
         jnp.where(my_sources[None, :] == slot_ids[:, None], slot_ids[None, :], 0), axis=1
     )
-    inverse_slot = jnp.sum(
-        jnp.where(send_slot[None, :] == slot_ids[:, None], slot_ids[None, :], 0), axis=1
+    piece_rows = block_rows // view_count
+    logs = jnp.log(back).reshape(plane_count, block_count, view_count, piece_rows, lane_count)
+    outgoing = jnp.take(logs, dest_slot, axis=1).transpose(1, 2, 0, 3, 4)
+    outgoing = outgoing.reshape(block_count * view_count, plane_count, piece_rows, lane_count)
+    arrived_logs = lax.all_to_all(outgoing, ("dom", "view"), 0, 0, tiled=True)
+    all_grid = src_map.reshape(view_count, block_count, block_count)
+    all_dev = all_grid // block_count
+    all_slot = all_grid % block_count
+    slot_of = jnp.sum(jnp.where(all_dev == dom_index, all_slot, 0), axis=2)
+    cam_of = jnp.sum(
+        jnp.where(slot_of[:, :, None] == slot_ids[None, None, :], slot_ids[None, :, None], 0), axis=1
     )
-    back_blocks = back.reshape(plane_count, block_count, block_rows, lane_count)
-    returning = jnp.take(back_blocks, dest_slot, axis=1)
-    returned = lax.all_to_all(returning, "dom", split_axis=1, concat_axis=1, tiled=True)
-    log_corr = jnp.log(jnp.take(returned, inverse_slot, axis=1))
-    log_total = lax.psum(log_corr, "view")
-    updated = blocks * jnp.exp(log_total / view_count)
-    return updated.reshape(plane_count, row_count, lane_count)
+    view_ids = jnp.arange(view_count, dtype=jnp.int32)
+    flat_index = (cam_of * view_count + view_ids[:, None]).reshape(-1)
+    by_view = jnp.take(arrived_logs, flat_index, axis=0)
+    by_view = by_view.reshape(view_count, block_count, plane_count, piece_rows, lane_count)
+    log_total = by_view[0]
+    for v in range(1, view_count):
+        log_total = log_total + by_view[v]
+    est_rows = estimate.reshape(plane_count, block_count, view_count, piece_rows, lane_count)
+    est_piece = lax.dynamic_index_in_dim(est_rows, view_index, 2, keepdims=False)
+    updated = est_piece * jnp.exp(log_total.transpose(1, 0, 2, 3) / view_count)
+    joined = lax.all_gather(updated, "view", axis=2, tiled=False)
+    return joined.reshape(plane_count, row_count, lane_count)
 
 
 def solution(mesh):

time: 109 us -> 80.9 us (0.74)
  waiting for transfers between devices: 52.3 us -> 18.7 us
  blocking collectives: 0 us -> 15.8 us
  between operations: 13.7 us -> 0.4 us
  starting transfers between devices: 17 us -> 21 us
  other arithmetic: 8.56 us -> 6.08 us
  local copies, waits for them, and re-layouts: 15.6 us -> 16.9 us
    psum x1 -> x0, waiting for transfers between devices: 39.7 us -> none  [body(): log_total = lax.psum(log_corr, 'view')]
    all_gather x0 -> x1, blocking collectives: none -> 15.8 us  [body(): joined = lax.all_gather(updated, 'view', axis=2, tiled=False)]
    all_to_all x1, waiting for transfers between devices: 8.78 us -> 14.9 us  [body(): arrived_logs = lax.all_to_all(outgoing, ('dom', 'view'), 0, 0, tiled=True)]
    all_to_all x1, starting transfers between devices: 4.03 us -> 8 us  [body(): arrived_logs = lax.all_to_all(outgoing, ('dom', 'view'), 0, 0, tiled=True)]
    reshape x1 -> x0, other arithmetic: 1.93 us -> none  [body(): return updated.reshape(plane_count, row_count, lane_count)]
    reshape x1 -> x3, local copies, waits for them, and re-layouts: 0.31 us -> 1.49 us  [the longest x1 1.1 us: body(): return joined.reshape(plane_count, row_count, lane_count)]
    add x4 -> x3, other arithmetic: 3.03 us -> 1.87 us  [taps_along(): total = total + taps[:, offset][:, None, None] * piece]
  transfers between devices with their start and end apart: 7 -> 6, of which waited for: 3 -> 2; matrix products, arithmetic and copies ran while one was open for 9% -> 13% of each run, Pallas kernels for 0% -> 0%
where the time goes in v3:
time: 80.9 us; the launch traced here: 80.4 us
  starting transfers between devices  21 us (26%)
  waiting for transfers between devices  18.7 us (23%)
  local copies, waits for them, and re-layouts  16.9 us (21%)
  blocking collectives  15.8 us (20%)
  other arithmetic  6.08 us (8%)
  matrix products  1.55 us (2%)
    all_gather x1, blocking collectives, body(): joined = lax.all_gather(updated, 'view', axis=2, tiled=False)  15.8 us
    all_to_all x1, waiting for transfers between devices, body(): arrived_logs = lax.all_to_all(outgoing, ('dom', 'view'), 0, 0, tiled=True)  14.9 us
    all_to_all x1, starting transfers between devices, body(): arrived_logs = lax.all_to_all(outgoing, ('dom', 'view'), 0, 0, tiled=True)  8 us
    ppermute x2, starting transfers between devices, extended_2(): before = lax.ppermute(last, axis, up)  6.17 us
    all_to_all x1, starting transfers between devices, body(): lax.all_to_all(outgoing, 'dom', split_axis=1, concat_axis=1, tiled=True)  4.24 us
    all_to_all x1, waiting for transfers between devices, body(): lax.all_to_all(outgoing, 'dom', split_axis=1, concat_axis=1, tiled=True)  3.77 us
    gather x2, local copies, waits for them, and re-layouts, body(): taps_own[row_sel, jnp.clip(fwd_tap, 0, 2 * reach)]  2.96 us
    gather x2, local copies, waits for them, and re-layouts, body(): taps_ext[col_sel, jnp.clip(back_tap, 0, 2 * reach)]  2.96 us
  transfers between devices with their start and end apart: 6, of which 2 were waited for; matrix products, arithmetic and copies ran while one was open for 13% of the time, Pallas kernels for 0%

profile of v3, /device:TPU:0, one launch (start us, length us, event | category | flops | bytes accessed | tf_op | source)
XLA Modules:
  0.0 80.4 jit_solution(12745816058225194941)
XLA Ops:
  0.0 0.7 copy-done.3
  0.7 0.1 reshape.267
  0.8 0.1 fusion.110
  0.9 0.1 select_reduce_fusion.1
  1.1 1.6 %gather_fusion.9 = f32[4,16,8,256]{3,2,1,0:T(8,128)S(1)} fusion(f32[16,4,8,256]{3,2,1,0:T(8,128)} %bitcast.63, s32[1024]{0:T(1024)S(1)} %pad_clamp_fusion.3), kind=kCustom, calls=%fused_computation.1.clone | custom fusion | bytes 1048592 | tf_op jit(solution)/shard_map/jit(_take)/gather | solution.py:65
  2.7 0.9 %select_bitcast_fusion.1 = f32[16,4,8,256]{3,2,0,1:T(8,128)} fusion(f32[4,16,8,256]{3,2,1,0:T(8,128)S(1)} %gather_fusion.9, pred[4]{0:T(512)(128)(4,1)S(1)} %get-tuple-element.41), kind=kLoop, calls=%fused_computation.121 | loop fusion | flops 131072 | bytes 1048580 | tf_op jit(solution)/shard_map/jit(_take)/select_n | solution.py:65
  3.6 4.2 %all-to-all-start = ((f32[16,4,8,256]{3,2,0,1:T(8,128)}), f32[16,4,8,256]{3,2,0,1:T(8,128)S(1)}, u32[]{:S(2)}, u32[]{:S(2)}) async-start(f32[16,4,8,256]{3,2,0,1:T(8,128)} %select_bitcast_fusion.1), calls=%async_computation | async-start | bytes 1048576 | tf_op jit(solution)/shard_map/all_to_all | solution.py:66
  7.9 0.6 copy-done
  8.5 0.7 gather_fusion
  9.3 0.1 compare_and_fusion.2
  9.4 0.6 copy-done.2
  10.0 0.6 gather_fusion.8
  10.6 0.6 gather_fusion.6
  11.1 0.6 gather_fusion.7
  11.8 0.6 gather_fusion.1
  12.3 0.5 slice_reduce_fusion.16
  12.9 3.8 %all-to-all-done = f32[16,4,8,256]{3,2,0,1:T(8,128)S(1)} async-done(((f32[16,4,8,256]{3,2,0,1:T(8,128)}), f32[16,4,8,256]{3,2,0,1:T(8,128)S(1)}, u32[]{:S(2)}, u32[]{:S(2)}) %all-to-all-start) | async-done | bytes 524320 | tf_op jit(solution)/shard_map/all_to_all | solution.py:66
  16.7 0.6 gather_fusion.10
  17.3 0.1 select_bitcast_fusion
  17.4 0.2 copy.14
  17.6 1.2 %fusion.51 = f32[16,32,256]{2,0,1:T(8,128)S(1)} fusion(f32[16,32,256]{2,0,1:T(8,128)S(1)} %bitcast.64, f32[16]{0:T(128)S(1)} %get-tuple-element.50, f32[16]{0:T(128)S(1)} %get-tuple-element.49, f32[16]{0:T(128)S(1)} %get-tuple-element.48, f32[16]{0:T(128)S(1)} %get-tuple-element.47, f32[16]{0:T(128)S(1)} %get-tuple-element.46, f32[16]{0:T(128)S(1)} %get-tuple-element.45, ...), kind=kLoop, calls=%fused_computation.95 | loop fusion | flops 2228224 | bytes 1049152 | tf_op jit(solution)/shard_map/add | solution.py:36
  18.8 0.4 fusion.19
  19.2 1.3 %collective-permute-start = (f32[4,32,256]{2,0,1:T(4,128)S(1)}, f32[4,32,256]{2,0,1:T(4,128)S(1)}, u32[]{:S(2)}, u32[]{:S(2)}) collective-permute-start(f32[4,32,256]{2,0,1:T(4,128)S(1)} %get-tuple-element.33), channel_id=1, source_target_pairs={{0,4},{4,8},{8,12},{1,5},{5,9},{9,13},{2,6},{6,10},{10,14},{3,7},{... | collective-permute-start | bytes 393224 | tf_op jit(solution)/shard_map/ppermute | solution.py:19
  20.5 1.3 %collective-permute-start.1 = (f32[4,32,256]{2,0,1:T(4,128)S(1)}, f32[4,32,256]{2,0,1:T(4,128)S(1)}, u32[]{:S(2)}, u32[]{:S(2)}) collective-permute-start(f32[4,32,256]{2,0,1:T(4,128)S(1)} %get-tuple-element.34), channel_id=1, source_target_pairs={{4,0},{8,4},{12,8},{5,1},{9,5},{13,9},{6,2},{10,6},{14,10},{7,3},{... | collective-permute-start | bytes 393224 | tf_op jit(solution)/shard_map/ppermute | solution.py:20
  21.8 0.1 reshape.335
  21.9 2.9 %gather_fusion.3 = f32[384]{0:T(512)S(1)} fusion(f32[16,9]{1,0:T(8,128)S(1)} %get-tuple-element.38, s32[384]{0:T(512)S(1)} %reshape.335), kind=kCustom, calls=%fused_computation.8 | custom fusion | bytes 6144 | tf_op jit(solution)/shard_map/gather | solution.py:89
  24.9 0.9 %convolution_divide_fusion = f32[16,32,256]{2,0,1:T(8,128)S(1)} fusion(f32[4,32,256]{2,0,1:T(4,128)S(1)} %collective-permute-done.1, f32[16,32,256]{2,0,1:T(8,128)S(1)} %fusion.19, f32[4,32,256]{2,0,1:T(4,128)S(1)} %collective-permute-done, f32[1,16,32,256]{3,2,1,0:T(8,128)S(1)} %copy-done.4, f32[16,24]{1,0:T(8,128)S(1)} %reshape.338), kind=kOutput, calls=%fused_computation.27 | convolution fusion | flops 38274944 | bytes 1836544 | tf_op jit(solution)/shard_map/zs,syx->zyx/dot_general | solution.py:90
  25.9 4.9 %collective-permute-start.2 = (f32[4,32,256]{2,0,1:T(4,128)S(1)}, f32[4,32,256]{2,0,1:T(4,128)S(1)}, u32[]{:S(2)}, u32[]{:S(2)}) collective-permute-start(f32[4,32,256]{2,0,1:T(4,128)S(1)} %get-tuple-element.31), channel_id=1, source_target_pairs={{0,4},{4,8},{8,12},{1,5},{5,9},{9,13},{2,6},{6,10},{10,14},{3,7},{... | collective-permute-start | bytes 393224 | tf_op jit(solution)/shard_map/ppermute | solution.py:19
  30.8 1.3 %collective-permute-start.3 = (f32[4,32,256]{2,0,1:T(4,128)S(1)}, f32[4,32,256]{2,0,1:T(4,128)S(1)}, u32[]{:S(2)}, u32[]{:S(2)}) collective-permute-start(f32[4,32,256]{2,0,1:T(4,128)S(1)} %get-tuple-element.32), channel_id=1, source_target_pairs={{4,0},{8,4},{12,8},{5,1},{9,5},{13,9},{6,2},{10,6},{14,10},{7,3},{... | collective-permute-start | bytes 393224 | tf_op jit(solution)/shard_map/ppermute | solution.py:20
  32.1 0.1 reshape.266
  32.2 0.1 reshape.329
  32.3 2.9 %gather_fusion.2 = f32[384]{0:T(512)S(1)} fusion(f32[24,9]{1,0:T(8,128)S(1)} %broadcast_select_fusion.2, s32[384]{0:T(512)S(1)} %reshape.329), kind=kCustom, calls=%fused_computation.7 | custom fusion | bytes 6144 | tf_op jit(solution)/shard_map/gather | solution.py:97
  35.3 0.2 fusion.82
  35.4 0.6 fusion.5
  36.1 0.3 fusion.35
  36.4 1.2 %fusion.68 = f32[16,32,256]{2,0,1:T(8,128)S(1)} fusion(f32[16,32,256]{2,0,1:T(8,128)S(1)} %fusion.35, f32[16]{0:T(128)S(1)} %get-tuple-element.50, f32[16]{0:T(128)S(1)} %get-tuple-element.49, f32[16]{0:T(128)S(1)} %get-tuple-element.48, f32[16]{0:T(128)S(1)} %get-tuple-element.47, f32[16]{0:T(128)S(1)} %get-tuple-element.46, f32[16]{0:T(128)S(1)} %get-tuple-element.45, ...), kind=kLoop, calls=%fused_computation.112 | loop fusion | flops 2228224 | bytes 1049152 | tf_op jit(solution)/shard_map/log | solution.py:104
  37.6 0.6 gather_fusion.4
  38.2 0.9 %broadcast_select_fusion = f32[4,16,4,2,256]{4,1,3,2,0:T(8,128)} fusion(f32[4,16,4,2,256]{4,1,3,2,0:T(8,128)S(1)} %gather_fusion.4, pred[4]{0:T(512)(128)(4,1)S(1)} %get-tuple-element.42), kind=kLoop, calls=%fused_computation.122 | loop fusion | flops 131072 | bytes 1048580 | tf_op jit(solution)/shard_map/jit(_take)/select_n | solution.py:105
  39.2 8.0 %all-to-all-start.1 = ((f32[16,16,2,256]{3,1,2,0:T(8,128)}), f32[16,16,2,256]{3,1,2,0:T(8,128)S(1)}, u32[]{:S(2)}, u32[]{:S(2)}) async-start(f32[16,16,2,256]{3,1,2,0:T(8,128)} %bitcast.22), calls=%async_computation.1 | async-start | bytes 1048576 | tf_op jit(solution)/shard_map/all_to_all | solution.py:107
  47.2 0.1 select_reduce_fusion
  47.3 0.1 add.366
  47.4 0.3 reshape.265
  47.8 14.9 %all-to-all-done.1 = f32[16,16,2,256]{3,1,2,0:T(8,128)S(1)} async-done(((f32[16,16,2,256]{3,1,2,0:T(8,128)}), f32[16,16,2,256]{3,1,2,0:T(8,128)S(1)}, u32[]{:S(2)}, u32[]{:S(2)}) %all-to-all-start.1) | async-done | bytes 524320 | tf_op jit(solution)/shard_map/all_to_all | solution.py:107
  62.7 0.6 gather_fusion.5
  63.3 0.1 broadcast_select_fusion.1
  63.4 0.1 fusion.79
  63.5 15.8 %all-gather = f32[16,4,8,256]{3,0,2,1:T(8,128)S(1)} all-gather(f32[16,4,2,256]{3,0,2,1:T(8,128)S(1)} %fusion.79), channel_id=2, replica_groups=mesh['tile'=2,'dom'=4,'view'=4] {'view'}, dimensions={2}, use_global_device_ids=true | all-gather | bytes 655360 | tf_op jit(solution)/shard_map/all_gather | solution.py:125
  79.3 1.1 %copy.15 = f32[16,32,256]{2,1,0:T(8,128)} copy(f32[16,32,256]{2,0,1:T(8,128)S(1)} %bitcast.62) | data formatting | bytes 1048576 | tf_op jit(solution)/shard_map/reshape | solution.py:126
  (42 shorter events, 0.8 us)
Async XLA Ops:
  0.0 0.7 copy-start.3
  3.6 13.1 %all-to-all-start = ((f32[16,4,8,256]{3,2,0,1:T(8,128)}), f32[16,4,8,256]{3,2,0,1:T(8,128)S(1)}, u32[]{:S(2)}, u32[]{:S(2)}) async-start(f32[16,4,8,256]{3,2,0,1:T(8,128)} %select_bitcast_fusion.1), calls=%async_computation | async-start | bytes 1048576 | tf_op jit(solution)/shard_map/all_to_all | solution.py:66
  7.9 0.7 copy-start
  9.3 0.7 copy-start.2
  19.2 5.7 %collective-permute-start = (f32[4,32,256]{2,0,1:T(4,128)S(1)}, f32[4,32,256]{2,0,1:T(4,128)S(1)}, u32[]{:S(2)}, u32[]{:S(2)}) collective-permute-start(f32[4,32,256]{2,0,1:T(4,128)S(1)} %get-tuple-element.33), channel_id=1, source_target_pairs={{0,4},{4,8},{8,12},{1,5},{5,9},{9,13},{2,6},{6,10},{10,14},{3,7},{... | collective-permute-start | bytes 393224 | tf_op jit(solution)/shard_map/ppermute | solution.py:19
  20.5 4.4 %collective-permute-start.1 = (f32[4,32,256]{2,0,1:T(4,128)S(1)}, f32[4,32,256]{2,0,1:T(4,128)S(1)}, u32[]{:S(2)}, u32[]{:S(2)}) collective-permute-start(f32[4,32,256]{2,0,1:T(4,128)S(1)} %get-tuple-element.34), channel_id=1, source_target_pairs={{4,0},{8,4},{12,8},{5,1},{9,5},{13,9},{6,2},{10,6},{14,10},{7,3},{... | collective-permute-start | bytes 393224 | tf_op jit(solution)/shard_map/ppermute | solution.py:20
  21.9 3.0 %copy-start.4 = (f32[1,16,32,256]{3,2,1,0:T(8,128)S(1)}, f32[1,16,32,256]{3,2,1,0:T(8,128)}, u32[]{:S(2)}) copy-start(f32[1,16,32,256]{3,2,1,0:T(8,128)} %param.10) | copy-start | bytes 1572868
  25.9 9.5 %collective-permute-start.2 = (f32[4,32,256]{2,0,1:T(4,128)S(1)}, f32[4,32,256]{2,0,1:T(4,128)S(1)}, u32[]{:S(2)}, u32[]{:S(2)}) collective-permute-start(f32[4,32,256]{2,0,1:T(4,128)S(1)} %get-tuple-element.31), channel_id=1, source_target_pairs={{0,4},{4,8},{8,12},{1,5},{5,9},{9,13},{2,6},{6,10},{10,14},{3,7},{... | collective-permute-start | bytes 393224 | tf_op jit(solution)/shard_map/ppermute | solution.py:19
  30.8 4.6 %collective-permute-start.3 = (f32[4,32,256]{2,0,1:T(4,128)S(1)}, f32[4,32,256]{2,0,1:T(4,128)S(1)}, u32[]{:S(2)}, u32[]{:S(2)}) collective-permute-start(f32[4,32,256]{2,0,1:T(4,128)S(1)} %get-tuple-element.32), channel_id=1, source_target_pairs={{4,0},{8,4},{12,8},{5,1},{9,5},{13,9},{6,2},{10,6},{14,10},{7,3},{... | collective-permute-start | bytes 393224 | tf_op jit(solution)/shard_map/ppermute | solution.py:20
  39.2 8.3 %copy-start.1 = (f32[16,32,256]{2,1,0:T(8,128)S(1)}, f32[16,32,256]{2,1,0:T(8,128)}, u32[]{:S(2)}) copy-start(f32[16,32,256]{2,1,0:T(8,128)} %param.9) | copy-start | bytes 1572868
  39.2 23.6 %all-to-all-start.1 = ((f32[16,16,2,256]{3,1,2,0:T(8,128)}), f32[16,16,2,256]{3,1,2,0:T(8,128)S(1)}, u32[]{:S(2)}, u32[]{:S(2)}) async-start(f32[16,16,2,256]{3,1,2,0:T(8,128)} %bitcast.22), calls=%async_computation.1 | async-start | bytes 1048576 | tf_op jit(solution)/shard_map/all_to_all | solution.py:107

commit v4 on v3

--- a/solution.py
+++ b/solution.py
@@ -80,22 +80,16 @@
     y_own = jnp.take(kernels[:, 1], band_own, axis=0)
     lateral = lateral_fwd(camera, x_own, y_own)
     extended = extended_2(lateral, (("dom", 0),), RADIUS)
-    z_pos = jnp.arange(plane_count, dtype=jnp.int32)[:, None]
-    s_pos = jnp.arange(ext_count, dtype=jnp.int32)[None, :]
-    fwd_tap = s_pos - z_pos
-    fwd_valid = (fwd_tap >= 0) & (fwd_tap <= 2 * reach)
     taps_own = jnp.take(kernels[:, 0], band_own, axis=0)
-    row_sel = jnp.broadcast_to(z_pos, (plane_count, ext_count))
-    depth_fwd = jnp.where(fwd_valid, taps_own[row_sel, jnp.clip(fwd_tap, 0, 2 * reach)], 0.0)
-    blurred = jnp.einsum("zs,syx->zyx", depth_fwd, extended, precision=precise)
+    blurred = jnp.zeros(lateral.shape, jnp.float32)
+    for j in range(2 * reach + 1):
+        blurred = blurred + taps_own[:, j][:, None, None] * extended[j : j + plane_count]
     ratio_field = observed[0] / blurred
     ratio_ext = extended_2(ratio_field, (("dom", 0),), RADIUS)
-    back_tap = z_pos - s_pos + 2 * reach
-    back_valid = (back_tap >= 0) & (back_tap <= 2 * reach)
     taps_ext = jnp.take(kernels[:, 0], band_ext, axis=0)
-    col_sel = jnp.broadcast_to(s_pos, (plane_count, ext_count))
-    depth_back = jnp.where(back_valid, taps_ext[col_sel, jnp.clip(back_tap, 0, 2 * reach)], 0.0)
-    zback = jnp.einsum("zs,syx->zyx", depth_back, ratio_ext, precision=precise)
+    zback = jnp.zeros(ratio_field.shape, jnp.float32)
+    for m in range(2 * reach + 1):
+        zback = zback + taps_ext[m : m + plane_count, 2 * reach - m][:, None, None] * ratio_ext[m : m + plane_count]
     back = lateral_back(zback, x_own, y_own)
     dest_slot = jnp.sum(
         jnp.where(my_sources[None, :] == slot_ids[:, None], slot_ids[None, :], 0), axis=1

time: 80.9 us -> 80.4 us (level)
  local copies, waits for them, and re-layouts: 16.9 us -> 11.6 us
  waiting for transfers between devices: 18.7 us -> 22.3 us
  other arithmetic: 6.08 us -> 7.77 us
  matrix products: 1.55 us -> 0 us
  starting transfers between devices: 21 us -> 22.2 us
    gather x4 -> x0, local copies, waits for them, and re-layouts: 5.93 us -> none  [the longest x2 2.96 us: body(): taps_own[row_sel, jnp.clip(fwd_tap, 0, 2 * reach)]]
    ppermute x2, waiting for transfers between devices: 0.01 us -> 3.6 us  [extended_2(): after = lax.ppermute(initial, axis, down)]
    dot_general x2 -> x0, matrix products: 1.55 us -> none  [the longest x1 0.91 us: body(): blurred = jnp.einsum('zs,syx->zyx', depth_fwd, extended, precision=precise)]
  transfers between devices with their start and end apart: 6 -> 6, of which waited for: 2 -> 4; matrix products, arithmetic and copies ran while one was open for 13% -> 7% of each run, Pallas kernels for 0% -> 0%
where the time goes in v4:
time: 80.4 us; the launch traced here: 79.9 us
  waiting for transfers between devices  22.3 us (28%)
  starting transfers between devices  22.2 us (28%)
  blocking collectives  15.8 us (20%)
  local copies, waits for them, and re-layouts  11.6 us (14%)
  other arithmetic  7.77 us (10%)
    all_gather x1, blocking collectives, body(): joined = lax.all_gather(updated, 'view', axis=2, tiled=False)  15.8 us
    all_to_all x1, waiting for transfers between devices, body(): arrived_logs = lax.all_to_all(outgoing, ('dom', 'view'), 0, 0, tiled=True)  14.9 us
    all_to_all x1, starting transfers between devices, body(): arrived_logs = lax.all_to_all(outgoing, ('dom', 'view'), 0, 0, tiled=True)  8.45 us
    ppermute x2, starting transfers between devices, extended_2(): before = lax.ppermute(last, axis, up)  6.88 us
    all_to_all x1, starting transfers between devices, body(): lax.all_to_all(outgoing, 'dom', split_axis=1, concat_axis=1, tiled=True)  4.24 us
    all_to_all x1, waiting for transfers between devices, body(): lax.all_to_all(outgoing, 'dom', split_axis=1, concat_axis=1, tiled=True)  3.77 us
    ppermute x2, waiting for transfers between devices, extended_2(): after = lax.ppermute(initial, axis, down)  3.6 us
    ppermute x2, starting transfers between devices, extended_2(): after = lax.ppermute(initial, axis, down)  2.58 us
  transfers between devices with their start and end apart: 6, of which 4 were waited for; matrix products, arithmetic and copies ran while one was open for 7% of the time, Pallas kernels for 0%

profile of v4, /device:TPU:0, one launch (start us, length us, event | category | flops | bytes accessed | tf_op | source)
XLA Modules:
  0.0 79.9 jit_solution(9079512928382514942)
XLA Ops:
  0.0 0.7 copy-done.4
  0.7 0.1 reshape.204
  0.8 0.1 fusion.119
  0.9 0.1 select_reduce_fusion.1
  1.1 1.6 %gather_fusion.7 = f32[4,16,8,256]{3,2,1,0:T(8,128)S(1)} fusion(f32[16,4,8,256]{3,2,1,0:T(8,128)} %bitcast.55, s32[1024]{0:T(1024)S(1)} %pad_clamp_fusion.3), kind=kCustom, calls=%fused_computation.1.clone | custom fusion | bytes 1048592 | tf_op jit(solution)/shard_map/jit(_take)/gather | solution.py:65
  2.7 0.9 %select_bitcast_fusion.1 = f32[16,4,8,256]{3,2,0,1:T(8,128)} fusion(f32[4,16,8,256]{3,2,1,0:T(8,128)S(1)} %gather_fusion.7, pred[4]{0:T(512)(128)(4,1)S(1)} %get-tuple-element.59), kind=kLoop, calls=%fused_computation.181 | loop fusion | flops 131072 | bytes 1048580 | tf_op jit(solution)/shard_map/jit(_take)/select_n | solution.py:65
  3.6 4.2 %all-to-all-start = ((f32[16,4,8,256]{3,2,0,1:T(8,128)}), f32[16,4,8,256]{3,2,0,1:T(8,128)S(1)}, u32[]{:S(2)}, u32[]{:S(2)}) async-start(f32[16,4,8,256]{3,2,0,1:T(8,128)} %select_bitcast_fusion.1), calls=%async_computation | async-start | bytes 1048576 | tf_op jit(solution)/shard_map/all_to_all | solution.py:66
  7.9 0.6 copy-done
  8.5 0.7 gather_fusion
  9.3 0.1 compare_and_fusion.2
  9.4 0.6 copy-done.3
  10.0 0.6 gather_fusion.6
  10.6 0.6 gather_fusion.5
  11.1 0.6 gather_fusion.4
  11.8 0.6 gather_fusion.1
  12.3 0.5 slice_reduce_fusion.34
  12.9 3.8 %all-to-all-done = f32[16,4,8,256]{3,2,0,1:T(8,128)S(1)} async-done(((f32[16,4,8,256]{3,2,0,1:T(8,128)}), f32[16,4,8,256]{3,2,0,1:T(8,128)S(1)}, u32[]{:S(2)}, u32[]{:S(2)}) %all-to-all-start) | async-done | bytes 524320 | tf_op jit(solution)/shard_map/all_to_all | solution.py:66
  16.7 0.6 gather_fusion.8
  17.3 0.1 copy_bitcast_fusion
  17.4 1.4 %fusion.81 = f32[16,32,256]{2,1,0:T(8,128)S(1)} fusion(f32[16,32,256]{2,1,0:T(8,128)S(1)} %copy_bitcast_fusion, f32[16]{0:T(128)S(1)} %get-tuple-element.68, f32[16]{0:T(128)S(1)} %get-tuple-element.67, f32[16]{0:T(128)S(1)} %get-tuple-element.66, f32[16]{0:T(128)S(1)} %get-tuple-element.65, f32[16]{0:T(128)S(1)} %get-tuple-element.64, ...), kind=kLoop, calls=%fused_computation.146 | loop fusion | flops 2228224 | bytes 1049152 | tf_op jit(solution)/shard_map/add | solution.py:36
  18.8 0.6 fusion.49
  19.5 1.4 %collective-permute-start = (f32[4,32,256]{2,1,0:T(8,128)S(1)}, f32[4,32,256]{2,1,0:T(8,128)S(1)}, u32[]{:S(2)}, u32[]{:S(2)}) collective-permute-start(f32[4,32,256]{2,1,0:T(8,128)S(1)} %get-tuple-element.51), channel_id=1, source_target_pairs={{0,4},{4,8},{8,12},{1,5},{5,9},{9,13},{2,6},{6,10},{10,14},{3,7},{... | collective-permute-start | bytes 393224 | tf_op jit(solution)/shard_map/ppermute | solution.py:19
  20.9 1.3 %collective-permute-start.1 = (f32[4,32,256]{2,1,0:T(8,128)S(1)}, f32[4,32,256]{2,1,0:T(8,128)S(1)}, u32[]{:S(2)}, u32[]{:S(2)}) collective-permute-start(f32[4,32,256]{2,1,0:T(8,128)S(1)} %get-tuple-element.52), channel_id=1, source_target_pairs={{4,0},{8,4},{12,8},{5,1},{9,5},{13,9},{6,2},{10,6},{14,10},{7,3},{... | collective-permute-start | bytes 393224 | tf_op jit(solution)/shard_map/ppermute | solution.py:20
  22.2 0.3 slice_reduce_fusion.32
  22.5 0.3 slice_reduce_fusion.33
  22.9 1.9 %collective-permute-done.1 = f32[4,32,256]{2,1,0:T(8,128)S(1)} collective-permute-done((f32[4,32,256]{2,1,0:T(8,128)S(1)}, f32[4,32,256]{2,1,0:T(8,128)S(1)}, u32[]{:S(2)}, u32[]{:S(2)}) %collective-permute-start.1) | collective-permute-done | bytes 131104 | tf_op jit(solution)/shard_map/ppermute | solution.py:20
  24.8 0.4 fusion.24
  25.3 5.5 %collective-permute-start.2 = (f32[4,32,256]{2,1,0:T(8,128)S(1)}, f32[4,32,256]{2,1,0:T(8,128)S(1)}, u32[]{:S(2)}, u32[]{:S(2)}) collective-permute-start(f32[4,32,256]{2,1,0:T(8,128)S(1)} %get-tuple-element.49), channel_id=1, source_target_pairs={{0,4},{4,8},{8,12},{1,5},{5,9},{9,13},{2,6},{6,10},{10,14},{3,7},{... | collective-permute-start | bytes 393224 | tf_op jit(solution)/shard_map/ppermute | solution.py:19
  30.7 1.3 %collective-permute-start.3 = (f32[4,32,256]{2,1,0:T(8,128)S(1)}, f32[4,32,256]{2,1,0:T(8,128)S(1)}, u32[]{:S(2)}, u32[]{:S(2)}) collective-permute-start(f32[4,32,256]{2,1,0:T(8,128)S(1)} %get-tuple-element.50), channel_id=1, source_target_pairs={{4,0},{8,4},{12,8},{5,1},{9,5},{13,9},{6,2},{10,6},{14,10},{7,3},{... | collective-permute-start | bytes 393224 | tf_op jit(solution)/shard_map/ppermute | solution.py:20
  32.0 0.1 reshape.203
  32.1 0.2 fusion.116
  32.3 1.7 %collective-permute-done.3 = f32[4,32,256]{2,1,0:T(8,128)S(1)} collective-permute-done((f32[4,32,256]{2,1,0:T(8,128)S(1)}, f32[4,32,256]{2,1,0:T(8,128)S(1)}, u32[]{:S(2)}, u32[]{:S(2)}) %collective-permute-start.3) | collective-permute-done | bytes 131104 | tf_op jit(solution)/shard_map/ppermute | solution.py:20
  34.0 0.4 fusion.3
  34.4 0.6 fusion.65
  35.0 1.3 %fusion.98 = f32[16,32,256]{2,1,0:T(8,128)S(1)} fusion(f32[16,32,256]{2,1,0:T(8,128)S(1)} %fusion.65, f32[16]{0:T(128)S(1)} %get-tuple-element.68, f32[16]{0:T(128)S(1)} %get-tuple-element.67, f32[16]{0:T(128)S(1)} %get-tuple-element.66, f32[16]{0:T(128)S(1)} %get-tuple-element.65, f32[16]{0:T(128)S(1)} %get-tuple-element.64, f32[16]{0:T(128)S(1)} %get-tuple-element.63, ...), kind=kLoop, calls=%fused_computation.163 | loop fusion | flops 2228224 | bytes 1049152 | tf_op jit(solution)/shard_map/log | solution.py:98
  36.3 0.3 copy.11
  36.6 0.6 gather_fusion.2
  37.2 0.9 %broadcast_select_fusion = f32[4,16,4,2,256]{4,1,3,2,0:T(8,128)} fusion(f32[4,16,4,2,256]{4,1,3,2,0:T(8,128)S(1)} %gather_fusion.2, pred[4]{0:T(512)(128)(4,1)S(1)} %get-tuple-element.60), kind=kLoop, calls=%fused_computation.182 | loop fusion | flops 131072 | bytes 1048580 | tf_op jit(solution)/shard_map/jit(_take)/select_n | solution.py:99
  38.1 8.5 %all-to-all-start.1 = ((f32[16,16,2,256]{3,1,2,0:T(8,128)}), f32[16,16,2,256]{3,1,2,0:T(8,128)S(1)}, u32[]{:S(2)}, u32[]{:S(2)}) async-start(f32[16,16,2,256]{3,1,2,0:T(8,128)} %bitcast.20), calls=%async_computation.1 | async-start | bytes 1048576 | tf_op jit(solution)/shard_map/all_to_all | solution.py:101
  46.6 0.1 select_reduce_fusion
  46.7 0.1 add.388
  46.9 0.3 reshape.202
  47.3 14.9 %all-to-all-done.1 = f32[16,16,2,256]{3,1,2,0:T(8,128)S(1)} async-done(((f32[16,16,2,256]{3,1,2,0:T(8,128)}), f32[16,16,2,256]{3,1,2,0:T(8,128)S(1)}, u32[]{:S(2)}, u32[]{:S(2)}) %all-to-all-start.1) | async-done | bytes 524320 | tf_op jit(solution)/shard_map/all_to_all | solution.py:101
  62.2 0.6 gather_fusion.3
  62.8 0.1 broadcast_select_fusion.1
  62.9 0.1 fusion.113
  63.0 15.8 %all-gather = f32[16,4,8,256]{3,0,2,1:T(8,128)S(1)} all-gather(f32[16,4,2,256]{3,0,2,1:T(8,128)S(1)} %fusion.113), channel_id=2, replica_groups=mesh['tile'=2,'dom'=4,'view'=4] {'view'}, dimensions={2}, use_global_device_ids=true | all-gather | bytes 655360 | tf_op jit(solution)/shard_map/all_gather | solution.py:119
  78.8 1.1 %copy.12 = f32[16,32,256]{2,1,0:T(8,128)} copy(f32[16,32,256]{2,0,1:T(8,128)S(1)} %bitcast.54) | data formatting | bytes 1048576 | tf_op jit(solution)/shard_map/reshape | solution.py:120
  (36 shorter events, 0.5 us)
Async XLA Ops:
  0.0 0.7 copy-start.4
  3.6 13.1 %all-to-all-start = ((f32[16,4,8,256]{3,2,0,1:T(8,128)}), f32[16,4,8,256]{3,2,0,1:T(8,128)S(1)}, u32[]{:S(2)}, u32[]{:S(2)}) async-start(f32[16,4,8,256]{3,2,0,1:T(8,128)} %select_bitcast_fusion.1), calls=%async_computation | async-start | bytes 1048576 | tf_op jit(solution)/shard_map/all_to_all | solution.py:66
  7.9 0.7 copy-start
  9.3 0.7 copy-start.3
  19.4 5.3 %copy-start.2 = (f32[1,16,32,256]{3,2,1,0:T(8,128)S(1)}, f32[1,16,32,256]{3,2,1,0:T(8,128)}, u32[]{:S(2)}) copy-start(f32[1,16,32,256]{3,2,1,0:T(8,128)} %param.10) | copy-start | bytes 1572868
  19.5 3.4 %collective-permute-start = (f32[4,32,256]{2,1,0:T(8,128)S(1)}, f32[4,32,256]{2,1,0:T(8,128)S(1)}, u32[]{:S(2)}, u32[]{:S(2)}) collective-permute-start(f32[4,32,256]{2,1,0:T(8,128)S(1)} %get-tuple-element.51), channel_id=1, source_target_pairs={{0,4},{4,8},{8,12},{1,5},{5,9},{9,13},{2,6},{6,10},{10,14},{3,7},{... | collective-permute-start | bytes 393224 | tf_op jit(solution)/shard_map/ppermute | solution.py:19
  20.9 3.9 %collective-permute-start.1 = (f32[4,32,256]{2,1,0:T(8,128)S(1)}, f32[4,32,256]{2,1,0:T(8,128)S(1)}, u32[]{:S(2)}, u32[]{:S(2)}) collective-permute-start(f32[4,32,256]{2,1,0:T(8,128)S(1)} %get-tuple-element.52), channel_id=1, source_target_pairs={{4,0},{8,4},{12,8},{5,1},{9,5},{13,9},{6,2},{10,6},{14,10},{7,3},{... | collective-permute-start | bytes 393224 | tf_op jit(solution)/shard_map/ppermute | solution.py:20
  25.3 7.0 %collective-permute-start.2 = (f32[4,32,256]{2,1,0:T(8,128)S(1)}, f32[4,32,256]{2,1,0:T(8,128)S(1)}, u32[]{:S(2)}, u32[]{:S(2)}) collective-permute-start(f32[4,32,256]{2,1,0:T(8,128)S(1)} %get-tuple-element.49), channel_id=1, source_target_pairs={{0,4},{4,8},{8,12},{1,5},{5,9},{9,13},{2,6},{6,10},{10,14},{3,7},{... | collective-permute-start | bytes 393224 | tf_op jit(solution)/shard_map/ppermute | solution.py:19
  30.7 3.2 %collective-permute-start.3 = (f32[4,32,256]{2,1,0:T(8,128)S(1)}, f32[4,32,256]{2,1,0:T(8,128)S(1)}, u32[]{:S(2)}, u32[]{:S(2)}) collective-permute-start(f32[4,32,256]{2,1,0:T(8,128)S(1)} %get-tuple-element.50), channel_id=1, source_target_pairs={{4,0},{8,4},{12,8},{5,1},{9,5},{13,9},{6,2},{10,6},{14,10},{7,3},{... | collective-permute-start | bytes 393224 | tf_op jit(solution)/shard_map/ppermute | solution.py:20
  38.1 8.7 %copy-start.1 = (f32[16,32,256]{2,1,0:T(8,128)S(1)}, f32[16,32,256]{2,1,0:T(8,128)}, u32[]{:S(2)}) copy-start(f32[16,32,256]{2,1,0:T(8,128)} %param.9) | copy-start | bytes 1572868
  38.1 24.0 %all-to-all-start.1 = ((f32[16,16,2,256]{3,1,2,0:T(8,128)}), f32[16,16,2,256]{3,1,2,0:T(8,128)S(1)}, u32[]{:S(2)}, u32[]{:S(2)}) async-start(f32[16,16,2,256]{3,1,2,0:T(8,128)} %bitcast.20), calls=%async_computation.1 | async-start | bytes 1048576 | tf_op jit(solution)/shard_map/all_to_all | solution.py:101

commit v5 on v4

--- a/solution.py
+++ b/solution.py
@@ -94,10 +94,10 @@
     dest_slot = jnp.sum(
         jnp.where(my_sources[None, :] == slot_ids[:, None], slot_ids[None, :], 0), axis=1
     )
-    piece_rows = block_rows // view_count
-    logs = jnp.log(back).reshape(plane_count, block_count, view_count, piece_rows, lane_count)
-    outgoing = jnp.take(logs, dest_slot, axis=1).transpose(1, 2, 0, 3, 4)
-    outgoing = outgoing.reshape(block_count * view_count, plane_count, piece_rows, lane_count)
+    piece_planes = plane_count // view_count
+    logs = jnp.log(back).reshape(view_count, piece_planes, block_count, block_rows, lane_count)
+    outgoing = jnp.take(logs, dest_slot, axis=2).transpose(2, 0, 1, 3, 4)
+    outgoing = outgoing.reshape(block_count * view_count, piece_planes, block_rows, lane_count)
     arrived_logs = lax.all_to_all(outgoing, ("dom", "view"), 0, 0, tiled=True)
     all_grid = src_map.reshape(view_count, block_count, block_count)
     all_dev = all_grid // block_count
@@ -109,15 +109,14 @@
     view_ids = jnp.arange(view_count, dtype=jnp.int32)
     flat_index = (cam_of * view_count + view_ids[:, None]).reshape(-1)
     by_view = jnp.take(arrived_logs, flat_index, axis=0)
-    by_view = by_view.reshape(view_count, block_count, plane_count, piece_rows, lane_count)
+    by_view = by_view.reshape(view_count, block_count, piece_planes, block_rows, lane_count)
     log_total = by_view[0]
     for v in range(1, view_count):
         log_total = log_total + by_view[v]
-    est_rows = estimate.reshape(plane_count, block_count, view_count, piece_rows, lane_count)
-    est_piece = lax.dynamic_index_in_dim(est_rows, view_index, 2, keepdims=False)
-    updated = est_piece * jnp.exp(log_total.transpose(1, 0, 2, 3) / view_count)
-    joined = lax.all_gather(updated, "view", axis=2, tiled=False)
-    return joined.reshape(plane_count, row_count, lane_count)
+    log_total = log_total.transpose(1, 0, 2, 3).reshape(piece_planes, row_count, lane_count)
+    est_piece = lax.dynamic_slice_in_dim(estimate, view_index * piece_planes, piece_planes, 0)
+    updated = est_piece * jnp.exp(log_total / view_count)
+    return lax.all_gather(updated, "view", axis=0, tiled=True)
 
 
 def solution(mesh):

time: 80.4 us -> 80.5 us (level)
  local copies, waits for them, and re-layouts: 11.6 us -> 10.6 us
  other arithmetic: 7.77 us -> 8.61 us
    reshape x2 -> x0, local copies, waits for them, and re-layouts: 1.41 us -> none  [the longest x1 1.1 us: body(): return joined.reshape(plane_count, row_count, lane_count)]
    mul x1, other arithmetic: 0.11 us -> 0.96 us  [body(): updated = est_piece * jnp.exp(log_total / view_count)]
    unnamed x10 -> x9, local copies, waits for them, and re-layouts: 1.94 us -> 2.73 us
  transfers between devices with their start and end apart: 6 -> 6, of which waited for: 4 -> 4; matrix products, arithmetic and copies ran while one was open for 7% -> 6% of each run, Pallas kernels for 0% -> 0%
where the time goes in v5:
time: 80.5 us; the launch traced here: 80 us
  waiting for transfers between devices  22.6 us (28%)
  starting transfers between devices  22 us (27%)
  blocking collectives  15.8 us (20%)
  local copies, waits for them, and re-layouts  10.6 us (13%)
  other arithmetic  8.61 us (11%)
    all_gather x1, blocking collectives, body(): return lax.all_gather(updated, 'view', axis=0, tiled=True)  15.8 us
    all_to_all x1, waiting for transfers between devices, body(): arrived_logs = lax.all_to_all(outgoing, ('dom', 'view'), 0, 0, tiled=True)  15.1 us
    all_to_all x1, starting transfers between devices, body(): arrived_logs = lax.all_to_all(outgoing, ('dom', 'view'), 0, 0, tiled=True)  8.32 us
    ppermute x2, starting transfers between devices, extended_2(): before = lax.ppermute(last, axis, up)  6.88 us
    all_to_all x1, starting transfers between devices, body(): lax.all_to_all(outgoing, 'dom', split_axis=1, concat_axis=1, tiled=True)  4.24 us
    all_to_all x1, waiting for transfers between devices, body(): lax.all_to_all(outgoing, 'dom', split_axis=1, concat_axis=1, tiled=True)  3.78 us
    ppermute x2, waiting for transfers between devices, extended_2(): after = lax.ppermute(initial, axis, down)  3.75 us
    unnamed x9, local copies, waits for them, and re-layouts  2.73 us
  transfers between devices with their start and end apart: 6, of which 4 were waited for; matrix products, arithmetic and copies ran while one was open for 6% of the time, Pallas kernels for 0%

profile of v5, /device:TPU:0, one launch (start us, length us, event | category | flops | bytes accessed | tf_op | source)
XLA Modules:
  0.0 80.0 jit_solution(4203895795987436302)
XLA Ops:
  0.0 0.7 copy-done.3
  0.7 0.1 reshape.201
  0.8 0.1 fusion.118
  0.9 0.1 select_reduce_fusion.1
  1.1 1.6 %gather_fusion.7 = f32[4,16,8,256]{3,2,1,0:T(8,128)S(1)} fusion(f32[16,4,8,256]{3,2,1,0:T(8,128)} %bitcast.49, s32[1024]{0:T(1024)S(1)} %pad_clamp_fusion.3), kind=kCustom, calls=%fused_computation.1.clone | custom fusion | bytes 1048592 | tf_op jit(solution)/shard_map/jit(_take)/gather | solution.py:65
  2.7 0.9 %select_bitcast_fusion.1 = f32[16,4,8,256]{3,2,0,1:T(8,128)} fusion(f32[4,16,8,256]{3,2,1,0:T(8,128)S(1)} %gather_fusion.7, pred[4]{0:T(512)(128)(4,1)S(1)} %get-tuple-element.59), kind=kLoop, calls=%fused_computation.181 | loop fusion | flops 131072 | bytes 1048580 | tf_op jit(solution)/shard_map/jit(_take)/select_n | solution.py:65
  3.6 4.2 %all-to-all-start = ((f32[16,4,8,256]{3,2,0,1:T(8,128)}), f32[16,4,8,256]{3,2,0,1:T(8,128)S(1)}, u32[]{:S(2)}, u32[]{:S(2)}) async-start(f32[16,4,8,256]{3,2,0,1:T(8,128)} %select_bitcast_fusion.1), calls=%async_computation | async-start | bytes 1048576 | tf_op jit(solution)/shard_map/all_to_all | solution.py:66
  7.9 0.6 copy-done
  8.5 0.7 gather_fusion
  9.3 0.1 compare_and_fusion.2
  9.4 0.6 copy-done.2
  10.0 0.6 gather_fusion.6
  10.5 0.6 gather_fusion.5
  11.1 0.6 gather_fusion.4
  11.7 0.1 broadcast_select_fusion.3
  11.8 0.6 gather_fusion.1
  12.3 0.5 slice_reduce_fusion.34
  12.9 3.8 %all-to-all-done = f32[16,4,8,256]{3,2,0,1:T(8,128)S(1)} async-done(((f32[16,4,8,256]{3,2,0,1:T(8,128)}), f32[16,4,8,256]{3,2,0,1:T(8,128)S(1)}, u32[]{:S(2)}, u32[]{:S(2)}) %all-to-all-start) | async-done | bytes 524320 | tf_op jit(solution)/shard_map/all_to_all | solution.py:66
  16.7 0.6 gather_fusion.8
  17.3 0.1 copy_bitcast_fusion
  17.4 1.4 %fusion.81 = f32[16,32,256]{2,1,0:T(8,128)S(1)} fusion(f32[16,32,256]{2,1,0:T(8,128)S(1)} %copy_bitcast_fusion, f32[16]{0:T(128)S(1)} %get-tuple-element.68, f32[16]{0:T(128)S(1)} %get-tuple-element.67, f32[16]{0:T(128)S(1)} %get-tuple-element.66, f32[16]{0:T(128)S(1)} %get-tuple-element.65, f32[16]{0:T(128)S(1)} %get-tuple-element.64, ...), kind=kLoop, calls=%fused_computation.146 | loop fusion | flops 2228224 | bytes 1049152 | tf_op jit(solution)/shard_map/add | solution.py:36
  18.8 0.6 fusion.49
  19.5 1.4 %collective-permute-start = (f32[4,32,256]{2,1,0:T(8,128)S(1)}, f32[4,32,256]{2,1,0:T(8,128)S(1)}, u32[]{:S(2)}, u32[]{:S(2)}) collective-permute-start(f32[4,32,256]{2,1,0:T(8,128)S(1)} %get-tuple-element.51), channel_id=1, source_target_pairs={{0,4},{4,8},{8,12},{1,5},{5,9},{9,13},{2,6},{6,10},{10,14},{3,7},{... | collective-permute-start | bytes 393224 | tf_op jit(solution)/shard_map/ppermute | solution.py:19
  20.9 1.3 %collective-permute-start.1 = (f32[4,32,256]{2,1,0:T(8,128)S(1)}, f32[4,32,256]{2,1,0:T(8,128)S(1)}, u32[]{:S(2)}, u32[]{:S(2)}) collective-permute-start(f32[4,32,256]{2,1,0:T(8,128)S(1)} %get-tuple-element.52), channel_id=1, source_target_pairs={{4,0},{8,4},{12,8},{5,1},{9,5},{13,9},{6,2},{10,6},{14,10},{7,3},{... | collective-permute-start | bytes 393224 | tf_op jit(solution)/shard_map/ppermute | solution.py:20
  22.2 0.3 slice_reduce_fusion.32
  22.5 2.2 %collective-permute-done.1 = f32[4,32,256]{2,1,0:T(8,128)S(1)} collective-permute-done((f32[4,32,256]{2,1,0:T(8,128)S(1)}, f32[4,32,256]{2,1,0:T(8,128)S(1)}, u32[]{:S(2)}, u32[]{:S(2)}) %collective-permute-start.1) | collective-permute-done | bytes 131104 | tf_op jit(solution)/shard_map/ppermute | solution.py:20
  24.8 0.4 fusion.24
  25.3 5.5 %collective-permute-start.2 = (f32[4,32,256]{2,1,0:T(8,128)S(1)}, f32[4,32,256]{2,1,0:T(8,128)S(1)}, u32[]{:S(2)}, u32[]{:S(2)}) collective-permute-start(f32[4,32,256]{2,1,0:T(8,128)S(1)} %get-tuple-element.49), channel_id=1, source_target_pairs={{0,4},{4,8},{8,12},{1,5},{5,9},{9,13},{2,6},{6,10},{10,14},{3,7},{... | collective-permute-start | bytes 393224 | tf_op jit(solution)/shard_map/ppermute | solution.py:19
  30.7 1.3 %collective-permute-start.3 = (f32[4,32,256]{2,1,0:T(8,128)S(1)}, f32[4,32,256]{2,1,0:T(8,128)S(1)}, u32[]{:S(2)}, u32[]{:S(2)}) collective-permute-start(f32[4,32,256]{2,1,0:T(8,128)S(1)} %get-tuple-element.50), channel_id=1, source_target_pairs={{4,0},{8,4},{12,8},{5,1},{9,5},{13,9},{6,2},{10,6},{14,10},{7,3},{... | collective-permute-start | bytes 393224 | tf_op jit(solution)/shard_map/ppermute | solution.py:20
  32.0 0.1 reshape.200
  32.1 0.3 slice_reduce_fusion.33
  32.5 1.5 %collective-permute-done.3 = f32[4,32,256]{2,1,0:T(8,128)S(1)} collective-permute-done((f32[4,32,256]{2,1,0:T(8,128)S(1)}, f32[4,32,256]{2,1,0:T(8,128)S(1)}, u32[]{:S(2)}, u32[]{:S(2)}) %collective-permute-start.3) | collective-permute-done | bytes 131104 | tf_op jit(solution)/shard_map/ppermute | solution.py:20
  34.0 0.4 fusion.3
  34.4 0.6 fusion.65
  35.0 1.3 %fusion.98 = f32[16,32,256]{2,1,0:T(8,128)S(1)} fusion(f32[16,32,256]{2,1,0:T(8,128)S(1)} %fusion.65, f32[16]{0:T(128)S(1)} %get-tuple-element.68, f32[16]{0:T(128)S(1)} %get-tuple-element.67, f32[16]{0:T(128)S(1)} %get-tuple-element.66, f32[16]{0:T(128)S(1)} %get-tuple-element.65, f32[16]{0:T(128)S(1)} %get-tuple-element.64, f32[16]{0:T(128)S(1)} %get-tuple-element.63, ...), kind=kLoop, calls=%fused_computation.163 | loop fusion | flops 2228224 | bytes 1049152 | tf_op jit(solution)/shard_map/log | solution.py:98
  36.3 0.6 gather_fusion.2
  36.9 0.9 %broadcast_select_fusion = f32[4,4,4,8,256]{4,3,2,1,0:T(8,128)} fusion(f32[4,4,4,8,256]{4,3,2,1,0:T(8,128)S(1)} %gather_fusion.2, pred[4]{0:T(512)(128)(4,1)S(1)} %get-tuple-element.60), kind=kLoop, calls=%fused_computation.182 | loop fusion | flops 131072 | bytes 1048580 | tf_op jit(solution)/shard_map/jit(_take)/select_n | solution.py:99
  37.8 8.3 %all-to-all-start.1 = ((f32[16,4,8,256]{3,2,1,0:T(8,128)}), f32[16,4,8,256]{3,2,1,0:T(8,128)S(1)}, u32[]{:S(2)}, u32[]{:S(2)}) async-start(f32[16,4,8,256]{3,2,1,0:T(8,128)} %bitcast.18), calls=%async_computation.1 | async-start | bytes 1048576 | tf_op jit(solution)/shard_map/all_to_all | solution.py:101
  46.1 0.2 fusion.115
  46.3 0.1 select_reduce_fusion
  46.4 0.1 add.390
  46.5 0.1 add.325
  46.6 15.1 %all-to-all-done.1 = f32[16,4,8,256]{3,2,1,0:T(8,128)S(1)} async-done(((f32[16,4,8,256]{3,2,1,0:T(8,128)}), f32[16,4,8,256]{3,2,1,0:T(8,128)S(1)}, u32[]{:S(2)}, u32[]{:S(2)}) %all-to-all-start.1) | async-done | bytes 524320 | tf_op jit(solution)/shard_map/all_to_all | solution.py:101
  61.7 0.6 gather_fusion.3
  62.3 0.1 broadcast_select_fusion.1
  62.4 1.0 %bitcast_multiply_fusion = f32[4,32,256]{2,1,0:T(8,128)S(1)} fusion(f32[16,32,256]{2,1,0:T(8,128)} %param.9, s32[]{:T(128)S(6)} %select_n.177, f32[16,4,8,256]{3,2,1,0:T(8,128)S(1)} %broadcast_select_fusion.1), kind=kLoop, calls=%fused_computation.190 | loop fusion | flops 163840 | bytes 786436 | tf_op jit(solution)/shard_map/mul | solution.py:118
  63.4 15.8 %all_gather.3 = f32[16,32,256]{2,1,0:T(8,128)S(1)} all-gather(f32[4,32,256]{2,1,0:T(8,128)S(1)} %bitcast_multiply_fusion), channel_id=1, replica_groups=mesh['tile'=2,'dom'=4,'view'=4] {'view'}, dimensions={0}, use_global_device_ids=true | all-gather | bytes 655360 | tf_op jit(solution)/shard_map/all_gather | solution.py:119
  79.2 0.8 copy.15
  (31 shorter events, 0.3 us)
Async XLA Ops:
  0.0 0.7 copy-start.3
  3.6 13.1 %all-to-all-start = ((f32[16,4,8,256]{3,2,0,1:T(8,128)}), f32[16,4,8,256]{3,2,0,1:T(8,128)S(1)}, u32[]{:S(2)}, u32[]{:S(2)}) async-start(f32[16,4,8,256]{3,2,0,1:T(8,128)} %select_bitcast_fusion.1), calls=%async_computation | async-start | bytes 1048576 | tf_op jit(solution)/shard_map/all_to_all | solution.py:66
  7.9 0.7 copy-start
  9.3 0.7 copy-start.2
  19.4 5.3 %copy-start.1 = (f32[1,16,32,256]{3,2,1,0:T(8,128)S(1)}, f32[1,16,32,256]{3,2,1,0:T(8,128)}, u32[]{:S(2)}) copy-start(f32[1,16,32,256]{3,2,1,0:T(8,128)} %param.10) | copy-start | bytes 1572868
  19.5 3.0 %collective-permute-start = (f32[4,32,256]{2,1,0:T(8,128)S(1)}, f32[4,32,256]{2,1,0:T(8,128)S(1)}, u32[]{:S(2)}, u32[]{:S(2)}) collective-permute-start(f32[4,32,256]{2,1,0:T(8,128)S(1)} %get-tuple-element.51), channel_id=1, source_target_pairs={{0,4},{4,8},{8,12},{1,5},{5,9},{9,13},{2,6},{6,10},{10,14},{3,7},{... | collective-permute-start | bytes 393224 | tf_op jit(solution)/shard_map/ppermute | solution.py:19
  20.9 3.9 %collective-permute-start.1 = (f32[4,32,256]{2,1,0:T(8,128)S(1)}, f32[4,32,256]{2,1,0:T(8,128)S(1)}, u32[]{:S(2)}, u32[]{:S(2)}) collective-permute-start(f32[4,32,256]{2,1,0:T(8,128)S(1)} %get-tuple-element.52), channel_id=1, source_target_pairs={{4,0},{8,4},{12,8},{5,1},{9,5},{13,9},{6,2},{10,6},{14,10},{7,3},{... | collective-permute-start | bytes 393224 | tf_op jit(solution)/shard_map/ppermute | solution.py:20
  25.3 7.2 %collective-permute-start.2 = (f32[4,32,256]{2,1,0:T(8,128)S(1)}, f32[4,32,256]{2,1,0:T(8,128)S(1)}, u32[]{:S(2)}, u32[]{:S(2)}) collective-permute-start(f32[4,32,256]{2,1,0:T(8,128)S(1)} %get-tuple-element.49), channel_id=1, source_target_pairs={{0,4},{4,8},{8,12},{1,5},{5,9},{9,13},{2,6},{6,10},{10,14},{3,7},{... | collective-permute-start | bytes 393224 | tf_op jit(solution)/shard_map/ppermute | solution.py:19
  30.7 3.2 %collective-permute-start.3 = (f32[4,32,256]{2,1,0:T(8,128)S(1)}, f32[4,32,256]{2,1,0:T(8,128)S(1)}, u32[]{:S(2)}, u32[]{:S(2)}) collective-permute-start(f32[4,32,256]{2,1,0:T(8,128)S(1)} %get-tuple-element.50), channel_id=1, source_target_pairs={{4,0},{8,4},{12,8},{5,1},{9,5},{13,9},{6,2},{10,6},{14,10},{7,3},{... | collective-permute-start | bytes 393224 | tf_op jit(solution)/shard_map/ppermute | solution.py:20
  37.8 23.9 %all-to-all-start.1 = ((f32[16,4,8,256]{3,2,1,0:T(8,128)}), f32[16,4,8,256]{3,2,1,0:T(8,128)S(1)}, u32[]{:S(2)}, u32[]{:S(2)}) async-start(f32[16,4,8,256]{3,2,1,0:T(8,128)} %bitcast.18), calls=%async_computation.1 | async-start | bytes 1048576 | tf_op jit(solution)/shard_map/all_to_all | solution.py:101

commit v6 on v5

--- a/solution.py
+++ b/solution.py
@@ -62,10 +62,10 @@
     source_slot = grid_map % block_count
     send_slot = jnp.sum(jnp.where(source_dev == dom_index, source_slot, 0), axis=1)
     blocks = estimate.reshape(plane_count, block_count, block_rows, lane_count)
-    outgoing = jnp.take(blocks, send_slot, axis=1)
+    outgoing = jnp.take(blocks, send_slot, axis=1, mode="clip")
     arrived = lax.all_to_all(outgoing, "dom", split_axis=1, concat_axis=1, tiled=True)
     my_sources = lax.dynamic_index_in_dim(source_dev, dom_index, 0, keepdims=False)
-    camera = jnp.take(arrived, my_sources, axis=1).reshape(plane_count, row_count, lane_count)
+    camera = jnp.take(arrived, my_sources, axis=1, mode="clip").reshape(plane_count, row_count, lane_count)
     kernels = psf[0]
     band_all = depth_band[0]
     total_planes = band_all.shape[0]
@@ -74,19 +74,19 @@
     ext_index = jnp.clip(
         plane_start - reach + jnp.arange(ext_count, dtype=jnp.int32), 0, total_planes - 1
     )
-    band_ext = jnp.take(band_all, ext_index)
+    band_ext = jnp.take(band_all, ext_index, mode="clip")
     band_own = lax.dynamic_slice_in_dim(band_all, plane_start, plane_count)
-    x_own = jnp.take(kernels[:, 2], band_own, axis=0)
-    y_own = jnp.take(kernels[:, 1], band_own, axis=0)
+    x_own = jnp.take(kernels[:, 2], band_own, axis=0, mode="clip")
+    y_own = jnp.take(kernels[:, 1], band_own, axis=0, mode="clip")
     lateral = lateral_fwd(camera, x_own, y_own)
     extended = extended_2(lateral, (("dom", 0),), RADIUS)
-    taps_own = jnp.take(kernels[:, 0], band_own, axis=0)
+    taps_own = jnp.take(kernels[:, 0], band_own, axis=0, mode="clip")
     blurred = jnp.zeros(lateral.shape, jnp.float32)
     for j in range(2 * reach + 1):
         blurred = blurred + taps_own[:, j][:, None, None] * extended[j : j + plane_count]
     ratio_field = observed[0] / blurred
     ratio_ext = extended_2(ratio_field, (("dom", 0),), RADIUS)
-    taps_ext = jnp.take(kernels[:, 0], band_ext, axis=0)
+    taps_ext = jnp.take(kernels[:, 0], band_ext, axis=0, mode="clip")
     zback = jnp.zeros(ratio_field.shape, jnp.float32)
     for m in range(2 * reach + 1):
         zback = zback + taps_ext[m : m + plane_count, 2 * reach - m][:, None, None] * ratio_ext[m : m + plane_count]
@@ -96,7 +96,7 @@
     )
     piece_planes = plane_count // view_count
     logs = jnp.log(back).reshape(view_count, piece_planes, block_count, block_rows, lane_count)
-    outgoing = jnp.take(logs, dest_slot, axis=2).transpose(2, 0, 1, 3, 4)
+    outgoing = jnp.take(logs, dest_slot, axis=2, mode="clip").transpose(2, 0, 1, 3, 4)
     outgoing = outgoing.reshape(block_count * view_count, piece_planes, block_rows, lane_count)
     arrived_logs = lax.all_to_all(outgoing, ("dom", "view"), 0, 0, tiled=True)
     all_grid = src_map.reshape(view_count, block_count, block_count)
@@ -108,7 +108,7 @@
     )
     view_ids = jnp.arange(view_count, dtype=jnp.int32)
     flat_index = (cam_of * view_count + view_ids[:, None]).reshape(-1)
-    by_view = jnp.take(arrived_logs, flat_index, axis=0)
+    by_view = jnp.take(arrived_logs, flat_index, axis=0, mode="clip")
     by_view = by_view.reshape(view_count, block_count, piece_planes, block_rows, lane_count)
     log_total = by_view[0]
     for v in range(1, view_count):

time: 80.5 us -> 79.9 us (level)
  other arithmetic: 8.61 us -> 6.3 us
  local copies, waits for them, and re-layouts: 10.6 us -> 11.7 us
    select_n x11 -> x0, other arithmetic: 2.12 us -> none  [the longest x2 0.93 us: body(): outgoing = jnp.take(logs, dest_slot, axis=2).transpose(2, 0, 1, 3, 4)]
    all_to_all x1, waiting for transfers between devices: 3.78 us -> 5.53 us  [body(): lax.all_to_all(outgoing, 'dom', split_axis=1, concat_axis=1, tiled=True)]
    gather x9, local copies, waits for them, and re-layouts: 6.31 us -> 7.91 us  [the longest x1 2.42 us: body(): outgoing = jnp.take(blocks, send_slot, axis=1, mode='clip')]
    ppermute x2, waiting for transfers between devices: 3.75 us -> 2.7 us  [extended_2(): after = lax.ppermute(initial, axis, down)]
where the time goes in v6:
time: 79.9 us; the launch traced here: 79.4 us
  waiting for transfers between devices  23.4 us (29%)
  starting transfers between devices  22 us (28%)
  blocking collectives  15.8 us (20%)
  local copies, waits for them, and re-layouts  11.7 us (15%)
  other arithmetic  6.3 us (8%)
    all_gather x1, blocking collectives, body(): return lax.all_gather(updated, 'view', axis=0, tiled=True)  15.8 us
    all_to_all x1, waiting for transfers between devices, body(): arrived_logs = lax.all_to_all(outgoing, ('dom', 'view'), 0, 0, tiled=True)  15.1 us
    all_to_all x1, starting transfers between devices, body(): arrived_logs = lax.all_to_all(outgoing, ('dom', 'view'), 0, 0, tiled=True)  8.32 us
    ppermute x2, starting transfers between devices, extended_2(): before = lax.ppermute(last, axis, up)  6.88 us
    all_to_all x1, waiting for transfers between devices, body(): lax.all_to_all(outgoing, 'dom', split_axis=1, concat_axis=1, tiled=True)  5.53 us
    all_to_all x1, starting transfers between devices, body(): lax.all_to_all(outgoing, 'dom', split_axis=1, concat_axis=1, tiled=True)  4.24 us
    ppermute x2, waiting for transfers between devices, extended_2(): after = lax.ppermute(initial, axis, down)  2.7 us
    ppermute x2, starting transfers between devices, extended_2(): after = lax.ppermute(initial, axis, down)  2.58 us
  transfers between devices with their start and end apart: 6, of which 4 were waited for; matrix products, arithmetic and copies ran while one was open for 6% of the time, Pallas kernels for 0%

profile of v6, /device:TPU:0, one launch (start us, length us, event | category | flops | bytes accessed | tf_op | source)
XLA Modules:
  0.0 79.4 jit_solution(14208257533041825180)
XLA Ops:
  0.0 0.0 copy-start
  0.0 0.7 copy-done.3
  0.7 0.1 reshape.110
  0.8 0.1 fusion.118
  0.9 2.4 %gather_fusion.5 = f32[4,16,8,256]{3,2,1,0:T(8,128)} fusion(f32[16,4,8,256]{3,2,1,0:T(8,128)} %bitcast.32, s32[1024]{0:T(1024)S(1)} %pad_clamp_fusion.3), kind=kCustom, calls=%fused_computation.5 | custom fusion | bytes 1048592 | tf_op jit(solution)/shard_map/jit(_take)/gather | solution.py:65
  3.4 4.2 %all-to-all-start = ((f32[16,4,8,256]{3,2,0,1:T(8,128)}), f32[16,4,8,256]{3,2,0,1:T(8,128)S(1)}, u32[]{:S(2)}, u32[]{:S(2)}) async-start(f32[16,4,8,256]{3,2,0,1:T(8,128)} %bitcast.9), calls=%async_computation | async-start | bytes 1048576 | tf_op jit(solution)/shard_map/all_to_all | solution.py:66
  7.6 0.0 copy-start.2
  7.6 0.0 copy-done
  7.6 0.1 fusion.120
  7.7 0.6 copy-done.2
  8.3 0.6 gather_fusion
  8.9 0.6 gather_fusion.1
  9.5 0.7 gather_fusion.2
  10.2 0.1 select_reduce_fusion.1
  10.3 0.3 slice_reduce_fusion.35
  10.6 0.3 slice_reduce_fusion.34
  10.9 5.5 %all-to-all-done = f32[16,4,8,256]{3,2,0,1:T(8,128)S(1)} async-done(((f32[16,4,8,256]{3,2,0,1:T(8,128)}), f32[16,4,8,256]{3,2,0,1:T(8,128)S(1)}, u32[]{:S(2)}, u32[]{:S(2)}) %all-to-all-start) | async-done | bytes 524320 | tf_op jit(solution)/shard_map/all_to_all | solution.py:66
  16.5 0.6 gather_fusion.6
  17.1 1.4 %fusion.81 = f32[16,32,256]{2,1,0:T(8,128)S(1)} fusion(f32[16,32,256]{2,1,0:T(8,128)S(1)} %copy_bitcast_fusion, f32[16]{0:T(128)S(1)} %get-tuple-element.40, f32[16]{0:T(128)S(1)} %get-tuple-element.33, f32[16]{0:T(128)S(1)} %get-tuple-element.34, f32[16]{0:T(128)S(1)} %get-tuple-element.35, f32[16]{0:T(128)S(1)} %get-tuple-element.36, ...), kind=kLoop, calls=%fused_computation.146 | loop fusion | flops 2228224 | bytes 1049152 | tf_op jit(solution)/shard_map/add | solution.py:36
  18.5 0.6 fusion.49
  19.1 0.0 copy-start.1
  19.1 1.4 %collective-permute-start = (f32[4,32,256]{2,1,0:T(8,128)S(1)}, f32[4,32,256]{2,1,0:T(8,128)S(1)}, u32[]{:S(2)}, u32[]{:S(2)}) collective-permute-start(f32[4,32,256]{2,1,0:T(8,128)S(1)} %get-tuple-element.45), channel_id=1, source_target_pairs={{0,4},{4,8},{8,12},{1,5},{5,9},{9,13},{2,6},{6,10},{10,14},{3,7},{... | collective-permute-start | bytes 393224 | tf_op jit(solution)/shard_map/ppermute | solution.py:19
  20.6 1.3 %collective-permute-start.1 = (f32[4,32,256]{2,1,0:T(8,128)S(1)}, f32[4,32,256]{2,1,0:T(8,128)S(1)}, u32[]{:S(2)}, u32[]{:S(2)}) collective-permute-start(f32[4,32,256]{2,1,0:T(8,128)S(1)} %get-tuple-element.46), channel_id=1, source_target_pairs={{4,0},{8,4},{12,8},{5,1},{9,5},{13,9},{6,2},{10,6},{14,10},{7,3},{... | collective-permute-start | bytes 393224 | tf_op jit(solution)/shard_map/ppermute | solution.py:20
  21.9 0.6 gather_fusion.4
  22.4 0.3 slice_reduce_fusion.32
  22.7 0.0 collective-permute-done
  22.8 1.7 %collective-permute-done.1 = f32[4,32,256]{2,1,0:T(8,128)S(1)} collective-permute-done((f32[4,32,256]{2,1,0:T(8,128)S(1)}, f32[4,32,256]{2,1,0:T(8,128)S(1)}, u32[]{:S(2)}, u32[]{:S(2)}) %collective-permute-start.1) | collective-permute-done | bytes 131104 | tf_op jit(solution)/shard_map/ppermute | solution.py:20
  24.4 0.5 fusion.24
  24.9 5.5 %collective-permute-start.2 = (f32[4,32,256]{2,1,0:T(8,128)S(1)}, f32[4,32,256]{2,1,0:T(8,128)S(1)}, u32[]{:S(2)}, u32[]{:S(2)}) collective-permute-start(f32[4,32,256]{2,1,0:T(8,128)S(1)} %get-tuple-element.43), channel_id=1, source_target_pairs={{0,4},{4,8},{8,12},{1,5},{5,9},{9,13},{2,6},{6,10},{10,14},{3,7},{... | collective-permute-start | bytes 393224 | tf_op jit(solution)/shard_map/ppermute | solution.py:19
  30.4 1.3 %collective-permute-start.3 = (f32[4,32,256]{2,1,0:T(8,128)S(1)}, f32[4,32,256]{2,1,0:T(8,128)S(1)}, u32[]{:S(2)}, u32[]{:S(2)}) collective-permute-start(f32[4,32,256]{2,1,0:T(8,128)S(1)} %get-tuple-element.44), channel_id=1, source_target_pairs={{4,0},{8,4},{12,8},{5,1},{9,5},{13,9},{6,2},{10,6},{14,10},{7,3},{... | collective-permute-start | bytes 393224 | tf_op jit(solution)/shard_map/ppermute | solution.py:20
  31.7 0.6 gather_fusion.3
  32.3 0.3 slice_reduce_fusion.33
  32.6 0.0 collective-permute-done.2
  32.6 1.0 %collective-permute-done.3 = f32[4,32,256]{2,1,0:T(8,128)S(1)} collective-permute-done((f32[4,32,256]{2,1,0:T(8,128)S(1)}, f32[4,32,256]{2,1,0:T(8,128)S(1)}, u32[]{:S(2)}, u32[]{:S(2)}) %collective-permute-start.3) | collective-permute-done | bytes 131104 | tf_op jit(solution)/shard_map/ppermute | solution.py:20
  33.6 0.4 fusion.3
  34.1 0.6 fusion.65
  34.7 1.3 %fusion.98 = f32[16,32,256]{2,1,0:T(8,128)S(1)} fusion(f32[16,32,256]{2,1,0:T(8,128)S(1)} %fusion.65, f32[16]{0:T(128)S(1)} %get-tuple-element.40, f32[16]{0:T(128)S(1)} %get-tuple-element.33, f32[16]{0:T(128)S(1)} %get-tuple-element.34, f32[16]{0:T(128)S(1)} %get-tuple-element.35, f32[16]{0:T(128)S(1)} %get-tuple-element.36, f32[16]{0:T(128)S(1)} %get-tuple-element.37, ...), kind=kLoop, calls=%fused_computation.163 | loop fusion | flops 2228224 | bytes 1049152 | tf_op jit(solution)/shard_map/log | solution.py:98
  36.0 1.4 %gather_fusion.7 = f32[4,4,4,8,256]{4,3,2,1,0:T(8,128)} fusion(f32[4,4,4,8,256]{4,3,2,1,0:T(8,128)S(1)} %bitcast.31, s32[1024]{0:T(1024)S(1)} %pad_clamp_fusion.1), kind=kCustom, calls=%fused_computation.7 | custom fusion | bytes 1048592 | tf_op jit(solution)/shard_map/jit(_take)/gather | solution.py:99
  37.4 8.3 %all-to-all-start.1 = ((f32[16,4,8,256]{3,2,1,0:T(8,128)}), f32[16,4,8,256]{3,2,1,0:T(8,128)S(1)}, u32[]{:S(2)}, u32[]{:S(2)}) async-start(f32[16,4,8,256]{3,2,1,0:T(8,128)} %bitcast.14), calls=%async_computation.1 | async-start | bytes 1048576 | tf_op jit(solution)/shard_map/all_to_all | solution.py:101
  45.7 0.1 reshape.114
  45.8 0.2 fusion.115
  46.0 0.1 select_reduce_fusion
  46.1 0.1 reshape.181
  46.1 15.1 %all-to-all-done.1 = f32[16,4,8,256]{3,2,1,0:T(8,128)S(1)} async-done(((f32[16,4,8,256]{3,2,1,0:T(8,128)}), f32[16,4,8,256]{3,2,1,0:T(8,128)S(1)}, u32[]{:S(2)}, u32[]{:S(2)}) %all-to-all-start.1) | async-done | bytes 524320 | tf_op jit(solution)/shard_map/all_to_all | solution.py:101
  61.3 0.6 gather_fusion.8
  61.9 1.0 %bitcast_multiply_fusion = f32[4,32,256]{2,1,0:T(8,128)S(1)} fusion(f32[16,32,256]{2,1,0:T(8,128)} %param.5, s32[]{:T(128)S(6)} %select_n.65, f32[16,4,8,256]{3,2,1,0:T(8,128)S(1)} %gather_fusion.8), kind=kLoop, calls=%fused_computation.186 | loop fusion | flops 163840 | bytes 786436 | tf_op jit(solution)/shard_map/mul | solution.py:118
  62.8 15.8 %all_gather.3 = f32[16,32,256]{2,1,0:T(8,128)S(1)} all-gather(f32[4,32,256]{2,1,0:T(8,128)S(1)} %bitcast_multiply_fusion), channel_id=1, replica_groups=mesh['tile'=2,'dom'=4,'view'=4] {'view'}, dimensions={0}, use_global_device_ids=true | all-gather | bytes 655360 | tf_op jit(solution)/shard_map/all_gather | solution.py:119
  78.6 0.8 copy.15
  (18 shorter events, 0.2 us)
Async XLA Ops:
  0.0 7.6 %copy-start = (s32[1,64]{1,0:T(1,128)S(1)}, s32[1,64]{1,0:T(1,128)}, u32[]{:S(2)}) copy-start(s32[1,64]{1,0:T(1,128)} %param.9) | copy-start | bytes 772
  0.0 0.7 copy-start.3
  3.4 13.0 %all-to-all-start = ((f32[16,4,8,256]{3,2,0,1:T(8,128)}), f32[16,4,8,256]{3,2,0,1:T(8,128)S(1)}, u32[]{:S(2)}, u32[]{:S(2)}) async-start(f32[16,4,8,256]{3,2,0,1:T(8,128)} %bitcast.9), calls=%async_computation | async-start | bytes 1048576 | tf_op jit(solution)/shard_map/all_to_all | solution.py:66
  7.6 0.7 copy-start.2
  19.1 5.3 %copy-start.1 = (f32[1,16,32,256]{3,2,1,0:T(8,128)S(1)}, f32[1,16,32,256]{3,2,1,0:T(8,128)}, u32[]{:S(2)}) copy-start(f32[1,16,32,256]{3,2,1,0:T(8,128)} %param.6) | copy-start | bytes 1572868
  19.1 3.6 %collective-permute-start = (f32[4,32,256]{2,1,0:T(8,128)S(1)}, f32[4,32,256]{2,1,0:T(8,128)S(1)}, u32[]{:S(2)}, u32[]{:S(2)}) collective-permute-start(f32[4,32,256]{2,1,0:T(8,128)S(1)} %get-tuple-element.45), channel_id=1, source_target_pairs={{0,4},{4,8},{8,12},{1,5},{5,9},{9,13},{2,6},{6,10},{10,14},{3,7},{... | collective-permute-start | bytes 393224 | tf_op jit(solution)/shard_map/ppermute | solution.py:19
  20.6 3.9 %collective-permute-start.1 = (f32[4,32,256]{2,1,0:T(8,128)S(1)}, f32[4,32,256]{2,1,0:T(8,128)S(1)}, u32[]{:S(2)}, u32[]{:S(2)}) collective-permute-start(f32[4,32,256]{2,1,0:T(8,128)S(1)} %get-tuple-element.46), channel_id=1, source_target_pairs={{4,0},{8,4},{12,8},{5,1},{9,5},{13,9},{6,2},{10,6},{14,10},{7,3},{... | collective-permute-start | bytes 393224 | tf_op jit(solution)/shard_map/ppermute | solution.py:20
  24.9 7.7 %collective-permute-start.2 = (f32[4,32,256]{2,1,0:T(8,128)S(1)}, f32[4,32,256]{2,1,0:T(8,128)S(1)}, u32[]{:S(2)}, u32[]{:S(2)}) collective-permute-start(f32[4,32,256]{2,1,0:T(8,128)S(1)} %get-tuple-element.43), channel_id=1, source_target_pairs={{0,4},{4,8},{8,12},{1,5},{5,9},{9,13},{2,6},{6,10},{10,14},{3,7},{... | collective-permute-start | bytes 393224 | tf_op jit(solution)/shard_map/ppermute | solution.py:19
  30.4 3.2 %collective-permute-start.3 = (f32[4,32,256]{2,1,0:T(8,128)S(1)}, f32[4,32,256]{2,1,0:T(8,128)S(1)}, u32[]{:S(2)}, u32[]{:S(2)}) collective-permute-start(f32[4,32,256]{2,1,0:T(8,128)S(1)} %get-tuple-element.44), channel_id=1, source_target_pairs={{4,0},{8,4},{12,8},{5,1},{9,5},{13,9},{6,2},{10,6},{14,10},{7,3},{... | collective-permute-start | bytes 393224 | tf_op jit(solution)/shard_map/ppermute | solution.py:20
  37.4 23.9 %all-to-all-start.1 = ((f32[16,4,8,256]{3,2,1,0:T(8,128)}), f32[16,4,8,256]{3,2,1,0:T(8,128)S(1)}, u32[]{:S(2)}, u32[]{:S(2)}) async-start(f32[16,4,8,256]{3,2,1,0:T(8,128)} %bitcast.14), calls=%async_computation.1 | async-start | bytes 1048576 | tf_op jit(solution)/shard_map/all_to_all | solution.py:101

commit v7 on v6

--- a/solution.py
+++ b/solution.py
@@ -62,32 +62,57 @@
     source_slot = grid_map % block_count
     send_slot = jnp.sum(jnp.where(source_dev == dom_index, source_slot, 0), axis=1)
     blocks = estimate.reshape(plane_count, block_count, block_rows, lane_count)
-    outgoing = jnp.take(blocks, send_slot, axis=1, mode="clip")
-    arrived = lax.all_to_all(outgoing, "dom", split_axis=1, concat_axis=1, tiled=True)
-    my_sources = lax.dynamic_index_in_dim(source_dev, dom_index, 0, keepdims=False)
-    camera = jnp.take(arrived, my_sources, axis=1, mode="clip").reshape(plane_count, row_count, lane_count)
     kernels = psf[0]
     band_all = depth_band[0]
     total_planes = band_all.shape[0]
     reach = (kernels.shape[2] - 1) // 2
+    wide = 2 * reach
+    last = block_count - 1
+    above = jnp.take(send_slot, jnp.clip(slot_ids - 1, 0, last), mode="clip")
+    below = jnp.take(send_slot, jnp.clip(slot_ids + 1, 0, last), mode="clip")
+    outgoing = jnp.concatenate(
+        [
+            jnp.take(blocks[plane_count - wide :], above, axis=1, mode="clip"),
+            jnp.take(blocks, send_slot, axis=1, mode="clip"),
+            jnp.take(blocks[:wide], below, axis=1, mode="clip"),
+        ],
+        axis=0,
+    )
+    arrived = lax.all_to_all(outgoing, "dom", split_axis=1, concat_axis=1, tiled=True)
+    my_sources = lax.dynamic_index_in_dim(source_dev, dom_index, 0, keepdims=False)
+    src_above = lax.dynamic_index_in_dim(source_dev, jnp.maximum(dom_index - 1, 0), 0, keepdims=False)
+    src_below = lax.dynamic_index_in_dim(source_dev, jnp.minimum(dom_index + 1, last), 0, keepdims=False)
+    camera_ext = jnp.concatenate(
+        [
+            jnp.take(arrived[:wide], src_above, axis=1, mode="clip"),
+            jnp.take(arrived[wide : wide + plane_count], my_sources, axis=1, mode="clip"),
+            jnp.take(arrived[wide + plane_count :], src_below, axis=1, mode="clip"),
+        ],
+        axis=0,
+    )
+    wide_count = plane_count + 2 * wide
+    wide_planes = plane_start - wide + jnp.arange(wide_count, dtype=jnp.int32)
+    wide_inside = (wide_planes >= 0) & (wide_planes < total_planes)
+    camera_ext = jnp.where(wide_inside[:, None, None, None], camera_ext, 0.0)
+    camera_ext = camera_ext.reshape(wide_count, row_count, lane_count)
+    band_wide = jnp.take(band_all, jnp.clip(wide_planes, 0, total_planes - 1), mode="clip")
+    x_wide = jnp.take(kernels[:, 2], band_wide, axis=0, mode="clip")
+    y_wide = jnp.take(kernels[:, 1], band_wide, axis=0, mode="clip")
+    lateral_ext = lateral_fwd(camera_ext, x_wide, y_wide)
     ext_count = plane_count + 2 * reach
-    ext_index = jnp.clip(
-        plane_start - reach + jnp.arange(ext_count, dtype=jnp.int32), 0, total_planes - 1
-    )
-    band_ext = jnp.take(band_all, ext_index, mode="clip")
+    ext_planes = plane_start - reach + jnp.arange(ext_count, dtype=jnp.int32)
+    ext_inside = (ext_planes >= 0) & (ext_planes < total_planes)
+    band_ext = jnp.take(band_all, jnp.clip(ext_planes, 0, total_planes - 1), mode="clip")
+    taps_ext = jnp.take(kernels[:, 0], band_ext, axis=0, mode="clip")
+    blurred = jnp.zeros((ext_count, row_count, lane_count), jnp.float32)
+    for j in range(2 * reach + 1):
+        blurred = blurred + taps_ext[:, j][:, None, None] * lateral_ext[j : j + ext_count]
+    observed_ext = extended_2(observed[0], (("dom", 0),), reach)
+    ratio_ext = jnp.where(ext_inside[:, None, None], observed_ext / blurred, 0.0)
     band_own = lax.dynamic_slice_in_dim(band_all, plane_start, plane_count)
     x_own = jnp.take(kernels[:, 2], band_own, axis=0, mode="clip")
     y_own = jnp.take(kernels[:, 1], band_own, axis=0, mode="clip")
-    lateral = lateral_fwd(camera, x_own, y_own)
-    extended = extended_2(lateral, (("dom", 0),), RADIUS)
-    taps_own = jnp.take(kernels[:, 0], band_own, axis=0, mode="clip")
-    blurred = jnp.zeros(lateral.shape, jnp.float32)
-    for j in range(2 * reach + 1):
-        blurred = blurred + taps_own[:, j][:, None, None] * extended[j : j + plane_count]
-    ratio_field = observed[0] / blurred
-    ratio_ext = extended_2(ratio_field, (("dom", 0),), RADIUS)
-    taps_ext = jnp.take(kernels[:, 0], band_ext, axis=0, mode="clip")
-    zback = jnp.zeros(ratio_field.shape, jnp.float32)
+    zback = jnp.zeros((plane_count, row_count, lane_count), jnp.float32)
     for m in range(2 * reach + 1):
         zback = zback + taps_ext[m : m + plane_count, 2 * reach - m][:, None, None] * ratio_ext[m : m + plane_count]
     back = lateral_back(zback, x_own, y_own)

time: 79.9 us -> 78.4 us (0.981)
  waiting for transfers between devices: 23.4 us -> 15.9 us
  local copies, waits for them, and re-layouts: 11.7 us -> 18.9 us
  starting transfers between devices: 22 us -> 16.3 us
  other arithmetic: 6.3 us -> 10.2 us
    all_to_all x1, waiting for transfers between devices: 5.53 us -> 0.81 us  [body(): lax.all_to_all(outgoing, 'dom', split_axis=1, concat_axis=1, tiled=True)]
    ppermute x2 -> x1, starting transfers between devices: 6.88 us -> 2.42 us  [extended_2(): before = lax.ppermute(last, axis, up)]
    gather x4 -> x12, local copies, waits for them, and re-layouts: 4.26 us -> 7.23 us  [the longest x1 0.7 us: body(): jnp.take(band_all, jnp.clip(ext_planes, 0, total_planes - 1), mode='clip')]
    ppermute x2 -> x1, waiting for transfers between devices: 2.7 us -> 0.01 us  [extended_2(): after = lax.ppermute(initial, axis, down)]
    add x3, other arithmetic: 2.57 us -> 4.57 us  [taps_along(): total = total + taps[:, offset][:, None, None] * piece]
    slice x1 -> x7, local copies, waits for them, and re-layouts: 0.29 us -> 2.11 us  [the longest x1 1.07 us: body(): blocks[plane_count - wide:]]
    slice x2 -> x4, local copies, waits for them, and re-layouts: 0.6 us -> 2.37 us  [taps_along(): total = total + taps[:, offset][:, None, None] * piece]
    ppermute x2 -> x1, starting transfers between devices: 2.58 us -> 1.29 us  [extended_2(): after = lax.ppermute(initial, axis, down)]
  transfers between devices with their start and end apart: 6 -> 4, of which waited for: 4 -> 2; matrix products, arithmetic and copies ran while one was open for 6% -> 21% of each run, Pallas kernels for 0% -> 0%
where the time goes in v7:
time: 78.4 us; the launch traced here: 78 us
  local copies, waits for them, and re-layouts  18.9 us (24%)
  starting transfers between devices  16.3 us (21%)
  waiting for transfers between devices  15.9 us (20%)
  blocking collectives  15.8 us (20%)
  other arithmetic  10.2 us (13%)
  between operations  0.86 us (1%)
    all_gather x1, blocking collectives, body(): return lax.all_gather(updated, 'view', axis=0, tiled=True)  15.8 us
    all_to_all x1, waiting for transfers between devices, body(): arrived_logs = lax.all_to_all(outgoing, ('dom', 'view'), 0, 0, tiled=True)  15.1 us
    all_to_all x1, starting transfers between devices, body(): arrived_logs = lax.all_to_all(outgoing, ('dom', 'view'), 0, 0, tiled=True)  8.22 us
    add x3, other arithmetic, taps_along(): total = total + taps[:, offset][:, None, None] * piece  4.57 us
    all_to_all x1, starting transfers between devices, body(): lax.all_to_all(outgoing, 'dom', split_axis=1, concat_axis=1, tiled=True)  4.37 us
    ppermute x1, starting transfers between devices, extended_2(): before = lax.ppermute(last, axis, up)  2.42 us
    slice x4, local copies, waits for them, and re-layouts, taps_along(): total = total + taps[:, offset][:, None, None] * piece  2.37 us
  transfers between devices with their start and end apart: 4, of which 2 were waited for; matrix products, arithmetic and copies ran while one was open for 21% of the time, Pallas kernels for 0%

profile of v7, /device:TPU:0, one launch (start us, length us, event | category | flops | bytes accessed | tf_op | source)
XLA Modules:
  0.0 78.0 jit_solution(6321071205109233533)
XLA Ops:
  0.0 0.7 fusion.94
  0.8 0.1 fusion.91
  0.9 0.6 gather_fusion.7
  1.6 1.1 %slice_bitcast_fusion.1 = (f32[8,4,8,256]{3,2,1,0:T(8,128)S(1)}, f32[8,4,8,256]{3,2,1,0:T(8,128)S(1)}) fusion(f32[16,32,256]{2,1,0:T(8,128)} %param.5), kind=kLoop, calls=%fused_computation.156 | loop fusion | bytes 1048576 | tf_op jit(solution)/shard_map/slice | solution.py:75
  2.7 0.6 gather_fusion.10
  3.3 0.6 gather_fusion.8
  3.9 0.6 gather_fusion.11
  4.5 0.6 gather_fusion.9
  5.1 1.1 %pad_maximum_fusion = f32[32,4,8,256]{3,2,0,1:T(8,128)} fusion(f32[8,4,8,256]{3,2,0,1:T(8,128)S(1)} %bitcast.66, f32[16,4,8,256]{3,2,0,1:T(8,128)S(1)} %bitcast.63, f32[8,4,8,256]{3,2,0,1:T(8,128)S(1)} %bitcast.65), kind=kLoop, calls=%fused_computation.73 | loop fusion | flops 524288 | bytes 2097152 | tf_op jit(solution)/shard_map/concatenate | solution.py:73
  6.1 4.4 %all-to-all-start = ((f32[32,4,8,256]{3,2,0,1:T(8,128)}), f32[32,4,8,256]{3,2,0,1:T(8,128)S(1)}, u32[]{:S(2)}, u32[]{:S(2)}) async-start(f32[32,4,8,256]{3,2,0,1:T(8,128)} %pad_maximum_fusion), calls=%async_computation | async-start | bytes 2097152 | tf_op jit(solution)/shard_map/all_to_all | solution.py:81
  10.5 2.4 %collective-permute-start = (f32[4,32,256]{2,1,0:T(8,128)S(1)}, f32[4,32,256]{2,1,0:T(8,128)S(1)}, u32[]{:S(2)}, u32[]{:S(2)}) collective-permute-start(f32[4,32,256]{2,1,0:T(8,128)S(1)} %get-tuple-element.63), channel_id=1, source_target_pairs={{0,4},{4,8},{8,12},{1,5},{5,9},{9,13},{2,6},{6,10},{10,14},{3,7},{... | collective-permute-start | bytes 393224 | tf_op jit(solution)/shard_map/ppermute | solution.py:19
  13.0 1.3 %collective-permute-start.1 = (f32[4,32,256]{2,1,0:T(8,128)S(1)}, f32[4,32,256]{2,1,0:T(8,128)S(1)}, u32[]{:S(2)}, u32[]{:S(2)}) collective-permute-start(f32[4,32,256]{2,1,0:T(8,128)S(1)} %get-tuple-element.64), channel_id=1, source_target_pairs={{4,0},{8,4},{12,8},{5,1},{9,5},{13,9},{6,2},{10,6},{14,10},{7,3},{... | collective-permute-start | bytes 393224 | tf_op jit(solution)/shard_map/ppermute | solution.py:20
  14.3 0.5 compare_and_fusion
  14.8 0.7 gather_fusion.4
  15.5 0.6 gather_fusion.6
  16.1 0.6 gather_fusion.5
  16.8 0.6 gather_fusion.1
  17.3 0.6 gather_fusion
  17.9 0.1 select_reduce_fusion.1
  18.1 0.7 gather_fusion.2
  18.8 0.6 gather_fusion.3
  19.4 0.6 compare_and_fusion.1
  20.0 0.3 slice_reduce_fusion.52
  20.3 0.3 slice_reduce_fusion.53
  20.6 0.9 %slice_reduce_fusion.26 = (f32[24]{0:T(128)}, f32[24]{0:T(128)}, f32[24]{0:T(128)}, f32[24]{0:T(128)}, f32[24]{0:T(128)}, /*index=5*/f32[24]{0:T(128)}, f32[24]{0:T(128)}, f32[24]{0:T(128)}, f32[24]{0:T(128)}) fusion(f32[24,9]{1,0:T(8,128)S(1)} %gather_fusion.3), kind=kLoop, calls=%fused_computation.192 | loop fusion | bytes 1728 | tf_op jit(solution)/shard_map/slice | solution.py:109
  21.5 0.9 %slice_reduce_fusion.16 = (f32[32]{0:T(128)}, f32[32]{0:T(128)}, f32[32]{0:T(128)}, f32[32]{0:T(128)}, f32[32]{0:T(128)}, /*index=5*/f32[32]{0:T(128)}, f32[32]{0:T(128)}, f32[32]{0:T(128)}, f32[32]{0:T(128)}) fusion(f32[32,9]{1,0:T(8,128)S(1)} %gather_fusion.6), kind=kLoop, calls=%fused_computation.182 | loop fusion | bytes 2304 | tf_op jit(solution)/shard_map/slice | solution.py:36
  22.4 0.9 %slice_reduce_fusion.17 = (f32[32]{0:T(128)}, f32[32]{0:T(128)}, f32[32]{0:T(128)}, f32[32]{0:T(128)}, f32[32]{0:T(128)}, /*index=5*/f32[32]{0:T(128)}, f32[32]{0:T(128)}, f32[32]{0:T(128)}, f32[32]{0:T(128)}) fusion(f32[32,9]{1,0:T(8,128)S(1)} %gather_fusion.5), kind=kLoop, calls=%fused_computation.183 | loop fusion | bytes 2304 | tf_op jit(solution)/shard_map/slice | solution.py:36
  23.2 0.9 %slice_reduce_fusion.51 = (f32[16]{0:T(128)S(1)}, f32[16]{0:T(128)}, f32[16]{0:T(128)}, f32[16]{0:T(128)}, f32[16]{0:T(128)}, /*index=5*/f32[16]{0:T(128)}, f32[16]{0:T(128)}, f32[16]{0:T(128)}, f32[16]{0:T(128)}) fusion(f32[24,9]{1,0:T(8,128)S(1)} %gather_fusion.3), kind=kLoop, calls=%fused_computation.225 | loop fusion | bytes 1152 | tf_op jit(solution)/shard_map/slice | solution.py:117
  24.1 0.8 %all-to-all-done = f32[32,4,8,256]{3,2,0,1:T(8,128)S(1)} async-done(((f32[32,4,8,256]{3,2,0,1:T(8,128)}), f32[32,4,8,256]{3,2,0,1:T(8,128)S(1)}, u32[]{:S(2)}, u32[]{:S(2)}) %all-to-all-start) | async-done | bytes 1048608 | tf_op jit(solution)/shard_map/all_to_all | solution.py:81
  25.0 0.6 gather_fusion.12
  25.6 0.6 gather_fusion.14
  26.3 0.6 gather_fusion.13
  27.1 0.1 maximum_select_fusion
  27.2 0.4 copy-done.30
  27.8 2.7 %fusion.24 = f32[32,32,256]{2,1,0:T(8,128)S(1)} fusion(f32[32,32,256]{2,1,0:T(8,128)S(1)} %maximum_select_fusion, f32[32]{0:T(128)S(1)} %copy-done.38, f32[32]{0:T(128)S(1)} %copy-done.31, f32[32]{0:T(128)S(1)} %copy-done.32, f32[32]{0:T(128)S(1)} %copy-done.33, f32[32]{0:T(128)S(1)} %copy-done.34, f32[32]{0:T(128)S(1)} %copy-done.35, f32[32]{0:T(128)S(1)} %copy-done.36, ...), kind=kLoop, calls=%fused_computation.65 | loop fusion | flops 4456448 | bytes 2098304 | tf_op jit(solution)/shard_map/add | solution.py:36
  30.7 1.3 %fusion.8 = f32[32,32,256]{2,1,0:T(8,128)S(1)} fusion(f32[32,32,256]{2,1,0:T(8,128)S(1)} %fusion.24, f32[32]{0:T(128)S(1)} %copy-done.29, f32[32]{0:T(128)S(1)} %copy-done.22, f32[32]{0:T(128)S(1)} %copy-done.23, f32[32]{0:T(128)S(1)} %copy-done.24, f32[32]{0:T(128)S(1)} %copy-done.25, f32[32]{0:T(128)S(1)} %copy-done.26, f32[32]{0:T(128)S(1)} %copy-done.27, ...), kind=kLoop, calls=%fused_computation.49 | loop fusion | flops 4456448 | bytes 2098304 | tf_op jit(solution)/shard_map/add | solution.py:36
  32.2 0.9 %fusion.34 = f32[24,32,256]{2,1,0:T(8,128)S(1)} fusion(f32[32,32,256]{2,1,0:T(8,128)S(1)} %fusion.8, f32[4,32,256]{2,1,0:T(8,128)S(1)} %collective-permute-done.1, f32[16,32,256]{2,1,0:T(8,128)S(1)} %bitcast.64, f32[4,32,256]{2,1,0:T(8,128)S(1)} %collective-permute-done, f32[24]{0:T(128)S(1)} %copy-done.5, f32[24]{0:T(128)S(1)} %copy-done.6, ...), kind=kLoop, calls=%fused_computation.86 | loop fusion | flops 4128768 | bytes 8651640 | tf_op jit(solution)/shard_map/jit(_where)/select_n | solution.py:111
  33.2 0.4 fusion.75
  33.6 0.6 fusion.50
  34.2 1.3 %fusion.67 = f32[16,32,256]{2,1,0:T(8,128)S(1)} fusion(f32[16,32,256]{2,1,0:T(8,128)S(1)} %fusion.50, f32[16]{0:T(128)S(1)} %get-tuple-element.49, f32[16]{0:T(128)S(1)} %get-tuple-element.42, f32[16]{0:T(128)S(1)} %get-tuple-element.43, f32[16]{0:T(128)S(1)} %get-tuple-element.44, f32[16]{0:T(128)S(1)} %get-tuple-element.45, f32[16]{0:T(128)S(1)} %get-tuple-element.46, ...), kind=kLoop, calls=%fused_computation.127 | loop fusion | flops 2228224 | bytes 1049152 | tf_op jit(solution)/shard_map/log | solution.py:123
  35.6 1.4 %gather_fusion.15 = f32[4,4,4,8,256]{4,3,2,1,0:T(8,128)} fusion(f32[4,4,4,8,256]{4,3,2,1,0:T(8,128)S(1)} %bitcast.62, s32[1024]{0:T(1024)S(1)} %pad_clamp_fusion.1), kind=kCustom, calls=%fused_computation.15 | custom fusion | bytes 1048592 | tf_op jit(solution)/shard_map/jit(_take)/gather | solution.py:124
  36.9 8.2 %all-to-all-start.1 = ((f32[16,4,8,256]{3,2,1,0:T(8,128)}), f32[16,4,8,256]{3,2,1,0:T(8,128)S(1)}, u32[]{:S(2)}, u32[]{:S(2)}) async-start(f32[16,4,8,256]{3,2,1,0:T(8,128)} %bitcast.29), calls=%async_computation.1 | async-start | bytes 1048576 | tf_op jit(solution)/shard_map/all_to_all | solution.py:126
  45.3 0.2 fusion.88
  45.4 0.1 select_reduce_fusion
  45.6 15.1 %all-to-all-done.1 = f32[16,4,8,256]{3,2,1,0:T(8,128)S(1)} async-done(((f32[16,4,8,256]{3,2,1,0:T(8,128)}), f32[16,4,8,256]{3,2,1,0:T(8,128)S(1)}, u32[]{:S(2)}, u32[]{:S(2)}) %all-to-all-start.1) | async-done | bytes 524320 | tf_op jit(solution)/shard_map/all_to_all | solution.py:126
  60.7 0.6 gather_fusion.16
  61.4 15.8 %all_gather.3 = f32[16,32,256]{2,1,0:T(8,128)S(1)} all-gather(f32[4,32,256]{2,1,0:T(8,128)S(1)} %bitcast_multiply_fusion), channel_id=1, replica_groups=mesh['tile'=2,'dom'=4,'view'=4] {'view'}, dimensions={0}, use_global_device_ids=true | all-gather | bytes 655360 | tf_op jit(solution)/shard_map/all_gather | solution.py:144
  77.2 0.8 %copy.25 = f32[16,32,256]{2,1,0:T(8,128)} copy(f32[16,32,256]{2,1,0:T(8,128)S(1)} %all_gather.3) | data formatting | bytes 1048576
  (119 shorter events, 1.0 us)
Async XLA Ops:
  0.0 14.8 %copy-start = (s32[1,64]{1,0:T(1,128)S(1)}, s32[1,64]{1,0:T(1,128)}, u32[]{:S(2)}) copy-start(s32[1,64]{1,0:T(1,128)} %param.9) | copy-start | bytes 772
  2.7 1.8 %copy-start.1 = (f32[16,32,256]{2,1,0:T(8,128)S(1)}, f32[16,32,256]{2,1,0:T(8,128)}, u32[]{:S(2)}) copy-start(f32[16,32,256]{2,1,0:T(8,128)} %param.5) | copy-start | bytes 1572868
  6.1 4.4 %copy-start.2 = (f32[1,16,32,256]{3,2,1,0:T(8,128)S(1)}, f32[1,16,32,256]{3,2,1,0:T(8,128)}, u32[]{:S(2)}) copy-start(f32[1,16,32,256]{3,2,1,0:T(8,128)} %param.6) | copy-start | bytes 1572868
  6.1 18.8 %all-to-all-start = ((f32[32,4,8,256]{3,2,0,1:T(8,128)}), f32[32,4,8,256]{3,2,0,1:T(8,128)S(1)}, u32[]{:S(2)}, u32[]{:S(2)}) async-start(f32[32,4,8,256]{3,2,0,1:T(8,128)} %pad_maximum_fusion), calls=%async_computation | async-start | bytes 2097152 | tf_op jit(solution)/shard_map/all_to_all | solution.py:81
  10.5 5.0 %copy-start.3 = (f32[1,4,3,9]{3,1,2,0:T(4,128)S(1)}, f32[1,4,3,9]{3,1,2,0:T(4,128)}, u32[]{:S(2)}) copy-start(f32[1,4,3,9]{3,1,2,0:T(4,128)} %param.7) | copy-start | bytes 1300
  10.5 21.5 %collective-permute-start = (f32[4,32,256]{2,1,0:T(8,128)S(1)}, f32[4,32,256]{2,1,0:T(8,128)S(1)}, u32[]{:S(2)}, u32[]{:S(2)}) collective-permute-start(f32[4,32,256]{2,1,0:T(8,128)S(1)} %get-tuple-element.63), channel_id=1, source_target_pairs={{0,4},{4,8},{8,12},{1,5},{5,9},{9,13},{2,6},{6,10},{10,14},{3,7},{... | collective-permute-start | bytes 393224 | tf_op jit(solution)/shard_map/ppermute | solution.py:19
  13.0 19.0 %collective-permute-start.1 = (f32[4,32,256]{2,1,0:T(8,128)S(1)}, f32[4,32,256]{2,1,0:T(8,128)S(1)}, u32[]{:S(2)}, u32[]{:S(2)}) collective-permute-start(f32[4,32,256]{2,1,0:T(8,128)S(1)} %get-tuple-element.64), channel_id=1, source_target_pairs={{4,0},{8,4},{12,8},{5,1},{9,5},{13,9},{6,2},{10,6},{14,10},{7,3},{... | collective-permute-start | bytes 393224 | tf_op jit(solution)/shard_map/ppermute | solution.py:20
  26.3 0.7 copy-start.40
  27.0 0.7 copy-start.30
  27.0 0.7 copy-start.31
  27.0 0.7 copy-start.32
  27.0 0.7 copy-start.33
  27.0 0.7 copy-start.34
  27.1 0.7 copy-start.35
  27.1 0.7 copy-start.36
  27.1 0.7 copy-start.37
  27.1 0.7 copy-start.38
  27.7 2.8 %copy-start.21 = (f32[32]{0:T(128)S(1)}, f32[32]{0:T(128)}, u32[]{:S(2)}) copy-start(f32[32]{0:T(128)} %get-tuple-element.5) | copy-start | bytes 388
  27.7 2.8 %copy-start.22 = (f32[32]{0:T(128)S(1)}, f32[32]{0:T(128)}, u32[]{:S(2)}) copy-start(f32[32]{0:T(128)} %get-tuple-element.6) | copy-start | bytes 388
  27.7 2.8 %copy-start.23 = (f32[32]{0:T(128)S(1)}, f32[32]{0:T(128)}, u32[]{:S(2)}) copy-start(f32[32]{0:T(128)} %get-tuple-element.7) | copy-start | bytes 388
  27.8 2.8 %copy-start.24 = (f32[32]{0:T(128)S(1)}, f32[32]{0:T(128)}, u32[]{:S(2)}) copy-start(f32[32]{0:T(128)} %get-tuple-element.8) | copy-start | bytes 388
  27.8 2.8 %copy-start.25 = (f32[32]{0:T(128)S(1)}, f32[32]{0:T(128)}, u32[]{:S(2)}) copy-start(f32[32]{0:T(128)} %get-tuple-element.9) | copy-start | bytes 388
  27.8 2.8 %copy-start.26 = (f32[32]{0:T(128)S(1)}, f32[32]{0:T(128)}, u32[]{:S(2)}) copy-start(f32[32]{0:T(128)} %get-tuple-element.10) | copy-start | bytes 388
  27.8 2.8 %copy-start.27 = (f32[32]{0:T(128)S(1)}, f32[32]{0:T(128)}, u32[]{:S(2)}) copy-start(f32[32]{0:T(128)} %get-tuple-element.11) | copy-start | bytes 388
  27.8 2.8 %copy-start.28 = (f32[32]{0:T(128)S(1)}, f32[32]{0:T(128)}, u32[]{:S(2)}) copy-start(f32[32]{0:T(128)} %get-tuple-element.12) | copy-start | bytes 388
  27.8 2.8 %copy-start.29 = (f32[32]{0:T(128)S(1)}, f32[32]{0:T(128)}, u32[]{:S(2)}) copy-start(f32[32]{0:T(128)} %get-tuple-element.13) | copy-start | bytes 388
  30.6 1.4 %copy-start.4 = (f32[24]{0:T(128)S(1)}, f32[24]{0:T(128)}, u32[]{:S(2)}) copy-start(f32[24]{0:T(128)} %get-tuple-element.32) | copy-start | bytes 292
  30.6 1.4 %copy-start.5 = (f32[24]{0:T(128)S(1)}, f32[24]{0:T(128)}, u32[]{:S(2)}) copy-start(f32[24]{0:T(128)} %get-tuple-element.33) | copy-start | bytes 292
  30.6 1.4 %copy-start.6 = (f32[24]{0:T(128)S(1)}, f32[24]{0:T(128)}, u32[]{:S(2)}) copy-start(f32[24]{0:T(128)} %get-tuple-element.34) | copy-start | bytes 292
  30.6 1.4 %copy-start.7 = (f32[24]{0:T(128)S(1)}, f32[24]{0:T(128)}, u32[]{:S(2)}) copy-start(f32[24]{0:T(128)} %get-tuple-element.35) | copy-start | bytes 292
  30.6 1.4 %copy-start.8 = (f32[24]{0:T(128)S(1)}, f32[24]{0:T(128)}, u32[]{:S(2)}) copy-start(f32[24]{0:T(128)} %get-tuple-element.36) | copy-start | bytes 292
  30.6 1.4 %copy-start.9 = (f32[24]{0:T(128)S(1)}, f32[24]{0:T(128)}, u32[]{:S(2)}) copy-start(f32[24]{0:T(128)} %get-tuple-element.37) | copy-start | bytes 292
  30.7 1.4 %copy-start.10 = (f32[24]{0:T(128)S(1)}, f32[24]{0:T(128)}, u32[]{:S(2)}) copy-start(f32[24]{0:T(128)} %get-tuple-element.38) | copy-start | bytes 292
  30.7 1.4 %copy-start.11 = (f32[24]{0:T(128)S(1)}, f32[24]{0:T(128)}, u32[]{:S(2)}) copy-start(f32[24]{0:T(128)} %get-tuple-element.39) | copy-start | bytes 292
  30.7 1.4 %copy-start.12 = (f32[24]{0:T(128)S(1)}, f32[24]{0:T(128)}, u32[]{:S(2)}) copy-start(f32[24]{0:T(128)} %get-tuple-element.40) | copy-start | bytes 292
  30.7 1.4 %copy-start.41 = (pred[24]{0:T(512)(128)(4,1)S(1)}, pred[24]{0:T(512)(128)(4,1)}, u32[]{:S(2)}) copy-start(pred[24]{0:T(512)(128)(4,1)} %compare_and_fusion.1) | copy-start | bytes 76
  32.1 1.0 %copy-start.13 = (f32[16]{0:T(128)S(1)}, f32[16]{0:T(128)}, u32[]{:S(2)}) copy-start(f32[16]{0:T(128)} %get-tuple-element.24) | copy-start | bytes 196
  32.1 1.0 %copy-start.14 = (f32[16]{0:T(128)S(1)}, f32[16]{0:T(128)}, u32[]{:S(2)}) copy-start(f32[16]{0:T(128)} %get-tuple-element.25) | copy-start | bytes 196
  32.1 1.0 %copy-start.15 = (f32[16]{0:T(128)S(1)}, f32[16]{0:T(128)}, u32[]{:S(2)}) copy-start(f32[16]{0:T(128)} %get-tuple-element.26) | copy-start | bytes 196
  32.1 1.0 %copy-start.16 = (f32[16]{0:T(128)S(1)}, f32[16]{0:T(128)}, u32[]{:S(2)}) copy-start(f32[16]{0:T(128)} %get-tuple-element.27) | copy-start | bytes 196
  32.2 1.0 %copy-start.17 = (f32[16]{0:T(128)S(1)}, f32[16]{0:T(128)}, u32[]{:S(2)}) copy-start(f32[16]{0:T(128)} %get-tuple-element.28) | copy-start | bytes 196
  32.2 1.0 %copy-start.18 = (f32[16]{0:T(128)S(1)}, f32[16]{0:T(128)}, u32[]{:S(2)}) copy-start(f32[16]{0:T(128)} %get-tuple-element.29) | copy-start | bytes 196
  32.2 1.0 %copy-start.19 = (f32[16]{0:T(128)S(1)}, f32[16]{0:T(128)}, u32[]{:S(2)}) copy-start(f32[16]{0:T(128)} %get-tuple-element.30) | copy-start | bytes 196
  32.2 1.0 %copy-start.20 = (f32[16]{0:T(128)S(1)}, f32[16]{0:T(128)}, u32[]{:S(2)}) copy-start(f32[16]{0:T(128)} %get-tuple-element.31) | copy-start | bytes 196
  35.5 9.6 %copy-start.39 = (s32[4,16]{1,0:T(4,128)S(1)}, s32[4,16]{1,0:T(4,128)}, u32[]{:S(2)}) copy-start(s32[4,16]{1,0:T(4,128)} %param.8) | copy-start | bytes 772
  36.9 23.8 %all-to-all-start.1 = ((f32[16,4,8,256]{3,2,1,0:T(8,128)}), f32[16,4,8,256]{3,2,1,0:T(8,128)S(1)}, u32[]{:S(2)}, u32[]{:S(2)}) async-start(f32[16,4,8,256]{3,2,1,0:T(8,128)} %bitcast.29), calls=%async_computation.1 | async-start | bytes 1048576 | tf_op jit(solution)/shard_map/all_to_all | solution.py:126

commit v8 on v7

--- a/solution.py
+++ b/solution.py
@@ -61,7 +61,6 @@
     source_dev = grid_map // block_count
     source_slot = grid_map % block_count
     send_slot = jnp.sum(jnp.where(source_dev == dom_index, source_slot, 0), axis=1)
-    blocks = estimate.reshape(plane_count, block_count, block_rows, lane_count)
     kernels = psf[0]
     band_all = depth_band[0]
     total_planes = band_all.shape[0]
@@ -70,27 +69,32 @@
     last = block_count - 1
     above = jnp.take(send_slot, jnp.clip(slot_ids - 1, 0, last), mode="clip")
     below = jnp.take(send_slot, jnp.clip(slot_ids + 1, 0, last), mode="clip")
-    outgoing = jnp.concatenate(
-        [
-            jnp.take(blocks[plane_count - wide :], above, axis=1, mode="clip"),
-            jnp.take(blocks, send_slot, axis=1, mode="clip"),
-            jnp.take(blocks[:wide], below, axis=1, mode="clip"),
-        ],
-        axis=0,
+    wide_count = plane_count + 2 * wide
+    chunk_plane = jnp.arange(wide_count, dtype=jnp.int32)
+    in_top = chunk_plane < wide
+    in_bottom = chunk_plane >= wide + plane_count
+    source_plane = jnp.where(
+        in_top, chunk_plane + plane_count - wide,
+        jnp.where(in_bottom, chunk_plane - wide - plane_count, chunk_plane - wide),
     )
+    source_block = jnp.where(
+        in_top[:, None], above[None, :], jnp.where(in_bottom[:, None], below[None, :], send_slot[None, :])
+    )
+    send_index = (source_plane[:, None] * block_count + source_block).reshape(-1)
+    flat_blocks = estimate.reshape(plane_count * block_count, block_rows, lane_count)
+    outgoing = jnp.take(flat_blocks, send_index, axis=0, mode="clip")
+    outgoing = outgoing.reshape(wide_count, block_count, block_rows, lane_count)
     arrived = lax.all_to_all(outgoing, "dom", split_axis=1, concat_axis=1, tiled=True)
     my_sources = lax.dynamic_index_in_dim(source_dev, dom_index, 0, keepdims=False)
     src_above = lax.dynamic_index_in_dim(source_dev, jnp.maximum(dom_index - 1, 0), 0, keepdims=False)
     src_below = lax.dynamic_index_in_dim(source_dev, jnp.minimum(dom_index + 1, last), 0, keepdims=False)
-    camera_ext = jnp.concatenate(
-        [
-            jnp.take(arrived[:wide], src_above, axis=1, mode="clip"),
-            jnp.take(arrived[wide : wide + plane_count], my_sources, axis=1, mode="clip"),
-            jnp.take(arrived[wide + plane_count :], src_below, axis=1, mode="clip"),
-        ],
-        axis=0,
+    from_block = jnp.where(
+        in_top[:, None], src_above[None, :], jnp.where(in_bottom[:, None], src_below[None, :], my_sources[None, :])
     )
-    wide_count = plane_count + 2 * wide
+    recv_index = (chunk_plane[:, None] * block_count + from_block).reshape(-1)
+    flat_arrived = arrived.reshape(wide_count * block_count, block_rows, lane_count)
+    camera_ext = jnp.take(flat_arrived, recv_index, axis=0, mode="clip")
+    camera_ext = camera_ext.reshape(wide_count, block_count, block_rows, lane_count)
     wide_planes = plane_start - wide + jnp.arange(wide_count, dtype=jnp.int32)
     wide_inside = (wide_planes >= 0) & (wide_planes < total_planes)
     camera_ext = jnp.where(wide_inside[:, None, None, None], camera_ext, 0.0)
@@ -120,8 +124,9 @@
         jnp.where(my_sources[None, :] == slot_ids[:, None], slot_ids[None, :], 0), axis=1
     )
     piece_planes = plane_count // view_count
-    logs = jnp.log(back).reshape(view_count, piece_planes, block_count, block_rows, lane_count)
-    outgoing = jnp.take(logs, dest_slot, axis=2, mode="clip").transpose(2, 0, 1, 3, 4)
+    logs = jnp.log(back).reshape(plane_count * block_count, block_rows, lane_count)
+    piece_index = jnp.arange(plane_count, dtype=jnp.int32)[None, :] * block_count + dest_slot[:, None]
+    outgoing = jnp.take(logs, piece_index.reshape(-1), axis=0, mode="clip")
     outgoing = outgoing.reshape(block_count * view_count, piece_planes, block_rows, lane_count)
     arrived_logs = lax.all_to_all(outgoing, ("dom", "view"), 0, 0, tiled=True)
     all_grid = src_map.reshape(view_count, block_count, block_count)

time: 78.4 us -> 78.8 us (level)
  starting transfers between devices: 16.3 us -> 17.1 us
  waiting for transfers between devices: 15.9 us -> 15.1 us
    gather x7 -> x3, local copies, waits for them, and re-layouts: 4.79 us -> 2.94 us  [the longest x1 1.43 us: body(): outgoing = jnp.take(logs, piece_index.reshape(-1), axis=0, mode='clip')]
    slice x6 -> x0, local copies, waits for them, and re-layouts: 1.23 us -> none  [the longest x1 1.07 us: body(): blocks[plane_count - wide:]]
    slice x4, local copies, waits for them, and re-layouts: 2.37 us -> 3.49 us  [taps_along(): total = total + taps[:, offset][:, None, None] * piece]
    reshape x0 -> x1, local copies, waits for them, and re-layouts: none -> 1.07 us  [body(): outgoing = outgoing.reshape(wide_count, block_count, block_rows, lane_count)]
    concatenate x1 -> x0, other arithmetic: 1.06 us -> none  [body(): jnp.concatenate([jnp.take(blocks[plane_count - wide:], above, axis=1, mod...]
    mul x1, other arithmetic: 0.06 us -> 0.96 us  [body(): updated = est_piece * jnp.exp(log_total / view_count)]
    all_to_all x1, waiting for transfers between devices: 0.81 us -> 0.01 us  [body(): lax.all_to_all(outgoing, 'dom', split_axis=1, concat_axis=1, tiled=True)]
    all_to_all x1, starting transfers between devices: 8.22 us -> 9.02 us  [body(): arrived_logs = lax.all_to_all(outgoing, ('dom', 'view'), 0, 0, tiled=True)]
  transfers between devices with their start and end apart: 4 -> 4, of which waited for: 2 -> 1; matrix products, arithmetic and copies ran while one was open for 21% -> 22% of each run, Pallas kernels for 0% -> 0%
where the time goes in v8:
time: 78.8 us; the launch traced here: 78.4 us
  local copies, waits for them, and re-layouts  19.2 us (24%)
  starting transfers between devices  17.1 us (22%)
  blocking collectives  15.8 us (20%)
  waiting for transfers between devices  15.1 us (19%)
  other arithmetic  10.2 us (13%)
  between operations  1.05 us (1%)
    all_gather x1, blocking collectives, body(): return lax.all_gather(updated, 'view', axis=0, tiled=True)  15.8 us
    all_to_all x1, waiting for transfers between devices, body(): arrived_logs = lax.all_to_all(outgoing, ('dom', 'view'), 0, 0, tiled=True)  15.1 us
    all_to_all x1, starting transfers between devices, body(): arrived_logs = lax.all_to_all(outgoing, ('dom', 'view'), 0, 0, tiled=True)  9.02 us
    add x3, other arithmetic, taps_along(): total = total + taps[:, offset][:, None, None] * piece  4.57 us
    all_to_all x1, starting transfers between devices, body(): lax.all_to_all(outgoing, 'dom', split_axis=1, concat_axis=1, tiled=True)  4.37 us
    slice x4, local copies, waits for them, and re-layouts, taps_along(): total = total + taps[:, offset][:, None, None] * piece  3.49 us
    ppermute x1, starting transfers between devices, extended_2(): before = lax.ppermute(last, axis, up)  2.41 us
    unnamed x123, local copies, waits for them, and re-layouts  1.66 us
  transfers between devices with their start and end apart: 4, of which 1 were waited for; matrix products, arithmetic and copies ran while one was open for 22% of the time, Pallas kernels for 0%

profile of v8, /device:TPU:0, one launch (start us, length us, event | category | flops | bytes accessed | tf_op | source)
XLA Modules:
  0.0 78.4 jit_solution(14651750233157888259)
XLA Ops:
  0.0 0.8 fusion.97
  0.9 0.1 fusion.91
  1.0 0.6 gather_fusion.7
  1.7 0.6 gather_fusion.8
  2.4 0.1 reshape.456
  2.5 0.8 gather_fusion.9
  3.3 1.1 %copy.8 = f32[32,4,8,256]{3,2,0,1:T(8,128)} copy(f32[32,4,8,256]{3,2,1,0:T(8,128)S(1)} %bitcast.46) | data formatting | bytes 2097152 | tf_op jit(solution)/shard_map/reshape | solution.py:86
  4.4 4.4 %all-to-all-start = ((f32[32,4,8,256]{3,2,0,1:T(8,128)}), f32[32,4,8,256]{3,2,0,1:T(8,128)S(1)}, u32[]{:S(2)}, u32[]{:S(2)}) async-start(f32[32,4,8,256]{3,2,0,1:T(8,128)} %copy.8), calls=%async_computation | async-start | bytes 2097152 | tf_op jit(solution)/shard_map/all_to_all | solution.py:87
  8.8 0.7 slice_bitcast_fusion.1
  9.4 2.4 %collective-permute-start = (f32[4,32,256]{2,1,0:T(8,128)}, f32[4,32,256]{2,1,0:T(8,128)S(1)}, u32[]{:S(2)}, u32[]{:S(2)}) collective-permute-start(f32[4,32,256]{2,1,0:T(8,128)} %get-tuple-element.61), channel_id=1, source_target_pairs={{0,4},{4,8},{8,12},{1,5},{5,9},{9,13},{2,6},{6,10},{10,14},{3,7},{... | collective-permute-start | bytes 393224 | tf_op jit(solution)/shard_map/ppermute | solution.py:19
  11.8 1.3 %collective-permute-start.1 = (f32[4,32,256]{2,1,0:T(8,128)S(1)}, f32[4,32,256]{2,1,0:T(8,128)S(1)}, u32[]{:S(2)}, u32[]{:S(2)}) collective-permute-start(f32[4,32,256]{2,1,0:T(8,128)S(1)} %get-tuple-element.62), channel_id=1, source_target_pairs={{4,0},{8,4},{12,8},{5,1},{9,5},{13,9},{6,2},{10,6},{14,10},{7,3},{... | collective-permute-start | bytes 393224 | tf_op jit(solution)/shard_map/ppermute | solution.py:20
  13.1 0.6 compare_and_fusion
  13.8 0.7 gather_fusion.4
  14.5 0.6 gather_fusion.6
  15.1 0.6 gather_fusion.5
  15.7 0.6 gather_fusion.1
  16.3 0.6 gather_fusion
  16.8 0.1 select_reduce_fusion.1
  17.0 0.1 reshape.464
  17.1 0.7 gather_fusion.2
  18.0 0.6 gather_fusion.3
  18.6 0.5 compare_and_fusion.1
  19.1 0.9 %slice_reduce_fusion.52 = (f32[16]{0:T(128)}, f32[16]{0:T(128)}, f32[16]{0:T(128)}, f32[16]{0:T(128)}, f32[16]{0:T(128)}, /*index=5*/f32[16]{0:T(128)}, f32[16]{0:T(128)}, f32[16]{0:T(128)}, f32[16]{0:T(128)}) fusion(f32[16,9]{1,0:T(8,128)S(1)} %gather_fusion.1), kind=kLoop, calls=%fused_computation.218 | loop fusion | bytes 1152 | tf_op jit(solution)/shard_map/slice | solution.py:36
  20.0 0.9 %slice_reduce_fusion.53 = (f32[16]{0:T(128)S(1)}, f32[16]{0:T(128)}, f32[16]{0:T(128)}, f32[16]{0:T(128)}, f32[16]{0:T(128)}, /*index=5*/f32[16]{0:T(128)}, f32[16]{0:T(128)}, f32[16]{0:T(128)}, f32[16]{0:T(128)}) fusion(f32[16,9]{1,0:T(8,128)S(1)} %gather_fusion), kind=kLoop, calls=%fused_computation.219 | loop fusion | bytes 1152 | tf_op jit(solution)/shard_map/slice | solution.py:36
  20.9 0.9 %slice_reduce_fusion.26 = (f32[24]{0:T(128)}, f32[24]{0:T(128)}, f32[24]{0:T(128)}, f32[24]{0:T(128)}, f32[24]{0:T(128)}, /*index=5*/f32[24]{0:T(128)}, f32[24]{0:T(128)}, f32[24]{0:T(128)}, f32[24]{0:T(128)}) fusion(f32[24,9]{1,0:T(8,128)S(1)} %gather_fusion.3), kind=kLoop, calls=%fused_computation.184 | loop fusion | bytes 1728 | tf_op jit(solution)/shard_map/slice | solution.py:113
  21.7 0.9 %slice_reduce_fusion.16 = (f32[32]{0:T(128)}, f32[32]{0:T(128)}, f32[32]{0:T(128)}, f32[32]{0:T(128)}, f32[32]{0:T(128)}, /*index=5*/f32[32]{0:T(128)}, f32[32]{0:T(128)}, f32[32]{0:T(128)}, f32[32]{0:T(128)}) fusion(f32[32,9]{1,0:T(8,128)S(1)} %gather_fusion.6), kind=kLoop, calls=%fused_computation.172 | loop fusion | bytes 2304 | tf_op jit(solution)/shard_map/slice | solution.py:36
  22.6 0.9 %slice_reduce_fusion.17 = (f32[32]{0:T(128)}, f32[32]{0:T(128)}, f32[32]{0:T(128)}, f32[32]{0:T(128)}, f32[32]{0:T(128)}, /*index=5*/f32[32]{0:T(128)}, f32[32]{0:T(128)}, f32[32]{0:T(128)}, f32[32]{0:T(128)}) fusion(f32[32,9]{1,0:T(8,128)S(1)} %gather_fusion.5), kind=kLoop, calls=%fused_computation.173 | loop fusion | bytes 2304 | tf_op jit(solution)/shard_map/slice | solution.py:36
  23.5 0.9 %slice_reduce_fusion.51 = (f32[16]{0:T(128)}, f32[16]{0:T(128)}, f32[16]{0:T(128)}, f32[16]{0:T(128)}, f32[16]{0:T(128)}, /*index=5*/f32[16]{0:T(128)}, f32[16]{0:T(128)}, f32[16]{0:T(128)}, f32[16]{0:T(128)}) fusion(f32[24,9]{1,0:T(8,128)S(1)} %gather_fusion.3), kind=kLoop, calls=%fused_computation.217 | loop fusion | bytes 1152 | tf_op jit(solution)/shard_map/slice | solution.py:121
  24.3 0.1 copy.9
  24.5 0.8 gather_fusion.10
  25.4 0.1 bitcast_select_fusion
  25.5 0.4 copy-done.49
  26.1 2.7 %fusion.24 = f32[32,32,256]{2,1,0:T(8,128)S(1)} fusion(f32[32,32,256]{2,1,0:T(8,128)S(1)} %bitcast_select_fusion, f32[32]{0:T(128)S(1)} %copy-done.57, f32[32]{0:T(128)S(1)} %copy-done.50, f32[32]{0:T(128)S(1)} %copy-done.51, f32[32]{0:T(128)S(1)} %copy-done.52, f32[32]{0:T(128)S(1)} %copy-done.53, f32[32]{0:T(128)S(1)} %copy-done.54, f32[32]{0:T(128)S(1)} %copy-done.55, ...), kind=kLoop, calls=%fused_computation.61 | loop fusion | flops 4456448 | bytes 2098304 | tf_op jit(solution)/shard_map/add | solution.py:36
  29.0 1.3 %fusion.8 = f32[32,32,256]{2,1,0:T(8,128)S(1)} fusion(f32[32,32,256]{2,1,0:T(8,128)S(1)} %fusion.24, f32[32]{0:T(128)S(1)} %copy-done.48, f32[32]{0:T(128)S(1)} %copy-done.41, f32[32]{0:T(128)S(1)} %copy-done.42, f32[32]{0:T(128)S(1)} %copy-done.43, f32[32]{0:T(128)S(1)} %copy-done.44, f32[32]{0:T(128)S(1)} %copy-done.45, f32[32]{0:T(128)S(1)} %copy-done.46, ...), kind=kLoop, calls=%fused_computation.45 | loop fusion | flops 4456448 | bytes 2098304 | tf_op jit(solution)/shard_map/add | solution.py:36
  30.5 0.9 %fusion.34 = f32[24,32,256]{2,1,0:T(8,128)S(1)} fusion(f32[32,32,256]{2,1,0:T(8,128)S(1)} %fusion.8, f32[4,32,256]{2,1,0:T(8,128)S(1)} %collective-permute-done.1, f32[16,32,256]{2,1,0:T(8,128)S(1)} %bitcast.49, f32[4,32,256]{2,1,0:T(8,128)S(1)} %collective-permute-done, f32[24]{0:T(128)S(1)} %copy-done.23, f32[24]{0:T(128)S(1)} %copy-done.24, ...), kind=kLoop, calls=%fused_computation.81 | loop fusion | flops 4128768 | bytes 8651640 | tf_op jit(solution)/shard_map/jit(_where)/select_n | solution.py:115
  31.6 0.4 fusion.75
  32.1 0.1 copy-done.13
  32.2 0.6 fusion.50
  32.9 1.3 %fusion.67 = f32[16,32,256]{2,1,0:T(8,128)S(1)} fusion(f32[16,32,256]{2,1,0:T(8,128)S(1)} %fusion.50, f32[16]{0:T(128)S(1)} %copy-done.12, f32[16]{0:T(128)S(1)} %copy-done.5, f32[16]{0:T(128)S(1)} %copy-done.6, f32[16]{0:T(128)S(1)} %copy-done.7, f32[16]{0:T(128)S(1)} %copy-done.8, f32[16]{0:T(128)S(1)} %copy-done.9, f32[16]{0:T(128)S(1)} %copy-done.10, ...), kind=kLoop, calls=%fused_computation.122 | loop fusion | flops 2228224 | bytes 1049152 | tf_op jit(solution)/shard_map/log | solution.py:127
  34.3 1.4 %gather_fusion.11 = f32[64,8,256]{2,1,0:T(8,128)} fusion(f32[64,8,256]{2,1,0:T(8,128)S(1)} %bitcast.48, s32[1024]{0:T(1024)S(1)} %pad_clamp_fusion.1), kind=kCustom, calls=%fused_computation.11 | custom fusion | bytes 1048832 | tf_op jit(solution)/shard_map/jit(_take)/gather | solution.py:129
  35.7 9.0 %all-to-all-start.1 = ((f32[16,4,8,256]{3,2,1,0:T(8,128)}), f32[16,4,8,256]{3,2,1,0:T(8,128)S(1)}, u32[]{:S(2)}, u32[]{:S(2)}) async-start(f32[16,4,8,256]{3,2,1,0:T(8,128)} %bitcast.21), calls=%async_computation.1 | async-start | bytes 1048576 | tf_op jit(solution)/shard_map/all_to_all | solution.py:131
  44.8 0.2 fusion.88
  45.0 0.1 select_reduce_fusion
  45.2 15.1 %all-to-all-done.1 = f32[16,4,8,256]{3,2,1,0:T(8,128)S(1)} async-done(((f32[16,4,8,256]{3,2,1,0:T(8,128)}), f32[16,4,8,256]{3,2,1,0:T(8,128)S(1)}, u32[]{:S(2)}, u32[]{:S(2)}) %all-to-all-start.1) | async-done | bytes 524320 | tf_op jit(solution)/shard_map/all_to_all | solution.py:131
  60.3 0.6 gather_fusion.12
  60.9 1.0 %bitcast_multiply_fusion = f32[4,32,256]{2,1,0:T(8,128)S(1)} fusion(f32[16,32,256]{2,1,0:T(8,128)} %param.5, s32[]{:T(128)S(6)} %select_n.139, f32[16,4,8,256]{3,2,1,0:T(8,128)S(1)} %gather_fusion.12), kind=kLoop, calls=%fused_computation.153 | loop fusion | flops 163840 | bytes 786436 | tf_op jit(solution)/shard_map/mul | solution.py:148
  61.8 15.8 %all_gather.3 = f32[16,32,256]{2,1,0:T(8,128)S(1)} all-gather(f32[4,32,256]{2,1,0:T(8,128)S(1)} %bitcast_multiply_fusion), channel_id=1, replica_groups=mesh['tile'=2,'dom'=4,'view'=4] {'view'}, dimensions={0}, use_global_device_ids=true | all-gather | bytes 655360 | tf_op jit(solution)/shard_map/all_gather | solution.py:149
  77.6 0.8 %copy.13 = f32[16,32,256]{2,1,0:T(8,128)} copy(f32[16,32,256]{2,1,0:T(8,128)S(1)} %all_gather.3) | data formatting | bytes 1048576
  (150 shorter events, 1.0 us)
Async XLA Ops:
  0.0 13.8 %copy-start = (s32[1,64]{1,0:T(1,128)S(1)}, s32[1,64]{1,0:T(1,128)}, u32[]{:S(2)}) copy-start(s32[1,64]{1,0:T(1,128)} %param.9) | copy-start | bytes 772
  0.0 2.5 %copy-start.1 = (f32[16,32,256]{2,1,0:T(8,128)S(1)}, f32[16,32,256]{2,1,0:T(8,128)}, u32[]{:S(2)}) copy-start(f32[16,32,256]{2,1,0:T(8,128)} %param.5) | copy-start | bytes 1572868
  4.4 4.4 %copy-start.2 = (f32[1,16,32,256]{3,2,1,0:T(8,128)S(1)}, f32[1,16,32,256]{3,2,1,0:T(8,128)}, u32[]{:S(2)}) copy-start(f32[1,16,32,256]{3,2,1,0:T(8,128)} %param.6) | copy-start | bytes 1572868
  4.4 20.0 %all-to-all-start = ((f32[32,4,8,256]{3,2,0,1:T(8,128)}), f32[32,4,8,256]{3,2,0,1:T(8,128)S(1)}, u32[]{:S(2)}, u32[]{:S(2)}) async-start(f32[32,4,8,256]{3,2,0,1:T(8,128)} %copy.8), calls=%async_computation | async-start | bytes 2097152 | tf_op jit(solution)/shard_map/all_to_all | solution.py:87
  8.8 5.7 %copy-start.4 = (f32[1,4,3,9]{3,1,2,0:T(4,128)S(1)}, f32[1,4,3,9]{3,1,2,0:T(4,128)}, u32[]{:S(2)}) copy-start(f32[1,4,3,9]{3,1,2,0:T(4,128)} %param.7) | copy-start | bytes 1300
  9.4 20.9 %collective-permute-start = (f32[4,32,256]{2,1,0:T(8,128)}, f32[4,32,256]{2,1,0:T(8,128)S(1)}, u32[]{:S(2)}, u32[]{:S(2)}) collective-permute-start(f32[4,32,256]{2,1,0:T(8,128)} %get-tuple-element.61), channel_id=1, source_target_pairs={{0,4},{4,8},{8,12},{1,5},{5,9},{9,13},{2,6},{6,10},{10,14},{3,7},{... | collective-permute-start | bytes 393224 | tf_op jit(solution)/shard_map/ppermute | solution.py:19
  11.8 18.5 %collective-permute-start.1 = (f32[4,32,256]{2,1,0:T(8,128)S(1)}, f32[4,32,256]{2,1,0:T(8,128)S(1)}, u32[]{:S(2)}, u32[]{:S(2)}) collective-permute-start(f32[4,32,256]{2,1,0:T(8,128)S(1)} %get-tuple-element.62), channel_id=1, source_target_pairs={{4,0},{8,4},{12,8},{5,1},{9,5},{13,9},{6,2},{10,6},{14,10},{7,3},{... | collective-permute-start | bytes 393224 | tf_op jit(solution)/shard_map/ppermute | solution.py:20
  24.5 0.8 copy-start.59
  25.3 0.7 copy-start.49
  26.0 2.8 %copy-start.40 = (f32[32]{0:T(128)S(1)}, f32[32]{0:T(128)}, u32[]{:S(2)}) copy-start(f32[32]{0:T(128)} %get-tuple-element.5) | copy-start | bytes 388
  26.0 2.8 %copy-start.41 = (f32[32]{0:T(128)S(1)}, f32[32]{0:T(128)}, u32[]{:S(2)}) copy-start(f32[32]{0:T(128)} %get-tuple-element.6) | copy-start | bytes 388
  26.0 2.8 %copy-start.42 = (f32[32]{0:T(128)S(1)}, f32[32]{0:T(128)}, u32[]{:S(2)}) copy-start(f32[32]{0:T(128)} %get-tuple-element.7) | copy-start | bytes 388
  26.0 2.8 %copy-start.43 = (f32[32]{0:T(128)S(1)}, f32[32]{0:T(128)}, u32[]{:S(2)}) copy-start(f32[32]{0:T(128)} %get-tuple-element.8) | copy-start | bytes 388
  26.0 2.8 %copy-start.44 = (f32[32]{0:T(128)S(1)}, f32[32]{0:T(128)}, u32[]{:S(2)}) copy-start(f32[32]{0:T(128)} %get-tuple-element.9) | copy-start | bytes 388
  26.1 2.8 %copy-start.45 = (f32[32]{0:T(128)S(1)}, f32[32]{0:T(128)}, u32[]{:S(2)}) copy-start(f32[32]{0:T(128)} %get-tuple-element.10) | copy-start | bytes 388
  26.1 2.8 %copy-start.46 = (f32[32]{0:T(128)S(1)}, f32[32]{0:T(128)}, u32[]{:S(2)}) copy-start(f32[32]{0:T(128)} %get-tuple-element.11) | copy-start | bytes 388
  26.1 2.8 %copy-start.47 = (f32[32]{0:T(128)S(1)}, f32[32]{0:T(128)}, u32[]{:S(2)}) copy-start(f32[32]{0:T(128)} %get-tuple-element.12) | copy-start | bytes 388
  26.1 2.8 %copy-start.48 = (f32[32]{0:T(128)S(1)}, f32[32]{0:T(128)}, u32[]{:S(2)}) copy-start(f32[32]{0:T(128)} %get-tuple-element.13) | copy-start | bytes 388
  28.9 1.4 %copy-start.3 = (f32[1,16,32,256]{3,2,1,0:T(8,128)S(1)}, f32[1,16,32,256]{3,2,1,0:T(8,128)}, u32[]{:S(2)}) copy-start(f32[1,16,32,256]{3,2,1,0:T(8,128)} %param.6) | copy-start | bytes 1572868
  28.9 1.4 %copy-start.22 = (f32[24]{0:T(128)S(1)}, f32[24]{0:T(128)}, u32[]{:S(2)}) copy-start(f32[24]{0:T(128)} %get-tuple-element.32) | copy-start | bytes 292
  28.9 1.4 %copy-start.23 = (f32[24]{0:T(128)S(1)}, f32[24]{0:T(128)}, u32[]{:S(2)}) copy-start(f32[24]{0:T(128)} %get-tuple-element.33) | copy-start | bytes 292
  28.9 1.4 %copy-start.24 = (f32[24]{0:T(128)S(1)}, f32[24]{0:T(128)}, u32[]{:S(2)}) copy-start(f32[24]{0:T(128)} %get-tuple-element.34) | copy-start | bytes 292
  28.9 1.4 %copy-start.25 = (f32[24]{0:T(128)S(1)}, f32[24]{0:T(128)}, u32[]{:S(2)}) copy-start(f32[24]{0:T(128)} %get-tuple-element.35) | copy-start | bytes 292
  28.9 1.4 %copy-start.26 = (f32[24]{0:T(128)S(1)}, f32[24]{0:T(128)}, u32[]{:S(2)}) copy-start(f32[24]{0:T(128)} %get-tuple-element.36) | copy-start | bytes 292
  28.9 1.4 %copy-start.27 = (f32[24]{0:T(128)S(1)}, f32[24]{0:T(128)}, u32[]{:S(2)}) copy-start(f32[24]{0:T(128)} %get-tuple-element.37) | copy-start | bytes 292
  28.9 1.4 %copy-start.28 = (f32[24]{0:T(128)S(1)}, f32[24]{0:T(128)}, u32[]{:S(2)}) copy-start(f32[24]{0:T(128)} %get-tuple-element.38) | copy-start | bytes 292
  29.0 1.4 %copy-start.29 = (f32[24]{0:T(128)S(1)}, f32[24]{0:T(128)}, u32[]{:S(2)}) copy-start(f32[24]{0:T(128)} %get-tuple-element.39) | copy-start | bytes 292
  29.0 1.4 %copy-start.30 = (f32[24]{0:T(128)S(1)}, f32[24]{0:T(128)}, u32[]{:S(2)}) copy-start(f32[24]{0:T(128)} %get-tuple-element.40) | copy-start | bytes 292
  29.0 1.4 %copy-start.60 = (pred[24]{0:T(512)(128)(4,1)S(1)}, pred[24]{0:T(512)(128)(4,1)}, u32[]{:S(2)}) copy-start(pred[24]{0:T(512)(128)(4,1)} %compare_and_fusion.1) | copy-start | bytes 76
  30.4 1.0 %copy-start.31 = (f32[16]{0:T(128)S(1)}, f32[16]{0:T(128)}, u32[]{:S(2)}) copy-start(f32[16]{0:T(128)} %get-tuple-element.23) | copy-start | bytes 196
  30.4 1.0 %copy-start.32 = (f32[16]{0:T(128)S(1)}, f32[16]{0:T(128)}, u32[]{:S(2)}) copy-start(f32[16]{0:T(128)} %get-tuple-element.24) | copy-start | bytes 196
  30.4 1.0 %copy-start.33 = (f32[16]{0:T(128)S(1)}, f32[16]{0:T(128)}, u32[]{:S(2)}) copy-start(f32[16]{0:T(128)} %get-tuple-element.25) | copy-start | bytes 196
  30.4 1.0 %copy-start.34 = (f32[16]{0:T(128)S(1)}, f32[16]{0:T(128)}, u32[]{:S(2)}) copy-start(f32[16]{0:T(128)} %get-tuple-element.26) | copy-start | bytes 196
  30.5 1.0 %copy-start.35 = (f32[16]{0:T(128)S(1)}, f32[16]{0:T(128)}, u32[]{:S(2)}) copy-start(f32[16]{0:T(128)} %get-tuple-element.27) | copy-start | bytes 196
  30.5 1.0 %copy-start.36 = (f32[16]{0:T(128)S(1)}, f32[16]{0:T(128)}, u32[]{:S(2)}) copy-start(f32[16]{0:T(128)} %get-tuple-element.28) | copy-start | bytes 196
  30.5 1.0 %copy-start.37 = (f32[16]{0:T(128)S(1)}, f32[16]{0:T(128)}, u32[]{:S(2)}) copy-start(f32[16]{0:T(128)} %get-tuple-element.29) | copy-start | bytes 196
  30.5 1.0 %copy-start.38 = (f32[16]{0:T(128)S(1)}, f32[16]{0:T(128)}, u32[]{:S(2)}) copy-start(f32[16]{0:T(128)} %get-tuple-element.30) | copy-start | bytes 196
  30.5 1.0 %copy-start.39 = (f32[16]{0:T(128)S(1)}, f32[16]{0:T(128)}, u32[]{:S(2)}) copy-start(f32[16]{0:T(128)} %get-tuple-element.31) | copy-start | bytes 196
  32.0 0.8 %copy-start.5 = (f32[16]{0:T(128)S(1)}, f32[16]{0:T(128)}, u32[]{:S(2)}) copy-start(f32[16]{0:T(128)} %get-tuple-element.42) | copy-start | bytes 196
  32.0 0.8 %copy-start.6 = (f32[16]{0:T(128)S(1)}, f32[16]{0:T(128)}, u32[]{:S(2)}) copy-start(f32[16]{0:T(128)} %get-tuple-element.43) | copy-start | bytes 196
  32.0 0.8 %copy-start.7 = (f32[16]{0:T(128)S(1)}, f32[16]{0:T(128)}, u32[]{:S(2)}) copy-start(f32[16]{0:T(128)} %get-tuple-element.44) | copy-start | bytes 196
  32.0 0.8 %copy-start.8 = (f32[16]{0:T(128)S(1)}, f32[16]{0:T(128)}, u32[]{:S(2)}) copy-start(f32[16]{0:T(128)} %get-tuple-element.45) | copy-start | bytes 196
  32.0 0.8 %copy-start.9 = (f32[16]{0:T(128)S(1)}, f32[16]{0:T(128)}, u32[]{:S(2)}) copy-start(f32[16]{0:T(128)} %get-tuple-element.46) | copy-start | bytes 196
  32.1 0.8 %copy-start.10 = (f32[16]{0:T(128)S(1)}, f32[16]{0:T(128)}, u32[]{:S(2)}) copy-start(f32[16]{0:T(128)} %get-tuple-element.47) | copy-start | bytes 196
  32.1 0.8 %copy-start.11 = (f32[16]{0:T(128)S(1)}, f32[16]{0:T(128)}, u32[]{:S(2)}) copy-start(f32[16]{0:T(128)} %get-tuple-element.48) | copy-start | bytes 196
  32.1 0.8 %copy-start.12 = (f32[16]{0:T(128)S(1)}, f32[16]{0:T(128)}, u32[]{:S(2)}) copy-start(f32[16]{0:T(128)} %get-tuple-element.49) | copy-start | bytes 196
  34.3 10.5 %copy-start.58 = (s32[4,16]{1,0:T(4,128)S(1)}, s32[4,16]{1,0:T(4,128)}, u32[]{:S(2)}) copy-start(s32[4,16]{1,0:T(4,128)} %param.8) | copy-start | bytes 772
  35.7 24.6 %all-to-all-start.1 = ((f32[16,4,8,256]{3,2,1,0:T(8,128)}), f32[16,4,8,256]{3,2,1,0:T(8,128)S(1)}, u32[]{:S(2)}, u32[]{:S(2)}) async-start(f32[16,4,8,256]{3,2,1,0:T(8,128)} %bitcast.21), calls=%async_computation.1 | async-start | bytes 1048576 | tf_op jit(solution)/shard_map/all_to_all | solution.py:131
  (17 other events, 11.3 us)

commit v9 on v8

--- a/solution.py
+++ b/solution.py
@@ -23,7 +23,7 @@
 
 
 def taps_along(field, taps, axis, flipped):
-    tap_count = taps.shape[1]
+    tap_count = taps.shape[0]
     reach = (tap_count - 1) // 2
     length = field.shape[axis]
     widths = [(0, 0), (0, 0), (0, 0)]
@@ -33,7 +33,7 @@
     for offset in range(tap_count):
         start = 2 * reach - offset if flipped else offset
         piece = lax.slice_in_dim(padded, start, start + length, axis=axis)
-        total = total + taps[:, offset][:, None, None] * piece
+        total = total + taps[offset][:, None, None] * piece
     return total
 
 
@@ -80,45 +80,46 @@
     source_block = jnp.where(
         in_top[:, None], above[None, :], jnp.where(in_bottom[:, None], below[None, :], send_slot[None, :])
     )
-    send_index = (source_plane[:, None] * block_count + source_block).reshape(-1)
+    send_index = (source_plane[None, :] * block_count + source_block.T).reshape(-1)
     flat_blocks = estimate.reshape(plane_count * block_count, block_rows, lane_count)
     outgoing = jnp.take(flat_blocks, send_index, axis=0, mode="clip")
-    outgoing = outgoing.reshape(wide_count, block_count, block_rows, lane_count)
-    arrived = lax.all_to_all(outgoing, "dom", split_axis=1, concat_axis=1, tiled=True)
+    outgoing = outgoing.reshape(block_count * wide_count, block_rows, lane_count)
+    arrived = lax.all_to_all(outgoing, "dom", split_axis=0, concat_axis=0, tiled=True)
     my_sources = lax.dynamic_index_in_dim(source_dev, dom_index, 0, keepdims=False)
     src_above = lax.dynamic_index_in_dim(source_dev, jnp.maximum(dom_index - 1, 0), 0, keepdims=False)
     src_below = lax.dynamic_index_in_dim(source_dev, jnp.minimum(dom_index + 1, last), 0, keepdims=False)
     from_block = jnp.where(
         in_top[:, None], src_above[None, :], jnp.where(in_bottom[:, None], src_below[None, :], my_sources[None, :])
     )
-    recv_index = (chunk_plane[:, None] * block_count + from_block).reshape(-1)
-    flat_arrived = arrived.reshape(wide_count * block_count, block_rows, lane_count)
-    camera_ext = jnp.take(flat_arrived, recv_index, axis=0, mode="clip")
+    recv_index = (from_block * wide_count + chunk_plane[:, None]).reshape(-1)
+    camera_ext = jnp.take(arrived, recv_index, axis=0, mode="clip")
     camera_ext = camera_ext.reshape(wide_count, block_count, block_rows, lane_count)
     wide_planes = plane_start - wide + jnp.arange(wide_count, dtype=jnp.int32)
     wide_inside = (wide_planes >= 0) & (wide_planes < total_planes)
     camera_ext = jnp.where(wide_inside[:, None, None, None], camera_ext, 0.0)
     camera_ext = camera_ext.reshape(wide_count, row_count, lane_count)
-    band_wide = jnp.take(band_all, jnp.clip(wide_planes, 0, total_planes - 1), mode="clip")
-    x_wide = jnp.take(kernels[:, 2], band_wide, axis=0, mode="clip")
-    y_wide = jnp.take(kernels[:, 1], band_wide, axis=0, mode="clip")
+    band_pad = jnp.pad(band_all, wide, mode="edge")
+    band_wide = lax.dynamic_slice_in_dim(band_pad, plane_start, wide_count)
+    band_ids = jnp.arange(kernels.shape[0], dtype=jnp.int32)
+    in_band = band_wide[None, :] == band_ids[:, None]
+    tables = jnp.sum(jnp.where(in_band[:, None, None, :], kernels[:, :, :, None], 0.0), axis=0)
+    x_wide = tables[2]
+    y_wide = tables[1]
     lateral_ext = lateral_fwd(camera_ext, x_wide, y_wide)
     ext_count = plane_count + 2 * reach
     ext_planes = plane_start - reach + jnp.arange(ext_count, dtype=jnp.int32)
     ext_inside = (ext_planes >= 0) & (ext_planes < total_planes)
-    band_ext = jnp.take(band_all, jnp.clip(ext_planes, 0, total_planes - 1), mode="clip")
-    taps_ext = jnp.take(kernels[:, 0], band_ext, axis=0, mode="clip")
+    taps_ext = tables[0][:, reach : reach + ext_count]
     blurred = jnp.zeros((ext_count, row_count, lane_count), jnp.float32)
     for j in range(2 * reach + 1):
-        blurred = blurred + taps_ext[:, j][:, None, None] * lateral_ext[j : j + ext_count]
+        blurred = blurred + taps_ext[j][:, None, None] * lateral_ext[j : j + ext_count]
     observed_ext = extended_2(observed[0], (("dom", 0),), reach)
     ratio_ext = jnp.where(ext_inside[:, None, None], observed_ext / blurred, 0.0)
-    band_own = lax.dynamic_slice_in_dim(band_all, plane_start, plane_count)
-    x_own = jnp.take(kernels[:, 2], band_own, axis=0, mode="clip")
-    y_own = jnp.take(kernels[:, 1], band_own, axis=0, mode="clip")
+    x_own = tables[2][:, wide : wide + plane_count]
+    y_own = tables[1][:, wide : wide + plane_count]
     zback = jnp.zeros((plane_count, row_count, lane_count), jnp.float32)
     for m in range(2 * reach + 1):
-        zback = zback + taps_ext[m : m + plane_count, 2 * reach - m][:, None, None] * ratio_ext[m : m + plane_count]
+        zback = zback + taps_ext[2 * reach - m, m : m + plane_count][:, None, None] * ratio_ext[m : m + plane_count]
     back = lateral_back(zback, x_own, y_own)
     dest_slot = jnp.sum(
         jnp.where(my_sources[None, :] == slot_ids[:, None], slot_ids[None, :], 0), axis=1

time: 78.8 us -> 73.4 us (0.931)
  local copies, waits for them, and re-layouts: 19.2 us -> 13.8 us
  starting transfers between devices: 17.1 us -> 13.8 us
  waiting for transfers between devices: 15.1 us -> 18.4 us
    slice x6 -> x1, local copies, waits for them, and re-layouts: 5.25 us -> 0.65 us  [body(): band_pad = jnp.pad(band_all, wide, mode='edge')]
    gather x8 -> x1, local copies, waits for them, and re-layouts: 5 us -> 0.76 us  [body(): camera_ext = jnp.take(arrived, recv_index, axis=0, mode='clip')]
    all_to_all x1, waiting for transfers between devices: 0.01 us -> 3.3 us  [body(): lax.all_to_all(outgoing, 'dom', split_axis=0, concat_axis=0, tiled=True)]
    all_to_all x1, starting transfers between devices: 9.02 us -> 5.74 us  [body(): arrived_logs = lax.all_to_all(outgoing, ('dom', 'view'), 0, 0, tiled=True)]
    mul x0 -> x4, local copies, waits for them, and re-layouts: none -> 2.74 us  [the longest x2 1.34 us: taps_along(): total = total + taps[offset][:, None, None] * piece]
    gather x1, local copies, waits for them, and re-layouts: 0.76 us -> 1.77 us  [body(): outgoing = jnp.take(flat_blocks, send_index, axis=0, mode='clip')]
    mul x1, other arithmetic: 0.96 us -> 0.05 us  [body(): updated = est_piece * jnp.exp(log_total / view_count)]
    unnamed x123 -> x117, local copies, waits for them, and re-layouts: 1.66 us -> 1.17 us
  transfers between devices with their start and end apart: 4 -> 4, of which waited for: 1 -> 2; matrix products, arithmetic and copies ran while one was open for 22% -> 18% of each run, Pallas kernels for 0% -> 0%
where the time goes in v9:
time: 73.4 us; the launch traced here: 73 us
  waiting for transfers between devices  18.4 us (25%)
  blocking collectives  15.8 us (22%)
  local copies, waits for them, and re-layouts  13.8 us (19%)
  starting transfers between devices  13.8 us (19%)
  other arithmetic  10.2 us (14%)
  between operations  1.02 us (1%)
    all_gather x1, blocking collectives, body(): return lax.all_gather(updated, 'view', axis=0, tiled=True)  15.8 us
    all_to_all x1, waiting for transfers between devices, body(): arrived_logs = lax.all_to_all(outgoing, ('dom', 'view'), 0, 0, tiled=True)  15.1 us
    all_to_all x1, starting transfers between devices, body(): arrived_logs = lax.all_to_all(outgoing, ('dom', 'view'), 0, 0, tiled=True)  5.74 us
    add x3, other arithmetic, taps_along(): total = total + taps[offset][:, None, None] * piece  4.57 us
    all_to_all x1, starting transfers between devices, body(): lax.all_to_all(outgoing, 'dom', split_axis=0, concat_axis=0, tiled=True)  4.37 us
    all_to_all x1, waiting for transfers between devices, body(): lax.all_to_all(outgoing, 'dom', split_axis=0, concat_axis=0, tiled=True)  3.3 us
    ppermute x1, starting transfers between devices, extended_2(): before = lax.ppermute(last, axis, up)  2.41 us
    gather x1, local copies, waits for them, and re-layouts, body(): outgoing = jnp.take(flat_blocks, send_index, axis=0, mode='clip')  1.77 us
  transfers between devices with their start and end apart: 4, of which 2 were waited for; matrix products, arithmetic and copies ran while one was open for 18% of the time, Pallas kernels for 0%

profile of v9, /device:TPU:0, one launch (start us, length us, event | category | flops | bytes accessed | tf_op | source)
XLA Modules:
  0.0 73.0 jit_solution(18144831445187569646)
XLA Ops:
  0.0 0.8 %fusion.93 = s32[16]{0:T(128)S(1)} fusion(s32[4,16]{1,0:T(4,128)} %param.8, s32[]{:T(128)S(6)} %select_n.150), kind=kLoop, calls=%fused_computation.199 | loop fusion | bytes 132 | tf_op jit(solution)/shard_map/jit(dynamic_index_in_dim)/dynamic_slice | solution.py:59
  0.8 0.1 reshape.423
  0.9 0.1 fusion.91
  1.0 0.6 gather_fusion
  1.7 0.6 gather_fusion.1
  2.4 0.1 reshape.446
  2.5 1.8 %gather_fusion.2 = f32[128,8,256]{2,1,0:T(8,128)} fusion(f32[64,8,256]{2,1,0:T(8,128)S(1)} %bitcast.145, s32[1024]{0:T(1024)S(1)} %pad_clamp_fusion.3), kind=kCustom, calls=%fused_computation.2 | custom fusion | bytes 2097664 | tf_op jit(solution)/shard_map/jit(_take)/gather | solution.py:85
  4.2 4.4 %all-to-all-start = ((f32[128,8,256]{2,1,0:T(8,128)}), f32[128,8,256]{2,1,0:T(8,128)S(1)}, u32[]{:S(2)}, u32[]{:S(2)}) async-start(f32[128,8,256]{2,1,0:T(8,128)} %gather_fusion.2), calls=%async_computation | async-start | bytes 2097152 | tf_op jit(solution)/shard_map/all_to_all | solution.py:87
  8.6 0.7 slice_bitcast_fusion.1
  9.3 2.4 %collective-permute-start = (f32[4,32,256]{2,1,0:T(8,128)}, f32[4,32,256]{2,1,0:T(8,128)S(1)}, u32[]{:S(2)}, u32[]{:S(2)}) collective-permute-start(f32[4,32,256]{2,1,0:T(8,128)} %get-tuple-element.7), channel_id=1, source_target_pairs={{0,4},{4,8},{8,12},{1,5},{5,9},{9,13},{2,6},{6,10},{10,14},{3,7},{... | collective-permute-start | bytes 393224 | tf_op jit(solution)/shard_map/ppermute | solution.py:19
  11.7 1.3 %collective-permute-start.1 = (f32[4,32,256]{2,1,0:T(8,128)S(1)}, f32[4,32,256]{2,1,0:T(8,128)S(1)}, u32[]{:S(2)}, u32[]{:S(2)}) collective-permute-start(f32[4,32,256]{2,1,0:T(8,128)S(1)} %get-tuple-element.8), channel_id=1, source_target_pairs={{4,0},{8,4},{12,8},{5,1},{9,5},{13,9},{6,2},{10,6},{14,10},{7,3},{... | collective-permute-start | bytes 393224 | tf_op jit(solution)/shard_map/ppermute | solution.py:20
  13.1 0.1 select_reduce_fusion.2
  13.2 0.1 iota_add_fusion
  13.2 0.1 reshape.454
  13.4 0.6 compare_and_fusion
  14.0 0.6 fusion.100
  14.6 0.6 reshape.420
  15.2 0.6 reshape.421
  15.9 0.1 pad_add_fusion
  15.9 0.1 dynamic_slice.21
  16.0 0.1 copy.12
  16.1 0.1 select_reduce_fusion
  16.3 0.7 slice_bitcast_fusion.55
  17.0 0.6 compare_and_fusion.1
  17.6 0.1 reshape.462
  17.7 0.7 slice_bitcast_fusion.58
  18.4 0.7 slice_bitcast_fusion.54
  19.0 0.7 slice_bitcast_fusion.56
  19.8 3.3 %all-to-all-done = f32[128,8,256]{2,1,0:T(8,128)S(1)} async-done(((f32[128,8,256]{2,1,0:T(8,128)}), f32[128,8,256]{2,1,0:T(8,128)S(1)}, u32[]{:S(2)}, u32[]{:S(2)}) %all-to-all-start) | async-done | bytes 1048608 | tf_op jit(solution)/shard_map/all_to_all | solution.py:87
  23.1 0.8 %gather_fusion.3 = f32[128,8,256]{2,1,0:T(8,128)S(1)} fusion(f32[128,8,256]{2,1,0:T(8,128)S(1)} %all-to-all-done, s32[1024]{0:T(1024)S(1)} %pad_clamp_fusion.2), kind=kCustom, calls=%fused_computation.3 | custom fusion | bytes 2097664 | tf_op jit(solution)/shard_map/jit(_take)/gather | solution.py:95
  23.9 0.8 %bitcast_select_fusion = f32[32,32,256]{2,1,0:T(8,128)S(1)} fusion(pred[32]{0:T(512)(128)(4,1)} %compare_and_fusion, f32[32,32,256]{2,1,0:T(8,128)S(1)} %bitcast.144), kind=kLoop, calls=%fused_computation.62 | loop fusion | flops 262144 | bytes 2097184 | tf_op jit(solution)/shard_map/jit(_where)/select_n | solution.py:99
  24.9 2.7 %fusion.24 = f32[32,32,256]{2,1,0:T(8,128)S(1)} fusion(f32[32,32,256]{2,1,0:T(8,128)S(1)} %bitcast_select_fusion, f32[32]{0:T(128)S(1)} %copy-done.47, f32[32]{0:T(128)S(1)} %copy-done.48, f32[32]{0:T(128)S(1)} %copy-done.49, f32[32]{0:T(128)S(1)} %copy-done.50, f32[32]{0:T(128)S(1)} %copy-done.51, f32[32]{0:T(128)S(1)} %copy-done.52, f32[32]{0:T(128)S(1)} %copy-done.53, ...), kind=kLoop, calls=%fused_computation.54 | loop fusion | flops 4456448 | bytes 2098304 | tf_op jit(solution)/shard_map/add | solution.py:36
  27.8 1.3 %fusion.8 = f32[32,32,256]{2,1,0:T(8,128)S(1)} fusion(f32[32,32,256]{2,1,0:T(8,128)S(1)} %fusion.24, f32[32]{0:T(128)S(1)} %copy-done.39, f32[32]{0:T(128)S(1)} %copy-done.40, f32[32]{0:T(128)S(1)} %copy-done.41, f32[32]{0:T(128)S(1)} %copy-done.42, f32[32]{0:T(128)S(1)} %copy-done.43, f32[32]{0:T(128)S(1)} %copy-done.44, f32[32]{0:T(128)S(1)} %copy-done.45, ...), kind=kLoop, calls=%fused_computation.38 | loop fusion | flops 4456448 | bytes 2098304 | tf_op jit(solution)/shard_map/add | solution.py:36
  29.3 0.9 %fusion.34 = f32[24,32,256]{2,1,0:T(8,128)S(1)} fusion(f32[32,32,256]{2,1,0:T(8,128)S(1)} %fusion.8, f32[4,32,256]{2,1,0:T(8,128)S(1)} %collective-permute-done.1, f32[16,32,256]{2,1,0:T(8,128)S(1)} %bitcast.147, f32[4,32,256]{2,1,0:T(8,128)S(1)} %collective-permute-done, f32[24]{0:T(128)S(1)} %copy-done.12, f32[24]{0:T(128)S(1)} %copy-done.13, ...), kind=kLoop, calls=%fused_computation.74 | loop fusion | flops 4128768 | bytes 8651640 | tf_op jit(solution)/shard_map/jit(_where)/select_n | solution.py:117
  30.4 0.4 fusion.75
  30.9 0.1 copy-done.21
  31.0 0.6 fusion.50
  31.7 1.3 %fusion.67 = f32[16,32,256]{2,1,0:T(8,128)S(1)} fusion(f32[16,32,256]{2,1,0:T(8,128)S(1)} %fusion.50, f32[16]{0:T(128)S(1)} %get-tuple-element.31, f32[16]{0:T(128)S(1)} %copy-done.4, f32[16]{0:T(128)S(1)} %copy-done.5, f32[16]{0:T(128)S(1)} %copy-done.6, f32[16]{0:T(128)S(1)} %copy-done.7, f32[16]{0:T(128)S(1)} %copy-done.8, f32[16]{0:T(128)S(1)} %copy-done.9, ...), kind=kLoop, calls=%fused_computation.115 | loop fusion | flops 2228224 | bytes 1049152 | tf_op jit(solution)/shard_map/log | solution.py:128
  33.0 1.4 %gather_fusion.4 = f32[64,8,256]{2,1,0:T(8,128)} fusion(f32[64,8,256]{2,1,0:T(8,128)S(1)} %bitcast.146, s32[1024]{0:T(1024)S(1)} %pad_clamp_fusion.1), kind=kCustom, calls=%fused_computation.4 | custom fusion | bytes 1048832 | tf_op jit(solution)/shard_map/jit(_take)/gather | solution.py:130
  34.5 5.7 %all-to-all-start.1 = ((f32[16,4,8,256]{3,2,1,0:T(8,128)}), f32[16,4,8,256]{3,2,1,0:T(8,128)S(1)}, u32[]{:S(2)}, u32[]{:S(2)}) async-start(f32[16,4,8,256]{3,2,1,0:T(8,128)} %bitcast.72), calls=%async_computation.1 | async-start | bytes 1048576 | tf_op jit(solution)/shard_map/all_to_all | solution.py:132
  40.2 0.1 reshape.427
  40.3 0.2 fusion.88
  40.5 0.1 select_reduce_fusion.1
  40.6 0.1 reshape.470
  40.7 15.1 %all-to-all-done.1 = f32[16,4,8,256]{3,2,1,0:T(8,128)S(1)} async-done(((f32[16,4,8,256]{3,2,1,0:T(8,128)}), f32[16,4,8,256]{3,2,1,0:T(8,128)S(1)}, u32[]{:S(2)}, u32[]{:S(2)}) %all-to-all-start.1) | async-done | bytes 524320 | tf_op jit(solution)/shard_map/all_to_all | solution.py:132
  55.8 0.6 gather_fusion.5
  56.4 15.8 %all_gather.3 = f32[16,32,256]{2,1,0:T(8,128)S(1)} all-gather(f32[4,32,256]{2,1,0:T(8,128)S(1)} %bitcast_multiply_fusion), channel_id=1, replica_groups=mesh['tile'=2,'dom'=4,'view'=4] {'view'}, dimensions={0}, use_global_device_ids=true | all-gather | bytes 655360 | tf_op jit(solution)/shard_map/all_gather | solution.py:150
  72.2 0.8 %copy.16 = f32[16,32,256]{2,1,0:T(8,128)} copy(f32[16,32,256]{2,1,0:T(8,128)S(1)} %all_gather.3) | data formatting | bytes 1048576
  (134 shorter events, 0.6 us)
Async XLA Ops:
  0.0 2.5 %copy-start = (f32[16,32,256]{2,1,0:T(8,128)S(1)}, f32[16,32,256]{2,1,0:T(8,128)}, u32[]{:S(2)}) copy-start(f32[16,32,256]{2,1,0:T(8,128)} %param.5) | copy-start | bytes 1572868
  4.2 4.4 %copy-start.1 = (f32[1,16,32,256]{3,2,1,0:T(8,128)S(1)}, f32[1,16,32,256]{3,2,1,0:T(8,128)}, u32[]{:S(2)}) copy-start(f32[1,16,32,256]{3,2,1,0:T(8,128)} %param.6) | copy-start | bytes 1572868
  4.2 9.7 %copy-start.3 = (s32[1,64]{1,0:T(1,128)S(1)}, s32[1,64]{1,0:T(1,128)}, u32[]{:S(2)}) copy-start(s32[1,64]{1,0:T(1,128)} %param.9) | copy-start | bytes 772
  4.2 11.8 %copy-start.2 = (f32[1,4,3,9]{3,1,2,0:T(4,128)S(1)}, f32[1,4,3,9]{3,1,2,0:T(4,128)}, u32[]{:S(2)}) copy-start(f32[1,4,3,9]{3,1,2,0:T(4,128)} %param.7) | copy-start | bytes 1300
  4.2 18.8 %all-to-all-start = ((f32[128,8,256]{2,1,0:T(8,128)}), f32[128,8,256]{2,1,0:T(8,128)S(1)}, u32[]{:S(2)}, u32[]{:S(2)}) async-start(f32[128,8,256]{2,1,0:T(8,128)} %gather_fusion.2), calls=%async_computation | async-start | bytes 2097152 | tf_op jit(solution)/shard_map/all_to_all | solution.py:87
  9.3 19.8 %collective-permute-start = (f32[4,32,256]{2,1,0:T(8,128)}, f32[4,32,256]{2,1,0:T(8,128)S(1)}, u32[]{:S(2)}, u32[]{:S(2)}) collective-permute-start(f32[4,32,256]{2,1,0:T(8,128)} %get-tuple-element.7), channel_id=1, source_target_pairs={{0,4},{4,8},{8,12},{1,5},{5,9},{9,13},{2,6},{6,10},{10,14},{3,7},{... | collective-permute-start | bytes 393224 | tf_op jit(solution)/shard_map/ppermute | solution.py:19
  11.7 17.4 %collective-permute-start.1 = (f32[4,32,256]{2,1,0:T(8,128)S(1)}, f32[4,32,256]{2,1,0:T(8,128)S(1)}, u32[]{:S(2)}, u32[]{:S(2)}) collective-permute-start(f32[4,32,256]{2,1,0:T(8,128)S(1)} %get-tuple-element.8), channel_id=1, source_target_pairs={{4,0},{8,4},{12,8},{5,1},{9,5},{13,9},{6,2},{10,6},{14,10},{7,3},{... | collective-permute-start | bytes 393224 | tf_op jit(solution)/shard_map/ppermute | solution.py:20
  23.8 0.9 %copy-start.47 = (f32[32]{0:T(128)S(1)}, f32[32]{0:T(128)}, u32[]{:S(2)}) copy-start(f32[32]{0:T(128)} %get-tuple-element.21) | copy-start | bytes 388
  23.8 0.9 %copy-start.48 = (f32[32]{0:T(128)S(1)}, f32[32]{0:T(128)}, u32[]{:S(2)}) copy-start(f32[32]{0:T(128)} %get-tuple-element.22) | copy-start | bytes 388
  23.8 0.9 %copy-start.49 = (f32[32]{0:T(128)S(1)}, f32[32]{0:T(128)}, u32[]{:S(2)}) copy-start(f32[32]{0:T(128)} %get-tuple-element.23) | copy-start | bytes 388
  23.8 0.9 %copy-start.50 = (f32[32]{0:T(128)S(1)}, f32[32]{0:T(128)}, u32[]{:S(2)}) copy-start(f32[32]{0:T(128)} %get-tuple-element.24) | copy-start | bytes 388
  23.9 0.9 %copy-start.51 = (f32[32]{0:T(128)S(1)}, f32[32]{0:T(128)}, u32[]{:S(2)}) copy-start(f32[32]{0:T(128)} %get-tuple-element.25) | copy-start | bytes 388
  23.9 0.9 %copy-start.52 = (f32[32]{0:T(128)S(1)}, f32[32]{0:T(128)}, u32[]{:S(2)}) copy-start(f32[32]{0:T(128)} %get-tuple-element.26) | copy-start | bytes 388
  23.9 0.9 %copy-start.53 = (f32[32]{0:T(128)S(1)}, f32[32]{0:T(128)}, u32[]{:S(2)}) copy-start(f32[32]{0:T(128)} %get-tuple-element.27) | copy-start | bytes 388
  23.9 0.9 %copy-start.54 = (f32[32]{0:T(128)S(1)}, f32[32]{0:T(128)}, u32[]{:S(2)}) copy-start(f32[32]{0:T(128)} %get-tuple-element.28) | copy-start | bytes 388
  23.9 0.9 %copy-start.55 = (f32[32]{0:T(128)S(1)}, f32[32]{0:T(128)}, u32[]{:S(2)}) copy-start(f32[32]{0:T(128)} %get-tuple-element.29) | copy-start | bytes 388
  24.8 2.8 %copy-start.38 = (f32[32]{0:T(128)S(1)}, f32[32]{0:T(128)}, u32[]{:S(2)}) copy-start(f32[32]{0:T(128)} %get-tuple-element.12) | copy-start | bytes 388
  24.8 2.8 %copy-start.39 = (f32[32]{0:T(128)S(1)}, f32[32]{0:T(128)}, u32[]{:S(2)}) copy-start(f32[32]{0:T(128)} %get-tuple-element.13) | copy-start | bytes 388
  24.8 2.8 %copy-start.40 = (f32[32]{0:T(128)S(1)}, f32[32]{0:T(128)}, u32[]{:S(2)}) copy-start(f32[32]{0:T(128)} %get-tuple-element.14) | copy-start | bytes 388
  24.8 2.8 %copy-start.41 = (f32[32]{0:T(128)S(1)}, f32[32]{0:T(128)}, u32[]{:S(2)}) copy-start(f32[32]{0:T(128)} %get-tuple-element.15) | copy-start | bytes 388
  24.8 2.8 %copy-start.42 = (f32[32]{0:T(128)S(1)}, f32[32]{0:T(128)}, u32[]{:S(2)}) copy-start(f32[32]{0:T(128)} %get-tuple-element.16) | copy-start | bytes 388
  24.9 2.8 %copy-start.43 = (f32[32]{0:T(128)S(1)}, f32[32]{0:T(128)}, u32[]{:S(2)}) copy-start(f32[32]{0:T(128)} %get-tuple-element.17) | copy-start | bytes 388
  24.9 2.8 %copy-start.44 = (f32[32]{0:T(128)S(1)}, f32[32]{0:T(128)}, u32[]{:S(2)}) copy-start(f32[32]{0:T(128)} %get-tuple-element.18) | copy-start | bytes 388
  24.9 2.8 %copy-start.45 = (f32[32]{0:T(128)S(1)}, f32[32]{0:T(128)}, u32[]{:S(2)}) copy-start(f32[32]{0:T(128)} %get-tuple-element.19) | copy-start | bytes 388
  24.9 2.8 %copy-start.46 = (f32[32]{0:T(128)S(1)}, f32[32]{0:T(128)}, u32[]{:S(2)}) copy-start(f32[32]{0:T(128)} %get-tuple-element.20) | copy-start | bytes 388
  27.7 1.4 %copy-start.11 = (f32[24]{0:T(128)S(1)}, f32[24]{0:T(128)}, u32[]{:S(2)}) copy-start(f32[24]{0:T(128)} %get-tuple-element.57) | copy-start | bytes 292
  27.7 1.4 %copy-start.12 = (f32[24]{0:T(128)S(1)}, f32[24]{0:T(128)}, u32[]{:S(2)}) copy-start(f32[24]{0:T(128)} %get-tuple-element.58) | copy-start | bytes 292
  27.7 1.4 %copy-start.13 = (f32[24]{0:T(128)S(1)}, f32[24]{0:T(128)}, u32[]{:S(2)}) copy-start(f32[24]{0:T(128)} %get-tuple-element.59) | copy-start | bytes 292
  27.7 1.4 %copy-start.14 = (f32[24]{0:T(128)S(1)}, f32[24]{0:T(128)}, u32[]{:S(2)}) copy-start(f32[24]{0:T(128)} %get-tuple-element.60) | copy-start | bytes 292
  27.7 1.4 %copy-start.15 = (f32[24]{0:T(128)S(1)}, f32[24]{0:T(128)}, u32[]{:S(2)}) copy-start(f32[24]{0:T(128)} %get-tuple-element.61) | copy-start | bytes 292
  27.7 1.4 %copy-start.16 = (f32[24]{0:T(128)S(1)}, f32[24]{0:T(128)}, u32[]{:S(2)}) copy-start(f32[24]{0:T(128)} %get-tuple-element.62) | copy-start | bytes 292
  27.7 1.4 %copy-start.17 = (f32[24]{0:T(128)S(1)}, f32[24]{0:T(128)}, u32[]{:S(2)}) copy-start(f32[24]{0:T(128)} %get-tuple-element.63) | copy-start | bytes 292
  27.7 1.4 %copy-start.18 = (f32[24]{0:T(128)S(1)}, f32[24]{0:T(128)}, u32[]{:S(2)}) copy-start(f32[24]{0:T(128)} %get-tuple-element.64) | copy-start | bytes 292
  27.8 1.4 %copy-start.19 = (f32[24]{0:T(128)S(1)}, f32[24]{0:T(128)}, u32[]{:S(2)}) copy-start(f32[24]{0:T(128)} %get-tuple-element.65) | copy-start | bytes 292
  27.8 1.4 %copy-start.57 = (pred[24]{0:T(512)(128)(4,1)S(1)}, pred[24]{0:T(512)(128)(4,1)}, u32[]{:S(2)}) copy-start(pred[24]{0:T(512)(128)(4,1)} %compare_and_fusion.1) | copy-start | bytes 76
  29.2 1.0 %copy-start.29 = (f32[16]{0:T(128)S(1)}, f32[16]{0:T(128)}, u32[]{:S(2)}) copy-start(f32[16]{0:T(128)} %get-tuple-element.48) | copy-start | bytes 196
  29.2 1.0 %copy-start.30 = (f32[16]{0:T(128)S(1)}, f32[16]{0:T(128)}, u32[]{:S(2)}) copy-start(f32[16]{0:T(128)} %get-tuple-element.49) | copy-start | bytes 196
  29.2 1.0 %copy-start.31 = (f32[16]{0:T(128)S(1)}, f32[16]{0:T(128)}, u32[]{:S(2)}) copy-start(f32[16]{0:T(128)} %get-tuple-element.50) | copy-start | bytes 196
  29.2 1.0 %copy-start.32 = (f32[16]{0:T(128)S(1)}, f32[16]{0:T(128)}, u32[]{:S(2)}) copy-start(f32[16]{0:T(128)} %get-tuple-element.51) | copy-start | bytes 196
  29.2 1.0 %copy-start.33 = (f32[16]{0:T(128)S(1)}, f32[16]{0:T(128)}, u32[]{:S(2)}) copy-start(f32[16]{0:T(128)} %get-tuple-element.52) | copy-start | bytes 196
  29.2 1.0 %copy-start.34 = (f32[16]{0:T(128)S(1)}, f32[16]{0:T(128)}, u32[]{:S(2)}) copy-start(f32[16]{0:T(128)} %get-tuple-element.53) | copy-start | bytes 196
  29.2 1.0 %copy-start.35 = (f32[16]{0:T(128)S(1)}, f32[16]{0:T(128)}, u32[]{:S(2)}) copy-start(f32[16]{0:T(128)} %get-tuple-element.54) | copy-start | bytes 196
  29.3 1.0 %copy-start.36 = (f32[16]{0:T(128)S(1)}, f32[16]{0:T(128)}, u32[]{:S(2)}) copy-start(f32[16]{0:T(128)} %get-tuple-element.55) | copy-start | bytes 196
  29.3 1.0 %copy-start.37 = (f32[16]{0:T(128)S(1)}, f32[16]{0:T(128)}, u32[]{:S(2)}) copy-start(f32[16]{0:T(128)} %get-tuple-element.56) | copy-start | bytes 196
  30.8 0.8 %copy-start.4 = (f32[16]{0:T(128)S(1)}, f32[16]{0:T(128)}, u32[]{:S(2)}) copy-start(f32[16]{0:T(128)} %get-tuple-element.32) | copy-start | bytes 196
  30.8 0.8 %copy-start.5 = (f32[16]{0:T(128)S(1)}, f32[16]{0:T(128)}, u32[]{:S(2)}) copy-start(f32[16]{0:T(128)} %get-tuple-element.33) | copy-start | bytes 196
  33.0 7.2 %copy-start.56 = (s32[4,16]{1,0:T(4,128)S(1)}, s32[4,16]{1,0:T(4,128)}, u32[]{:S(2)}) copy-start(s32[4,16]{1,0:T(4,128)} %param.8) | copy-start | bytes 772
  34.5 21.3 %all-to-all-start.1 = ((f32[16,4,8,256]{3,2,1,0:T(8,128)}), f32[16,4,8,256]{3,2,1,0:T(8,128)S(1)}, u32[]{:S(2)}, u32[]{:S(2)}) async-start(f32[16,4,8,256]{3,2,1,0:T(8,128)} %bitcast.72), calls=%async_computation.1 | async-start | bytes 1048576 | tf_op jit(solution)/shard_map/all_to_all | solution.py:132
  (14 other events, 10.1 us)

commit v10 on v9

--- a/solution.py
+++ b/solution.py
@@ -60,15 +60,23 @@
     grid_map = my_map.reshape(block_count, block_count)
     source_dev = grid_map // block_count
     source_slot = grid_map % block_count
-    send_slot = jnp.sum(jnp.where(source_dev == dom_index, source_slot, 0), axis=1)
+    near_rows = jnp.stack(
+        [
+            jnp.concatenate([grid_map[:1], grid_map[:-1]], axis=0),
+            grid_map,
+            jnp.concatenate([grid_map[1:], grid_map[-1:]], axis=0),
+        ]
+    )
+    near_slots = jnp.sum(
+        jnp.where(near_rows // block_count == dom_index, near_rows % block_count, 0), axis=2
+    )
+    above, send_slot, below = near_slots[0], near_slots[1], near_slots[2]
     kernels = psf[0]
     band_all = depth_band[0]
     total_planes = band_all.shape[0]
     reach = (kernels.shape[2] - 1) // 2
     wide = 2 * reach
     last = block_count - 1
-    above = jnp.take(send_slot, jnp.clip(slot_ids - 1, 0, last), mode="clip")
-    below = jnp.take(send_slot, jnp.clip(slot_ids + 1, 0, last), mode="clip")
     wide_count = plane_count + 2 * wide
     chunk_plane = jnp.arange(wide_count, dtype=jnp.int32)
     in_top = chunk_plane < wide
@@ -96,7 +104,6 @@
     camera_ext = camera_ext.reshape(wide_count, block_count, block_rows, lane_count)
     wide_planes = plane_start - wide + jnp.arange(wide_count, dtype=jnp.int32)
     wide_inside = (wide_planes >= 0) & (wide_planes < total_planes)
-    camera_ext = jnp.where(wide_inside[:, None, None, None], camera_ext, 0.0)
     camera_ext = camera_ext.reshape(wide_count, row_count, lane_count)
     band_pad = jnp.pad(band_all, wide, mode="edge")
     band_wide = lax.dynamic_slice_in_dim(band_pad, plane_start, wide_count)
@@ -106,6 +113,7 @@
     x_wide = tables[2]
     y_wide = tables[1]
     lateral_ext = lateral_fwd(camera_ext, x_wide, y_wide)
+    lateral_ext = jnp.where(wide_inside[:, None, None], lateral_ext, 0.0)
     ext_count = plane_count + 2 * reach
     ext_planes = plane_start - reach + jnp.arange(ext_count, dtype=jnp.int32)
     ext_inside = (ext_planes >= 0) & (ext_planes < total_planes)

time: 73.4 us -> 73.6 us (level)
  waiting for transfers between devices: 18.4 us -> 22.7 us
  local copies, waits for them, and re-layouts: 13.8 us -> 11.3 us
  other arithmetic: 10.2 us -> 9.29 us
  between operations: 1.02 us -> 0.23 us
    all_to_all x1, waiting for transfers between devices: 3.3 us -> 7.57 us  [body(): lax.all_to_all(outgoing, 'dom', split_axis=0, concat_axis=0, tiled=True)]
    add x3 -> x2, other arithmetic: 4.57 us -> 3.26 us  [taps_along(): total = total + taps[offset][:, None, None] * piece]
    gather x2 -> x0, local copies, waits for them, and re-layouts: 1.28 us -> none  [the longest x1 0.64 us: body(): above = jnp.take(send_slot, jnp.clip(slot_ids - 1, 0, last), mode='clip')]
    mul x2, local copies, waits for them, and re-layouts: 1.34 us -> 0.09 us  [taps_along(): total = total + taps[offset][:, None, None] * piece]
    dynamic_slice x1 -> x2, local copies, waits for them, and re-layouts: 0.76 us -> 1.86 us  [body(): my_map = lax.dynamic_index_in_dim(src_map, view_index, 0, keepdims=False)]
    gather x1, local copies, waits for them, and re-layouts: 1.77 us -> 2.68 us  [body(): outgoing = jnp.take(flat_blocks, send_index, axis=0, mode='clip')]
    mul x1, other arithmetic: 0.05 us -> 0.96 us  [body(): updated = est_piece * jnp.exp(log_total / view_count)]
  transfers between devices with their start and end apart: 4 -> 4, of which waited for: 2 -> 2; matrix products, arithmetic and copies ran while one was open for 18% -> 11% of each run, Pallas kernels for 0% -> 0%
where the time goes in v10:
time: 73.6 us; the launch traced here: 73.1 us
  waiting for transfers between devices  22.7 us (31%)
  blocking collectives  15.8 us (21%)
  starting transfers between devices  13.8 us (19%)
  local copies, waits for them, and re-layouts  11.3 us (15%)
  other arithmetic  9.29 us (13%)
    all_gather x1, blocking collectives, body(): return lax.all_gather(updated, 'view', axis=0, tiled=True)  15.8 us
    all_to_all x1, waiting for transfers between devices, body(): arrived_logs = lax.all_to_all(outgoing, ('dom', 'view'), 0, 0, tiled=True)  15.1 us
    all_to_all x1, waiting for transfers between devices, body(): lax.all_to_all(outgoing, 'dom', split_axis=0, concat_axis=0, tiled=True)  7.57 us
    all_to_all x1, starting transfers between devices, body(): arrived_logs = lax.all_to_all(outgoing, ('dom', 'view'), 0, 0, tiled=True)  5.74 us
    all_to_all x1, starting transfers between devices, body(): lax.all_to_all(outgoing, 'dom', split_axis=0, concat_axis=0, tiled=True)  4.37 us
    add x2, other arithmetic, taps_along(): total = total + taps[offset][:, None, None] * piece  3.26 us
    gather x1, local copies, waits for them, and re-layouts, body(): outgoing = jnp.take(flat_blocks, send_index, axis=0, mode='clip')  2.68 us
    ppermute x1, starting transfers between devices, extended_2(): before = lax.ppermute(last, axis, up)  2.42 us
  transfers between devices with their start and end apart: 4, of which 2 were waited for; matrix products, arithmetic and copies ran while one was open for 11% of the time, Pallas kernels for 0%

profile of v10, /device:TPU:0, one launch (start us, length us, event | category | flops | bytes accessed | tf_op | source)
XLA Modules:
  0.0 73.1 jit_solution(16696185603385979386)
XLA Ops:
  0.0 0.5 broadcast.258
  0.5 1.3 %fusion.103 = (s32[16]{0:T(128)S(1)}, s32[1,16]{1,0:T(1,128)S(1)}) fusion(s32[]{:T(128)} %broadcast.258, s32[4,16]{1,0:T(4,128)} %param.8, s32[]{:T(128)S(6)} %select_n.142), kind=kLoop, calls=%fused_computation.272 | loop fusion | bytes 200 | tf_op jit(solution)/shard_map/jit(dynamic_index_in_dim)/dynamic_slice | solution.py:59
  1.9 0.1 slice_reduce_fusion.1
  1.9 0.1 fusion.105
  2.0 0.1 slice.492
  2.1 0.1 slice.494
  2.2 0.1 stack_reshape.3
  2.3 0.2 fusion.93
  2.5 0.1 select_add_fusion
  2.5 0.1 reshape.406
  2.6 2.7 %gather_fusion = f32[128,8,256]{2,1,0:T(8,128)} fusion(f32[64,8,256]{2,1,0:T(8,128)} %bitcast.150, s32[1024]{0:T(1024)S(1)} %pad_clamp_fusion.3), kind=kCustom, calls=%fused_computation | custom fusion | bytes 2097664 | tf_op jit(solution)/shard_map/jit(_take)/gather | solution.py:93
  5.3 4.4 %all-to-all-start = ((f32[128,8,256]{2,1,0:T(8,128)}), f32[128,8,256]{2,1,0:T(8,128)S(1)}, u32[]{:S(2)}, u32[]{:S(2)}) async-start(f32[128,8,256]{2,1,0:T(8,128)} %gather_fusion), calls=%async_computation | async-start | bytes 2097152 | tf_op jit(solution)/shard_map/all_to_all | solution.py:95
  9.7 2.4 %collective-permute-start = (f32[4,32,256]{2,1,0:T(8,128)S(1)}, f32[4,32,256]{2,1,0:T(8,128)S(1)}, u32[]{:S(2)}, u32[]{:S(2)}) collective-permute-start(f32[4,32,256]{2,1,0:T(8,128)S(1)} %get-tuple-element.9), channel_id=1, source_target_pairs={{0,4},{4,8},{8,12},{1,5},{5,9},{9,13},{2,6},{6,10},{10,14},{3,7},{... | collective-permute-start | bytes 393224 | tf_op jit(solution)/shard_map/ppermute | solution.py:19
  12.1 1.3 %collective-permute-start.1 = (f32[4,32,256]{2,1,0:T(8,128)S(1)}, f32[4,32,256]{2,1,0:T(8,128)S(1)}, u32[]{:S(2)}, u32[]{:S(2)}) collective-permute-start(f32[4,32,256]{2,1,0:T(8,128)S(1)} %get-tuple-element.10), channel_id=1, source_target_pairs={{4,0},{8,4},{12,8},{5,1},{9,5},{13,9},{6,2},{10,6},{14,10},{7,3},{... | collective-permute-start | bytes 393224 | tf_op jit(solution)/shard_map/ppermute | solution.py:20
  13.4 0.1 reshape.400
  13.6 0.1 select_reduce_fusion.2
  13.7 0.1 iota_add_fusion
  13.8 0.1 reshape.414
  13.9 0.6 fusion.104
  14.5 0.6 reshape.397
  15.1 0.6 reshape.398
  15.7 0.1 pad_add_fusion.1
  15.8 0.1 dynamic_slice.21
  15.9 0.1 copy.12
  16.0 0.1 select_reduce_fusion
  16.1 0.1 slice_bitcast_fusion.55
  16.3 0.1 reshape.422
  16.4 0.1 slice_bitcast_fusion.58
  16.5 0.1 slice_bitcast_fusion.56
  16.5 7.6 %all-to-all-done = f32[128,8,256]{2,1,0:T(8,128)S(1)} async-done(((f32[128,8,256]{2,1,0:T(8,128)}), f32[128,8,256]{2,1,0:T(8,128)S(1)}, u32[]{:S(2)}, u32[]{:S(2)}) %all-to-all-start) | async-done | bytes 1048608 | tf_op jit(solution)/shard_map/all_to_all | solution.py:95
  24.1 0.8 %gather_fusion.1 = f32[128,8,256]{2,1,0:T(8,128)S(1)} fusion(f32[128,8,256]{2,1,0:T(8,128)S(1)} %all-to-all-done, s32[1024]{0:T(1024)S(1)} %pad_clamp_fusion.2), kind=kCustom, calls=%fused_computation.1 | custom fusion | bytes 2097664 | tf_op jit(solution)/shard_map/jit(_take)/gather | solution.py:103
  24.9 2.7 %fusion.25 = f32[32,32,256]{2,1,0:T(8,128)S(1)} fusion(f32[32,32,256]{2,1,0:T(8,128)S(1)} %bitcast.149, f32[32]{0:T(128)S(1)} %get-tuple-element.23, f32[32]{0:T(128)S(1)} %get-tuple-element.24, f32[32]{0:T(128)S(1)} %get-tuple-element.25, f32[32]{0:T(128)S(1)} %get-tuple-element.26, f32[32]{0:T(128)S(1)} %get-tuple-element.27, f32[32]{0:T(128)S(1)} %get-tuple-element.28, ...), kind=kLoop, calls=%fused_computation.53 | loop fusion | flops 4456448 | bytes 2098304 | tf_op jit(solution)/shard_map/add | solution.py:36
  27.5 1.4 %fusion.9 = f32[32,32,256]{2,1,0:T(8,128)S(1)} fusion(f32[32,32,256]{2,1,0:T(8,128)S(1)} %fusion.25, f32[32]{0:T(128)S(1)} %get-tuple-element.15, f32[32]{0:T(128)S(1)} %get-tuple-element.16, f32[32]{0:T(128)S(1)} %get-tuple-element.17, f32[32]{0:T(128)S(1)} %get-tuple-element.18, f32[32]{0:T(128)S(1)} %get-tuple-element.19, f32[32]{0:T(128)S(1)} %get-tuple-element.20, ...), kind=kLoop, calls=%fused_computation.37 | loop fusion | flops 4718592 | bytes 2098336 | tf_op jit(solution)/shard_map/jit(_where)/select_n | solution.py:116
  29.0 0.9 %fusion.35 = f32[24,32,256]{2,1,0:T(8,128)S(1)} fusion(f32[32,32,256]{2,1,0:T(8,128)S(1)} %fusion.9, f32[4,32,256]{2,1,0:T(8,128)S(1)} %collective-permute-done.1, f32[16,32,256]{2,1,0:T(8,128)S(1)} %bitcast.152, f32[4,32,256]{2,1,0:T(8,128)S(1)} %collective-permute-done, f32[24]{0:T(128)S(1)} %get-tuple-element.60, f32[24]{0:T(128)S(1)} %get-tuple-element.61, ...), kind=kLoop, calls=%fused_computation.72 | loop fusion | flops 4128768 | bytes 8651640 | tf_op jit(solution)/shard_map/jit(_where)/select_n | solution.py:125
  29.9 0.4 fusion.76
  30.3 0.6 fusion.51
  30.9 1.3 %fusion.68 = f32[16,32,256]{2,1,0:T(8,128)S(1)} fusion(f32[16,32,256]{2,1,0:T(8,128)S(1)} %fusion.51, f32[16]{0:T(128)S(1)} %get-tuple-element.33, f32[16]{0:T(128)S(1)} %get-tuple-element.34, f32[16]{0:T(128)S(1)} %get-tuple-element.35, f32[16]{0:T(128)S(1)} %get-tuple-element.36, f32[16]{0:T(128)S(1)} %get-tuple-element.37, f32[16]{0:T(128)S(1)} %get-tuple-element.38, ...), kind=kLoop, calls=%fused_computation.113 | loop fusion | flops 2228224 | bytes 1049152 | tf_op jit(solution)/shard_map/log | solution.py:136
  32.3 1.4 %gather_fusion.2 = f32[64,8,256]{2,1,0:T(8,128)} fusion(f32[64,8,256]{2,1,0:T(8,128)S(1)} %bitcast.151, s32[1024]{0:T(1024)S(1)} %pad_clamp_fusion.1), kind=kCustom, calls=%fused_computation.2 | custom fusion | bytes 1048832 | tf_op jit(solution)/shard_map/jit(_take)/gather | solution.py:138
  33.7 5.7 %all-to-all-start.1 = ((f32[16,4,8,256]{3,2,1,0:T(8,128)}), f32[16,4,8,256]{3,2,1,0:T(8,128)S(1)}, u32[]{:S(2)}, u32[]{:S(2)}) async-start(f32[16,4,8,256]{3,2,1,0:T(8,128)} %bitcast.75), calls=%async_computation.1 | async-start | bytes 1048576 | tf_op jit(solution)/shard_map/all_to_all | solution.py:140
  39.4 0.1 reshape.403
  39.5 0.2 fusion.89
  39.7 0.1 select_reduce_fusion.1
  39.8 0.1 reshape.430
  39.9 15.1 %all-to-all-done.1 = f32[16,4,8,256]{3,2,1,0:T(8,128)S(1)} async-done(((f32[16,4,8,256]{3,2,1,0:T(8,128)}), f32[16,4,8,256]{3,2,1,0:T(8,128)S(1)}, u32[]{:S(2)}, u32[]{:S(2)}) %all-to-all-start.1) | async-done | bytes 524320 | tf_op jit(solution)/shard_map/all_to_all | solution.py:140
  55.0 0.6 gather_fusion.3
  55.6 1.0 %bitcast_multiply_fusion = f32[4,32,256]{2,1,0:T(8,128)S(1)} fusion(f32[16,32,256]{2,1,0:T(8,128)} %param.5, s32[]{:T(128)S(6)} %select_n.137, f32[16,4,8,256]{3,2,1,0:T(8,128)S(1)} %gather_fusion.3), kind=kLoop, calls=%fused_computation.144 | loop fusion | flops 163840 | bytes 786436 | tf_op jit(solution)/shard_map/mul | solution.py:157
  56.5 15.8 %all_gather.3 = f32[16,32,256]{2,1,0:T(8,128)S(1)} all-gather(f32[4,32,256]{2,1,0:T(8,128)S(1)} %bitcast_multiply_fusion), channel_id=1, replica_groups=mesh['tile'=2,'dom'=4,'view'=4] {'view'}, dimensions={0}, use_global_device_ids=true | all-gather | bytes 655360 | tf_op jit(solution)/shard_map/all_gather | solution.py:158
  72.3 0.8 %copy.16 = f32[16,32,256]{2,1,0:T(8,128)} copy(f32[16,32,256]{2,1,0:T(8,128)S(1)} %all_gather.3) | data formatting | bytes 1048576
  (29 shorter events, 0.2 us)
Async XLA Ops:
  5.3 4.4 %copy-start = (f32[1,16,32,256]{3,2,1,0:T(8,128)S(1)}, f32[1,16,32,256]{3,2,1,0:T(8,128)}, u32[]{:S(2)}) copy-start(f32[1,16,32,256]{3,2,1,0:T(8,128)} %param.6) | copy-start | bytes 1572868
  5.3 8.6 %copy-start.2 = (s32[1,64]{1,0:T(1,128)S(1)}, s32[1,64]{1,0:T(1,128)}, u32[]{:S(2)}) copy-start(s32[1,64]{1,0:T(1,128)} %param.9) | copy-start | bytes 772
  5.3 10.6 %copy-start.1 = (f32[1,4,3,9]{3,1,2,0:T(4,128)S(1)}, f32[1,4,3,9]{3,1,2,0:T(4,128)}, u32[]{:S(2)}) copy-start(f32[1,4,3,9]{3,1,2,0:T(4,128)} %param.7) | copy-start | bytes 1300
  5.3 18.8 %all-to-all-start = ((f32[128,8,256]{2,1,0:T(8,128)}), f32[128,8,256]{2,1,0:T(8,128)S(1)}, u32[]{:S(2)}, u32[]{:S(2)}) async-start(f32[128,8,256]{2,1,0:T(8,128)} %gather_fusion), calls=%async_computation | async-start | bytes 2097152 | tf_op jit(solution)/shard_map/all_to_all | solution.py:95
  9.7 19.2 %collective-permute-start = (f32[4,32,256]{2,1,0:T(8,128)S(1)}, f32[4,32,256]{2,1,0:T(8,128)S(1)}, u32[]{:S(2)}, u32[]{:S(2)}) collective-permute-start(f32[4,32,256]{2,1,0:T(8,128)S(1)} %get-tuple-element.9), channel_id=1, source_target_pairs={{0,4},{4,8},{8,12},{1,5},{5,9},{9,13},{2,6},{6,10},{10,14},{3,7},{... | collective-permute-start | bytes 393224 | tf_op jit(solution)/shard_map/ppermute | solution.py:19
  12.1 16.8 %collective-permute-start.1 = (f32[4,32,256]{2,1,0:T(8,128)S(1)}, f32[4,32,256]{2,1,0:T(8,128)S(1)}, u32[]{:S(2)}, u32[]{:S(2)}) collective-permute-start(f32[4,32,256]{2,1,0:T(8,128)S(1)} %get-tuple-element.10), channel_id=1, source_target_pairs={{4,0},{8,4},{12,8},{5,1},{9,5},{13,9},{6,2},{10,6},{14,10},{7,3},{... | collective-permute-start | bytes 393224 | tf_op jit(solution)/shard_map/ppermute | solution.py:20
  32.2 7.2 %copy-start.3 = (s32[4,16]{1,0:T(4,128)S(1)}, s32[4,16]{1,0:T(4,128)}, u32[]{:S(2)}) copy-start(s32[4,16]{1,0:T(4,128)} %param.8) | copy-start | bytes 772
  33.7 21.3 %all-to-all-start.1 = ((f32[16,4,8,256]{3,2,1,0:T(8,128)}), f32[16,4,8,256]{3,2,1,0:T(8,128)S(1)}, u32[]{:S(2)}, u32[]{:S(2)}) async-start(f32[16,4,8,256]{3,2,1,0:T(8,128)} %bitcast.75), calls=%async_computation.1 | async-start | bytes 1048576 | tf_op jit(solution)/shard_map/all_to_all | solution.py:140

commit v11 on v10

--- a/solution.py
+++ b/solution.py
@@ -37,13 +37,26 @@
     return total
 
 
+def rows_mixed(field, taps, flipped):
+    tap_count = taps.shape[0]
+    reach = (tap_count - 1) // 2
+    length = field.shape[1]
+    out_pos = jnp.arange(length, dtype=jnp.int32)[:, None]
+    in_pos = jnp.arange(length, dtype=jnp.int32)[None, :]
+    offset = out_pos - in_pos if flipped else in_pos - out_pos
+    mix = jnp.zeros((taps.shape[1], length, length), jnp.float32)
+    for tap in range(tap_count):
+        mix = mix + jnp.where((offset == tap - reach)[None], taps[tap][:, None, None], 0.0)
+    return jnp.einsum("pri,pix->prx", mix, field, precision=precise)
+
+
 def lateral_fwd(field, x_taps, y_taps):
     inner = taps_along(field, x_taps, 2, False)
-    return taps_along(inner, y_taps, 1, False)
+    return rows_mixed(inner, y_taps, False)
 
 
 def lateral_back(field, x_taps, y_taps):
-    inner = taps_along(field, y_taps, 1, True)
+    inner = rows_mixed(field, y_taps, True)
     return taps_along(inner, x_taps, 2, True)
 
 

time: 73.6 us -> 73.4 us (level)
  matrix products: 0 us -> 4.99 us
  other arithmetic: 9.29 us -> 4.3 us
    dot_general x0 -> x2, matrix products: none -> 4.99 us  [rows_mixed(): return jnp.einsum('pri,pix->prx', mix, field, precision=precise)]
    add x3 -> x0, other arithmetic: 3.67 us -> none  [the longest x2 3.26 us: taps_along(): total = total + taps[offset][:, None, None] * piece]
    select_n x1 -> x0, other arithmetic: 1.4 us -> none  [body(): lateral_ext = jnp.where(wide_inside[:, None, None], lateral_ext, 0.0)]
where the time goes in v11:
time: 73.4 us; the launch traced here: 73 us
  waiting for transfers between devices  22.4 us (31%)
  blocking collectives  15.8 us (22%)
  starting transfers between devices  13.8 us (19%)
  local copies, waits for them, and re-layouts  11.4 us (16%)
  matrix products  4.99 us (7%)
  other arithmetic  4.3 us (6%)
    all_gather x1, blocking collectives, body(): return lax.all_gather(updated, 'view', axis=0, tiled=True)  15.8 us
    all_to_all x1, waiting for transfers between devices, body(): arrived_logs = lax.all_to_all(outgoing, ('dom', 'view'), 0, 0, tiled=True)  15.1 us
    all_to_all x1, waiting for transfers between devices, body(): lax.all_to_all(outgoing, 'dom', split_axis=0, concat_axis=0, tiled=True)  7.32 us
    all_to_all x1, starting transfers between devices, body(): arrived_logs = lax.all_to_all(outgoing, ('dom', 'view'), 0, 0, tiled=True)  5.73 us
    dot_general x2, matrix products, rows_mixed(): return jnp.einsum('pri,pix->prx', mix, field, precision=precise)  4.99 us
    all_to_all x1, starting transfers between devices, body(): lax.all_to_all(outgoing, 'dom', split_axis=0, concat_axis=0, tiled=True)  4.37 us
    gather x1, local copies, waits for them, and re-layouts, body(): outgoing = jnp.take(flat_blocks, send_index, axis=0, mode='clip')  2.66 us
    ppermute x1, starting transfers between devices, extended_2(): before = lax.ppermute(last, axis, up)  2.42 us
  transfers between devices with their start and end apart: 4, of which 2 were waited for; matrix products, arithmetic and copies ran while one was open for 11% of the time, Pallas kernels for 0%

profile of v11, /device:TPU:0, one launch (start us, length us, event | category | flops | bytes accessed | tf_op | source)
XLA Modules:
  0.0 73.0 jit_solution(17212269546347175408)
XLA Ops:
  0.0 0.5 broadcast.470
  0.5 1.3 %fusion.198 = (s32[16]{0:T(128)S(1)}, s32[1,16]{1,0:T(1,128)S(1)}) fusion(s32[]{:T(128)} %broadcast.470, s32[4,16]{1,0:T(4,128)} %param.8, s32[]{:T(128)S(6)} %select_n.216), kind=kLoop, calls=%fused_computation.338 | loop fusion | bytes 200 | tf_op jit(solution)/shard_map/jit(dynamic_index_in_dim)/dynamic_slice | solution.py:72
  1.9 0.1 slice_reduce_fusion.1
  1.9 0.1 fusion.200
  2.0 0.1 slice.458
  2.1 0.1 slice.460
  2.2 0.1 stack_reshape.3
  2.3 0.2 fusion.186
  2.5 0.1 select_add_fusion
  2.5 0.1 reshape.592
  2.6 2.7 %gather_fusion = f32[128,8,256]{2,1,0:T(8,128)} fusion(f32[64,8,256]{2,1,0:T(8,128)} %bitcast.149, s32[1024]{0:T(1024)S(1)} %pad_clamp_fusion.3), kind=kCustom, calls=%fused_computation | custom fusion | bytes 2097664 | tf_op jit(solution)/shard_map/jit(_take)/gather | solution.py:106
  5.3 4.4 %all-to-all-start = ((f32[128,8,256]{2,1,0:T(8,128)}), f32[128,8,256]{2,1,0:T(8,128)S(1)}, u32[]{:S(2)}, u32[]{:S(2)}) async-start(f32[128,8,256]{2,1,0:T(8,128)} %gather_fusion), calls=%async_computation | async-start | bytes 2097152 | tf_op jit(solution)/shard_map/all_to_all | solution.py:108
  9.7 2.4 %collective-permute-start = (f32[4,32,256]{2,1,0:T(8,128)S(1)}, f32[4,32,256]{2,1,0:T(8,128)S(1)}, u32[]{:S(2)}, u32[]{:S(2)}) collective-permute-start(f32[4,32,256]{2,1,0:T(8,128)S(1)} %get-tuple-element.9), channel_id=1, source_target_pairs={{0,4},{4,8},{8,12},{1,5},{5,9},{9,13},{2,6},{6,10},{10,14},{3,7},{... | collective-permute-start | bytes 393224 | tf_op jit(solution)/shard_map/ppermute | solution.py:19
  12.1 1.3 %collective-permute-start.1 = (f32[4,32,256]{2,1,0:T(8,128)S(1)}, f32[4,32,256]{2,1,0:T(8,128)S(1)}, u32[]{:S(2)}, u32[]{:S(2)}) collective-permute-start(f32[4,32,256]{2,1,0:T(8,128)S(1)} %get-tuple-element.10), channel_id=1, source_target_pairs={{4,0},{8,4},{12,8},{5,1},{9,5},{13,9},{6,2},{10,6},{14,10},{7,3},{... | collective-permute-start | bytes 393224 | tf_op jit(solution)/shard_map/ppermute | solution.py:20
  13.6 0.1 reshape.586
  13.7 0.1 select_reduce_fusion.2
  13.8 0.1 iota_add_fusion
  13.9 0.1 reshape.600
  14.0 0.6 fusion.199
  14.6 0.6 reshape.583
  15.3 0.6 reshape.584
  15.9 0.1 pad_add_fusion.1
  16.0 0.1 dynamic_slice.21
  16.1 0.1 copy.12
  16.2 0.1 select_reduce_fusion
  16.3 0.1 slice_bitcast_fusion.47
  16.4 0.1 broadcast_add_fusion
  16.5 0.1 reshape.608
  16.6 0.1 slice_bitcast_fusion.58
  16.7 0.1 slice_bitcast_fusion.48
  16.8 7.3 %all-to-all-done = f32[128,8,256]{2,1,0:T(8,128)S(1)} async-done(((f32[128,8,256]{2,1,0:T(8,128)}), f32[128,8,256]{2,1,0:T(8,128)S(1)}, u32[]{:S(2)}, u32[]{:S(2)}) %all-to-all-start) | async-done | bytes 1048608 | tf_op jit(solution)/shard_map/all_to_all | solution.py:108
  24.1 0.8 %gather_fusion.1 = f32[128,8,256]{2,1,0:T(8,128)S(1)} fusion(f32[128,8,256]{2,1,0:T(8,128)S(1)} %all-to-all-done, s32[1024]{0:T(1024)S(1)} %pad_clamp_fusion.2), kind=kCustom, calls=%fused_computation.1 | custom fusion | bytes 2097664 | tf_op jit(solution)/shard_map/jit(_take)/gather | solution.py:116
  24.9 3.8 %convolution_select_fusion = f32[32,32,256]{2,1,0:T(8,128)S(1)} fusion(f32[32,32,256]{2,1,0:T(8,128)S(1)} %bitcast.152, f32[32]{0:T(128)S(1)} %get-tuple-element.15, f32[32]{0:T(128)S(1)} %get-tuple-element.16, f32[32]{0:T(128)S(1)} %get-tuple-element.17, f32[32]{0:T(128)S(1)} %get-tuple-element.18, f32[32]{0:T(128)S(1)} %get-tuple-element.19, ...), kind=kOutput, calls=%fused_computation.20 | convolution fusion | flops 105938944 | bytes 2108704 | tf_op jit(solution)/shard_map/pri,pix->prx/dot_general | solution.py:50
  28.7 0.9 %fusion.27 = f32[24,32,256]{2,1,0:T(8,128)S(1)} fusion(f32[32,32,256]{2,1,0:T(8,128)S(1)} %convolution_select_fusion, f32[4,32,256]{2,1,0:T(8,128)S(1)} %collective-permute-done.1, f32[16,32,256]{2,1,0:T(8,128)S(1)} %bitcast.151, f32[4,32,256]{2,1,0:T(8,128)S(1)} %collective-permute-done, f32[24]{0:T(128)S(1)} %get-tuple-element.60, ...), kind=kLoop, calls=%fused_computation.41 | loop fusion | flops 4128768 | bytes 8651640 | tf_op jit(solution)/shard_map/jit(_where)/select_n | solution.py:138
  29.5 1.2 %fusion.53 = f32[16,32,256]{2,1,0:T(8,128)S(1)} fusion(f32[24,32,256]{2,1,0:T(8,128)S(1)} %fusion.27, f32[16]{0:T(128)S(1)} %get-tuple-element.51, f32[16]{0:T(128)S(1)} %get-tuple-element.52, f32[16]{0:T(128)S(1)} %get-tuple-element.53, f32[16]{0:T(128)S(1)} %get-tuple-element.54, f32[16]{0:T(128)S(1)} %get-tuple-element.55, f32[16]{0:T(128)S(1)} %get-tuple-element.56, ...), kind=kOutput, calls=%fused_computation.76 | convolution fusion | flops 52838400 | bytes 5288960 | tf_op jit(solution)/shard_map/pri,pix->prx/dot_general | solution.py:50
  30.8 1.3 %fusion.44 = f32[16,32,256]{2,1,0:T(8,128)S(1)} fusion(f32[16,32,256]{2,1,0:T(8,128)S(1)} %fusion.53, f32[16]{0:T(128)S(1)} %get-tuple-element.33, f32[16]{0:T(128)S(1)} %get-tuple-element.34, f32[16]{0:T(128)S(1)} %get-tuple-element.35, f32[16]{0:T(128)S(1)} %get-tuple-element.36, f32[16]{0:T(128)S(1)} %get-tuple-element.37, f32[16]{0:T(128)S(1)} %get-tuple-element.38, ...), kind=kLoop, calls=%fused_computation.66 | loop fusion | flops 2228224 | bytes 1049152 | tf_op jit(solution)/shard_map/log | solution.py:149
  32.1 0.0 copy-start.3
  32.1 1.4 %gather_fusion.2 = f32[64,8,256]{2,1,0:T(8,128)} fusion(f32[64,8,256]{2,1,0:T(8,128)S(1)} %bitcast.150, s32[1024]{0:T(1024)S(1)} %pad_clamp_fusion.1), kind=kCustom, calls=%fused_computation.2 | custom fusion | bytes 1048832 | tf_op jit(solution)/shard_map/jit(_take)/gather | solution.py:151
  33.5 5.7 %all-to-all-start.1 = ((f32[16,4,8,256]{3,2,1,0:T(8,128)}), f32[16,4,8,256]{3,2,1,0:T(8,128)S(1)}, u32[]{:S(2)}, u32[]{:S(2)}) async-start(f32[16,4,8,256]{3,2,1,0:T(8,128)} %bitcast.75), calls=%async_computation.1 | async-start | bytes 1048576 | tf_op jit(solution)/shard_map/all_to_all | solution.py:153
  39.3 0.1 reshape.589
  39.4 0.2 fusion.182
  39.5 0.1 select_reduce_fusion.1
  39.6 0.1 reshape.616
  39.7 15.1 %all-to-all-done.1 = f32[16,4,8,256]{3,2,1,0:T(8,128)S(1)} async-done(((f32[16,4,8,256]{3,2,1,0:T(8,128)}), f32[16,4,8,256]{3,2,1,0:T(8,128)S(1)}, u32[]{:S(2)}, u32[]{:S(2)}) %all-to-all-start.1) | async-done | bytes 524320 | tf_op jit(solution)/shard_map/all_to_all | solution.py:153
  54.8 0.6 gather_fusion.3
  55.4 1.0 %bitcast_multiply_fusion = f32[4,32,256]{2,1,0:T(8,128)S(1)} fusion(f32[16,32,256]{2,1,0:T(8,128)} %param.5, s32[]{:T(128)S(6)} %select_n.193, f32[16,4,8,256]{3,2,1,0:T(8,128)S(1)} %gather_fusion.3), kind=kLoop, calls=%fused_computation.169 | loop fusion | flops 163840 | bytes 786436 | tf_op jit(solution)/shard_map/mul | solution.py:170
  56.4 15.8 %all_gather.3 = f32[16,32,256]{2,1,0:T(8,128)S(1)} all-gather(f32[4,32,256]{2,1,0:T(8,128)S(1)} %bitcast_multiply_fusion), channel_id=1, replica_groups=mesh['tile'=2,'dom'=4,'view'=4] {'view'}, dimensions={0}, use_global_device_ids=true | all-gather | bytes 655360 | tf_op jit(solution)/shard_map/all_gather | solution.py:171
  72.2 0.8 %copy.16 = f32[16,32,256]{2,1,0:T(8,128)} copy(f32[16,32,256]{2,1,0:T(8,128)S(1)} %all_gather.3) | data formatting | bytes 1048576
  (37 shorter events, 0.3 us)
Async XLA Ops:
  5.3 4.4 %copy-start = (f32[1,16,32,256]{3,2,1,0:T(8,128)S(1)}, f32[1,16,32,256]{3,2,1,0:T(8,128)}, u32[]{:S(2)}) copy-start(f32[1,16,32,256]{3,2,1,0:T(8,128)} %param.6) | copy-start | bytes 1572868
  5.3 8.7 %copy-start.2 = (s32[1,64]{1,0:T(1,128)S(1)}, s32[1,64]{1,0:T(1,128)}, u32[]{:S(2)}) copy-start(s32[1,64]{1,0:T(1,128)} %param.9) | copy-start | bytes 772
  5.3 10.8 %copy-start.1 = (f32[1,4,3,9]{3,1,2,0:T(4,128)S(1)}, f32[1,4,3,9]{3,1,2,0:T(4,128)}, u32[]{:S(2)}) copy-start(f32[1,4,3,9]{3,1,2,0:T(4,128)} %param.7) | copy-start | bytes 1300
  5.3 18.8 %all-to-all-start = ((f32[128,8,256]{2,1,0:T(8,128)}), f32[128,8,256]{2,1,0:T(8,128)S(1)}, u32[]{:S(2)}, u32[]{:S(2)}) async-start(f32[128,8,256]{2,1,0:T(8,128)} %gather_fusion), calls=%async_computation | async-start | bytes 2097152 | tf_op jit(solution)/shard_map/all_to_all | solution.py:108
  9.7 19.0 %collective-permute-start = (f32[4,32,256]{2,1,0:T(8,128)S(1)}, f32[4,32,256]{2,1,0:T(8,128)S(1)}, u32[]{:S(2)}, u32[]{:S(2)}) collective-permute-start(f32[4,32,256]{2,1,0:T(8,128)S(1)} %get-tuple-element.9), channel_id=1, source_target_pairs={{0,4},{4,8},{8,12},{1,5},{5,9},{9,13},{2,6},{6,10},{10,14},{3,7},{... | collective-permute-start | bytes 393224 | tf_op jit(solution)/shard_map/ppermute | solution.py:19
  12.1 16.6 %collective-permute-start.1 = (f32[4,32,256]{2,1,0:T(8,128)S(1)}, f32[4,32,256]{2,1,0:T(8,128)S(1)}, u32[]{:S(2)}, u32[]{:S(2)}) collective-permute-start(f32[4,32,256]{2,1,0:T(8,128)S(1)} %get-tuple-element.10), channel_id=1, source_target_pairs={{4,0},{8,4},{12,8},{5,1},{9,5},{13,9},{6,2},{10,6},{14,10},{7,3},{... | collective-permute-start | bytes 393224 | tf_op jit(solution)/shard_map/ppermute | solution.py:20
  32.1 7.2 %copy-start.3 = (s32[4,16]{1,0:T(4,128)S(1)}, s32[4,16]{1,0:T(4,128)}, u32[]{:S(2)}) copy-start(s32[4,16]{1,0:T(4,128)} %param.8) | copy-start | bytes 772
  33.5 21.3 %all-to-all-start.1 = ((f32[16,4,8,256]{3,2,1,0:T(8,128)}), f32[16,4,8,256]{3,2,1,0:T(8,128)S(1)}, u32[]{:S(2)}, u32[]{:S(2)}) async-start(f32[16,4,8,256]{3,2,1,0:T(8,128)} %bitcast.75), calls=%async_computation.1 | async-start | bytes 1048576 | tf_op jit(solution)/shard_map/all_to_all | solution.py:153

commit v12 on v10

--- a/solution.py
+++ b/solution.py
@@ -135,9 +135,10 @@
     piece_planes = plane_count // view_count
     logs = jnp.log(back).reshape(plane_count * block_count, block_rows, lane_count)
     piece_index = jnp.arange(plane_count, dtype=jnp.int32)[None, :] * block_count + dest_slot[:, None]
+    piece_index = piece_index.reshape(block_count, view_count, piece_planes).transpose(1, 0, 2)
     outgoing = jnp.take(logs, piece_index.reshape(-1), axis=0, mode="clip")
     outgoing = outgoing.reshape(block_count * view_count, piece_planes, block_rows, lane_count)
-    arrived_logs = lax.all_to_all(outgoing, ("dom", "view"), 0, 0, tiled=True)
+    arrived_logs = lax.all_to_all(outgoing, ("view", "dom"), 0, 0, tiled=True)
     all_grid = src_map.reshape(view_count, block_count, block_count)
     all_dev = all_grid // block_count
     all_slot = all_grid % block_count
@@ -146,7 +147,7 @@
         jnp.where(slot_of[:, :, None] == slot_ids[None, None, :], slot_ids[None, :, None], 0), axis=1
     )
     view_ids = jnp.arange(view_count, dtype=jnp.int32)
-    flat_index = (cam_of * view_count + view_ids[:, None]).reshape(-1)
+    flat_index = (view_ids[:, None] * block_count + cam_of).reshape(-1)
     by_view = jnp.take(arrived_logs, flat_index, axis=0, mode="clip")
     by_view = by_view.reshape(view_count, block_count, piece_planes, block_rows, lane_count)
     log_total = by_view[0]

time: 73.6 us -> 72.2 us (0.981)
  waiting for transfers between devices: 22.7 us -> 21.2 us
    all_to_all x1, waiting for transfers between devices: 15.1 us -> 13.8 us  [body(): arrived_logs = lax.all_to_all(outgoing, ('view', 'dom'), 0, 0, tiled=True)]
  transfers between devices with their start and end apart: 4 -> 4, of which waited for: 2 -> 2; matrix products, arithmetic and copies ran while one was open for 11% -> 12% of each run, Pallas kernels for 0% -> 0%
where the time goes in v12:
time: 72.2 us; the launch traced here: 71.7 us
  waiting for transfers between devices  21.2 us (29%)
  blocking collectives  15.7 us (22%)
  starting transfers between devices  13.8 us (19%)
  local copies, waits for them, and re-layouts  11.4 us (16%)
  other arithmetic  9.35 us (13%)
    all_gather x1, blocking collectives, body(): return lax.all_gather(updated, 'view', axis=0, tiled=True)  15.7 us
    all_to_all x1, waiting for transfers between devices, body(): arrived_logs = lax.all_to_all(outgoing, ('view', 'dom'), 0, 0, tiled=True)  13.8 us
    all_to_all x1, waiting for transfers between devices, body(): lax.all_to_all(outgoing, 'dom', split_axis=0, concat_axis=0, tiled=True)  7.46 us
    all_to_all x1, starting transfers between devices, body(): arrived_logs = lax.all_to_all(outgoing, ('view', 'dom'), 0, 0, tiled=True)  5.74 us
    all_to_all x1, starting transfers between devices, body(): lax.all_to_all(outgoing, 'dom', split_axis=0, concat_axis=0, tiled=True)  4.37 us
    add x2, other arithmetic, taps_along(): total = total + taps[offset][:, None, None] * piece  3.26 us
    gather x1, local copies, waits for them, and re-layouts, body(): outgoing = jnp.take(flat_blocks, send_index, axis=0, mode='clip')  2.67 us
    ppermute x1, starting transfers between devices, extended_2(): before = lax.ppermute(last, axis, up)  2.42 us
  transfers between devices with their start and end apart: 4, of which 2 were waited for; matrix products, arithmetic and copies ran while one was open for 12% of the time, Pallas kernels for 0%

profile of v12, /device:TPU:0, one launch (start us, length us, event | category | flops | bytes accessed | tf_op | source)
XLA Modules:
  0.0 71.7 jit_solution(1133903943272569751)
XLA Ops:
  0.0 0.5 broadcast.264
  0.5 1.3 %fusion.103 = (s32[16]{0:T(128)S(1)}, s32[1,16]{1,0:T(1,128)S(1)}) fusion(s32[]{:T(128)} %broadcast.264, s32[4,16]{1,0:T(4,128)} %param.8, s32[]{:T(128)S(6)} %select_n.142), kind=kLoop, calls=%fused_computation.273 | loop fusion | bytes 200 | tf_op jit(solution)/shard_map/jit(dynamic_index_in_dim)/dynamic_slice | solution.py:59
  1.9 0.1 slice_reduce_fusion.1
  2.0 0.1 slice.492
  2.1 0.1 slice.494
  2.2 0.1 stack_reshape.3
  2.3 0.2 fusion.93
  2.5 0.1 select_add_fusion
  2.5 0.1 reshape.412
  2.6 2.7 %gather_fusion = f32[128,8,256]{2,1,0:T(8,128)} fusion(f32[64,8,256]{2,1,0:T(8,128)} %bitcast.150, s32[1024]{0:T(1024)S(1)} %pad_clamp_fusion.3), kind=kCustom, calls=%fused_computation | custom fusion | bytes 2097664 | tf_op jit(solution)/shard_map/jit(_take)/gather | solution.py:93
  5.3 4.4 %all-to-all-start = ((f32[128,8,256]{2,1,0:T(8,128)}), f32[128,8,256]{2,1,0:T(8,128)S(1)}, u32[]{:S(2)}, u32[]{:S(2)}) async-start(f32[128,8,256]{2,1,0:T(8,128)} %gather_fusion), calls=%async_computation | async-start | bytes 2097152 | tf_op jit(solution)/shard_map/all_to_all | solution.py:95
  9.7 2.4 %collective-permute-start = (f32[4,32,256]{2,1,0:T(8,128)S(1)}, f32[4,32,256]{2,1,0:T(8,128)S(1)}, u32[]{:S(2)}, u32[]{:S(2)}) collective-permute-start(f32[4,32,256]{2,1,0:T(8,128)S(1)} %get-tuple-element.9), channel_id=1, source_target_pairs={{0,4},{4,8},{8,12},{1,5},{5,9},{9,13},{2,6},{6,10},{10,14},{3,7},{... | collective-permute-start | bytes 393224 | tf_op jit(solution)/shard_map/ppermute | solution.py:19
  12.1 1.3 %collective-permute-start.1 = (f32[4,32,256]{2,1,0:T(8,128)S(1)}, f32[4,32,256]{2,1,0:T(8,128)S(1)}, u32[]{:S(2)}, u32[]{:S(2)}) collective-permute-start(f32[4,32,256]{2,1,0:T(8,128)S(1)} %get-tuple-element.10), channel_id=1, source_target_pairs={{4,0},{8,4},{12,8},{5,1},{9,5},{13,9},{6,2},{10,6},{14,10},{7,3},{... | collective-permute-start | bytes 393224 | tf_op jit(solution)/shard_map/ppermute | solution.py:20
  13.4 0.1 reshape.406
  13.5 0.1 select_reduce_fusion.2
  13.7 0.1 iota_add_fusion
  13.7 0.1 reshape.420
  13.9 0.6 fusion.104
  14.5 0.6 reshape.403
  15.1 0.6 reshape.404
  15.8 0.1 pad_add_fusion.1
  15.9 0.1 dynamic_slice.21
  15.9 0.1 copy.12
  16.1 0.1 select_reduce_fusion
  16.2 0.1 slice_bitcast_fusion.55
  16.3 0.1 reshape.428
  16.5 0.1 slice_bitcast_fusion.58
  16.6 0.1 slice_bitcast_fusion.56
  16.6 7.5 %all-to-all-done = f32[128,8,256]{2,1,0:T(8,128)S(1)} async-done(((f32[128,8,256]{2,1,0:T(8,128)}), f32[128,8,256]{2,1,0:T(8,128)S(1)}, u32[]{:S(2)}, u32[]{:S(2)}) %all-to-all-start) | async-done | bytes 1048608 | tf_op jit(solution)/shard_map/all_to_all | solution.py:95
  24.1 0.8 %gather_fusion.1 = f32[128,8,256]{2,1,0:T(8,128)S(1)} fusion(f32[128,8,256]{2,1,0:T(8,128)S(1)} %all-to-all-done, s32[1024]{0:T(1024)S(1)} %pad_clamp_fusion.2), kind=kCustom, calls=%fused_computation.1 | custom fusion | bytes 2097664 | tf_op jit(solution)/shard_map/jit(_take)/gather | solution.py:103
  24.9 2.7 %fusion.25 = f32[32,32,256]{2,1,0:T(8,128)S(1)} fusion(f32[32,32,256]{2,1,0:T(8,128)S(1)} %bitcast.149, f32[32]{0:T(128)S(1)} %get-tuple-element.23, f32[32]{0:T(128)S(1)} %get-tuple-element.24, f32[32]{0:T(128)S(1)} %get-tuple-element.25, f32[32]{0:T(128)S(1)} %get-tuple-element.26, f32[32]{0:T(128)S(1)} %get-tuple-element.27, f32[32]{0:T(128)S(1)} %get-tuple-element.28, ...), kind=kLoop, calls=%fused_computation.53 | loop fusion | flops 4456448 | bytes 2098304 | tf_op jit(solution)/shard_map/add | solution.py:36
  27.5 1.4 %fusion.9 = f32[32,32,256]{2,1,0:T(8,128)S(1)} fusion(f32[32,32,256]{2,1,0:T(8,128)S(1)} %fusion.25, f32[32]{0:T(128)S(1)} %get-tuple-element.15, f32[32]{0:T(128)S(1)} %get-tuple-element.16, f32[32]{0:T(128)S(1)} %get-tuple-element.17, f32[32]{0:T(128)S(1)} %get-tuple-element.18, f32[32]{0:T(128)S(1)} %get-tuple-element.19, f32[32]{0:T(128)S(1)} %get-tuple-element.20, ...), kind=kLoop, calls=%fused_computation.37 | loop fusion | flops 4718592 | bytes 2098336 | tf_op jit(solution)/shard_map/jit(_where)/select_n | solution.py:116
  29.0 0.9 %fusion.35 = f32[24,32,256]{2,1,0:T(8,128)S(1)} fusion(f32[32,32,256]{2,1,0:T(8,128)S(1)} %fusion.9, f32[4,32,256]{2,1,0:T(8,128)S(1)} %collective-permute-done.1, f32[16,32,256]{2,1,0:T(8,128)S(1)} %bitcast.152, f32[4,32,256]{2,1,0:T(8,128)S(1)} %collective-permute-done, f32[24]{0:T(128)S(1)} %get-tuple-element.60, f32[24]{0:T(128)S(1)} %get-tuple-element.61, ...), kind=kLoop, calls=%fused_computation.72 | loop fusion | flops 4128768 | bytes 8651640 | tf_op jit(solution)/shard_map/jit(_where)/select_n | solution.py:125
  29.9 0.4 fusion.76
  30.3 0.6 fusion.51
  30.9 1.3 %fusion.68 = f32[16,32,256]{2,1,0:T(8,128)S(1)} fusion(f32[16,32,256]{2,1,0:T(8,128)S(1)} %fusion.51, f32[16]{0:T(128)S(1)} %get-tuple-element.33, f32[16]{0:T(128)S(1)} %get-tuple-element.34, f32[16]{0:T(128)S(1)} %get-tuple-element.35, f32[16]{0:T(128)S(1)} %get-tuple-element.36, f32[16]{0:T(128)S(1)} %get-tuple-element.37, f32[16]{0:T(128)S(1)} %get-tuple-element.38, ...), kind=kLoop, calls=%fused_computation.113 | loop fusion | flops 2228224 | bytes 1049152 | tf_op jit(solution)/shard_map/log | solution.py:136
  32.2 1.4 %gather_fusion.2 = f32[64,8,256]{2,1,0:T(8,128)} fusion(f32[64,8,256]{2,1,0:T(8,128)S(1)} %bitcast.151, s32[1024]{0:T(1024)S(1)} %pad_clamp_fusion.1), kind=kCustom, calls=%fused_computation.2 | custom fusion | bytes 1048832 | tf_op jit(solution)/shard_map/jit(_take)/gather | solution.py:139
  33.7 5.7 %all-to-all-start.1 = ((f32[16,4,8,256]{3,2,1,0:T(8,128)}), f32[16,4,8,256]{3,2,1,0:T(8,128)S(1)}, u32[]{:S(2)}, u32[]{:S(2)}) async-start(f32[16,4,8,256]{3,2,1,0:T(8,128)} %bitcast.75), calls=%async_computation.1 | async-start | bytes 1048576 | tf_op jit(solution)/shard_map/all_to_all | solution.py:141
  39.4 0.1 reshape.409
  39.5 0.2 fusion.89
  39.7 0.1 select_reduce_fusion.1
  39.8 0.1 broadcast_add_fusion.1
  39.8 0.1 reshape.436
  39.9 13.8 %all-to-all-done.1 = f32[16,4,8,256]{3,2,1,0:T(8,128)S(1)} async-done(((f32[16,4,8,256]{3,2,1,0:T(8,128)}), f32[16,4,8,256]{3,2,1,0:T(8,128)S(1)}, u32[]{:S(2)}, u32[]{:S(2)}) %all-to-all-start.1) | async-done | bytes 524320 | tf_op jit(solution)/shard_map/all_to_all | solution.py:141
  53.7 0.6 gather_fusion.3
  54.3 1.0 %bitcast_multiply_fusion = f32[4,32,256]{2,1,0:T(8,128)S(1)} fusion(f32[16,32,256]{2,1,0:T(8,128)} %param.5, s32[]{:T(128)S(6)} %select_n.137, f32[16,4,8,256]{3,2,1,0:T(8,128)S(1)} %gather_fusion.3), kind=kLoop, calls=%fused_computation.144 | loop fusion | flops 163840 | bytes 786436 | tf_op jit(solution)/shard_map/mul | solution.py:158
  55.2 15.7 %all_gather.3 = f32[16,32,256]{2,1,0:T(8,128)S(1)} all-gather(f32[4,32,256]{2,1,0:T(8,128)S(1)} %bitcast_multiply_fusion), channel_id=1, replica_groups=mesh['tile'=2,'dom'=4,'view'=4] {'view'}, dimensions={0}, use_global_device_ids=true | all-gather | bytes 655360 | tf_op jit(solution)/shard_map/all_gather | solution.py:159
  70.9 0.8 %copy.16 = f32[16,32,256]{2,1,0:T(8,128)} copy(f32[16,32,256]{2,1,0:T(8,128)S(1)} %all_gather.3) | data formatting | bytes 1048576
  (29 shorter events, 0.3 us)
Async XLA Ops:
  5.3 4.4 %copy-start = (f32[1,16,32,256]{3,2,1,0:T(8,128)S(1)}, f32[1,16,32,256]{3,2,1,0:T(8,128)}, u32[]{:S(2)}) copy-start(f32[1,16,32,256]{3,2,1,0:T(8,128)} %param.6) | copy-start | bytes 1572868
  5.3 8.6 %copy-start.2 = (s32[1,64]{1,0:T(1,128)S(1)}, s32[1,64]{1,0:T(1,128)}, u32[]{:S(2)}) copy-start(s32[1,64]{1,0:T(1,128)} %param.9) | copy-start | bytes 772
  5.3 10.6 %copy-start.1 = (f32[1,4,3,9]{3,1,2,0:T(4,128)S(1)}, f32[1,4,3,9]{3,1,2,0:T(4,128)}, u32[]{:S(2)}) copy-start(f32[1,4,3,9]{3,1,2,0:T(4,128)} %param.7) | copy-start | bytes 1300
  5.3 18.8 %all-to-all-start = ((f32[128,8,256]{2,1,0:T(8,128)}), f32[128,8,256]{2,1,0:T(8,128)S(1)}, u32[]{:S(2)}, u32[]{:S(2)}) async-start(f32[128,8,256]{2,1,0:T(8,128)} %gather_fusion), calls=%async_computation | async-start | bytes 2097152 | tf_op jit(solution)/shard_map/all_to_all | solution.py:95
  9.7 19.2 %collective-permute-start = (f32[4,32,256]{2,1,0:T(8,128)S(1)}, f32[4,32,256]{2,1,0:T(8,128)S(1)}, u32[]{:S(2)}, u32[]{:S(2)}) collective-permute-start(f32[4,32,256]{2,1,0:T(8,128)S(1)} %get-tuple-element.9), channel_id=1, source_target_pairs={{0,4},{4,8},{8,12},{1,5},{5,9},{9,13},{2,6},{6,10},{10,14},{3,7},{... | collective-permute-start | bytes 393224 | tf_op jit(solution)/shard_map/ppermute | solution.py:19
  12.1 16.8 %collective-permute-start.1 = (f32[4,32,256]{2,1,0:T(8,128)S(1)}, f32[4,32,256]{2,1,0:T(8,128)S(1)}, u32[]{:S(2)}, u32[]{:S(2)}) collective-permute-start(f32[4,32,256]{2,1,0:T(8,128)S(1)} %get-tuple-element.10), channel_id=1, source_target_pairs={{4,0},{8,4},{12,8},{5,1},{9,5},{13,9},{6,2},{10,6},{14,10},{7,3},{... | collective-permute-start | bytes 393224 | tf_op jit(solution)/shard_map/ppermute | solution.py:20
  32.2 7.2 %copy-start.3 = (s32[4,16]{1,0:T(4,128)S(1)}, s32[4,16]{1,0:T(4,128)}, u32[]{:S(2)}) copy-start(s32[4,16]{1,0:T(4,128)} %param.8) | copy-start | bytes 772
  33.7 20.0 %all-to-all-start.1 = ((f32[16,4,8,256]{3,2,1,0:T(8,128)}), f32[16,4,8,256]{3,2,1,0:T(8,128)S(1)}, u32[]{:S(2)}, u32[]{:S(2)}) async-start(f32[16,4,8,256]{3,2,1,0:T(8,128)} %bitcast.75), calls=%async_computation.1 | async-start | bytes 1048576 | tf_op jit(solution)/shard_map/all_to_all | solution.py:141

commit v13 on v12

--- a/solution.py
+++ b/solution.py
@@ -40,11 +40,6 @@
 def lateral_fwd(field, x_taps, y_taps):
     inner = taps_along(field, x_taps, 2, False)
     return taps_along(inner, y_taps, 1, False)
-
-
-def lateral_back(field, x_taps, y_taps):
-    inner = taps_along(field, y_taps, 1, True)
-    return taps_along(inner, x_taps, 2, True)
 
 
 def body(estimate, observed, psf, src_map, depth_band):
@@ -128,16 +123,20 @@
     zback = jnp.zeros((plane_count, row_count, lane_count), jnp.float32)
     for m in range(2 * reach + 1):
         zback = zback + taps_ext[2 * reach - m, m : m + plane_count][:, None, None] * ratio_ext[m : m + plane_count]
-    back = lateral_back(zback, x_own, y_own)
     dest_slot = jnp.sum(
         jnp.where(my_sources[None, :] == slot_ids[:, None], slot_ids[None, :], 0), axis=1
     )
+    row_ids = jnp.arange(block_rows, dtype=jnp.int32)
+    out_rows = (dest_slot[:, None] * block_rows + row_ids[None, :]).reshape(row_count)
+    offset = out_rows[:, None] - jnp.arange(row_count, dtype=jnp.int32)[None, :]
+    mix = jnp.zeros((plane_count, row_count, row_count), jnp.float32)
+    for tap in range(2 * reach + 1):
+        mix = mix + jnp.where((offset == tap - reach)[None], y_own[tap][:, None, None], 0.0)
+    by_source = jnp.einsum("pri,pix->prx", mix, zback, precision=lax.Precision.HIGHEST)
+    back = taps_along(by_source, x_own, 2, True)
     piece_planes = plane_count // view_count
-    logs = jnp.log(back).reshape(plane_count * block_count, block_rows, lane_count)
-    piece_index = jnp.arange(plane_count, dtype=jnp.int32)[None, :] * block_count + dest_slot[:, None]
-    piece_index = piece_index.reshape(block_count, view_count, piece_planes).transpose(1, 0, 2)
-    outgoing = jnp.take(logs, piece_index.reshape(-1), axis=0, mode="clip")
-    outgoing = outgoing.reshape(block_count * view_count, piece_planes, block_rows, lane_count)
+    logs = jnp.log(back).reshape(view_count, piece_planes, block_count, block_rows, lane_count)
+    outgoing = logs.transpose(0, 2, 1, 3, 4).reshape(view_count * block_count, piece_planes, block_rows, lane_count)
     arrived_logs = lax.all_to_all(outgoing, ("view", "dom"), 0, 0, tiled=True)
     all_grid = src_map.reshape(view_count, block_count, block_count)
     all_dev = all_grid // block_count

time: 72.2 us -> 71.8 us (level)
  matrix products: 0 us -> 1.21 us
  other arithmetic: 9.35 us -> 8.44 us
    gather x1 -> x0, local copies, waits for them, and re-layouts: 1.43 us -> none  [body(): outgoing = jnp.take(logs, piece_index.reshape(-1), axis=0, mode='clip')]
    dot_general x0 -> x1, matrix products: none -> 1.21 us  [body(): jnp.einsum('pri,pix->prx', mix, zback, precision=lax.Precision.HIGHEST)]
    reshape x0 -> x1, local copies, waits for them, and re-layouts: none -> 0.85 us  [body(): jnp.log(back)]
    add x2 -> x1, other arithmetic: 3.26 us -> 2.66 us  [taps_along(): total = total + taps[offset][:, None, None] * piece]
where the time goes in v13:
time: 71.8 us; the launch traced here: 71.3 us
  waiting for transfers between devices  21.2 us (30%)
  blocking collectives  15.7 us (22%)
  starting transfers between devices  13.8 us (19%)
  local copies, waits for them, and re-layouts  10.8 us (15%)
  other arithmetic  8.44 us (12%)
  matrix products  1.21 us (2%)
    all_gather x1, blocking collectives, body(): return lax.all_gather(updated, 'view', axis=0, tiled=True)  15.7 us
    all_to_all x1, waiting for transfers between devices, body(): arrived_logs = lax.all_to_all(outgoing, ('view', 'dom'), 0, 0, tiled=True)  13.8 us
    all_to_all x1, waiting for transfers between devices, body(): lax.all_to_all(outgoing, 'dom', split_axis=0, concat_axis=0, tiled=True)  7.39 us
    all_to_all x1, starting transfers between devices, body(): arrived_logs = lax.all_to_all(outgoing, ('view', 'dom'), 0, 0, tiled=True)  5.74 us
    all_to_all x1, starting transfers between devices, body(): lax.all_to_all(outgoing, 'dom', split_axis=0, concat_axis=0, tiled=True)  4.37 us
    gather x1, local copies, waits for them, and re-layouts, body(): outgoing = jnp.take(flat_blocks, send_index, axis=0, mode='clip')  2.67 us
    add x1, other arithmetic, taps_along(): total = total + taps[offset][:, None, None] * piece  2.66 us
    ppermute x1, starting transfers between devices, extended_2(): before = lax.ppermute(last, axis, up)  2.42 us
  transfers between devices with their start and end apart: 4, of which 2 were waited for; matrix products, arithmetic and copies ran while one was open for 12% of the time, Pallas kernels for 0%

profile of v13, /device:TPU:0, one launch (start us, length us, event | category | flops | bytes accessed | tf_op | source)
XLA Modules:
  0.0 71.3 jit_solution(5513227237306217971)
XLA Ops:
  0.0 0.5 broadcast.369
  0.5 1.3 %fusion.151 = (s32[16]{0:T(128)S(1)}, s32[1,16]{1,0:T(1,128)S(1)}) fusion(s32[]{:T(128)} %broadcast.369, s32[4,16]{1,0:T(4,128)} %param.8, s32[]{:T(128)S(6)} %select_n.168), kind=kLoop, calls=%fused_computation.304 | loop fusion | bytes 200 | tf_op jit(solution)/shard_map/jit(dynamic_index_in_dim)/dynamic_slice | solution.py:54
  1.9 0.1 slice_reduce_fusion.1
  2.0 0.1 slice.475
  2.1 0.1 slice.477
  2.2 0.1 stack_reshape.3
  2.3 0.2 fusion.140
  2.5 0.1 select_add_fusion
  2.5 0.1 reshape.558
  2.6 2.7 %gather_fusion = f32[128,8,256]{2,1,0:T(8,128)} fusion(f32[64,8,256]{2,1,0:T(8,128)} %bitcast.152, s32[1024]{0:T(1024)S(1)} %pad_clamp_fusion.2), kind=kCustom, calls=%fused_computation | custom fusion | bytes 2097664 | tf_op jit(solution)/shard_map/jit(_take)/gather | solution.py:88
  5.3 4.4 %all-to-all-start = ((f32[128,8,256]{2,1,0:T(8,128)}), f32[128,8,256]{2,1,0:T(8,128)S(1)}, u32[]{:S(2)}, u32[]{:S(2)}) async-start(f32[128,8,256]{2,1,0:T(8,128)} %gather_fusion), calls=%async_computation | async-start | bytes 2097152 | tf_op jit(solution)/shard_map/all_to_all | solution.py:90
  9.7 2.4 %collective-permute-start = (f32[4,32,256]{2,1,0:T(8,128)S(1)}, f32[4,32,256]{2,1,0:T(8,128)S(1)}, u32[]{:S(2)}, u32[]{:S(2)}) collective-permute-start(f32[4,32,256]{2,1,0:T(8,128)S(1)} %get-tuple-element.9), channel_id=1, source_target_pairs={{0,4},{4,8},{8,12},{1,5},{5,9},{9,13},{2,6},{6,10},{10,14},{3,7},{... | collective-permute-start | bytes 393224 | tf_op jit(solution)/shard_map/ppermute | solution.py:19
  12.1 1.3 %collective-permute-start.1 = (f32[4,32,256]{2,1,0:T(8,128)S(1)}, f32[4,32,256]{2,1,0:T(8,128)S(1)}, u32[]{:S(2)}, u32[]{:S(2)}) collective-permute-start(f32[4,32,256]{2,1,0:T(8,128)S(1)} %get-tuple-element.10), channel_id=1, source_target_pairs={{4,0},{8,4},{12,8},{5,1},{9,5},{13,9},{6,2},{10,6},{14,10},{7,3},{... | collective-permute-start | bytes 393224 | tf_op jit(solution)/shard_map/ppermute | solution.py:20
  13.4 0.1 reshape.551
  13.5 0.6 fusion.152
  14.1 0.6 reshape.549
  14.8 0.6 reshape.550
  15.4 0.1 pad_add_fusion.1
  15.5 0.1 dynamic_slice.21
  15.6 0.1 copy.15
  15.7 0.1 select_reduce_fusion
  15.9 0.1 slice_bitcast_fusion.47
  15.9 0.1 select_reduce_fusion.2
  16.1 0.1 iota_add_fusion.1
  16.1 0.1 slice_bitcast_fusion.58
  16.2 0.1 iota_add_fusion
  16.3 0.1 reshape.566
  16.4 0.1 add.320
  16.5 0.1 slice_bitcast_fusion.48
  16.6 0.1 fusion.133
  16.7 7.4 %all-to-all-done = f32[128,8,256]{2,1,0:T(8,128)S(1)} async-done(((f32[128,8,256]{2,1,0:T(8,128)}), f32[128,8,256]{2,1,0:T(8,128)S(1)}, u32[]{:S(2)}, u32[]{:S(2)}) %all-to-all-start) | async-done | bytes 1048608 | tf_op jit(solution)/shard_map/all_to_all | solution.py:90
  24.1 0.8 %gather_fusion.1 = f32[128,8,256]{2,1,0:T(8,128)S(1)} fusion(f32[128,8,256]{2,1,0:T(8,128)S(1)} %all-to-all-done, s32[1024]{0:T(1024)S(1)} %pad_clamp_fusion.1), kind=kCustom, calls=%fused_computation.1 | custom fusion | bytes 2097664 | tf_op jit(solution)/shard_map/jit(_take)/gather | solution.py:98
  24.9 2.7 %fusion.25 = f32[32,32,256]{2,1,0:T(8,128)S(1)} fusion(f32[32,32,256]{2,1,0:T(8,128)S(1)} %bitcast.151, f32[32]{0:T(128)S(1)} %get-tuple-element.23, f32[32]{0:T(128)S(1)} %get-tuple-element.24, f32[32]{0:T(128)S(1)} %get-tuple-element.25, f32[32]{0:T(128)S(1)} %get-tuple-element.26, f32[32]{0:T(128)S(1)} %get-tuple-element.27, f32[32]{0:T(128)S(1)} %get-tuple-element.28, ...), kind=kLoop, calls=%fused_computation.52 | loop fusion | flops 4456448 | bytes 2098304 | tf_op jit(solution)/shard_map/add | solution.py:36
  27.5 1.4 %fusion.9 = f32[32,32,256]{2,1,0:T(8,128)S(1)} fusion(f32[32,32,256]{2,1,0:T(8,128)S(1)} %fusion.25, f32[32]{0:T(128)S(1)} %get-tuple-element.15, f32[32]{0:T(128)S(1)} %get-tuple-element.16, f32[32]{0:T(128)S(1)} %get-tuple-element.17, f32[32]{0:T(128)S(1)} %get-tuple-element.18, f32[32]{0:T(128)S(1)} %get-tuple-element.19, f32[32]{0:T(128)S(1)} %get-tuple-element.20, ...), kind=kLoop, calls=%fused_computation.36 | loop fusion | flops 4718592 | bytes 2098336 | tf_op jit(solution)/shard_map/jit(_where)/select_n | solution.py:111
  29.0 0.9 %fusion.35 = f32[24,32,256]{2,1,0:T(8,128)S(1)} fusion(f32[32,32,256]{2,1,0:T(8,128)S(1)} %fusion.9, f32[4,32,256]{2,1,0:T(8,128)S(1)} %collective-permute-done.1, f32[16,32,256]{2,1,0:T(8,128)S(1)} %bitcast.154, f32[4,32,256]{2,1,0:T(8,128)S(1)} %collective-permute-done, f32[24]{0:T(128)S(1)} %get-tuple-element.60, f32[24]{0:T(128)S(1)} %get-tuple-element.61, ...), kind=kLoop, calls=%fused_computation.63 | loop fusion | flops 4128768 | bytes 8651640 | tf_op jit(solution)/shard_map/jit(_where)/select_n | solution.py:120
  29.9 1.2 %fusion.61 = f32[16,32,256]{2,1,0:T(8,128)S(1)} fusion(f32[24,32,256]{2,1,0:T(8,128)S(1)} %fusion.35, f32[16]{0:T(128)S(1)} %get-tuple-element.51, f32[16]{0:T(128)S(1)} %get-tuple-element.52, f32[16]{0:T(128)S(1)} %get-tuple-element.53, f32[16]{0:T(128)S(1)} %get-tuple-element.54, f32[16]{0:T(128)S(1)} %get-tuple-element.55, f32[16]{0:T(128)S(1)} %get-tuple-element.56, ...), kind=kOutput, calls=%fused_computation.98 | convolution fusion | flops 52838400 | bytes 5288960 | tf_op jit(solution)/shard_map/pri,pix->prx/dot_general | solution.py:135
  31.1 1.3 %fusion.52 = f32[16,32,256]{2,1,0:T(8,128)S(1)} fusion(f32[16,32,256]{2,1,0:T(8,128)S(1)} %fusion.61, f32[16]{0:T(128)S(1)} %get-tuple-element.33, f32[16]{0:T(128)S(1)} %get-tuple-element.34, f32[16]{0:T(128)S(1)} %get-tuple-element.35, f32[16]{0:T(128)S(1)} %get-tuple-element.36, f32[16]{0:T(128)S(1)} %get-tuple-element.37, f32[16]{0:T(128)S(1)} %get-tuple-element.38, ...), kind=kLoop, calls=%fused_computation.88 | loop fusion | flops 2228224 | bytes 1049152 | tf_op jit(solution)/shard_map/log | solution.py:138
  32.4 0.8 %copy.16 = f32[4,4,4,8,256]{4,3,1,2,0:T(8,128)} copy(f32[4,4,4,8,256]{4,3,2,1,0:T(8,128)S(1)} %bitcast.153) | data formatting | bytes 1048576 | tf_op jit(solution)/shard_map/reshape | solution.py:138
  33.3 5.7 %all-to-all-start.1 = ((f32[16,4,8,256]{3,2,1,0:T(8,128)}), f32[16,4,8,256]{3,2,1,0:T(8,128)S(1)}, u32[]{:S(2)}, u32[]{:S(2)}) async-start(f32[16,4,8,256]{3,2,1,0:T(8,128)} %bitcast.76), calls=%async_computation.1 | async-start | bytes 1048576 | tf_op jit(solution)/shard_map/all_to_all | solution.py:140
  39.0 0.1 reshape.555
  39.1 0.2 fusion.136
  39.3 0.1 select_reduce_fusion.1
  39.4 0.1 reshape.574
  39.5 13.8 %all-to-all-done.1 = f32[16,4,8,256]{3,2,1,0:T(8,128)S(1)} async-done(((f32[16,4,8,256]{3,2,1,0:T(8,128)}), f32[16,4,8,256]{3,2,1,0:T(8,128)S(1)}, u32[]{:S(2)}, u32[]{:S(2)}) %all-to-all-start.1) | async-done | bytes 524320 | tf_op jit(solution)/shard_map/all_to_all | solution.py:140
  53.3 0.6 gather_fusion.2
  53.9 1.0 %bitcast_multiply_fusion = f32[4,32,256]{2,1,0:T(8,128)S(1)} fusion(f32[16,32,256]{2,1,0:T(8,128)} %param.5, s32[]{:T(128)S(6)} %select_n.165, f32[16,4,8,256]{3,2,1,0:T(8,128)S(1)} %gather_fusion.2), kind=kLoop, calls=%fused_computation.146 | loop fusion | flops 163840 | bytes 786436 | tf_op jit(solution)/shard_map/mul | solution.py:157
  54.8 15.7 %all_gather.3 = f32[16,32,256]{2,1,0:T(8,128)S(1)} all-gather(f32[4,32,256]{2,1,0:T(8,128)S(1)} %bitcast_multiply_fusion), channel_id=1, replica_groups=mesh['tile'=2,'dom'=4,'view'=4] {'view'}, dimensions={0}, use_global_device_ids=true | all-gather | bytes 655360 | tf_op jit(solution)/shard_map/all_gather | solution.py:158
  70.5 0.8 %copy.20 = f32[16,32,256]{2,1,0:T(8,128)} copy(f32[16,32,256]{2,1,0:T(8,128)S(1)} %all_gather.3) | data formatting | bytes 1048576
  (29 shorter events, 0.3 us)
Async XLA Ops:
  5.3 4.4 %copy-start = (f32[1,16,32,256]{3,2,1,0:T(8,128)S(1)}, f32[1,16,32,256]{3,2,1,0:T(8,128)}, u32[]{:S(2)}) copy-start(f32[1,16,32,256]{3,2,1,0:T(8,128)} %param.6) | copy-start | bytes 1572868
  5.3 8.2 %copy-start.2 = (s32[1,64]{1,0:T(1,128)S(1)}, s32[1,64]{1,0:T(1,128)}, u32[]{:S(2)}) copy-start(s32[1,64]{1,0:T(1,128)} %param.9) | copy-start | bytes 772
  5.3 10.3 %copy-start.1 = (f32[1,4,3,9]{3,1,2,0:T(4,128)S(1)}, f32[1,4,3,9]{3,1,2,0:T(4,128)}, u32[]{:S(2)}) copy-start(f32[1,4,3,9]{3,1,2,0:T(4,128)} %param.7) | copy-start | bytes 1300
  5.3 18.8 %all-to-all-start = ((f32[128,8,256]{2,1,0:T(8,128)}), f32[128,8,256]{2,1,0:T(8,128)S(1)}, u32[]{:S(2)}, u32[]{:S(2)}) async-start(f32[128,8,256]{2,1,0:T(8,128)} %gather_fusion), calls=%async_computation | async-start | bytes 2097152 | tf_op jit(solution)/shard_map/all_to_all | solution.py:90
  9.7 19.2 %collective-permute-start = (f32[4,32,256]{2,1,0:T(8,128)S(1)}, f32[4,32,256]{2,1,0:T(8,128)S(1)}, u32[]{:S(2)}, u32[]{:S(2)}) collective-permute-start(f32[4,32,256]{2,1,0:T(8,128)S(1)} %get-tuple-element.9), channel_id=1, source_target_pairs={{0,4},{4,8},{8,12},{1,5},{5,9},{9,13},{2,6},{6,10},{10,14},{3,7},{... | collective-permute-start | bytes 393224 | tf_op jit(solution)/shard_map/ppermute | solution.py:19
  12.1 16.8 %collective-permute-start.1 = (f32[4,32,256]{2,1,0:T(8,128)S(1)}, f32[4,32,256]{2,1,0:T(8,128)S(1)}, u32[]{:S(2)}, u32[]{:S(2)}) collective-permute-start(f32[4,32,256]{2,1,0:T(8,128)S(1)} %get-tuple-element.10), channel_id=1, source_target_pairs={{4,0},{8,4},{12,8},{5,1},{9,5},{13,9},{6,2},{10,6},{14,10},{7,3},{... | collective-permute-start | bytes 393224 | tf_op jit(solution)/shard_map/ppermute | solution.py:20
  32.4 6.6 %copy-start.3 = (s32[4,16]{1,0:T(4,128)S(1)}, s32[4,16]{1,0:T(4,128)}, u32[]{:S(2)}) copy-start(s32[4,16]{1,0:T(4,128)} %param.8) | copy-start | bytes 772
  33.3 20.0 %all-to-all-start.1 = ((f32[16,4,8,256]{3,2,1,0:T(8,128)}), f32[16,4,8,256]{3,2,1,0:T(8,128)S(1)}, u32[]{:S(2)}, u32[]{:S(2)}) async-start(f32[16,4,8,256]{3,2,1,0:T(8,128)} %bitcast.76), calls=%async_computation.1 | async-start | bytes 1048576 | tf_op jit(solution)/shard_map/all_to_all | solution.py:140

commit v14 on v13

--- a/solution.py
+++ b/solution.py
@@ -153,9 +153,8 @@
     for v in range(1, view_count):
         log_total = log_total + by_view[v]
     log_total = log_total.transpose(1, 0, 2, 3).reshape(piece_planes, row_count, lane_count)
-    est_piece = lax.dynamic_slice_in_dim(estimate, view_index * piece_planes, piece_planes, 0)
-    updated = est_piece * jnp.exp(log_total / view_count)
-    return lax.all_gather(updated, "view", axis=0, tiled=True)
+    log_joined = lax.all_gather(log_total, "view", axis=0, tiled=True)
+    return estimate * jnp.exp(log_joined / view_count)
 
 
 def solution(mesh):

time: 71.8 us -> 70.9 us (0.987)
  local copies, waits for them, and re-layouts: 10.8 us -> 10 us
    unnamed x9 -> x10, local copies, waits for them, and re-layouts: 0.81 us -> 0.02 us
where the time goes in v14:
time: 70.9 us; the launch traced here: 70.5 us
  waiting for transfers between devices  21.1 us (30%)
  blocking collectives  15.7 us (22%)
  starting transfers between devices  13.8 us (19%)
  local copies, waits for them, and re-layouts  10 us (14%)
  other arithmetic  8.39 us (12%)
  matrix products  1.2 us (2%)
    all_gather x1, blocking collectives, body(): log_joined = lax.all_gather(log_total, 'view', axis=0, tiled=True)  15.7 us
    all_to_all x1, waiting for transfers between devices, body(): arrived_logs = lax.all_to_all(outgoing, ('view', 'dom'), 0, 0, tiled=True)  13.8 us
    all_to_all x1, waiting for transfers between devices, body(): lax.all_to_all(outgoing, 'dom', split_axis=0, concat_axis=0, tiled=True)  7.36 us
    all_to_all x1, starting transfers between devices, body(): arrived_logs = lax.all_to_all(outgoing, ('view', 'dom'), 0, 0, tiled=True)  5.74 us
    all_to_all x1, starting transfers between devices, body(): lax.all_to_all(outgoing, 'dom', split_axis=0, concat_axis=0, tiled=True)  4.37 us
    gather x1, local copies, waits for them, and re-layouts, body(): outgoing = jnp.take(flat_blocks, send_index, axis=0, mode='clip')  2.66 us
    add x1, other arithmetic, taps_along(): total = total + taps[offset][:, None, None] * piece  2.66 us
    ppermute x1, starting transfers between devices, extended_2(): before = lax.ppermute(last, axis, up)  2.42 us
  transfers between devices with their start and end apart: 4, of which 2 were waited for; matrix products, arithmetic and copies ran while one was open for 12% of the time, Pallas kernels for 0%

profile of v14, /device:TPU:0, one launch (start us, length us, event | category | flops | bytes accessed | tf_op | source)
XLA Modules:
  0.0 70.5 jit_solution(7177254492454294667)
XLA Ops:
  0.0 0.5 broadcast.365
  0.5 1.3 %fusion.149 = (s32[16]{0:T(128)S(1)}, s32[1,16]{1,0:T(1,128)S(1)}) fusion(s32[]{:T(128)} %broadcast.365, s32[4,16]{1,0:T(4,128)} %param.8, s32[]{:T(128)S(6)} %select_n.164), kind=kLoop, calls=%fused_computation.303 | loop fusion | bytes 200 | tf_op jit(solution)/shard_map/jit(dynamic_index_in_dim)/dynamic_slice | solution.py:54
  1.9 0.1 slice_reduce_fusion.1
  2.0 0.1 slice.475
  2.1 0.1 slice.477
  2.2 0.1 stack_reshape.3
  2.3 0.2 fusion.138
  2.5 0.1 select_add_fusion
  2.5 0.1 reshape.558
  2.6 2.7 %gather_fusion = f32[128,8,256]{2,1,0:T(8,128)} fusion(f32[64,8,256]{2,1,0:T(8,128)} %bitcast.151, s32[1024]{0:T(1024)S(1)} %pad_clamp_fusion.2), kind=kCustom, calls=%fused_computation | custom fusion | bytes 2097664 | tf_op jit(solution)/shard_map/jit(_take)/gather | solution.py:88
  5.3 4.4 %all-to-all-start = ((f32[128,8,256]{2,1,0:T(8,128)}), f32[128,8,256]{2,1,0:T(8,128)S(1)}, u32[]{:S(2)}, u32[]{:S(2)}) async-start(f32[128,8,256]{2,1,0:T(8,128)} %gather_fusion), calls=%async_computation | async-start | bytes 2097152 | tf_op jit(solution)/shard_map/all_to_all | solution.py:90
  9.7 2.4 %collective-permute-start = (f32[4,32,256]{2,1,0:T(8,128)S(1)}, f32[4,32,256]{2,1,0:T(8,128)S(1)}, u32[]{:S(2)}, u32[]{:S(2)}) collective-permute-start(f32[4,32,256]{2,1,0:T(8,128)S(1)} %get-tuple-element.9), channel_id=1, source_target_pairs={{0,4},{4,8},{8,12},{1,5},{5,9},{9,13},{2,6},{6,10},{10,14},{3,7},{... | collective-permute-start | bytes 393224 | tf_op jit(solution)/shard_map/ppermute | solution.py:19
  12.1 1.3 %collective-permute-start.1 = (f32[4,32,256]{2,1,0:T(8,128)S(1)}, f32[4,32,256]{2,1,0:T(8,128)S(1)}, u32[]{:S(2)}, u32[]{:S(2)}) collective-permute-start(f32[4,32,256]{2,1,0:T(8,128)S(1)} %get-tuple-element.10), channel_id=1, source_target_pairs={{4,0},{8,4},{12,8},{5,1},{9,5},{13,9},{6,2},{10,6},{14,10},{7,3},{... | collective-permute-start | bytes 393224 | tf_op jit(solution)/shard_map/ppermute | solution.py:20
  13.4 0.1 reshape.550
  13.5 0.6 fusion.150
  14.2 0.6 reshape.548
  14.8 0.6 reshape.549
  15.5 0.1 pad_add_fusion.1
  15.5 0.1 dynamic_slice.17
  15.6 0.1 copy.15
  15.8 0.1 select_reduce_fusion
  15.9 0.1 slice_bitcast_fusion.47
  16.0 0.1 select_reduce_fusion.2
  16.1 0.1 iota_add_fusion.1
  16.2 0.1 slice_bitcast_fusion.58
  16.2 0.1 iota_add_fusion
  16.3 0.1 reshape.566
  16.4 0.1 add.316
  16.6 0.1 slice_bitcast_fusion.48
  16.6 0.1 fusion.131
  16.7 7.4 %all-to-all-done = f32[128,8,256]{2,1,0:T(8,128)S(1)} async-done(((f32[128,8,256]{2,1,0:T(8,128)}), f32[128,8,256]{2,1,0:T(8,128)S(1)}, u32[]{:S(2)}, u32[]{:S(2)}) %all-to-all-start) | async-done | bytes 1048608 | tf_op jit(solution)/shard_map/all_to_all | solution.py:90
  24.1 0.8 %gather_fusion.1 = f32[128,8,256]{2,1,0:T(8,128)S(1)} fusion(f32[128,8,256]{2,1,0:T(8,128)S(1)} %all-to-all-done, s32[1024]{0:T(1024)S(1)} %pad_clamp_fusion.1), kind=kCustom, calls=%fused_computation.1 | custom fusion | bytes 2097664 | tf_op jit(solution)/shard_map/jit(_take)/gather | solution.py:98
  24.9 2.7 %fusion.25 = f32[32,32,256]{2,1,0:T(8,128)S(1)} fusion(f32[32,32,256]{2,1,0:T(8,128)S(1)} %bitcast.152, f32[32]{0:T(128)S(1)} %get-tuple-element.23, f32[32]{0:T(128)S(1)} %get-tuple-element.24, f32[32]{0:T(128)S(1)} %get-tuple-element.25, f32[32]{0:T(128)S(1)} %get-tuple-element.26, f32[32]{0:T(128)S(1)} %get-tuple-element.27, f32[32]{0:T(128)S(1)} %get-tuple-element.28, ...), kind=kLoop, calls=%fused_computation.52 | loop fusion | flops 4456448 | bytes 2098304 | tf_op jit(solution)/shard_map/add | solution.py:36
  27.5 1.4 %fusion.9 = f32[32,32,256]{2,1,0:T(8,128)S(1)} fusion(f32[32,32,256]{2,1,0:T(8,128)S(1)} %fusion.25, f32[32]{0:T(128)S(1)} %get-tuple-element.15, f32[32]{0:T(128)S(1)} %get-tuple-element.16, f32[32]{0:T(128)S(1)} %get-tuple-element.17, f32[32]{0:T(128)S(1)} %get-tuple-element.18, f32[32]{0:T(128)S(1)} %get-tuple-element.19, f32[32]{0:T(128)S(1)} %get-tuple-element.20, ...), kind=kLoop, calls=%fused_computation.36 | loop fusion | flops 4718592 | bytes 2098336 | tf_op jit(solution)/shard_map/jit(_where)/select_n | solution.py:111
  29.0 0.9 %fusion.35 = f32[24,32,256]{2,1,0:T(8,128)S(1)} fusion(f32[32,32,256]{2,1,0:T(8,128)S(1)} %fusion.9, f32[4,32,256]{2,1,0:T(8,128)S(1)} %collective-permute-done.1, f32[16,32,256]{2,1,0:T(8,128)S(1)} %bitcast.154, f32[4,32,256]{2,1,0:T(8,128)S(1)} %collective-permute-done, f32[24]{0:T(128)S(1)} %get-tuple-element.60, f32[24]{0:T(128)S(1)} %get-tuple-element.61, ...), kind=kLoop, calls=%fused_computation.63 | loop fusion | flops 4128768 | bytes 8651640 | tf_op jit(solution)/shard_map/jit(_where)/select_n | solution.py:120
  29.9 1.2 %fusion.61 = f32[16,32,256]{2,1,0:T(8,128)S(1)} fusion(f32[24,32,256]{2,1,0:T(8,128)S(1)} %fusion.35, f32[16]{0:T(128)S(1)} %get-tuple-element.51, f32[16]{0:T(128)S(1)} %get-tuple-element.52, f32[16]{0:T(128)S(1)} %get-tuple-element.53, f32[16]{0:T(128)S(1)} %get-tuple-element.54, f32[16]{0:T(128)S(1)} %get-tuple-element.55, f32[16]{0:T(128)S(1)} %get-tuple-element.56, ...), kind=kOutput, calls=%fused_computation.98 | convolution fusion | flops 52838400 | bytes 5288960 | tf_op jit(solution)/shard_map/pri,pix->prx/dot_general | solution.py:135
  31.1 1.3 %fusion.52 = f32[16,32,256]{2,1,0:T(8,128)S(1)} fusion(f32[16,32,256]{2,1,0:T(8,128)S(1)} %fusion.61, f32[16]{0:T(128)S(1)} %get-tuple-element.33, f32[16]{0:T(128)S(1)} %get-tuple-element.34, f32[16]{0:T(128)S(1)} %get-tuple-element.35, f32[16]{0:T(128)S(1)} %get-tuple-element.36, f32[16]{0:T(128)S(1)} %get-tuple-element.37, f32[16]{0:T(128)S(1)} %get-tuple-element.38, ...), kind=kLoop, calls=%fused_computation.88 | loop fusion | flops 2228224 | bytes 1049152 | tf_op jit(solution)/shard_map/log | solution.py:138
  32.4 0.8 %copy.16 = f32[4,4,4,8,256]{4,3,1,2,0:T(8,128)} copy(f32[4,4,4,8,256]{4,3,2,1,0:T(8,128)S(1)} %bitcast.153) | data formatting | bytes 1048576 | tf_op jit(solution)/shard_map/reshape | solution.py:138
  33.3 5.7 %all-to-all-start.1 = ((f32[16,4,8,256]{3,2,1,0:T(8,128)}), f32[16,4,8,256]{3,2,1,0:T(8,128)S(1)}, u32[]{:S(2)}, u32[]{:S(2)}) async-start(f32[16,4,8,256]{3,2,1,0:T(8,128)} %bitcast.76), calls=%async_computation.1 | async-start | bytes 1048576 | tf_op jit(solution)/shard_map/all_to_all | solution.py:140
  39.0 0.1 reshape.554
  39.1 0.2 fusion.134
  39.3 0.1 select_reduce_fusion.1
  39.4 0.1 broadcast_add_fusion
  39.4 0.1 reshape.574
  39.5 13.8 %all-to-all-done.1 = f32[16,4,8,256]{3,2,1,0:T(8,128)S(1)} async-done(((f32[16,4,8,256]{3,2,1,0:T(8,128)}), f32[16,4,8,256]{3,2,1,0:T(8,128)S(1)}, u32[]{:S(2)}, u32[]{:S(2)}) %all-to-all-start.1) | async-done | bytes 524320 | tf_op jit(solution)/shard_map/all_to_all | solution.py:140
  53.3 0.6 gather_fusion.2
  53.9 15.7 %all_gather.3 = f32[16,32,256]{2,1,0:T(8,128)S(1)} all-gather(f32[4,32,256]{2,1,0:T(8,128)S(1)} %copy_bitcast_fusion), channel_id=1, replica_groups=mesh['tile'=2,'dom'=4,'view'=4] {'view'}, dimensions={0}, use_global_device_ids=true | all-gather | bytes 655360 | tf_op jit(solution)/shard_map/all_gather | solution.py:156
  69.6 0.9 %exponential_multiply_fusion = f32[16,32,256]{2,1,0:T(8,128)} fusion(f32[16,32,256]{2,1,0:T(8,128)S(1)} %copy-done, f32[16,32,256]{2,1,0:T(8,128)S(1)} %all_gather.3), kind=kLoop, calls=%fused_computation.114 | loop fusion | flops 262144 | bytes 1572864 | tf_op jit(solution)/shard_map/mul | solution.py:157
  (31 shorter events, 0.3 us)
Async XLA Ops:
  5.3 4.4 %copy-start.1 = (f32[1,16,32,256]{3,2,1,0:T(8,128)S(1)}, f32[1,16,32,256]{3,2,1,0:T(8,128)}, u32[]{:S(2)}) copy-start(f32[1,16,32,256]{3,2,1,0:T(8,128)} %param.6) | copy-start | bytes 1572868
  5.3 8.2 %copy-start.3 = (s32[1,64]{1,0:T(1,128)S(1)}, s32[1,64]{1,0:T(1,128)}, u32[]{:S(2)}) copy-start(s32[1,64]{1,0:T(1,128)} %param.9) | copy-start | bytes 772
  5.3 10.3 %copy-start.2 = (f32[1,4,3,9]{3,1,2,0:T(4,128)S(1)}, f32[1,4,3,9]{3,1,2,0:T(4,128)}, u32[]{:S(2)}) copy-start(f32[1,4,3,9]{3,1,2,0:T(4,128)} %param.7) | copy-start | bytes 1300
  5.3 18.8 %all-to-all-start = ((f32[128,8,256]{2,1,0:T(8,128)}), f32[128,8,256]{2,1,0:T(8,128)S(1)}, u32[]{:S(2)}, u32[]{:S(2)}) async-start(f32[128,8,256]{2,1,0:T(8,128)} %gather_fusion), calls=%async_computation | async-start | bytes 2097152 | tf_op jit(solution)/shard_map/all_to_all | solution.py:90
  9.7 19.2 %collective-permute-start = (f32[4,32,256]{2,1,0:T(8,128)S(1)}, f32[4,32,256]{2,1,0:T(8,128)S(1)}, u32[]{:S(2)}, u32[]{:S(2)}) collective-permute-start(f32[4,32,256]{2,1,0:T(8,128)S(1)} %get-tuple-element.9), channel_id=1, source_target_pairs={{0,4},{4,8},{8,12},{1,5},{5,9},{9,13},{2,6},{6,10},{10,14},{3,7},{... | collective-permute-start | bytes 393224 | tf_op jit(solution)/shard_map/ppermute | solution.py:19
  12.1 16.8 %collective-permute-start.1 = (f32[4,32,256]{2,1,0:T(8,128)S(1)}, f32[4,32,256]{2,1,0:T(8,128)S(1)}, u32[]{:S(2)}, u32[]{:S(2)}) collective-permute-start(f32[4,32,256]{2,1,0:T(8,128)S(1)} %get-tuple-element.10), channel_id=1, source_target_pairs={{4,0},{8,4},{12,8},{5,1},{9,5},{13,9},{6,2},{10,6},{14,10},{7,3},{... | collective-permute-start | bytes 393224 | tf_op jit(solution)/shard_map/ppermute | solution.py:20
  32.4 6.6 %copy-start.4 = (s32[4,16]{1,0:T(4,128)S(1)}, s32[4,16]{1,0:T(4,128)}, u32[]{:S(2)}) copy-start(s32[4,16]{1,0:T(4,128)} %param.8) | copy-start | bytes 772
  33.3 20.0 %all-to-all-start.1 = ((f32[16,4,8,256]{3,2,1,0:T(8,128)}), f32[16,4,8,256]{3,2,1,0:T(8,128)S(1)}, u32[]{:S(2)}, u32[]{:S(2)}) async-start(f32[16,4,8,256]{3,2,1,0:T(8,128)} %bitcast.76), calls=%async_computation.1 | async-start | bytes 1048576 | tf_op jit(solution)/shard_map/all_to_all | solution.py:140
  39.5 30.1 %copy-start = (f32[16,32,256]{2,1,0:T(8,128)S(1)}, f32[16,32,256]{2,1,0:T(8,128)}, u32[]{:S(2)}) copy-start(f32[16,32,256]{2,1,0:T(8,128)} %param.5) | copy-start | bytes 1572868

commit v15 on v14

--- a/solution.py
+++ b/solution.py
@@ -51,7 +51,8 @@
     view_count = lax.axis_size("view")
     plane_start = dom_index * plane_count
     slot_ids = jnp.arange(block_count, dtype=jnp.int32)
-    my_map = lax.dynamic_index_in_dim(src_map, view_index, 0, keepdims=False)
+    view_ids = jnp.arange(view_count, dtype=jnp.int32)
+    my_map = jnp.sum(jnp.where((view_ids == view_index)[:, None], src_map, 0), axis=0)
     grid_map = my_map.reshape(block_count, block_count)
     source_dev = grid_map // block_count
     source_slot = grid_map % block_count
@@ -145,7 +146,6 @@
     cam_of = jnp.sum(
         jnp.where(slot_of[:, :, None] == slot_ids[None, None, :], slot_ids[None, :, None], 0), axis=1
     )
-    view_ids = jnp.arange(view_count, dtype=jnp.int32)
     flat_index = (view_ids[:, None] * block_count + cam_of).reshape(-1)
     by_view = jnp.take(arrived_logs, flat_index, axis=0, mode="clip")
     by_view = by_view.reshape(view_count, block_count, piece_planes, block_rows, lane_count)

time: 70.9 us -> 69.8 us (0.984)
  local copies, waits for them, and re-layouts: 10 us -> 8.15 us
  other arithmetic: 8.39 us -> 9.17 us
    dynamic_slice x2 -> x0, local copies, waits for them, and re-layouts: 1.86 us -> none  [body(): my_map = lax.dynamic_index_in_dim(src_map, view_index, 0, keepdims=False)]
    reduce_sum x0 -> x1, other arithmetic: none -> 0.77 us  [body(): jnp.sum(jnp.where((view_ids == view_index)[:, None], src_map, 0), axis=0)]
where the time goes in v15:
time: 69.8 us; the launch traced here: 69.4 us
  waiting for transfers between devices  21.1 us (30%)
  blocking collectives  15.7 us (22%)
  starting transfers between devices  13.8 us (20%)
  other arithmetic  9.17 us (13%)
  local copies, waits for them, and re-layouts  8.15 us (12%)
  matrix products  1.21 us (2%)
    all_gather x1, blocking collectives, body(): log_joined = lax.all_gather(log_total, 'view', axis=0, tiled=True)  15.7 us
    all_to_all x1, waiting for transfers between devices, body(): arrived_logs = lax.all_to_all(outgoing, ('view', 'dom'), 0, 0, tiled=True)  13.8 us
    all_to_all x1, waiting for transfers between devices, body(): lax.all_to_all(outgoing, 'dom', split_axis=0, concat_axis=0, tiled=True)  7.37 us
    all_to_all x1, starting transfers between devices, body(): arrived_logs = lax.all_to_all(outgoing, ('view', 'dom'), 0, 0, tiled=True)  5.74 us
    all_to_all x1, starting transfers between devices, body(): lax.all_to_all(outgoing, 'dom', split_axis=0, concat_axis=0, tiled=True)  4.37 us
    add x1, other arithmetic, taps_along(): total = total + taps[offset][:, None, None] * piece  2.66 us
    gather x1, local copies, waits for them, and re-layouts, body(): outgoing = jnp.take(flat_blocks, send_index, axis=0, mode='clip')  2.66 us
    ppermute x1, starting transfers between devices, extended_2(): before = lax.ppermute(last, axis, up)  2.42 us
  transfers between devices with their start and end apart: 4, of which 2 were waited for; matrix products, arithmetic and copies ran while one was open for 12% of the time, Pallas kernels for 0%

profile of v15, /device:TPU:0, one launch (start us, length us, event | category | flops | bytes accessed | tf_op | source)
XLA Modules:
  0.0 69.4 jit_solution(13107891842594487650)
XLA Ops:
  0.0 0.8 %select_reduce_fusion.3 = s32[16]{0:T(128)S(1)} fusion(s32[4,16]{1,0:T(4,128)} %param.8, pred[4]{0:T(512)(128)(4,1)S(1)} %iota_compare_fusion.5), kind=kLoop, calls=%fused_computation.220 | loop fusion | flops 112 | bytes 324 | tf_op jit(solution)/shard_map/reduce_sum | solution.py:55
  0.8 0.1 fusion.150
  0.9 0.1 slice_bitcast_fusion.63
  0.9 0.1 stack_reshape.3
  1.0 0.1 slice.496
  1.1 0.1 slice.498
  1.2 0.2 fusion.138
  1.4 0.1 select_add_fusion
  1.4 0.1 reshape.576
  1.5 2.7 %gather_fusion = f32[128,8,256]{2,1,0:T(8,128)} fusion(f32[64,8,256]{2,1,0:T(8,128)} %bitcast.154, s32[1024]{0:T(1024)S(1)} %pad_clamp_fusion.2), kind=kCustom, calls=%fused_computation | custom fusion | bytes 2097664 | tf_op jit(solution)/shard_map/jit(_take)/gather | solution.py:89
  4.2 4.4 %all-to-all-start = ((f32[128,8,256]{2,1,0:T(8,128)}), f32[128,8,256]{2,1,0:T(8,128)S(1)}, u32[]{:S(2)}, u32[]{:S(2)}) async-start(f32[128,8,256]{2,1,0:T(8,128)} %gather_fusion), calls=%async_computation | async-start | bytes 2097152 | tf_op jit(solution)/shard_map/all_to_all | solution.py:91
  8.6 2.4 %collective-permute-start = (f32[4,32,256]{2,1,0:T(8,128)S(1)}, f32[4,32,256]{2,1,0:T(8,128)S(1)}, u32[]{:S(2)}, u32[]{:S(2)}) collective-permute-start(f32[4,32,256]{2,1,0:T(8,128)S(1)} %get-tuple-element.5), channel_id=1, source_target_pairs={{0,4},{4,8},{8,12},{1,5},{5,9},{9,13},{2,6},{6,10},{10,14},{3,7},{... | collective-permute-start | bytes 393224 | tf_op jit(solution)/shard_map/ppermute | solution.py:19
  11.0 1.3 %collective-permute-start.1 = (f32[4,32,256]{2,1,0:T(8,128)S(1)}, f32[4,32,256]{2,1,0:T(8,128)S(1)}, u32[]{:S(2)}, u32[]{:S(2)}) collective-permute-start(f32[4,32,256]{2,1,0:T(8,128)S(1)} %get-tuple-element.6), channel_id=1, source_target_pairs={{4,0},{8,4},{12,8},{5,1},{9,5},{13,9},{6,2},{10,6},{14,10},{7,3},{... | collective-permute-start | bytes 393224 | tf_op jit(solution)/shard_map/ppermute | solution.py:20
  12.3 0.1 reshape.568
  12.4 0.6 fusion.149
  13.1 0.6 reshape.566
  13.7 0.6 reshape.567
  14.4 0.1 pad_add_fusion.1
  14.4 0.1 dynamic_slice.13
  14.5 0.1 copy.15
  14.6 0.1 select_reduce_fusion
  14.8 0.1 slice_bitcast_fusion.47
  14.9 0.1 select_reduce_fusion.2
  15.0 0.1 iota_add_fusion.1
  15.1 0.1 slice_bitcast_fusion.58
  15.1 0.1 iota_add_fusion
  15.2 0.1 reshape.584
  15.3 0.1 add.311
  15.4 0.1 slice_bitcast_fusion.48
  15.5 0.1 fusion.131
  15.6 7.4 %all-to-all-done = f32[128,8,256]{2,1,0:T(8,128)S(1)} async-done(((f32[128,8,256]{2,1,0:T(8,128)}), f32[128,8,256]{2,1,0:T(8,128)S(1)}, u32[]{:S(2)}, u32[]{:S(2)}) %all-to-all-start) | async-done | bytes 1048608 | tf_op jit(solution)/shard_map/all_to_all | solution.py:91
  23.0 0.8 %gather_fusion.1 = f32[128,8,256]{2,1,0:T(8,128)S(1)} fusion(f32[128,8,256]{2,1,0:T(8,128)S(1)} %all-to-all-done, s32[1024]{0:T(1024)S(1)} %pad_clamp_fusion.1), kind=kCustom, calls=%fused_computation.1 | custom fusion | bytes 2097664 | tf_op jit(solution)/shard_map/jit(_take)/gather | solution.py:99
  23.8 2.7 %fusion.25 = f32[32,32,256]{2,1,0:T(8,128)S(1)} fusion(f32[32,32,256]{2,1,0:T(8,128)S(1)} %bitcast.155, f32[32]{0:T(128)S(1)} %get-tuple-element.19, f32[32]{0:T(128)S(1)} %get-tuple-element.20, f32[32]{0:T(128)S(1)} %get-tuple-element.21, f32[32]{0:T(128)S(1)} %get-tuple-element.22, f32[32]{0:T(128)S(1)} %get-tuple-element.23, f32[32]{0:T(128)S(1)} %get-tuple-element.24, ...), kind=kLoop, calls=%fused_computation.52 | loop fusion | flops 4456448 | bytes 2098304 | tf_op jit(solution)/shard_map/add | solution.py:36
  26.4 1.4 %fusion.9 = f32[32,32,256]{2,1,0:T(8,128)S(1)} fusion(f32[32,32,256]{2,1,0:T(8,128)S(1)} %fusion.25, f32[32]{0:T(128)S(1)} %get-tuple-element.11, f32[32]{0:T(128)S(1)} %get-tuple-element.12, f32[32]{0:T(128)S(1)} %get-tuple-element.13, f32[32]{0:T(128)S(1)} %get-tuple-element.14, f32[32]{0:T(128)S(1)} %get-tuple-element.15, f32[32]{0:T(128)S(1)} %get-tuple-element.16, ...), kind=kLoop, calls=%fused_computation.36 | loop fusion | flops 4718592 | bytes 2098336 | tf_op jit(solution)/shard_map/jit(_where)/select_n | solution.py:112
  27.9 0.9 %fusion.35 = f32[24,32,256]{2,1,0:T(8,128)S(1)} fusion(f32[32,32,256]{2,1,0:T(8,128)S(1)} %fusion.9, f32[4,32,256]{2,1,0:T(8,128)S(1)} %collective-permute-done.1, f32[16,32,256]{2,1,0:T(8,128)S(1)} %bitcast.157, f32[4,32,256]{2,1,0:T(8,128)S(1)} %collective-permute-done, f32[24]{0:T(128)S(1)} %get-tuple-element.56, f32[24]{0:T(128)S(1)} %get-tuple-element.57, ...), kind=kLoop, calls=%fused_computation.63 | loop fusion | flops 4128768 | bytes 8651640 | tf_op jit(solution)/shard_map/jit(_where)/select_n | solution.py:121
  28.8 1.2 %fusion.61 = f32[16,32,256]{2,1,0:T(8,128)S(1)} fusion(f32[24,32,256]{2,1,0:T(8,128)S(1)} %fusion.35, f32[16]{0:T(128)S(1)} %get-tuple-element.47, f32[16]{0:T(128)S(1)} %get-tuple-element.48, f32[16]{0:T(128)S(1)} %get-tuple-element.49, f32[16]{0:T(128)S(1)} %get-tuple-element.50, f32[16]{0:T(128)S(1)} %get-tuple-element.51, f32[16]{0:T(128)S(1)} %get-tuple-element.52, ...), kind=kOutput, calls=%fused_computation.98 | convolution fusion | flops 52838400 | bytes 5288960 | tf_op jit(solution)/shard_map/pri,pix->prx/dot_general | solution.py:136
  30.0 1.3 %fusion.52 = f32[16,32,256]{2,1,0:T(8,128)S(1)} fusion(f32[16,32,256]{2,1,0:T(8,128)S(1)} %fusion.61, f32[16]{0:T(128)S(1)} %get-tuple-element.29, f32[16]{0:T(128)S(1)} %get-tuple-element.30, f32[16]{0:T(128)S(1)} %get-tuple-element.31, f32[16]{0:T(128)S(1)} %get-tuple-element.32, f32[16]{0:T(128)S(1)} %get-tuple-element.33, f32[16]{0:T(128)S(1)} %get-tuple-element.34, ...), kind=kLoop, calls=%fused_computation.88 | loop fusion | flops 2228224 | bytes 1049152 | tf_op jit(solution)/shard_map/log | solution.py:139
  31.3 0.8 %copy.16 = f32[4,4,4,8,256]{4,3,1,2,0:T(8,128)} copy(f32[4,4,4,8,256]{4,3,2,1,0:T(8,128)S(1)} %bitcast.156) | data formatting | bytes 1048576 | tf_op jit(solution)/shard_map/reshape | solution.py:139
  32.2 5.7 %all-to-all-start.1 = ((f32[16,4,8,256]{3,2,1,0:T(8,128)}), f32[16,4,8,256]{3,2,1,0:T(8,128)S(1)}, u32[]{:S(2)}, u32[]{:S(2)}) async-start(f32[16,4,8,256]{3,2,1,0:T(8,128)} %bitcast.78), calls=%async_computation.1 | async-start | bytes 1048576 | tf_op jit(solution)/shard_map/all_to_all | solution.py:141
  37.9 0.1 reshape.572
  38.0 0.2 fusion.134
  38.2 0.1 select_reduce_fusion.1
  38.3 0.1 broadcast_add_fusion
  38.3 0.1 reshape.592
  38.4 13.8 %all-to-all-done.1 = f32[16,4,8,256]{3,2,1,0:T(8,128)S(1)} async-done(((f32[16,4,8,256]{3,2,1,0:T(8,128)}), f32[16,4,8,256]{3,2,1,0:T(8,128)S(1)}, u32[]{:S(2)}, u32[]{:S(2)}) %all-to-all-start.1) | async-done | bytes 524320 | tf_op jit(solution)/shard_map/all_to_all | solution.py:141
  52.2 0.6 gather_fusion.2
  52.8 15.7 %all_gather.3 = f32[16,32,256]{2,1,0:T(8,128)S(1)} all-gather(f32[4,32,256]{2,1,0:T(8,128)S(1)} %copy_bitcast_fusion), channel_id=1, replica_groups=mesh['tile'=2,'dom'=4,'view'=4] {'view'}, dimensions={0}, use_global_device_ids=true | all-gather | bytes 655360 | tf_op jit(solution)/shard_map/all_gather | solution.py:156
  68.5 0.9 %exponential_multiply_fusion = f32[16,32,256]{2,1,0:T(8,128)} fusion(f32[16,32,256]{2,1,0:T(8,128)S(1)} %copy-done, f32[16,32,256]{2,1,0:T(8,128)S(1)} %all_gather.3), kind=kLoop, calls=%fused_computation.114 | loop fusion | flops 262144 | bytes 1572864 | tf_op jit(solution)/shard_map/mul | solution.py:157
  (31 shorter events, 0.2 us)
Async XLA Ops:
  4.2 4.4 %copy-start.1 = (f32[1,16,32,256]{3,2,1,0:T(8,128)S(1)}, f32[1,16,32,256]{3,2,1,0:T(8,128)}, u32[]{:S(2)}) copy-start(f32[1,16,32,256]{3,2,1,0:T(8,128)} %param.6) | copy-start | bytes 1572868
  4.2 8.2 %copy-start.4 = (s32[1,64]{1,0:T(1,128)S(1)}, s32[1,64]{1,0:T(1,128)}, u32[]{:S(2)}) copy-start(s32[1,64]{1,0:T(1,128)} %param.9) | copy-start | bytes 772
  4.2 10.3 %copy-start.3 = (f32[1,4,3,9]{3,1,2,0:T(4,128)S(1)}, f32[1,4,3,9]{3,1,2,0:T(4,128)}, u32[]{:S(2)}) copy-start(f32[1,4,3,9]{3,1,2,0:T(4,128)} %param.7) | copy-start | bytes 1300
  4.2 18.8 %all-to-all-start = ((f32[128,8,256]{2,1,0:T(8,128)}), f32[128,8,256]{2,1,0:T(8,128)S(1)}, u32[]{:S(2)}, u32[]{:S(2)}) async-start(f32[128,8,256]{2,1,0:T(8,128)} %gather_fusion), calls=%async_computation | async-start | bytes 2097152 | tf_op jit(solution)/shard_map/all_to_all | solution.py:91
  8.6 19.2 %collective-permute-start = (f32[4,32,256]{2,1,0:T(8,128)S(1)}, f32[4,32,256]{2,1,0:T(8,128)S(1)}, u32[]{:S(2)}, u32[]{:S(2)}) collective-permute-start(f32[4,32,256]{2,1,0:T(8,128)S(1)} %get-tuple-element.5), channel_id=1, source_target_pairs={{0,4},{4,8},{8,12},{1,5},{5,9},{9,13},{2,6},{6,10},{10,14},{3,7},{... | collective-permute-start | bytes 393224 | tf_op jit(solution)/shard_map/ppermute | solution.py:19
  11.0 16.8 %collective-permute-start.1 = (f32[4,32,256]{2,1,0:T(8,128)S(1)}, f32[4,32,256]{2,1,0:T(8,128)S(1)}, u32[]{:S(2)}, u32[]{:S(2)}) collective-permute-start(f32[4,32,256]{2,1,0:T(8,128)S(1)} %get-tuple-element.6), channel_id=1, source_target_pairs={{4,0},{8,4},{12,8},{5,1},{9,5},{13,9},{6,2},{10,6},{14,10},{7,3},{... | collective-permute-start | bytes 393224 | tf_op jit(solution)/shard_map/ppermute | solution.py:20
  31.3 6.6 %copy-start.2 = (s32[4,16]{1,0:T(4,128)S(1)}, s32[4,16]{1,0:T(4,128)}, u32[]{:S(2)}) copy-start(s32[4,16]{1,0:T(4,128)} %param.8) | copy-start | bytes 772
  32.2 20.0 %all-to-all-start.1 = ((f32[16,4,8,256]{3,2,1,0:T(8,128)}), f32[16,4,8,256]{3,2,1,0:T(8,128)S(1)}, u32[]{:S(2)}, u32[]{:S(2)}) async-start(f32[16,4,8,256]{3,2,1,0:T(8,128)} %bitcast.78), calls=%async_computation.1 | async-start | bytes 1048576 | tf_op jit(solution)/shard_map/all_to_all | solution.py:141
  38.4 30.1 %copy-start = (f32[16,32,256]{2,1,0:T(8,128)S(1)}, f32[16,32,256]{2,1,0:T(8,128)}, u32[]{:S(2)}) copy-start(f32[16,32,256]{2,1,0:T(8,128)} %param.5) | copy-start | bytes 1572868

commit v16 on v15

--- a/solution.py
+++ b/solution.py
@@ -74,30 +74,40 @@
     wide = 2 * reach
     last = block_count - 1
     wide_count = plane_count + 2 * wide
-    chunk_plane = jnp.arange(wide_count, dtype=jnp.int32)
-    in_top = chunk_plane < wide
-    in_bottom = chunk_plane >= wide + plane_count
-    source_plane = jnp.where(
-        in_top, chunk_plane + plane_count - wide,
-        jnp.where(in_bottom, chunk_plane - wide - plane_count, chunk_plane - wide),
+    blocks = estimate.reshape(plane_count, block_count, block_rows, lane_count)
+    tops = blocks[plane_count - wide :]
+    bottoms = blocks[:wide]
+
+    def column(field, index):
+        return lax.dynamic_index_in_dim(field, index, 1, keepdims=False)
+
+    outgoing = jnp.stack(
+        [
+            jnp.concatenate(
+                [column(tops, above[d]), column(blocks, send_slot[d]), column(bottoms, below[d])], axis=0
+            )
+            for d in range(block_count)
+        ]
     )
-    source_block = jnp.where(
-        in_top[:, None], above[None, :], jnp.where(in_bottom[:, None], below[None, :], send_slot[None, :])
-    )
-    send_index = (source_plane[None, :] * block_count + source_block.T).reshape(-1)
-    flat_blocks = estimate.reshape(plane_count * block_count, block_rows, lane_count)
-    outgoing = jnp.take(flat_blocks, send_index, axis=0, mode="clip")
     outgoing = outgoing.reshape(block_count * wide_count, block_rows, lane_count)
     arrived = lax.all_to_all(outgoing, "dom", split_axis=0, concat_axis=0, tiled=True)
+    arrived = arrived.reshape(block_count, wide_count, block_rows, lane_count)
     my_sources = lax.dynamic_index_in_dim(source_dev, dom_index, 0, keepdims=False)
     src_above = lax.dynamic_index_in_dim(source_dev, jnp.maximum(dom_index - 1, 0), 0, keepdims=False)
     src_below = lax.dynamic_index_in_dim(source_dev, jnp.minimum(dom_index + 1, last), 0, keepdims=False)
-    from_block = jnp.where(
-        in_top[:, None], src_above[None, :], jnp.where(in_bottom[:, None], src_below[None, :], my_sources[None, :])
+
+    def pick(index, start, count):
+        chunk = lax.dynamic_index_in_dim(arrived, index, 0, keepdims=False)
+        return chunk[start : start + count]
+
+    camera_ext = jnp.concatenate(
+        [
+            jnp.stack([pick(src_above[t], 0, wide) for t in range(block_count)], axis=1),
+            jnp.stack([pick(my_sources[t], wide, plane_count) for t in range(block_count)], axis=1),
+            jnp.stack([pick(src_below[t], wide + plane_count, wide) for t in range(block_count)], axis=1),
+        ],
+        axis=0,
     )
-    recv_index = (from_block * wide_count + chunk_plane[:, None]).reshape(-1)
-    camera_ext = jnp.take(arrived, recv_index, axis=0, mode="clip")
-    camera_ext = camera_ext.reshape(wide_count, block_count, block_rows, lane_count)
     wide_planes = plane_start - wide + jnp.arange(wide_count, dtype=jnp.int32)
     wide_inside = (wide_planes >= 0) & (wide_planes < total_planes)
     camera_ext = camera_ext.reshape(wide_count, row_count, lane_count)

time: 69.8 us -> 113 us (1.62)
  between operations: 0.23 us -> 45.7 us
  waiting for transfers between devices: 21.1 us -> 13.8 us
  starting transfers between devices: 13.8 us -> 17.1 us
  other arithmetic: 9.17 us -> 10.3 us
    all_to_all x1, waiting for transfers between devices: 7.37 us -> 0.01 us  [body(): lax.all_to_all(outgoing, 'dom', split_axis=0, concat_axis=0, tiled=True)]
    gather x2 -> x0, local copies, waits for them, and re-layouts: 3.41 us -> none  [the longest x1 2.66 us: body(): outgoing = jnp.take(flat_blocks, send_index, axis=0, mode='clip')]
    all_to_all x1, starting transfers between devices: 5.74 us -> 9.02 us  [body(): arrived_logs = lax.all_to_all(outgoing, ('view', 'dom'), 0, 0, tiled=True)]
    slice x0 -> x4, local copies, waits for them, and re-layouts: none -> 3.1 us  [the longest x1 1.07 us: body(): tops = blocks[plane_count - wide:]]
    another operation x0 -> x6, other arithmetic: none -> 1.17 us  [the longest x5 1.13 us: body(): jnp.stack([jnp.concatenate([column(tops, above[d]), column(blocks, send_s...]
  transfers between devices with their start and end apart: 4 -> 4, of which waited for: 2 -> 1; matrix products, arithmetic and copies ran while one was open for 12% -> 8% of each run, Pallas kernels for 0% -> 0%
where the time goes in v16:
time: 113 us; the launch traced here: 112 us
  between operations  45.7 us (40%)
  starting transfers between devices  17.1 us (15%)
  blocking collectives  15.7 us (14%)
  waiting for transfers between devices  13.8 us (12%)
  other arithmetic  10.3 us (9%)
  local copies, waits for them, and re-layouts  7.83 us (7%)
  matrix products  1.18 us (1%)
    all_gather x1, blocking collectives, body(): log_joined = lax.all_gather(log_total, 'view', axis=0, tiled=True)  15.7 us
    all_to_all x1, waiting for transfers between devices, body(): arrived_logs = lax.all_to_all(outgoing, ('view', 'dom'), 0, 0, tiled=True)  13.8 us
    all_to_all x1, starting transfers between devices, body(): arrived_logs = lax.all_to_all(outgoing, ('view', 'dom'), 0, 0, tiled=True)  9.02 us
    all_to_all x1, starting transfers between devices, body(): lax.all_to_all(outgoing, 'dom', split_axis=0, concat_axis=0, tiled=True)  4.37 us
    add x1, other arithmetic, taps_along(): total = total + taps[offset][:, None, None] * piece  2.69 us
    ppermute x1, starting transfers between devices, extended_2(): before = lax.ppermute(last, axis, up)  2.42 us
  transfers between devices with their start and end apart: 4, of which 1 were waited for; matrix products, arithmetic and copies ran while one was open for 8% of the time, Pallas kernels for 0%

profile of v16, /device:TPU:0, one launch (start us, length us, event | category | flops | bytes accessed | tf_op | source)
XLA Modules:
  0.0 111.6 jit_solution(1082341908261400748)
XLA Ops:
  0.0 0.8 select_reduce_fusion.3
  0.8 0.1 fusion.148
  0.9 0.1 slice_bitcast_fusion.62
  1.0 0.1 stack_reshape.3
  1.1 0.1 slice.660
  1.1 0.1 slice.662
  1.2 0.2 fusion.138
  1.4 0.7 fusion.143
  17.1 1.1 slice_bitcast_fusion.1
  26.0 1.1 pad_maximum_fusion
  27.0 4.4 %all-to-all-start = ((f32[128,8,256]{2,1,0:T(8,128)}), f32[128,8,256]{2,1,0:T(8,128)S(1)}, u32[]{:S(2)}, u32[]{:S(2)}) async-start(f32[128,8,256]{2,1,0:T(8,128)} %bitcast.60), calls=%async_computation | async-start | bytes 2097152 | tf_op jit(solution)/shard_map/all_to_all | solution.py:93
  31.4 2.4 %collective-permute-start = (f32[4,32,256]{2,1,0:T(8,128)S(1)}, f32[4,32,256]{2,1,0:T(8,128)S(1)}, u32[]{:S(2)}, u32[]{:S(2)}) collective-permute-start(f32[4,32,256]{2,1,0:T(8,128)S(1)} %get-tuple-element.17), channel_id=1, source_target_pairs={{0,4},{4,8},{8,12},{1,5},{5,9},{9,13},{2,6},{6,10},{10,14},{3,7},{... | collective-permute-start | bytes 393224 | tf_op jit(solution)/shard_map/ppermute | solution.py:19
  33.9 1.3 %collective-permute-start.1 = (f32[4,32,256]{2,1,0:T(8,128)S(1)}, f32[4,32,256]{2,1,0:T(8,128)S(1)}, u32[]{:S(2)}, u32[]{:S(2)}) collective-permute-start(f32[4,32,256]{2,1,0:T(8,128)S(1)} %get-tuple-element.18), channel_id=1, source_target_pairs={{4,0},{8,4},{12,8},{5,1},{9,5},{13,9},{6,2},{10,6},{14,10},{7,3},{... | collective-permute-start | bytes 393224 | tf_op jit(solution)/shard_map/ppermute | solution.py:20
  35.2 0.1 reshape.484
  35.3 0.7 fusion.145
  46.2 0.7 fusion.147
  51.8 0.6 fusion.144
  52.5 0.6 reshape.482
  53.1 0.6 reshape.483
  53.7 0.1 pad_add_fusion.1
  53.8 0.1 dynamic_slice.88
  53.9 0.1 copy.35
  54.0 0.1 select_reduce_fusion
  54.1 0.1 slice_bitcast_fusion.49
  54.2 0.1 select_reduce_fusion.2
  54.3 0.1 iota_add_fusion
  54.4 0.1 add.329
  54.5 0.1 slice_bitcast_fusion.60
  62.2 0.1 slice_bitcast_fusion.50
  62.3 0.1 fusion.131
  62.5 0.1 dynamic-slice_bitcast_fusion.15
  62.6 0.1 maximum_bitcast_fusion
  62.7 2.7 %fusion.25 = f32[32,32,256]{2,1,0:T(8,128)S(1)} fusion(f32[32,32,256]{2,1,0:T(8,128)S(1)} %maximum_bitcast_fusion, f32[32]{0:T(128)S(1)} %get-tuple-element.45, f32[32]{0:T(128)S(1)} %get-tuple-element.46, f32[32]{0:T(128)S(1)} %get-tuple-element.47, f32[32]{0:T(128)S(1)} %get-tuple-element.48, f32[32]{0:T(128)S(1)} %get-tuple-element.49, ...), kind=kLoop, calls=%fused_computation.50 | loop fusion | flops 4456448 | bytes 2098304 | tf_op jit(solution)/shard_map/add | solution.py:36
  65.4 1.4 %fusion.9 = f32[32,32,256]{2,1,0:T(8,128)S(1)} fusion(f32[32,32,256]{2,1,0:T(8,128)S(1)} %fusion.25, f32[32]{0:T(128)S(1)} %get-tuple-element.37, f32[32]{0:T(128)S(1)} %get-tuple-element.38, f32[32]{0:T(128)S(1)} %get-tuple-element.39, f32[32]{0:T(128)S(1)} %get-tuple-element.40, f32[32]{0:T(128)S(1)} %get-tuple-element.41, f32[32]{0:T(128)S(1)} %get-tuple-element.42, ...), kind=kLoop, calls=%fused_computation.34 | loop fusion | flops 4718592 | bytes 2098336 | tf_op jit(solution)/shard_map/jit(_where)/select_n | solution.py:122
  66.8 0.9 fusion.35
  67.7 1.2 %fusion.61 = f32[16,32,256]{2,1,0:T(8,128)S(1)} fusion(f32[24,32,256]{2,1,0:T(8,128)S(1)} %fusion.35, f32[16]{0:T(128)S(1)} %get-tuple-element.73, f32[16]{0:T(128)S(1)} %get-tuple-element.74, f32[16]{0:T(128)S(1)} %get-tuple-element.75, f32[16]{0:T(128)S(1)} %get-tuple-element.76, f32[16]{0:T(128)S(1)} %get-tuple-element.77, f32[16]{0:T(128)S(1)} %get-tuple-element.78, ...), kind=kOutput, calls=%fused_computation.98 | convolution fusion | flops 52838400 | bytes 5288960 | tf_op jit(solution)/shard_map/pri,pix->prx/dot_general | solution.py:146
  68.9 1.3 %fusion.52 = f32[16,32,256]{2,1,0:T(8,128)S(1)} fusion(f32[16,32,256]{2,1,0:T(8,128)S(1)} %fusion.61, f32[16]{0:T(128)S(1)} %get-tuple-element.55, f32[16]{0:T(128)S(1)} %get-tuple-element.56, f32[16]{0:T(128)S(1)} %get-tuple-element.57, f32[16]{0:T(128)S(1)} %get-tuple-element.58, f32[16]{0:T(128)S(1)} %get-tuple-element.59, f32[16]{0:T(128)S(1)} %get-tuple-element.60, ...), kind=kLoop, calls=%fused_computation.88 | loop fusion | flops 2228224 | bytes 1049152 | tf_op jit(solution)/shard_map/log | solution.py:149
  70.2 0.8 copy.41
  71.1 9.0 %all-to-all-start.1 = ((f32[16,4,8,256]{3,2,1,0:T(8,128)}), f32[16,4,8,256]{3,2,1,0:T(8,128)S(1)}, u32[]{:S(2)}, u32[]{:S(2)}) async-start(f32[16,4,8,256]{3,2,1,0:T(8,128)} %bitcast.132), calls=%async_computation.1 | async-start | bytes 1048576 | tf_op jit(solution)/shard_map/all_to_all | solution.py:151
  80.1 0.1 reshape.491
  80.2 0.2 fusion.134
  80.4 0.1 select_reduce_fusion.1
  80.5 0.1 broadcast_add_fusion
  80.5 0.1 reshape.495
  80.6 13.8 %all-to-all-done.1 = f32[16,4,8,256]{3,2,1,0:T(8,128)S(1)} async-done(((f32[16,4,8,256]{3,2,1,0:T(8,128)}), f32[16,4,8,256]{3,2,1,0:T(8,128)S(1)}, u32[]{:S(2)}, u32[]{:S(2)}) %all-to-all-start.1) | async-done | bytes 524320 | tf_op jit(solution)/shard_map/all_to_all | solution.py:151
  94.4 0.6 gather_fusion
  95.0 15.7 %all_gather.3 = f32[16,32,256]{2,1,0:T(8,128)S(1)} all-gather(f32[4,32,256]{2,1,0:T(8,128)S(1)} %copy_bitcast_fusion), channel_id=1, replica_groups=mesh['tile'=2,'dom'=4,'view'=4] {'view'}, dimensions={0}, use_global_device_ids=true | all-gather | bytes 655360 | tf_op jit(solution)/shard_map/all_gather | solution.py:166
  110.7 0.9 exponential_multiply_fusion
  (36 shorter events, 0.4 us)
Async XLA Ops:
  0.0 25.8 %copy-start = (f32[16,32,256]{2,1,0:T(8,128)S(1)}, f32[16,32,256]{2,1,0:T(8,128)}, u32[]{:S(2)}) copy-start(f32[16,32,256]{2,1,0:T(8,128)} %param.5) | copy-start | bytes 1572868
  27.0 4.4 %copy-start.1 = (f32[1,16,32,256]{3,2,1,0:T(8,128)S(1)}, f32[1,16,32,256]{3,2,1,0:T(8,128)}, u32[]{:S(2)}) copy-start(f32[1,16,32,256]{3,2,1,0:T(8,128)} %param.6) | copy-start | bytes 1572868
  27.0 24.8 %copy-start.4 = (s32[1,64]{1,0:T(1,128)S(1)}, s32[1,64]{1,0:T(1,128)}, u32[]{:S(2)}) copy-start(s32[1,64]{1,0:T(1,128)} %param.9) | copy-start | bytes 772
  27.0 26.9 %copy-start.3 = (f32[1,4,3,9]{3,1,2,0:T(4,128)S(1)}, f32[1,4,3,9]{3,1,2,0:T(4,128)}, u32[]{:S(2)}) copy-start(f32[1,4,3,9]{3,1,2,0:T(4,128)} %param.7) | copy-start | bytes 1300
  27.0 35.4 %all-to-all-start = ((f32[128,8,256]{2,1,0:T(8,128)}), f32[128,8,256]{2,1,0:T(8,128)S(1)}, u32[]{:S(2)}, u32[]{:S(2)}) async-start(f32[128,8,256]{2,1,0:T(8,128)} %bitcast.60), calls=%async_computation | async-start | bytes 2097152 | tf_op jit(solution)/shard_map/all_to_all | solution.py:93
  31.4 35.3 %collective-permute-start = (f32[4,32,256]{2,1,0:T(8,128)S(1)}, f32[4,32,256]{2,1,0:T(8,128)S(1)}, u32[]{:S(2)}, u32[]{:S(2)}) collective-permute-start(f32[4,32,256]{2,1,0:T(8,128)S(1)} %get-tuple-element.17), channel_id=1, source_target_pairs={{0,4},{4,8},{8,12},{1,5},{5,9},{9,13},{2,6},{6,10},{10,14},{3,7},{... | collective-permute-start | bytes 393224 | tf_op jit(solution)/shard_map/ppermute | solution.py:19
  33.9 32.9 %collective-permute-start.1 = (f32[4,32,256]{2,1,0:T(8,128)S(1)}, f32[4,32,256]{2,1,0:T(8,128)S(1)}, u32[]{:S(2)}, u32[]{:S(2)}) collective-permute-start(f32[4,32,256]{2,1,0:T(8,128)S(1)} %get-tuple-element.18), channel_id=1, source_target_pairs={{4,0},{8,4},{12,8},{5,1},{9,5},{13,9},{6,2},{10,6},{14,10},{7,3},{... | collective-permute-start | bytes 393224 | tf_op jit(solution)/shard_map/ppermute | solution.py:20
  70.2 9.9 %copy-start.2 = (s32[4,16]{1,0:T(4,128)S(1)}, s32[4,16]{1,0:T(4,128)}, u32[]{:S(2)}) copy-start(s32[4,16]{1,0:T(4,128)} %param.8) | copy-start | bytes 772
  71.1 23.3 %all-to-all-start.1 = ((f32[16,4,8,256]{3,2,1,0:T(8,128)}), f32[16,4,8,256]{3,2,1,0:T(8,128)S(1)}, u32[]{:S(2)}, u32[]{:S(2)}) async-start(f32[16,4,8,256]{3,2,1,0:T(8,128)} %bitcast.132), calls=%async_computation.1 | async-start | bytes 1048576 | tf_op jit(solution)/shard_map/all_to_all | solution.py:151

commit v17 on v15

--- a/solution.py
+++ b/solution.py
@@ -109,14 +109,14 @@
     x_wide = tables[2]
     y_wide = tables[1]
     lateral_ext = lateral_fwd(camera_ext, x_wide, y_wide)
-    lateral_ext = jnp.where(wide_inside[:, None, None], lateral_ext, 0.0)
     ext_count = plane_count + 2 * reach
     ext_planes = plane_start - reach + jnp.arange(ext_count, dtype=jnp.int32)
     ext_inside = (ext_planes >= 0) & (ext_planes < total_planes)
     taps_ext = tables[0][:, reach : reach + ext_count]
     blurred = jnp.zeros((ext_count, row_count, lane_count), jnp.float32)
     for j in range(2 * reach + 1):
-        blurred = blurred + taps_ext[j][:, None, None] * lateral_ext[j : j + ext_count]
+        weight = jnp.where(wide_inside[j : j + ext_count], taps_ext[j], 0.0)
+        blurred = blurred + weight[:, None, None] * lateral_ext[j : j + ext_count]
     observed_ext = extended_2(observed[0], (("dom", 0),), reach)
     ratio_ext = jnp.where(ext_inside[:, None, None], observed_ext / blurred, 0.0)
     x_own = tables[2][:, wide : wide + plane_count]

time: 69.8 us -> 69.7 us (level)
    select_n x1, other arithmetic: 1.39 us -> 0.1 us  [body(): weight = jnp.where(wide_inside[j:j + ext_count], taps_ext[j], 0.0)]
    add x1 -> x2, other arithmetic: 2.66 us -> 3.95 us  [taps_along(): total = total + taps[offset][:, None, None] * piece]
where the time goes in v17:
time: 69.7 us; the launch traced here: 69.3 us
  waiting for transfers between devices  21.1 us (30%)
  blocking collectives  15.7 us (23%)
  starting transfers between devices  13.8 us (20%)
  other arithmetic  9.17 us (13%)
  local copies, waits for them, and re-layouts  8.08 us (12%)
  matrix products  1.2 us (2%)
    all_gather x1, blocking collectives, body(): log_joined = lax.all_gather(log_total, 'view', axis=0, tiled=True)  15.7 us
    all_to_all x1, waiting for transfers between devices, body(): arrived_logs = lax.all_to_all(outgoing, ('view', 'dom'), 0, 0, tiled=True)  13.8 us
    all_to_all x1, waiting for transfers between devices, body(): lax.all_to_all(outgoing, 'dom', split_axis=0, concat_axis=0, tiled=True)  7.33 us
    all_to_all x1, starting transfers between devices, body(): arrived_logs = lax.all_to_all(outgoing, ('view', 'dom'), 0, 0, tiled=True)  5.74 us
    all_to_all x1, starting transfers between devices, body(): lax.all_to_all(outgoing, 'dom', split_axis=0, concat_axis=0, tiled=True)  4.37 us
    add x2, other arithmetic, taps_along(): total = total + taps[offset][:, None, None] * piece  3.95 us
    gather x1, local copies, waits for them, and re-layouts, body(): outgoing = jnp.take(flat_blocks, send_index, axis=0, mode='clip')  2.66 us
    ppermute x1, starting transfers between devices, extended_2(): before = lax.ppermute(last, axis, up)  2.42 us
  transfers between devices with their start and end apart: 4, of which 2 were waited for; matrix products, arithmetic and copies ran while one was open for 12% of the time, Pallas kernels for 0%

profile of v17, /device:TPU:0, one launch (start us, length us, event | category | flops | bytes accessed | tf_op | source)
XLA Modules:
  0.0 69.3 jit_solution(12184630448701241668)
XLA Ops:
  0.0 0.8 %select_reduce_fusion.3 = s32[16]{0:T(128)S(1)} fusion(s32[4,16]{1,0:T(4,128)} %param.8, pred[4]{0:T(512)(128)(4,1)S(1)} %iota_compare_fusion.5), kind=kLoop, calls=%fused_computation.219 | loop fusion | flops 112 | bytes 324 | tf_op jit(solution)/shard_map/reduce_sum | solution.py:55
  0.8 0.1 fusion.149
  0.9 0.1 slice_bitcast_fusion.63
  0.9 0.1 stack_reshape.3
  1.0 0.1 slice.524
  1.1 0.1 slice.526
  1.2 0.2 fusion.137
  1.4 0.1 select_add_fusion
  1.4 0.1 reshape.569
  1.5 2.7 %gather_fusion = f32[128,8,256]{2,1,0:T(8,128)} fusion(f32[64,8,256]{2,1,0:T(8,128)} %bitcast.172, s32[1024]{0:T(1024)S(1)} %pad_clamp_fusion.2), kind=kCustom, calls=%fused_computation | custom fusion | bytes 2097664 | tf_op jit(solution)/shard_map/jit(_take)/gather | solution.py:89
  4.2 4.4 %all-to-all-start = ((f32[128,8,256]{2,1,0:T(8,128)}), f32[128,8,256]{2,1,0:T(8,128)S(1)}, u32[]{:S(2)}, u32[]{:S(2)}) async-start(f32[128,8,256]{2,1,0:T(8,128)} %gather_fusion), calls=%async_computation | async-start | bytes 2097152 | tf_op jit(solution)/shard_map/all_to_all | solution.py:91
  8.6 2.4 %collective-permute-start = (f32[4,32,256]{2,1,0:T(8,128)S(1)}, f32[4,32,256]{2,1,0:T(8,128)S(1)}, u32[]{:S(2)}, u32[]{:S(2)}) collective-permute-start(f32[4,32,256]{2,1,0:T(8,128)S(1)} %get-tuple-element.5), channel_id=1, source_target_pairs={{0,4},{4,8},{8,12},{1,5},{5,9},{9,13},{2,6},{6,10},{10,14},{3,7},{... | collective-permute-start | bytes 393224 | tf_op jit(solution)/shard_map/ppermute | solution.py:19
  11.0 1.3 %collective-permute-start.1 = (f32[4,32,256]{2,1,0:T(8,128)S(1)}, f32[4,32,256]{2,1,0:T(8,128)S(1)}, u32[]{:S(2)}, u32[]{:S(2)}) collective-permute-start(f32[4,32,256]{2,1,0:T(8,128)S(1)} %get-tuple-element.6), channel_id=1, source_target_pairs={{4,0},{8,4},{12,8},{5,1},{9,5},{13,9},{6,2},{10,6},{14,10},{7,3},{... | collective-permute-start | bytes 393224 | tf_op jit(solution)/shard_map/ppermute | solution.py:20
  12.3 0.1 reshape.561
  12.4 0.6 fusion.148
  13.1 0.6 reshape.559
  13.7 0.6 reshape.560
  14.4 0.1 pad_add_fusion.1
  14.4 0.1 dynamic_slice.13
  14.5 0.1 copy.15
  14.6 0.1 select_reduce_fusion
  14.8 0.1 select_reduce_fusion.2
  14.9 0.1 iota_add_fusion.1
  15.0 0.1 slice_bitcast_fusion.58
  15.1 0.1 iota_add_fusion
  15.1 0.1 slice_select_fusion.8
  15.3 0.1 reshape.577
  15.4 0.1 add.307
  15.5 0.1 slice_bitcast_fusion.48
  15.6 0.1 fusion.130
  15.7 7.3 %all-to-all-done = f32[128,8,256]{2,1,0:T(8,128)S(1)} async-done(((f32[128,8,256]{2,1,0:T(8,128)}), f32[128,8,256]{2,1,0:T(8,128)S(1)}, u32[]{:S(2)}, u32[]{:S(2)}) %all-to-all-start) | async-done | bytes 1048608 | tf_op jit(solution)/shard_map/all_to_all | solution.py:91
  23.0 0.8 %gather_fusion.1 = f32[128,8,256]{2,1,0:T(8,128)S(1)} fusion(f32[128,8,256]{2,1,0:T(8,128)S(1)} %all-to-all-done, s32[1024]{0:T(1024)S(1)} %pad_clamp_fusion.1), kind=kCustom, calls=%fused_computation.1 | custom fusion | bytes 2097664 | tf_op jit(solution)/shard_map/jit(_take)/gather | solution.py:99
  23.8 2.7 %fusion.24 = f32[32,32,256]{2,1,0:T(8,128)S(1)} fusion(f32[32,32,256]{2,1,0:T(8,128)S(1)} %bitcast.173, f32[32]{0:T(128)S(1)} %get-tuple-element.19, f32[32]{0:T(128)S(1)} %get-tuple-element.20, f32[32]{0:T(128)S(1)} %get-tuple-element.21, f32[32]{0:T(128)S(1)} %get-tuple-element.22, f32[32]{0:T(128)S(1)} %get-tuple-element.23, f32[32]{0:T(128)S(1)} %get-tuple-element.24, ...), kind=kLoop, calls=%fused_computation.51 | loop fusion | flops 4456448 | bytes 2098304 | tf_op jit(solution)/shard_map/add | solution.py:36
  26.4 1.3 %fusion.8 = f32[32,32,256]{2,1,0:T(8,128)S(1)} fusion(f32[32,32,256]{2,1,0:T(8,128)S(1)} %fusion.24, f32[32]{0:T(128)S(1)} %get-tuple-element.11, f32[32]{0:T(128)S(1)} %get-tuple-element.12, f32[32]{0:T(128)S(1)} %get-tuple-element.13, f32[32]{0:T(128)S(1)} %get-tuple-element.14, f32[32]{0:T(128)S(1)} %get-tuple-element.15, f32[32]{0:T(128)S(1)} %get-tuple-element.16, ...), kind=kLoop, calls=%fused_computation.35 | loop fusion | flops 4456448 | bytes 2098304 | tf_op jit(solution)/shard_map/add | solution.py:36
  27.8 0.9 %fusion.34 = f32[24,32,256]{2,1,0:T(8,128)S(1)} fusion(f32[32,32,256]{2,1,0:T(8,128)S(1)} %fusion.8, f32[4,32,256]{2,1,0:T(8,128)S(1)} %collective-permute-done.1, f32[16,32,256]{2,1,0:T(8,128)S(1)} %bitcast.175, f32[4,32,256]{2,1,0:T(8,128)S(1)} %collective-permute-done, f32[24]{0:T(128)S(1)} %get-tuple-element.29, f32[24]{0:T(128)S(1)} %get-tuple-element.30, ...), kind=kLoop, calls=%fused_computation.62 | loop fusion | flops 4128768 | bytes 8651640 | tf_op jit(solution)/shard_map/jit(_where)/select_n | solution.py:121
  28.7 1.2 %fusion.60 = f32[16,32,256]{2,1,0:T(8,128)S(1)} fusion(f32[24,32,256]{2,1,0:T(8,128)S(1)} %fusion.34, f32[16]{0:T(128)S(1)} %get-tuple-element.56, f32[16]{0:T(128)S(1)} %get-tuple-element.57, f32[16]{0:T(128)S(1)} %get-tuple-element.58, f32[16]{0:T(128)S(1)} %get-tuple-element.59, f32[16]{0:T(128)S(1)} %get-tuple-element.60, f32[16]{0:T(128)S(1)} %get-tuple-element.61, ...), kind=kOutput, calls=%fused_computation.97 | convolution fusion | flops 52838400 | bytes 5288960 | tf_op jit(solution)/shard_map/pri,pix->prx/dot_general | solution.py:136
  29.9 1.3 %fusion.51 = f32[16,32,256]{2,1,0:T(8,128)S(1)} fusion(f32[16,32,256]{2,1,0:T(8,128)S(1)} %fusion.60, f32[16]{0:T(128)S(1)} %get-tuple-element.38, f32[16]{0:T(128)S(1)} %get-tuple-element.39, f32[16]{0:T(128)S(1)} %get-tuple-element.40, f32[16]{0:T(128)S(1)} %get-tuple-element.41, f32[16]{0:T(128)S(1)} %get-tuple-element.42, f32[16]{0:T(128)S(1)} %get-tuple-element.43, ...), kind=kLoop, calls=%fused_computation.87 | loop fusion | flops 2228224 | bytes 1049152 | tf_op jit(solution)/shard_map/log | solution.py:139
  31.2 0.8 %copy.16 = f32[4,4,4,8,256]{4,3,1,2,0:T(8,128)} copy(f32[4,4,4,8,256]{4,3,2,1,0:T(8,128)S(1)} %bitcast.174) | data formatting | bytes 1048576 | tf_op jit(solution)/shard_map/reshape | solution.py:139
  32.1 5.7 %all-to-all-start.1 = ((f32[16,4,8,256]{3,2,1,0:T(8,128)}), f32[16,4,8,256]{3,2,1,0:T(8,128)S(1)}, u32[]{:S(2)}, u32[]{:S(2)}) async-start(f32[16,4,8,256]{3,2,1,0:T(8,128)} %bitcast.78), calls=%async_computation.1 | async-start | bytes 1048576 | tf_op jit(solution)/shard_map/all_to_all | solution.py:141
  37.8 0.1 reshape.565
  37.9 0.2 fusion.133
  38.1 0.1 select_reduce_fusion.1
  38.2 0.1 broadcast_add_fusion
  38.2 0.1 reshape.585
  38.3 13.8 %all-to-all-done.1 = f32[16,4,8,256]{3,2,1,0:T(8,128)S(1)} async-done(((f32[16,4,8,256]{3,2,1,0:T(8,128)}), f32[16,4,8,256]{3,2,1,0:T(8,128)S(1)}, u32[]{:S(2)}, u32[]{:S(2)}) %all-to-all-start.1) | async-done | bytes 524320 | tf_op jit(solution)/shard_map/all_to_all | solution.py:141
  52.1 0.6 gather_fusion.2
  52.7 15.7 %all_gather.3 = f32[16,32,256]{2,1,0:T(8,128)S(1)} all-gather(f32[4,32,256]{2,1,0:T(8,128)S(1)} %copy_bitcast_fusion), channel_id=1, replica_groups=mesh['tile'=2,'dom'=4,'view'=4] {'view'}, dimensions={0}, use_global_device_ids=true | all-gather | bytes 655360 | tf_op jit(solution)/shard_map/all_gather | solution.py:156
  68.4 0.9 %exponential_multiply_fusion = f32[16,32,256]{2,1,0:T(8,128)} fusion(f32[16,32,256]{2,1,0:T(8,128)S(1)} %copy-done, f32[16,32,256]{2,1,0:T(8,128)S(1)} %all_gather.3), kind=kLoop, calls=%fused_computation.113 | loop fusion | flops 262144 | bytes 1572864 | tf_op jit(solution)/shard_map/mul | solution.py:157
  (31 shorter events, 0.2 us)
Async XLA Ops:
  4.2 4.4 %copy-start.1 = (f32[1,16,32,256]{3,2,1,0:T(8,128)S(1)}, f32[1,16,32,256]{3,2,1,0:T(8,128)}, u32[]{:S(2)}) copy-start(f32[1,16,32,256]{3,2,1,0:T(8,128)} %param.6) | copy-start | bytes 1572868
  4.2 8.2 %copy-start.4 = (s32[1,64]{1,0:T(1,128)S(1)}, s32[1,64]{1,0:T(1,128)}, u32[]{:S(2)}) copy-start(s32[1,64]{1,0:T(1,128)} %param.9) | copy-start | bytes 772
  4.2 10.3 %copy-start.3 = (f32[1,4,3,9]{3,1,2,0:T(4,128)S(1)}, f32[1,4,3,9]{3,1,2,0:T(4,128)}, u32[]{:S(2)}) copy-start(f32[1,4,3,9]{3,1,2,0:T(4,128)} %param.7) | copy-start | bytes 1300
  4.2 18.8 %all-to-all-start = ((f32[128,8,256]{2,1,0:T(8,128)}), f32[128,8,256]{2,1,0:T(8,128)S(1)}, u32[]{:S(2)}, u32[]{:S(2)}) async-start(f32[128,8,256]{2,1,0:T(8,128)} %gather_fusion), calls=%async_computation | async-start | bytes 2097152 | tf_op jit(solution)/shard_map/all_to_all | solution.py:91
  8.6 19.1 %collective-permute-start = (f32[4,32,256]{2,1,0:T(8,128)S(1)}, f32[4,32,256]{2,1,0:T(8,128)S(1)}, u32[]{:S(2)}, u32[]{:S(2)}) collective-permute-start(f32[4,32,256]{2,1,0:T(8,128)S(1)} %get-tuple-element.5), channel_id=1, source_target_pairs={{0,4},{4,8},{8,12},{1,5},{5,9},{9,13},{2,6},{6,10},{10,14},{3,7},{... | collective-permute-start | bytes 393224 | tf_op jit(solution)/shard_map/ppermute | solution.py:19
  11.0 16.7 %collective-permute-start.1 = (f32[4,32,256]{2,1,0:T(8,128)S(1)}, f32[4,32,256]{2,1,0:T(8,128)S(1)}, u32[]{:S(2)}, u32[]{:S(2)}) collective-permute-start(f32[4,32,256]{2,1,0:T(8,128)S(1)} %get-tuple-element.6), channel_id=1, source_target_pairs={{4,0},{8,4},{12,8},{5,1},{9,5},{13,9},{6,2},{10,6},{14,10},{7,3},{... | collective-permute-start | bytes 393224 | tf_op jit(solution)/shard_map/ppermute | solution.py:20
  31.2 6.6 %copy-start.2 = (s32[4,16]{1,0:T(4,128)S(1)}, s32[4,16]{1,0:T(4,128)}, u32[]{:S(2)}) copy-start(s32[4,16]{1,0:T(4,128)} %param.8) | copy-start | bytes 772
  32.1 20.0 %all-to-all-start.1 = ((f32[16,4,8,256]{3,2,1,0:T(8,128)}), f32[16,4,8,256]{3,2,1,0:T(8,128)S(1)}, u32[]{:S(2)}, u32[]{:S(2)}) async-start(f32[16,4,8,256]{3,2,1,0:T(8,128)} %bitcast.78), calls=%async_computation.1 | async-start | bytes 1048576 | tf_op jit(solution)/shard_map/all_to_all | solution.py:141
  38.3 30.1 %copy-start = (f32[16,32,256]{2,1,0:T(8,128)S(1)}, f32[16,32,256]{2,1,0:T(8,128)}, u32[]{:S(2)}) copy-start(f32[16,32,256]{2,1,0:T(8,128)} %param.5) | copy-start | bytes 1572868

commit v18 on v17

--- a/solution.py
+++ b/solution.py
@@ -84,9 +84,19 @@
     source_block = jnp.where(
         in_top[:, None], above[None, :], jnp.where(in_bottom[:, None], below[None, :], send_slot[None, :])
     )
-    send_index = (source_plane[None, :] * block_count + source_block.T).reshape(-1)
-    flat_blocks = estimate.reshape(plane_count * block_count, block_rows, lane_count)
-    outgoing = jnp.take(flat_blocks, send_index, axis=0, mode="clip")
+    piece_count = wide_count // wide
+    piece_first = source_plane[::wide]
+    piece_block = source_block[::wide].T
+    starts = jnp.stack(
+        [jnp.broadcast_to(piece_first[None, :], piece_block.shape), piece_block], axis=-1
+    ).reshape(block_count * piece_count, 2)
+    numbers = lax.GatherDimensionNumbers(
+        offset_dims=(1, 2, 3), collapsed_slice_dims=(1,), start_index_map=(0, 1)
+    )
+    blocks = estimate.reshape(plane_count, block_count, block_rows, lane_count)
+    outgoing = lax.gather(
+        blocks, starts, numbers, (wide, 1, block_rows, lane_count), mode=lax.GatherScatterMode.CLIP
+    )
     outgoing = outgoing.reshape(block_count * wide_count, block_rows, lane_count)
     arrived = lax.all_to_all(outgoing, "dom", split_axis=0, concat_axis=0, tiled=True)
     my_sources = lax.dynamic_index_in_dim(source_dev, dom_index, 0, keepdims=False)

time: 69.7 us -> 70.1 us (level)
  no operation moved by 1% of the time
where the time goes in v18:
time: 70.1 us; the launch traced here: 69.7 us
  waiting for transfers between devices  21.3 us (30%)
  blocking collectives  15.7 us (22%)
  starting transfers between devices  13.8 us (20%)
  other arithmetic  9.15 us (13%)
  local copies, waits for them, and re-layouts  8.22 us (12%)
  matrix products  1.2 us (2%)
    all_gather x1, blocking collectives, body(): log_joined = lax.all_gather(log_total, 'view', axis=0, tiled=True)  15.7 us
    all_to_all x1, waiting for transfers between devices, body(): arrived_logs = lax.all_to_all(outgoing, ('view', 'dom'), 0, 0, tiled=True)  13.8 us
    all_to_all x1, waiting for transfers between devices, body(): lax.all_to_all(outgoing, 'dom', split_axis=0, concat_axis=0, tiled=True)  7.58 us
    all_to_all x1, starting transfers between devices, body(): arrived_logs = lax.all_to_all(outgoing, ('view', 'dom'), 0, 0, tiled=True)  5.74 us
    all_to_all x1, starting transfers between devices, body(): lax.all_to_all(outgoing, 'dom', split_axis=0, concat_axis=0, tiled=True)  4.37 us
    add x2, other arithmetic, taps_along(): total = total + taps[offset][:, None, None] * piece  3.95 us
    gather x1, local copies, waits for them, and re-layouts, body(): lax.gather(blocks, starts, numbers, (wide, 1, block_rows, lane_count), mo...  2.63 us
    ppermute x1, starting transfers between devices, extended_2(): before = lax.ppermute(last, axis, up)  2.42 us
  transfers between devices with their start and end apart: 4, of which 2 were waited for; matrix products, arithmetic and copies ran while one was open for 12% of the time, Pallas kernels for 0%

profile of v18, /device:TPU:0, one launch (start us, length us, event | category | flops | bytes accessed | tf_op | source)
XLA Modules:
  0.0 69.7 jit_solution(12028412703036950068)
XLA Ops:
  0.0 0.8 %select_reduce_fusion.3 = s32[16]{0:T(128)S(1)} fusion(s32[4,16]{1,0:T(4,128)} %param.8, pred[4]{0:T(512)(128)(4,1)S(1)} %iota_compare_fusion.5), kind=kLoop, calls=%fused_computation.219 | loop fusion | flops 112 | bytes 324 | tf_op jit(solution)/shard_map/reduce_sum | solution.py:55
  0.8 0.1 reshape.485
  0.9 0.1 fusion.148
  1.0 0.1 stack_reshape.3
  1.1 0.1 slice.531
  1.2 0.1 slice.533
  1.3 0.2 fusion.137
  1.5 0.1 iota_add_fusion
  1.6 0.1 slice.527
  1.7 0.1 or_bitcast_fusion
  1.8 0.1 copy.20
  1.9 0.1 reshape.492
  1.9 2.6 %gather_fusion = f32[16,8,8,256]{3,2,1,0:T(8,128)} fusion(f32[16,4,8,256]{3,2,1,0:T(8,128)} %bitcast.175, s32[16]{0:T(128)S(1)} %reshape.492), kind=kCustom, calls=%fused_computation | custom fusion | bytes 2097280 | tf_op jit(solution)/shard_map/gather | solution.py:97
  4.6 4.4 %all-to-all-start = ((f32[128,8,256]{2,1,0:T(8,128)}), f32[128,8,256]{2,1,0:T(8,128)S(1)}, u32[]{:S(2)}, u32[]{:S(2)}) async-start(f32[128,8,256]{2,1,0:T(8,128)} %bitcast.34), calls=%async_computation | async-start | bytes 2097152 | tf_op jit(solution)/shard_map/all_to_all | solution.py:101
  9.0 2.4 %collective-permute-start = (f32[4,32,256]{2,1,0:T(8,128)S(1)}, f32[4,32,256]{2,1,0:T(8,128)S(1)}, u32[]{:S(2)}, u32[]{:S(2)}) collective-permute-start(f32[4,32,256]{2,1,0:T(8,128)S(1)} %get-tuple-element.5), channel_id=1, source_target_pairs={{0,4},{4,8},{8,12},{1,5},{5,9},{9,13},{2,6},{6,10},{10,14},{3,7},{... | collective-permute-start | bytes 393224 | tf_op jit(solution)/shard_map/ppermute | solution.py:19
  11.4 1.3 %collective-permute-start.1 = (f32[4,32,256]{2,1,0:T(8,128)S(1)}, f32[4,32,256]{2,1,0:T(8,128)S(1)}, u32[]{:S(2)}, u32[]{:S(2)}) collective-permute-start(f32[4,32,256]{2,1,0:T(8,128)S(1)} %get-tuple-element.6), channel_id=1, source_target_pairs={{4,0},{8,4},{12,8},{5,1},{9,5},{13,9},{6,2},{10,6},{14,10},{7,3},{... | collective-permute-start | bytes 393224 | tf_op jit(solution)/shard_map/ppermute | solution.py:20
  12.7 0.1 select_reduce_fusion.2
  12.8 0.6 fusion.147
  13.4 0.6 reshape.483
  14.1 0.6 reshape.484
  14.7 0.1 pad_add_fusion.1
  14.8 0.1 dynamic_slice.13
  14.9 0.1 copy.19
  15.0 0.1 select_reduce_fusion
  15.2 0.1 slice_bitcast_fusion.58
  15.3 0.1 slice_select_fusion.8
  15.4 0.1 reshape.500
  15.5 0.1 add.276
  15.6 0.1 slice_bitcast_fusion.48
  15.7 0.1 fusion.130
  15.8 7.6 %all-to-all-done = f32[128,8,256]{2,1,0:T(8,128)S(1)} async-done(((f32[128,8,256]{2,1,0:T(8,128)}), f32[128,8,256]{2,1,0:T(8,128)S(1)}, u32[]{:S(2)}, u32[]{:S(2)}) %all-to-all-start) | async-done | bytes 1048608 | tf_op jit(solution)/shard_map/all_to_all | solution.py:101
  23.4 0.8 %gather_fusion.1 = f32[128,8,256]{2,1,0:T(8,128)S(1)} fusion(f32[128,8,256]{2,1,0:T(8,128)S(1)} %all-to-all-done, s32[1024]{0:T(1024)S(1)} %pad_clamp_fusion.1), kind=kCustom, calls=%fused_computation.1 | custom fusion | bytes 2097664 | tf_op jit(solution)/shard_map/jit(_take)/gather | solution.py:109
  24.1 2.7 %fusion.24 = f32[32,32,256]{2,1,0:T(8,128)S(1)} fusion(f32[32,32,256]{2,1,0:T(8,128)S(1)} %bitcast.176, f32[32]{0:T(128)S(1)} %get-tuple-element.19, f32[32]{0:T(128)S(1)} %get-tuple-element.20, f32[32]{0:T(128)S(1)} %get-tuple-element.21, f32[32]{0:T(128)S(1)} %get-tuple-element.22, f32[32]{0:T(128)S(1)} %get-tuple-element.23, f32[32]{0:T(128)S(1)} %get-tuple-element.24, ...), kind=kLoop, calls=%fused_computation.51 | loop fusion | flops 4456448 | bytes 2098304 | tf_op jit(solution)/shard_map/add | solution.py:36
  26.8 1.3 %fusion.8 = f32[32,32,256]{2,1,0:T(8,128)S(1)} fusion(f32[32,32,256]{2,1,0:T(8,128)S(1)} %fusion.24, f32[32]{0:T(128)S(1)} %get-tuple-element.11, f32[32]{0:T(128)S(1)} %get-tuple-element.12, f32[32]{0:T(128)S(1)} %get-tuple-element.13, f32[32]{0:T(128)S(1)} %get-tuple-element.14, f32[32]{0:T(128)S(1)} %get-tuple-element.15, f32[32]{0:T(128)S(1)} %get-tuple-element.16, ...), kind=kLoop, calls=%fused_computation.35 | loop fusion | flops 4456448 | bytes 2098304 | tf_op jit(solution)/shard_map/add | solution.py:36
  28.1 0.9 %fusion.34 = f32[24,32,256]{2,1,0:T(8,128)S(1)} fusion(f32[32,32,256]{2,1,0:T(8,128)S(1)} %fusion.8, f32[4,32,256]{2,1,0:T(8,128)S(1)} %collective-permute-done.1, f32[16,32,256]{2,1,0:T(8,128)S(1)} %bitcast.178, f32[4,32,256]{2,1,0:T(8,128)S(1)} %collective-permute-done, f32[24]{0:T(128)S(1)} %get-tuple-element.29, f32[24]{0:T(128)S(1)} %get-tuple-element.30, ...), kind=kLoop, calls=%fused_computation.62 | loop fusion | flops 4128768 | bytes 8651640 | tf_op jit(solution)/shard_map/jit(_where)/select_n | solution.py:131
  29.0 1.2 %fusion.60 = f32[16,32,256]{2,1,0:T(8,128)S(1)} fusion(f32[24,32,256]{2,1,0:T(8,128)S(1)} %fusion.34, f32[16]{0:T(128)S(1)} %get-tuple-element.56, f32[16]{0:T(128)S(1)} %get-tuple-element.57, f32[16]{0:T(128)S(1)} %get-tuple-element.58, f32[16]{0:T(128)S(1)} %get-tuple-element.59, f32[16]{0:T(128)S(1)} %get-tuple-element.60, f32[16]{0:T(128)S(1)} %get-tuple-element.61, ...), kind=kOutput, calls=%fused_computation.97 | convolution fusion | flops 52838400 | bytes 5288960 | tf_op jit(solution)/shard_map/pri,pix->prx/dot_general | solution.py:146
  30.3 1.3 %fusion.51 = f32[16,32,256]{2,1,0:T(8,128)S(1)} fusion(f32[16,32,256]{2,1,0:T(8,128)S(1)} %fusion.60, f32[16]{0:T(128)S(1)} %get-tuple-element.38, f32[16]{0:T(128)S(1)} %get-tuple-element.39, f32[16]{0:T(128)S(1)} %get-tuple-element.40, f32[16]{0:T(128)S(1)} %get-tuple-element.41, f32[16]{0:T(128)S(1)} %get-tuple-element.42, f32[16]{0:T(128)S(1)} %get-tuple-element.43, ...), kind=kLoop, calls=%fused_computation.87 | loop fusion | flops 2228224 | bytes 1049152 | tf_op jit(solution)/shard_map/log | solution.py:149
  31.6 0.8 %copy.21 = f32[4,4,4,8,256]{4,3,1,2,0:T(8,128)} copy(f32[4,4,4,8,256]{4,3,2,1,0:T(8,128)S(1)} %bitcast.177) | data formatting | bytes 1048576 | tf_op jit(solution)/shard_map/reshape | solution.py:149
  32.5 5.7 %all-to-all-start.1 = ((f32[16,4,8,256]{3,2,1,0:T(8,128)}), f32[16,4,8,256]{3,2,1,0:T(8,128)S(1)}, u32[]{:S(2)}, u32[]{:S(2)}) async-start(f32[16,4,8,256]{3,2,1,0:T(8,128)} %bitcast.80), calls=%async_computation.1 | async-start | bytes 1048576 | tf_op jit(solution)/shard_map/all_to_all | solution.py:151
  38.2 0.1 reshape.490
  38.3 0.2 fusion.133
  38.5 0.1 select_reduce_fusion.1
  38.5 0.1 broadcast_add_fusion
  38.6 0.1 reshape.508
  38.7 13.8 %all-to-all-done.1 = f32[16,4,8,256]{3,2,1,0:T(8,128)S(1)} async-done(((f32[16,4,8,256]{3,2,1,0:T(8,128)}), f32[16,4,8,256]{3,2,1,0:T(8,128)S(1)}, u32[]{:S(2)}, u32[]{:S(2)}) %all-to-all-start.1) | async-done | bytes 524320 | tf_op jit(solution)/shard_map/all_to_all | solution.py:151
  52.5 0.6 gather_fusion.2
  53.1 15.7 %all_gather.3 = f32[16,32,256]{2,1,0:T(8,128)S(1)} all-gather(f32[4,32,256]{2,1,0:T(8,128)S(1)} %copy_bitcast_fusion), channel_id=1, replica_groups=mesh['tile'=2,'dom'=4,'view'=4] {'view'}, dimensions={0}, use_global_device_ids=true | all-gather | bytes 655360 | tf_op jit(solution)/shard_map/all_gather | solution.py:166
  68.8 0.9 %exponential_multiply_fusion = f32[16,32,256]{2,1,0:T(8,128)} fusion(f32[16,32,256]{2,1,0:T(8,128)S(1)} %copy-done, f32[16,32,256]{2,1,0:T(8,128)S(1)} %all_gather.3), kind=kLoop, calls=%fused_computation.113 | loop fusion | flops 262144 | bytes 1572864 | tf_op jit(solution)/shard_map/mul | solution.py:167
  (34 shorter events, 0.4 us)
Async XLA Ops:
  4.6 4.4 %copy-start.1 = (f32[1,16,32,256]{3,2,1,0:T(8,128)S(1)}, f32[1,16,32,256]{3,2,1,0:T(8,128)}, u32[]{:S(2)}) copy-start(f32[1,16,32,256]{3,2,1,0:T(8,128)} %param.6) | copy-start | bytes 1572868
  4.6 8.2 %copy-start.4 = (s32[1,64]{1,0:T(1,128)S(1)}, s32[1,64]{1,0:T(1,128)}, u32[]{:S(2)}) copy-start(s32[1,64]{1,0:T(1,128)} %param.9) | copy-start | bytes 772
  4.6 10.3 %copy-start.3 = (f32[1,4,3,9]{3,1,2,0:T(4,128)S(1)}, f32[1,4,3,9]{3,1,2,0:T(4,128)}, u32[]{:S(2)}) copy-start(f32[1,4,3,9]{3,1,2,0:T(4,128)} %param.7) | copy-start | bytes 1300
  4.6 18.8 %all-to-all-start = ((f32[128,8,256]{2,1,0:T(8,128)}), f32[128,8,256]{2,1,0:T(8,128)S(1)}, u32[]{:S(2)}, u32[]{:S(2)}) async-start(f32[128,8,256]{2,1,0:T(8,128)} %bitcast.34), calls=%async_computation | async-start | bytes 2097152 | tf_op jit(solution)/shard_map/all_to_all | solution.py:101
  9.0 19.1 %collective-permute-start = (f32[4,32,256]{2,1,0:T(8,128)S(1)}, f32[4,32,256]{2,1,0:T(8,128)S(1)}, u32[]{:S(2)}, u32[]{:S(2)}) collective-permute-start(f32[4,32,256]{2,1,0:T(8,128)S(1)} %get-tuple-element.5), channel_id=1, source_target_pairs={{0,4},{4,8},{8,12},{1,5},{5,9},{9,13},{2,6},{6,10},{10,14},{3,7},{... | collective-permute-start | bytes 393224 | tf_op jit(solution)/shard_map/ppermute | solution.py:19
  11.4 16.7 %collective-permute-start.1 = (f32[4,32,256]{2,1,0:T(8,128)S(1)}, f32[4,32,256]{2,1,0:T(8,128)S(1)}, u32[]{:S(2)}, u32[]{:S(2)}) collective-permute-start(f32[4,32,256]{2,1,0:T(8,128)S(1)} %get-tuple-element.6), channel_id=1, source_target_pairs={{4,0},{8,4},{12,8},{5,1},{9,5},{13,9},{6,2},{10,6},{14,10},{7,3},{... | collective-permute-start | bytes 393224 | tf_op jit(solution)/shard_map/ppermute | solution.py:20
  31.6 6.6 %copy-start.2 = (s32[4,16]{1,0:T(4,128)S(1)}, s32[4,16]{1,0:T(4,128)}, u32[]{:S(2)}) copy-start(s32[4,16]{1,0:T(4,128)} %param.8) | copy-start | bytes 772
  32.5 20.0 %all-to-all-start.1 = ((f32[16,4,8,256]{3,2,1,0:T(8,128)}), f32[16,4,8,256]{3,2,1,0:T(8,128)S(1)}, u32[]{:S(2)}, u32[]{:S(2)}) async-start(f32[16,4,8,256]{3,2,1,0:T(8,128)} %bitcast.80), calls=%async_computation.1 | async-start | bytes 1048576 | tf_op jit(solution)/shard_map/all_to_all | solution.py:151
  38.7 30.1 %copy-start = (f32[16,32,256]{2,1,0:T(8,128)S(1)}, f32[16,32,256]{2,1,0:T(8,128)}, u32[]{:S(2)}) copy-start(f32[16,32,256]{2,1,0:T(8,128)} %param.5) | copy-start | bytes 1572868

commit v19 on v17

--- a/solution.py
+++ b/solution.py
@@ -71,7 +71,7 @@
     band_all = depth_band[0]
     total_planes = band_all.shape[0]
     reach = (kernels.shape[2] - 1) // 2
-    wide = 2 * reach
+    wide = reach
     last = block_count - 1
     wide_count = plane_count + 2 * wide
     chunk_plane = jnp.arange(wide_count, dtype=jnp.int32)
@@ -109,16 +109,14 @@
     x_wide = tables[2]
     y_wide = tables[1]
     lateral_ext = lateral_fwd(camera_ext, x_wide, y_wide)
-    ext_count = plane_count + 2 * reach
-    ext_planes = plane_start - reach + jnp.arange(ext_count, dtype=jnp.int32)
-    ext_inside = (ext_planes >= 0) & (ext_planes < total_planes)
-    taps_ext = tables[0][:, reach : reach + ext_count]
-    blurred = jnp.zeros((ext_count, row_count, lane_count), jnp.float32)
+    taps_own = tables[0][:, wide : wide + plane_count]
+    blurred = jnp.zeros((plane_count, row_count, lane_count), jnp.float32)
     for j in range(2 * reach + 1):
-        weight = jnp.where(wide_inside[j : j + ext_count], taps_ext[j], 0.0)
-        blurred = blurred + weight[:, None, None] * lateral_ext[j : j + ext_count]
-    observed_ext = extended_2(observed[0], (("dom", 0),), reach)
-    ratio_ext = jnp.where(ext_inside[:, None, None], observed_ext / blurred, 0.0)
+        weight = jnp.where(wide_inside[j : j + plane_count], taps_own[j], 0.0)
+        blurred = blurred + weight[:, None, None] * lateral_ext[j : j + plane_count]
+    ratio_field = observed[0] / blurred
+    ratio_ext = extended_2(ratio_field, (("dom", 0),), reach)
+    taps_ext = tables[0]
     x_own = tables[2][:, wide : wide + plane_count]
     y_own = tables[1][:, wide : wide + plane_count]
     zback = jnp.zeros((plane_count, row_count, lane_count), jnp.float32)

time: 69.7 us -> 74 us (1.062)
  waiting for transfers between devices: 21.1 us -> 24.7 us
  starting transfers between devices: 13.8 us -> 15.9 us
  other arithmetic: 9.17 us -> 7.66 us
    all_to_all x1, starting transfers between devices: 5.74 us -> 8.96 us  [body(): arrived_logs = lax.all_to_all(outgoing, ('view', 'dom'), 0, 0, tiled=True)]
    ppermute x1, waiting for transfers between devices: 0.01 us -> 2.48 us  [extended_2(): after = lax.ppermute(initial, axis, down)]
    ppermute x1, starting transfers between devices: 2.42 us -> 1.3 us  [extended_2(): before = lax.ppermute(last, axis, up)]
    all_to_all x1, waiting for transfers between devices: 7.33 us -> 8.43 us  [body(): lax.all_to_all(outgoing, 'dom', split_axis=0, concat_axis=0, tiled=True)]
    add x2, other arithmetic: 3.95 us -> 2.89 us  [taps_along(): total = total + taps[offset][:, None, None] * piece]
    select_n x2 -> x1, other arithmetic: 1 us -> 0.09 us  [body(): weight = jnp.where(wide_inside[j:j + plane_count], taps_own[j], 0.0)]
  transfers between devices with their start and end apart: 4 -> 4, of which waited for: 2 -> 3; matrix products, arithmetic and copies ran while one was open for 12% -> 5% of each run, Pallas kernels for 0% -> 0%
where the time goes in v19:
time: 74 us; the launch traced here: 73.5 us
  waiting for transfers between devices  24.7 us (33%)
  starting transfers between devices  15.9 us (21%)
  blocking collectives  15.8 us (21%)
  local copies, waits for them, and re-layouts  8.01 us (11%)
  other arithmetic  7.66 us (10%)
  matrix products  1.19 us (2%)
    all_gather x1, blocking collectives, body(): log_joined = lax.all_gather(log_total, 'view', axis=0, tiled=True)  15.8 us
    all_to_all x1, waiting for transfers between devices, body(): arrived_logs = lax.all_to_all(outgoing, ('view', 'dom'), 0, 0, tiled=True)  13.8 us
    all_to_all x1, starting transfers between devices, body(): arrived_logs = lax.all_to_all(outgoing, ('view', 'dom'), 0, 0, tiled=True)  8.96 us
    all_to_all x1, waiting for transfers between devices, body(): lax.all_to_all(outgoing, 'dom', split_axis=0, concat_axis=0, tiled=True)  8.43 us
    all_to_all x1, starting transfers between devices, body(): lax.all_to_all(outgoing, 'dom', split_axis=0, concat_axis=0, tiled=True)  4.37 us
    add x2, other arithmetic, taps_along(): total = total + taps[offset][:, None, None] * piece  2.89 us
    gather x1, local copies, waits for them, and re-layouts, body(): outgoing = jnp.take(flat_blocks, send_index, axis=0, mode='clip')  2.55 us
    ppermute x1, waiting for transfers between devices, extended_2(): after = lax.ppermute(initial, axis, down)  2.48 us
  transfers between devices with their start and end apart: 4, of which 3 were waited for; matrix products, arithmetic and copies ran while one was open for 5% of the time, Pallas kernels for 0%

profile of v19, /device:TPU:0, one launch (start us, length us, event | category | flops | bytes accessed | tf_op | source)
XLA Modules:
  0.0 73.5 jit_solution(2625204482322737211)
XLA Ops:
  0.0 0.8 %select_reduce_fusion.3 = s32[16]{0:T(128)S(1)} fusion(s32[4,16]{1,0:T(4,128)} %param.8, pred[4]{0:T(512)(128)(4,1)S(1)} %iota_compare_fusion.5), kind=kLoop, calls=%fused_computation.238 | loop fusion | flops 112 | bytes 324 | tf_op jit(solution)/shard_map/reduce_sum | solution.py:55
  0.8 0.1 fusion.167
  0.9 0.1 stack_reshape.3
  1.0 0.1 slice.509
  1.1 0.1 slice.511
  1.2 0.2 fusion.153
  1.4 0.1 select_add_fusion
  1.4 0.1 reshape.560
  1.5 2.5 %gather_fusion = f32[96,8,256]{2,1,0:T(8,128)} fusion(f32[64,8,256]{2,1,0:T(8,128)} %bitcast.167, s32[1024]{0:T(1024)S(1)} %pad_clamp_fusion.2), kind=kCustom, calls=%fused_computation | custom fusion | bytes 1573248 | tf_op jit(solution)/shard_map/jit(_take)/gather | solution.py:89
  4.1 4.4 %all-to-all-start = ((f32[96,8,256]{2,1,0:T(8,128)}), f32[96,8,256]{2,1,0:T(8,128)S(1)}, u32[]{:S(2)}, u32[]{:S(2)}) async-start(f32[96,8,256]{2,1,0:T(8,128)} %gather_fusion), calls=%async_computation | async-start | bytes 1572864 | tf_op jit(solution)/shard_map/all_to_all | solution.py:91
  8.5 0.1 reshape.552
  8.5 0.6 fusion.166
  9.2 0.6 reshape.550
  9.8 0.6 reshape.551
  10.4 0.1 pad_add_fusion.1
  10.5 0.1 dynamic_slice.13
  10.6 0.1 copy.15
  10.7 0.1 select_reduce_fusion
  10.9 0.1 select_reduce_fusion.2
  11.0 0.1 iota_add_fusion
  11.1 0.1 slice_select_fusion.8
  11.3 0.1 reshape.568
  11.4 0.1 add.296
  11.5 0.1 slice_bitcast_fusion.45
  11.5 0.1 fusion.146
  11.6 8.4 %all-to-all-done = f32[96,8,256]{2,1,0:T(8,128)S(1)} async-done(((f32[96,8,256]{2,1,0:T(8,128)}), f32[96,8,256]{2,1,0:T(8,128)S(1)}, u32[]{:S(2)}, u32[]{:S(2)}) %all-to-all-start) | async-done | bytes 786464 | tf_op jit(solution)/shard_map/all_to_all | solution.py:91
  20.1 0.7 gather_fusion.1
  20.8 2.0 %fusion.24 = f32[24,32,256]{2,1,0:T(8,128)S(1)} fusion(f32[24,32,256]{2,1,0:T(8,128)S(1)} %bitcast.168, f32[24]{0:T(128)S(1)} %get-tuple-element.19, f32[24]{0:T(128)S(1)} %get-tuple-element.20, f32[24]{0:T(128)S(1)} %get-tuple-element.21, f32[24]{0:T(128)S(1)} %get-tuple-element.22, f32[24]{0:T(128)S(1)} %get-tuple-element.23, f32[24]{0:T(128)S(1)} %get-tuple-element.24, ...), kind=kLoop, calls=%fused_computation.57 | loop fusion | flops 3342336 | bytes 1573728 | tf_op jit(solution)/shard_map/add | solution.py:36
  22.8 0.9 %fusion.8 = f32[24,32,256]{2,1,0:T(8,128)S(1)} fusion(f32[24,32,256]{2,1,0:T(8,128)S(1)} %fusion.24, f32[24]{0:T(128)S(1)} %get-tuple-element.11, f32[24]{0:T(128)S(1)} %get-tuple-element.12, f32[24]{0:T(128)S(1)} %get-tuple-element.13, f32[24]{0:T(128)S(1)} %get-tuple-element.14, f32[24]{0:T(128)S(1)} %get-tuple-element.15, f32[24]{0:T(128)S(1)} %get-tuple-element.16, ...), kind=kLoop, calls=%fused_computation.41 | loop fusion | flops 3342336 | bytes 1573728 | tf_op jit(solution)/shard_map/add | solution.py:36
  23.7 0.2 copy-done.1
  23.9 0.5 fusion.83
  24.4 1.3 %collective-permute-start = (f32[4,32,256]{2,1,0:T(8,128)S(1)}, f32[4,32,256]{2,1,0:T(8,128)S(1)}, u32[]{:S(2)}, u32[]{:S(2)}) collective-permute-start(f32[4,32,256]{2,1,0:T(8,128)S(1)} %get-tuple-element.5), channel_id=1, source_target_pairs={{0,4},{4,8},{8,12},{1,5},{5,9},{9,13},{2,6},{6,10},{10,14},{3,7},{... | collective-permute-start | bytes 393224 | tf_op jit(solution)/shard_map/ppermute | solution.py:19
  25.7 1.3 %collective-permute-start.1 = (f32[4,32,256]{2,1,0:T(8,128)S(1)}, f32[4,32,256]{2,1,0:T(8,128)S(1)}, u32[]{:S(2)}, u32[]{:S(2)}) collective-permute-start(f32[4,32,256]{2,1,0:T(8,128)S(1)} %get-tuple-element.6), channel_id=1, source_target_pairs={{4,0},{8,4},{12,8},{5,1},{9,5},{13,9},{6,2},{10,6},{14,10},{7,3},{... | collective-permute-start | bytes 393224 | tf_op jit(solution)/shard_map/ppermute | solution.py:20
  27.0 0.1 slice_bitcast_fusion.55
  27.0 2.5 %collective-permute-done.1 = f32[4,32,256]{2,1,0:T(8,128)S(1)} collective-permute-done((f32[4,32,256]{2,1,0:T(8,128)S(1)}, f32[4,32,256]{2,1,0:T(8,128)S(1)}, u32[]{:S(2)}, u32[]{:S(2)}) %collective-permute-start.1) | collective-permute-done | bytes 131104 | tf_op jit(solution)/shard_map/ppermute | solution.py:20
  29.5 1.2 %fusion.36 = f32[16,32,256]{2,1,0:T(8,128)S(1)} fusion(f32[16,32,256]{2,1,0:T(8,128)S(1)} %fusion.83, f32[4,32,256]{2,1,0:T(8,128)S(1)} %collective-permute-done.1, f32[4,32,256]{2,1,0:T(8,128)S(1)} %collective-permute-done, f32[16]{0:T(128)S(1)} %get-tuple-element.56, f32[16]{0:T(128)S(1)} %get-tuple-element.57, f32[16]{0:T(128)S(1)} %get-tuple-element.58, ...), kind=kOutput, calls=%fused_computation.75 | convolution fusion | flops 53886976 | bytes 1321088 | tf_op jit(solution)/shard_map/pri,pix->prx/dot_general | solution.py:134
  30.7 1.3 %fusion.68 = f32[16,32,256]{2,1,0:T(8,128)S(1)} fusion(f32[16,32,256]{2,1,0:T(8,128)S(1)} %fusion.36, f32[16]{0:T(128)S(1)} %get-tuple-element.38, f32[16]{0:T(128)S(1)} %get-tuple-element.39, f32[16]{0:T(128)S(1)} %get-tuple-element.40, f32[16]{0:T(128)S(1)} %get-tuple-element.41, f32[16]{0:T(128)S(1)} %get-tuple-element.42, f32[16]{0:T(128)S(1)} %get-tuple-element.43, ...), kind=kLoop, calls=%fused_computation.101 | loop fusion | flops 2228224 | bytes 1049152 | tf_op jit(solution)/shard_map/log | solution.py:137
  32.1 0.8 %copy.16 = f32[4,4,4,8,256]{4,3,1,2,0:T(8,128)} copy(f32[4,4,4,8,256]{4,3,2,1,0:T(8,128)S(1)} %bitcast.169) | data formatting | bytes 1048576 | tf_op jit(solution)/shard_map/reshape | solution.py:137
  32.9 9.0 %all-to-all-start.1 = ((f32[16,4,8,256]{3,2,1,0:T(8,128)}), f32[16,4,8,256]{3,2,1,0:T(8,128)S(1)}, u32[]{:S(2)}, u32[]{:S(2)}) async-start(f32[16,4,8,256]{3,2,1,0:T(8,128)} %bitcast.75), calls=%async_computation.1 | async-start | bytes 1048576 | tf_op jit(solution)/shard_map/all_to_all | solution.py:139
  41.9 0.1 reshape.556
  42.0 0.2 fusion.149
  42.1 0.1 select_reduce_fusion.1
  42.2 0.1 broadcast_add_fusion
  42.3 0.1 reshape.576
  42.4 13.8 %all-to-all-done.1 = f32[16,4,8,256]{3,2,1,0:T(8,128)S(1)} async-done(((f32[16,4,8,256]{3,2,1,0:T(8,128)}), f32[16,4,8,256]{3,2,1,0:T(8,128)S(1)}, u32[]{:S(2)}, u32[]{:S(2)}) %all-to-all-start.1) | async-done | bytes 524320 | tf_op jit(solution)/shard_map/all_to_all | solution.py:139
  56.2 0.6 gather_fusion.2
  56.8 15.8 %all_gather.3 = f32[16,32,256]{2,1,0:T(8,128)S(1)} all-gather(f32[4,32,256]{2,1,0:T(8,128)S(1)} %copy_bitcast_fusion), channel_id=1, replica_groups=mesh['tile'=2,'dom'=4,'view'=4] {'view'}, dimensions={0}, use_global_device_ids=true | all-gather | bytes 655360 | tf_op jit(solution)/shard_map/all_gather | solution.py:154
  72.6 0.9 %exponential_multiply_fusion = f32[16,32,256]{2,1,0:T(8,128)} fusion(f32[16,32,256]{2,1,0:T(8,128)S(1)} %copy-done, f32[16,32,256]{2,1,0:T(8,128)S(1)} %all_gather.3), kind=kLoop, calls=%fused_computation.133 | loop fusion | flops 262144 | bytes 1572864 | tf_op jit(solution)/shard_map/mul | solution.py:155
  (30 shorter events, 0.3 us)
Async XLA Ops:
  4.1 4.5 %copy-start.4 = (s32[1,64]{1,0:T(1,128)S(1)}, s32[1,64]{1,0:T(1,128)}, u32[]{:S(2)}) copy-start(s32[1,64]{1,0:T(1,128)} %param.9) | copy-start | bytes 772
  4.1 6.5 %copy-start.3 = (f32[1,4,3,9]{3,1,2,0:T(4,128)S(1)}, f32[1,4,3,9]{3,1,2,0:T(4,128)}, u32[]{:S(2)}) copy-start(f32[1,4,3,9]{3,1,2,0:T(4,128)} %param.7) | copy-start | bytes 1300
  4.1 16.0 %all-to-all-start = ((f32[96,8,256]{2,1,0:T(8,128)}), f32[96,8,256]{2,1,0:T(8,128)S(1)}, u32[]{:S(2)}, u32[]{:S(2)}) async-start(f32[96,8,256]{2,1,0:T(8,128)} %gather_fusion), calls=%async_computation | async-start | bytes 1572864 | tf_op jit(solution)/shard_map/all_to_all | solution.py:91
  22.8 1.0 %copy-start.1 = (f32[1,16,32,256]{3,2,1,0:T(8,128)S(1)}, f32[1,16,32,256]{3,2,1,0:T(8,128)}, u32[]{:S(2)}) copy-start(f32[1,16,32,256]{3,2,1,0:T(8,128)} %param.6) | copy-start | bytes 1572868
  24.4 2.7 %collective-permute-start = (f32[4,32,256]{2,1,0:T(8,128)S(1)}, f32[4,32,256]{2,1,0:T(8,128)S(1)}, u32[]{:S(2)}, u32[]{:S(2)}) collective-permute-start(f32[4,32,256]{2,1,0:T(8,128)S(1)} %get-tuple-element.5), channel_id=1, source_target_pairs={{0,4},{4,8},{8,12},{1,5},{5,9},{9,13},{2,6},{6,10},{10,14},{3,7},{... | collective-permute-start | bytes 393224 | tf_op jit(solution)/shard_map/ppermute | solution.py:19
  25.7 3.9 %collective-permute-start.1 = (f32[4,32,256]{2,1,0:T(8,128)S(1)}, f32[4,32,256]{2,1,0:T(8,128)S(1)}, u32[]{:S(2)}, u32[]{:S(2)}) collective-permute-start(f32[4,32,256]{2,1,0:T(8,128)S(1)} %get-tuple-element.6), channel_id=1, source_target_pairs={{4,0},{8,4},{12,8},{5,1},{9,5},{13,9},{6,2},{10,6},{14,10},{7,3},{... | collective-permute-start | bytes 393224 | tf_op jit(solution)/shard_map/ppermute | solution.py:20
  32.9 9.0 %copy-start.2 = (s32[4,16]{1,0:T(4,128)S(1)}, s32[4,16]{1,0:T(4,128)}, u32[]{:S(2)}) copy-start(s32[4,16]{1,0:T(4,128)} %param.8) | copy-start | bytes 772
  32.9 23.2 %all-to-all-start.1 = ((f32[16,4,8,256]{3,2,1,0:T(8,128)}), f32[16,4,8,256]{3,2,1,0:T(8,128)S(1)}, u32[]{:S(2)}, u32[]{:S(2)}) async-start(f32[16,4,8,256]{3,2,1,0:T(8,128)} %bitcast.75), calls=%async_computation.1 | async-start | bytes 1048576 | tf_op jit(solution)/shard_map/all_to_all | solution.py:139
  56.7 15.9 %copy-start = (f32[16,32,256]{2,1,0:T(8,128)S(1)}, f32[16,32,256]{2,1,0:T(8,128)}, u32[]{:S(2)}) copy-start(f32[16,32,256]{2,1,0:T(8,128)} %param.5) | copy-start | bytes 1572868

commit v20 on v17

--- a/solution.py
+++ b/solution.py
@@ -95,12 +95,12 @@
     from_block = jnp.where(
         in_top[:, None], src_above[None, :], jnp.where(in_bottom[:, None], src_below[None, :], my_sources[None, :])
     )
-    recv_index = (from_block * wide_count + chunk_plane[:, None]).reshape(-1)
-    camera_ext = jnp.take(arrived, recv_index, axis=0, mode="clip")
-    camera_ext = camera_ext.reshape(wide_count, block_count, block_rows, lane_count)
+    inverse = jnp.sum(
+        jnp.where(from_block[:, :, None] == slot_ids[None, None, :], slot_ids[None, :, None], 0), axis=1
+    )
+    arrived = arrived.reshape(block_count, wide_count, block_rows, lane_count)
     wide_planes = plane_start - wide + jnp.arange(wide_count, dtype=jnp.int32)
     wide_inside = (wide_planes >= 0) & (wide_planes < total_planes)
-    camera_ext = camera_ext.reshape(wide_count, row_count, lane_count)
     band_pad = jnp.pad(band_all, wide, mode="edge")
     band_wide = lax.dynamic_slice_in_dim(band_pad, plane_start, wide_count)
     band_ids = jnp.arange(kernels.shape[0], dtype=jnp.int32)
@@ -108,7 +108,17 @@
     tables = jnp.sum(jnp.where(in_band[:, None, None, :], kernels[:, :, :, None], 0.0), axis=0)
     x_wide = tables[2]
     y_wide = tables[1]
-    lateral_ext = lateral_fwd(camera_ext, x_wide, y_wide)
+    padded = jnp.pad(arrived, [(0, 0), (0, 0), (0, 0), (reach, reach)])
+    lanes_done = jnp.zeros(arrived.shape, jnp.float32)
+    for tap in range(2 * reach + 1):
+        lanes_done = lanes_done + x_wide[tap][None, :, None, None] * padded[..., tap : tap + lane_count]
+    row_ids = jnp.arange(block_rows, dtype=jnp.int32)
+    in_rows = inverse[:, :, None] * block_rows + row_ids[None, None, :]
+    offset = in_rows[:, None, :, :] - jnp.arange(row_count, dtype=jnp.int32)[None, :, None, None]
+    mix = jnp.zeros((wide_count, row_count, block_count, block_rows), jnp.float32)
+    for tap in range(2 * reach + 1):
+        mix = mix + jnp.where(offset == tap - reach, y_wide[tap][:, None, None, None], 0.0)
+    lateral_ext = jnp.einsum("prsk,spkx->prx", mix, lanes_done, precision=lax.Precision.HIGHEST)
     ext_count = plane_count + 2 * reach
     ext_planes = plane_start - reach + jnp.arange(ext_count, dtype=jnp.int32)
     ext_inside = (ext_planes >= 0) & (ext_planes < total_planes)

time: 69.7 us -> 70 us (level)
  matrix products: 1.2 us -> 6.27 us
  other arithmetic: 9.17 us -> 5.28 us
  local copies, waits for them, and re-layouts: 8.08 us -> 7.38 us
    dot_general x0 -> x1, matrix products: none -> 5.06 us  [body(): jnp.einsum('prsk,spkx->prx', mix, lanes_done, precision=lax.Precision.HIG...]
    add x3 -> x1, other arithmetic: 4.03 us -> 0.1 us  [body(): in_rows = inverse[:, :, None] * block_rows + row_ids[None, None, :]]
    gather x1 -> x0, local copies, waits for them, and re-layouts: 0.76 us -> none  [body(): camera_ext = jnp.take(arrived, recv_index, axis=0, mode='clip')]
  transfers between devices with their start and end apart: 4 -> 4, of which waited for: 2 -> 2; matrix products, arithmetic and copies ran while one was open for 12% -> 13% of each run, Pallas kernels for 0% -> 0%
where the time goes in v20:
time: 70 us; the launch traced here: 69.6 us
  waiting for transfers between devices  20.9 us (30%)
  blocking collectives  15.7 us (22%)
  starting transfers between devices  13.8 us (20%)
  local copies, waits for them, and re-layouts  7.38 us (11%)
  matrix products  6.27 us (9%)
  other arithmetic  5.28 us (8%)
    all_gather x1, blocking collectives, body(): log_joined = lax.all_gather(log_total, 'view', axis=0, tiled=True)  15.7 us
    all_to_all x1, waiting for transfers between devices, body(): arrived_logs = lax.all_to_all(outgoing, ('view', 'dom'), 0, 0, tiled=True)  13.8 us
    all_to_all x1, waiting for transfers between devices, body(): lax.all_to_all(outgoing, 'dom', split_axis=0, concat_axis=0, tiled=True)  7.16 us
    all_to_all x1, starting transfers between devices, body(): arrived_logs = lax.all_to_all(outgoing, ('view', 'dom'), 0, 0, tiled=True)  5.75 us
    dot_general x1, matrix products, body(): jnp.einsum('prsk,spkx->prx', mix, lanes_done, precision=lax.Precision.HIG...  5.06 us
    all_to_all x1, starting transfers between devices, body(): lax.all_to_all(outgoing, 'dom', split_axis=0, concat_axis=0, tiled=True)  4.37 us
    gather x1, local copies, waits for them, and re-layouts, body(): outgoing = jnp.take(flat_blocks, send_index, axis=0, mode='clip')  2.66 us
    ppermute x1, starting transfers between devices, extended_2(): before = lax.ppermute(last, axis, up)  2.42 us
  transfers between devices with their start and end apart: 4, of which 2 were waited for; matrix products, arithmetic and copies ran while one was open for 13% of the time, Pallas kernels for 0%

profile of v20, /device:TPU:0, one launch (start us, length us, event | category | flops | bytes accessed | tf_op | source)
XLA Modules:
  0.0 69.6 jit_solution(4864996820822223189)
XLA Ops:
  0.0 0.8 %select_reduce_fusion.4 = s32[16]{0:T(128)S(1)} fusion(s32[4,16]{1,0:T(4,128)} %param.8, pred[4]{0:T(512)(128)(4,1)S(1)} %iota_compare_fusion.6), kind=kLoop, calls=%fused_computation.245 | loop fusion | flops 112 | bytes 324 | tf_op jit(solution)/shard_map/reduce_sum | solution.py:55
  0.8 0.1 fusion.199
  0.9 0.1 slice_bitcast_fusion.63
  0.9 0.1 stack_reshape.3
  1.0 0.1 slice.507
  1.1 0.1 slice.509
  1.2 0.2 fusion.177
  1.4 0.1 select_add_fusion
  1.4 0.1 reshape.576
  1.5 2.7 %gather_fusion = f32[128,8,256]{2,1,0:T(8,128)} fusion(f32[64,8,256]{2,1,0:T(8,128)} %bitcast.175, s32[1024]{0:T(1024)S(1)} %pad_clamp_fusion.1), kind=kCustom, calls=%fused_computation | custom fusion | bytes 2097664 | tf_op jit(solution)/shard_map/jit(_take)/gather | solution.py:89
  4.2 4.4 %all-to-all-start = ((f32[128,8,256]{2,1,0:T(8,128)}), f32[128,8,256]{2,1,0:T(8,128)S(1)}, u32[]{:S(2)}, u32[]{:S(2)}) async-start(f32[128,8,256]{2,1,0:T(8,128)} %gather_fusion), calls=%async_computation | async-start | bytes 2097152 | tf_op jit(solution)/shard_map/all_to_all | solution.py:91
  8.6 2.4 %collective-permute-start = (f32[4,32,256]{2,1,0:T(8,128)S(1)}, f32[4,32,256]{2,1,0:T(8,128)S(1)}, u32[]{:S(2)}, u32[]{:S(2)}) collective-permute-start(f32[4,32,256]{2,1,0:T(8,128)S(1)} %get-tuple-element.5), channel_id=1, source_target_pairs={{0,4},{4,8},{8,12},{1,5},{5,9},{9,13},{2,6},{6,10},{10,14},{3,7},{... | collective-permute-start | bytes 393224 | tf_op jit(solution)/shard_map/ppermute | solution.py:19
  11.0 1.3 %collective-permute-start.1 = (f32[4,32,256]{2,1,0:T(8,128)S(1)}, f32[4,32,256]{2,1,0:T(8,128)S(1)}, u32[]{:S(2)}, u32[]{:S(2)}) collective-permute-start(f32[4,32,256]{2,1,0:T(8,128)S(1)} %get-tuple-element.6), channel_id=1, source_target_pairs={{4,0},{8,4},{12,8},{5,1},{9,5},{13,9},{6,2},{10,6},{14,10},{7,3},{... | collective-permute-start | bytes 393224 | tf_op jit(solution)/shard_map/ppermute | solution.py:20
  12.3 0.1 reshape.567
  12.4 0.7 fusion.198
  13.1 0.6 reshape.565
  13.7 0.7 reshape.566
  14.4 0.1 pad_add_fusion.1
  14.5 0.1 dynamic_slice.13
  14.6 0.1 copy.18
  14.7 0.1 select_reduce_fusion
  14.9 0.1 select_reduce_fusion.3
  15.0 0.1 select_select_fusion
  15.1 0.1 copy.19
  15.2 0.1 iota_add_fusion.1
  15.3 0.1 add.304
  15.3 0.1 slice_bitcast_fusion.58
  15.4 0.1 slice_select_fusion.8
  15.5 0.1 slice_bitcast_fusion.48
  15.6 0.1 fusion.170
  15.7 0.1 iota_add_fusion
  15.8 7.2 %all-to-all-done = f32[128,8,256]{2,1,0:T(8,128)S(1)} async-done(((f32[128,8,256]{2,1,0:T(8,128)}), f32[128,8,256]{2,1,0:T(8,128)S(1)}, u32[]{:S(2)}, u32[]{:S(2)}) %all-to-all-start) | async-done | bytes 1048608 | tf_op jit(solution)/shard_map/all_to_all | solution.py:91
  23.0 5.1 %convolution_bitcast_fusion = f32[32,32,256]{2,1,0:T(8,128)S(1)} fusion(f32[32]{0:T(128)S(1)} %get-tuple-element.20, f32[32]{0:T(128)S(1)} %get-tuple-element.21, f32[32]{0:T(128)S(1)} %get-tuple-element.22, f32[32]{0:T(128)S(1)} %get-tuple-element.23, f32[32]{0:T(128)S(1)} %get-tuple-element.24, f32[32]{0:T(128)S(1)} %get-tuple-element.25, ...), kind=kOutput, calls=%fused_computation.18 | convolution fusion | flops 106004480 | bytes 2103552 | tf_op jit(solution)/shard_map/prsk,spkx->prx/dot_general | solution.py:121
  28.1 0.9 %fusion.19 = f32[24,32,256]{2,1,0:T(8,128)S(1)} fusion(f32[32,32,256]{2,1,0:T(8,128)S(1)} %convolution_bitcast_fusion, f32[4,32,256]{2,1,0:T(8,128)S(1)} %collective-permute-done.1, f32[16,32,256]{2,1,0:T(8,128)S(1)} %bitcast.177, f32[4,32,256]{2,1,0:T(8,128)S(1)} %collective-permute-done, f32[24]{0:T(128)S(1)} %get-tuple-element.29, ...), kind=kLoop, calls=%fused_computation.39 | loop fusion | flops 4128768 | bytes 8651640 | tf_op jit(solution)/shard_map/jit(_where)/select_n | solution.py:131
  29.0 1.2 %fusion.45 = f32[16,32,256]{2,1,0:T(8,128)S(1)} fusion(f32[24,32,256]{2,1,0:T(8,128)S(1)} %fusion.19, f32[16]{0:T(128)S(1)} %get-tuple-element.56, f32[16]{0:T(128)S(1)} %get-tuple-element.57, f32[16]{0:T(128)S(1)} %get-tuple-element.58, f32[16]{0:T(128)S(1)} %get-tuple-element.59, f32[16]{0:T(128)S(1)} %get-tuple-element.60, f32[16]{0:T(128)S(1)} %get-tuple-element.61, ...), kind=kOutput, calls=%fused_computation.74 | convolution fusion | flops 52838400 | bytes 5288960 | tf_op jit(solution)/shard_map/pri,pix->prx/dot_general | solution.py:146
  30.2 1.3 %fusion.36 = f32[16,32,256]{2,1,0:T(8,128)S(1)} fusion(f32[16,32,256]{2,1,0:T(8,128)S(1)} %fusion.45, f32[16]{0:T(128)S(1)} %get-tuple-element.38, f32[16]{0:T(128)S(1)} %get-tuple-element.39, f32[16]{0:T(128)S(1)} %get-tuple-element.40, f32[16]{0:T(128)S(1)} %get-tuple-element.41, f32[16]{0:T(128)S(1)} %get-tuple-element.42, f32[16]{0:T(128)S(1)} %get-tuple-element.43, ...), kind=kLoop, calls=%fused_computation.64 | loop fusion | flops 2228224 | bytes 1049152 | tf_op jit(solution)/shard_map/log | solution.py:149
  31.5 0.0 copy-start.2
  31.5 0.8 %copy.21 = f32[4,4,4,8,256]{4,3,1,2,0:T(8,128)} copy(f32[4,4,4,8,256]{4,3,2,1,0:T(8,128)S(1)} %bitcast.176) | data formatting | bytes 1048576 | tf_op jit(solution)/shard_map/reshape | solution.py:149
  32.4 5.7 %all-to-all-start.1 = ((f32[16,4,8,256]{3,2,1,0:T(8,128)}), f32[16,4,8,256]{3,2,1,0:T(8,128)S(1)}, u32[]{:S(2)}, u32[]{:S(2)}) async-start(f32[16,4,8,256]{3,2,1,0:T(8,128)} %bitcast.80), calls=%async_computation.1 | async-start | bytes 1048576 | tf_op jit(solution)/shard_map/all_to_all | solution.py:151
  38.1 0.1 reshape.572
  38.2 0.2 fusion.173
  38.4 0.1 select_reduce_fusion.1
  38.5 0.1 broadcast_add_fusion
  38.5 0.1 reshape.584
  38.6 13.8 %all-to-all-done.1 = f32[16,4,8,256]{3,2,1,0:T(8,128)S(1)} async-done(((f32[16,4,8,256]{3,2,1,0:T(8,128)}), f32[16,4,8,256]{3,2,1,0:T(8,128)S(1)}, u32[]{:S(2)}, u32[]{:S(2)}) %all-to-all-start.1) | async-done | bytes 524320 | tf_op jit(solution)/shard_map/all_to_all | solution.py:151
  52.4 0.6 gather_fusion.1
  53.0 15.7 %all_gather.3 = f32[16,32,256]{2,1,0:T(8,128)S(1)} all-gather(f32[4,32,256]{2,1,0:T(8,128)S(1)} %copy_bitcast_fusion), channel_id=1, replica_groups=mesh['tile'=2,'dom'=4,'view'=4] {'view'}, dimensions={0}, use_global_device_ids=true | all-gather | bytes 655360 | tf_op jit(solution)/shard_map/all_gather | solution.py:166
  68.7 0.9 %exponential_multiply_fusion = f32[16,32,256]{2,1,0:T(8,128)} fusion(f32[16,32,256]{2,1,0:T(8,128)S(1)} %copy-done, f32[16,32,256]{2,1,0:T(8,128)S(1)} %all_gather.3), kind=kLoop, calls=%fused_computation.90 | loop fusion | flops 262144 | bytes 1572864 | tf_op jit(solution)/shard_map/mul | solution.py:167
  (31 shorter events, 0.2 us)
Async XLA Ops:
  4.2 4.4 %copy-start.1 = (f32[1,16,32,256]{3,2,1,0:T(8,128)S(1)}, f32[1,16,32,256]{3,2,1,0:T(8,128)}, u32[]{:S(2)}) copy-start(f32[1,16,32,256]{3,2,1,0:T(8,128)} %param.6) | copy-start | bytes 1572868
  4.2 8.2 %copy-start.4 = (s32[1,64]{1,0:T(1,128)S(1)}, s32[1,64]{1,0:T(1,128)}, u32[]{:S(2)}) copy-start(s32[1,64]{1,0:T(1,128)} %param.9) | copy-start | bytes 772
  4.2 10.4 %copy-start.3 = (f32[1,4,3,9]{3,1,2,0:T(4,128)S(1)}, f32[1,4,3,9]{3,1,2,0:T(4,128)}, u32[]{:S(2)}) copy-start(f32[1,4,3,9]{3,1,2,0:T(4,128)} %param.7) | copy-start | bytes 1300
  4.2 18.8 %all-to-all-start = ((f32[128,8,256]{2,1,0:T(8,128)}), f32[128,8,256]{2,1,0:T(8,128)S(1)}, u32[]{:S(2)}, u32[]{:S(2)}) async-start(f32[128,8,256]{2,1,0:T(8,128)} %gather_fusion), calls=%async_computation | async-start | bytes 2097152 | tf_op jit(solution)/shard_map/all_to_all | solution.py:91
  8.6 19.5 %collective-permute-start = (f32[4,32,256]{2,1,0:T(8,128)S(1)}, f32[4,32,256]{2,1,0:T(8,128)S(1)}, u32[]{:S(2)}, u32[]{:S(2)}) collective-permute-start(f32[4,32,256]{2,1,0:T(8,128)S(1)} %get-tuple-element.5), channel_id=1, source_target_pairs={{0,4},{4,8},{8,12},{1,5},{5,9},{9,13},{2,6},{6,10},{10,14},{3,7},{... | collective-permute-start | bytes 393224 | tf_op jit(solution)/shard_map/ppermute | solution.py:19
  11.0 17.1 %collective-permute-start.1 = (f32[4,32,256]{2,1,0:T(8,128)S(1)}, f32[4,32,256]{2,1,0:T(8,128)S(1)}, u32[]{:S(2)}, u32[]{:S(2)}) collective-permute-start(f32[4,32,256]{2,1,0:T(8,128)S(1)} %get-tuple-element.6), channel_id=1, source_target_pairs={{4,0},{8,4},{12,8},{5,1},{9,5},{13,9},{6,2},{10,6},{14,10},{7,3},{... | collective-permute-start | bytes 393224 | tf_op jit(solution)/shard_map/ppermute | solution.py:20
  31.5 6.6 %copy-start.2 = (s32[4,16]{1,0:T(4,128)S(1)}, s32[4,16]{1,0:T(4,128)}, u32[]{:S(2)}) copy-start(s32[4,16]{1,0:T(4,128)} %param.8) | copy-start | bytes 772
  32.4 20.0 %all-to-all-start.1 = ((f32[16,4,8,256]{3,2,1,0:T(8,128)}), f32[16,4,8,256]{3,2,1,0:T(8,128)S(1)}, u32[]{:S(2)}, u32[]{:S(2)}) async-start(f32[16,4,8,256]{3,2,1,0:T(8,128)} %bitcast.80), calls=%async_computation.1 | async-start | bytes 1048576 | tf_op jit(solution)/shard_map/all_to_all | solution.py:151
  38.6 30.1 %copy-start = (f32[16,32,256]{2,1,0:T(8,128)S(1)}, f32[16,32,256]{2,1,0:T(8,128)}, u32[]{:S(2)}) copy-start(f32[16,32,256]{2,1,0:T(8,128)} %param.5) | copy-start | bytes 1572868

commit v21 on v17

--- a/solution.py
+++ b/solution.py
@@ -134,10 +134,15 @@
     for tap in range(2 * reach + 1):
         mix = mix + jnp.where((offset == tap - reach)[None], y_own[tap][:, None, None], 0.0)
     by_source = jnp.einsum("pri,pix->prx", mix, zback, precision=lax.Precision.HIGHEST)
-    back = taps_along(by_source, x_own, 2, True)
     piece_planes = plane_count // view_count
-    logs = jnp.log(back).reshape(view_count, piece_planes, block_count, block_rows, lane_count)
-    outgoing = logs.transpose(0, 2, 1, 3, 4).reshape(view_count * block_count, piece_planes, block_rows, lane_count)
+    by_source = by_source.reshape(view_count, piece_planes, block_count, block_rows, lane_count)
+    by_source = by_source.transpose(0, 2, 1, 3, 4)
+    padded = jnp.pad(by_source, [(0, 0)] * 4 + [(reach, reach)])
+    back = jnp.zeros(by_source.shape, jnp.float32)
+    for tap in range(2 * reach + 1):
+        weight = x_own[tap].reshape(view_count, 1, piece_planes, 1, 1)
+        back = back + weight * padded[..., 2 * reach - tap : 2 * reach - tap + lane_count]
+    outgoing = jnp.log(back).reshape(view_count * block_count, piece_planes, block_rows, lane_count)
     arrived_logs = lax.all_to_all(outgoing, ("view", "dom"), 0, 0, tiled=True)
     all_grid = src_map.reshape(view_count, block_count, block_count)
     all_dev = all_grid // block_count

time: 69.7 us -> 69.7 us (level)
  waiting for transfers between devices: 21.1 us -> 20.2 us
  other arithmetic: 9.17 us -> 9.93 us
    all_to_all x1, waiting for transfers between devices: 7.33 us -> 6.47 us  [body(): lax.all_to_all(outgoing, 'dom', split_axis=0, concat_axis=0, tiled=True)]
    reshape x1, local copies, waits for them, and re-layouts: 0.85 us -> 0.05 us  [body(): by_source.reshape(view_count, piece_planes, block_count, block_rows, lane...]
    log x1, other arithmetic: 1.34 us -> 2.11 us  [body(): jnp.log(back)]
    mul x0 -> x9, local copies, waits for them, and re-layouts: none -> 0.74 us  [body(): weight * padded[..., 2 * reach - tap:2 * reach - tap + lane_count]]
  transfers between devices with their start and end apart: 4 -> 4, of which waited for: 2 -> 2; matrix products, arithmetic and copies ran while one was open for 12% -> 13% of each run, Pallas kernels for 0% -> 0%
where the time goes in v21:
time: 69.7 us; the launch traced here: 69.3 us
  waiting for transfers between devices  20.2 us (29%)
  blocking collectives  15.7 us (23%)
  starting transfers between devices  13.8 us (20%)
  other arithmetic  9.93 us (14%)
  local copies, waits for them, and re-layouts  8.16 us (12%)
  matrix products  1.21 us (2%)
    all_gather x1, blocking collectives, body(): log_joined = lax.all_gather(log_total, 'view', axis=0, tiled=True)  15.7 us
    all_to_all x1, waiting for transfers between devices, body(): arrived_logs = lax.all_to_all(outgoing, ('view', 'dom'), 0, 0, tiled=True)  13.8 us
    all_to_all x1, waiting for transfers between devices, body(): lax.all_to_all(outgoing, 'dom', split_axis=0, concat_axis=0, tiled=True)  6.47 us
    all_to_all x1, starting transfers between devices, body(): arrived_logs = lax.all_to_all(outgoing, ('view', 'dom'), 0, 0, tiled=True)  5.74 us
    all_to_all x1, starting transfers between devices, body(): lax.all_to_all(outgoing, 'dom', split_axis=0, concat_axis=0, tiled=True)  4.37 us
    add x2, other arithmetic, taps_along(): total = total + taps[offset][:, None, None] * piece  3.95 us
    gather x1, local copies, waits for them, and re-layouts, body(): outgoing = jnp.take(flat_blocks, send_index, axis=0, mode='clip')  2.68 us
    ppermute x1, starting transfers between devices, extended_2(): before = lax.ppermute(last, axis, up)  2.42 us
  transfers between devices with their start and end apart: 4, of which 2 were waited for; matrix products, arithmetic and copies ran while one was open for 13% of the time, Pallas kernels for 0%

profile of v21, /device:TPU:0, one launch (start us, length us, event | category | flops | bytes accessed | tf_op | source)
XLA Modules:
  0.0 69.3 jit_solution(6469087917205547116)
XLA Ops:
  0.0 0.8 %select_reduce_fusion.3 = s32[16]{0:T(128)S(1)} fusion(s32[4,16]{1,0:T(4,128)} %param.8, pred[4]{0:T(512)(128)(4,1)S(1)} %iota_compare_fusion.5), kind=kLoop, calls=%fused_computation.220 | loop fusion | flops 112 | bytes 324 | tf_op jit(solution)/shard_map/reduce_sum | solution.py:55
  0.9 0.1 stack_reshape.3
  1.0 0.1 slice.524
  1.1 0.1 slice.526
  1.2 0.2 fusion.137
  1.4 0.1 reshape.569
  1.5 2.7 %gather_fusion = f32[128,8,256]{2,1,0:T(8,128)} fusion(f32[64,8,256]{2,1,0:T(8,128)} %bitcast.155, s32[1024]{0:T(1024)S(1)} %pad_clamp_fusion.2), kind=kCustom, calls=%fused_computation | custom fusion | bytes 2097664 | tf_op jit(solution)/shard_map/jit(_take)/gather | solution.py:89
  4.2 4.4 %all-to-all-start = ((f32[128,8,256]{2,1,0:T(8,128)}), f32[128,8,256]{2,1,0:T(8,128)S(1)}, u32[]{:S(2)}, u32[]{:S(2)}) async-start(f32[128,8,256]{2,1,0:T(8,128)} %gather_fusion), calls=%async_computation | async-start | bytes 2097152 | tf_op jit(solution)/shard_map/all_to_all | solution.py:91
  8.6 2.4 %collective-permute-start = (f32[4,32,256]{2,1,0:T(8,128)S(1)}, f32[4,32,256]{2,1,0:T(8,128)S(1)}, u32[]{:S(2)}, u32[]{:S(2)}) collective-permute-start(f32[4,32,256]{2,1,0:T(8,128)S(1)} %get-tuple-element.14), channel_id=1, source_target_pairs={{0,4},{4,8},{8,12},{1,5},{5,9},{9,13},{2,6},{6,10},{10,14},{3,7},{... | collective-permute-start | bytes 393224 | tf_op jit(solution)/shard_map/ppermute | solution.py:19
  11.0 1.3 %collective-permute-start.1 = (f32[4,32,256]{2,1,0:T(8,128)S(1)}, f32[4,32,256]{2,1,0:T(8,128)S(1)}, u32[]{:S(2)}, u32[]{:S(2)}) collective-permute-start(f32[4,32,256]{2,1,0:T(8,128)S(1)} %get-tuple-element.15), channel_id=1, source_target_pairs={{4,0},{8,4},{12,8},{5,1},{9,5},{13,9},{6,2},{10,6},{14,10},{7,3},{... | collective-permute-start | bytes 393224 | tf_op jit(solution)/shard_map/ppermute | solution.py:20
  12.3 0.1 reshape.561
  12.5 0.1 select_reduce_fusion.2
  12.7 0.1 reshape.577
  12.8 0.7 fusion.148
  13.4 0.6 reshape.559
  14.1 0.7 reshape.560
  15.0 0.1 copy.15
  15.1 0.1 select_reduce_fusion
  15.3 0.1 add.307
  15.4 0.1 slice_reduce_fusion.8
  15.5 0.1 mul.480
  15.6 0.1 mul.587
  15.7 0.1 mul.590
  15.7 0.1 mul.593
  15.8 0.1 mul.596
  15.9 0.1 slice_select_fusion.8
  16.0 0.1 mul.599
  16.1 0.1 mul.602
  16.2 0.1 mul.605
  16.3 0.1 mul.608
  16.4 0.1 slice_bitcast_fusion.40
  16.4 0.1 fusion.130
  16.6 6.5 %all-to-all-done = f32[128,8,256]{2,1,0:T(8,128)S(1)} async-done(((f32[128,8,256]{2,1,0:T(8,128)}), f32[128,8,256]{2,1,0:T(8,128)S(1)}, u32[]{:S(2)}, u32[]{:S(2)}) %all-to-all-start) | async-done | bytes 1048608 | tf_op jit(solution)/shard_map/all_to_all | solution.py:91
  23.0 0.8 %gather_fusion.1 = f32[128,8,256]{2,1,0:T(8,128)S(1)} fusion(f32[128,8,256]{2,1,0:T(8,128)S(1)} %all-to-all-done, s32[1024]{0:T(1024)S(1)} %pad_clamp_fusion.1), kind=kCustom, calls=%fused_computation.1 | custom fusion | bytes 2097664 | tf_op jit(solution)/shard_map/jit(_take)/gather | solution.py:99
  23.8 2.7 %fusion.24 = f32[32,32,256]{2,1,0:T(8,128)S(1)} fusion(f32[32,32,256]{2,1,0:T(8,128)S(1)} %bitcast.156, f32[32]{0:T(128)S(1)} %get-tuple-element.28, f32[32]{0:T(128)S(1)} %get-tuple-element.29, f32[32]{0:T(128)S(1)} %get-tuple-element.30, f32[32]{0:T(128)S(1)} %get-tuple-element.31, f32[32]{0:T(128)S(1)} %get-tuple-element.32, f32[32]{0:T(128)S(1)} %get-tuple-element.33, ...), kind=kLoop, calls=%fused_computation.51 | loop fusion | flops 4456448 | bytes 2098304 | tf_op jit(solution)/shard_map/add | solution.py:36
  26.5 1.3 %fusion.8 = f32[32,32,256]{2,1,0:T(8,128)S(1)} fusion(f32[32,32,256]{2,1,0:T(8,128)S(1)} %fusion.24, f32[32]{0:T(128)S(1)} %get-tuple-element.20, f32[32]{0:T(128)S(1)} %get-tuple-element.21, f32[32]{0:T(128)S(1)} %get-tuple-element.22, f32[32]{0:T(128)S(1)} %get-tuple-element.23, f32[32]{0:T(128)S(1)} %get-tuple-element.24, f32[32]{0:T(128)S(1)} %get-tuple-element.25, ...), kind=kLoop, calls=%fused_computation.35 | loop fusion | flops 4456448 | bytes 2098304 | tf_op jit(solution)/shard_map/add | solution.py:36
  27.8 0.9 %fusion.34 = f32[24,32,256]{2,1,0:T(8,128)S(1)} fusion(f32[32,32,256]{2,1,0:T(8,128)S(1)} %fusion.8, f32[4,32,256]{2,1,0:T(8,128)S(1)} %collective-permute-done.1, f32[16,32,256]{2,1,0:T(8,128)S(1)} %bitcast.158, f32[4,32,256]{2,1,0:T(8,128)S(1)} %collective-permute-done, f32[24]{0:T(128)S(1)} %get-tuple-element.38, f32[24]{0:T(128)S(1)} %get-tuple-element.39, ...), kind=kLoop, calls=%fused_computation.62 | loop fusion | flops 4128768 | bytes 8651640 | tf_op jit(solution)/shard_map/jit(_where)/select_n | solution.py:121
  28.7 1.2 %fusion.60 = f32[16,32,256]{2,1,0:T(8,128)S(1)} fusion(f32[24,32,256]{2,1,0:T(8,128)S(1)} %fusion.34, f32[16]{0:T(128)S(1)} %get-tuple-element.56, f32[16]{0:T(128)S(1)} %get-tuple-element.57, f32[16]{0:T(128)S(1)} %get-tuple-element.58, f32[16]{0:T(128)S(1)} %get-tuple-element.59, f32[16]{0:T(128)S(1)} %get-tuple-element.60, f32[16]{0:T(128)S(1)} %get-tuple-element.61, ...), kind=kOutput, calls=%fused_computation.97 | convolution fusion | flops 52838400 | bytes 5288960 | tf_op jit(solution)/shard_map/pri,pix->prx/dot_general | solution.py:136
  30.0 2.1 %fusion.51 = f32[4,4,4,8,256]{4,3,2,1,0:T(8,128)} fusion(f32[4,4,4,8,256]{4,3,2,1,0:T(8,128)S(1)} %bitcast.157, f32[4,4]{1,0:T(4,128)S(1)} %mul.608, f32[4,4]{1,0:T(4,128)S(1)} %mul.605, f32[4,4]{1,0:T(4,128)S(1)} %mul.602, f32[4,4]{1,0:T(4,128)S(1)} %mul.599, f32[4,4]{1,0:T(4,128)S(1)} %mul.596, f32[4,4]{1,0:T(4,128)S(1)} %mul.593, f32[4,4]{1,0:T(4,128)S(1)} %mul.590, ...), kind=kLoop, calls=%fused_computation.87 | loop fusion | flops 2228224 | bytes 1049152 | tf_op jit(solution)/shard_map/log | solution.py:145
  32.1 5.7 %all-to-all-start.1 = ((f32[16,4,8,256]{3,2,1,0:T(8,128)}), f32[16,4,8,256]{3,2,1,0:T(8,128)S(1)}, u32[]{:S(2)}, u32[]{:S(2)}) async-start(f32[16,4,8,256]{3,2,1,0:T(8,128)} %bitcast.69), calls=%async_computation.1 | async-start | bytes 1048576 | tf_op jit(solution)/shard_map/all_to_all | solution.py:146
  37.8 0.1 reshape.565
  37.9 0.2 fusion.133
  38.1 0.1 select_reduce_fusion.1
  38.2 0.1 reshape.585
  38.3 13.8 %all-to-all-done.1 = f32[16,4,8,256]{3,2,1,0:T(8,128)S(1)} async-done(((f32[16,4,8,256]{3,2,1,0:T(8,128)}), f32[16,4,8,256]{3,2,1,0:T(8,128)S(1)}, u32[]{:S(2)}, u32[]{:S(2)}) %all-to-all-start.1) | async-done | bytes 524320 | tf_op jit(solution)/shard_map/all_to_all | solution.py:146
  52.1 0.6 gather_fusion.2
  52.7 15.7 %all_gather.3 = f32[16,32,256]{2,1,0:T(8,128)S(1)} all-gather(f32[4,32,256]{2,1,0:T(8,128)S(1)} %copy_bitcast_fusion.1), channel_id=1, replica_groups=mesh['tile'=2,'dom'=4,'view'=4] {'view'}, dimensions={0}, use_global_device_ids=true | all-gather | bytes 655360 | tf_op jit(solution)/shard_map/all_gather | solution.py:161
  68.4 0.9 %exponential_multiply_fusion = f32[16,32,256]{2,1,0:T(8,128)} fusion(f32[16,32,256]{2,1,0:T(8,128)S(1)} %copy-done, f32[16,32,256]{2,1,0:T(8,128)S(1)} %all_gather.3), kind=kLoop, calls=%fused_computation.114 | loop fusion | flops 262144 | bytes 1572864 | tf_op jit(solution)/shard_map/mul | solution.py:162
  (40 shorter events, 0.8 us)
Async XLA Ops:
  4.2 4.4 %copy-start.1 = (f32[1,16,32,256]{3,2,1,0:T(8,128)S(1)}, f32[1,16,32,256]{3,2,1,0:T(8,128)}, u32[]{:S(2)}) copy-start(f32[1,16,32,256]{3,2,1,0:T(8,128)} %param.6) | copy-start | bytes 1572868
  4.2 8.6 %copy-start.4 = (s32[1,64]{1,0:T(1,128)S(1)}, s32[1,64]{1,0:T(1,128)}, u32[]{:S(2)}) copy-start(s32[1,64]{1,0:T(1,128)} %param.9) | copy-start | bytes 772
  4.2 10.7 %copy-start.3 = (f32[1,4,3,9]{3,1,2,0:T(4,128)S(1)}, f32[1,4,3,9]{3,1,2,0:T(4,128)}, u32[]{:S(2)}) copy-start(f32[1,4,3,9]{3,1,2,0:T(4,128)} %param.7) | copy-start | bytes 1300
  4.2 18.8 %all-to-all-start = ((f32[128,8,256]{2,1,0:T(8,128)}), f32[128,8,256]{2,1,0:T(8,128)S(1)}, u32[]{:S(2)}, u32[]{:S(2)}) async-start(f32[128,8,256]{2,1,0:T(8,128)} %gather_fusion), calls=%async_computation | async-start | bytes 2097152 | tf_op jit(solution)/shard_map/all_to_all | solution.py:91
  8.6 19.1 %collective-permute-start = (f32[4,32,256]{2,1,0:T(8,128)S(1)}, f32[4,32,256]{2,1,0:T(8,128)S(1)}, u32[]{:S(2)}, u32[]{:S(2)}) collective-permute-start(f32[4,32,256]{2,1,0:T(8,128)S(1)} %get-tuple-element.14), channel_id=1, source_target_pairs={{0,4},{4,8},{8,12},{1,5},{5,9},{9,13},{2,6},{6,10},{10,14},{3,7},{... | collective-permute-start | bytes 393224 | tf_op jit(solution)/shard_map/ppermute | solution.py:19
  11.0 16.7 %collective-permute-start.1 = (f32[4,32,256]{2,1,0:T(8,128)S(1)}, f32[4,32,256]{2,1,0:T(8,128)S(1)}, u32[]{:S(2)}, u32[]{:S(2)}) collective-permute-start(f32[4,32,256]{2,1,0:T(8,128)S(1)} %get-tuple-element.15), channel_id=1, source_target_pairs={{4,0},{8,4},{12,8},{5,1},{9,5},{13,9},{6,2},{10,6},{14,10},{7,3},{... | collective-permute-start | bytes 393224 | tf_op jit(solution)/shard_map/ppermute | solution.py:20
  30.0 7.9 %copy-start.2 = (s32[4,16]{1,0:T(4,128)S(1)}, s32[4,16]{1,0:T(4,128)}, u32[]{:S(2)}) copy-start(s32[4,16]{1,0:T(4,128)} %param.8) | copy-start | bytes 772
  32.1 20.0 %all-to-all-start.1 = ((f32[16,4,8,256]{3,2,1,0:T(8,128)}), f32[16,4,8,256]{3,2,1,0:T(8,128)S(1)}, u32[]{:S(2)}, u32[]{:S(2)}) async-start(f32[16,4,8,256]{3,2,1,0:T(8,128)} %bitcast.69), calls=%async_computation.1 | async-start | bytes 1048576 | tf_op jit(solution)/shard_map/all_to_all | solution.py:146
  38.3 30.1 %copy-start = (f32[16,32,256]{2,1,0:T(8,128)S(1)}, f32[16,32,256]{2,1,0:T(8,128)}, u32[]{:S(2)}) copy-start(f32[16,32,256]{2,1,0:T(8,128)} %param.5) | copy-start | bytes 1572868

commit v22 on v17

--- a/solution.py
+++ b/solution.py
@@ -153,8 +153,8 @@
     for v in range(1, view_count):
         log_total = log_total + by_view[v]
     log_total = log_total.transpose(1, 0, 2, 3).reshape(piece_planes, row_count, lane_count)
-    log_joined = lax.all_gather(log_total, "view", axis=0, tiled=True)
-    return estimate * jnp.exp(log_joined / view_count)
+    scale_joined = lax.all_gather(jnp.exp(log_total / view_count), "view", axis=0, tiled=True)
+    return estimate * scale_joined
 
 
 def solution(mesh):

time: 69.7 us -> 69.7 us (level)
  no operation moved by 1% of the time
where the time goes in v22:
time: 69.7 us; the launch traced here: 69.3 us
  waiting for transfers between devices  21.1 us (30%)
  blocking collectives  15.7 us (23%)
  starting transfers between devices  13.8 us (20%)
  other arithmetic  9.17 us (13%)
  local copies, waits for them, and re-layouts  8.08 us (12%)
  matrix products  1.2 us (2%)
    all_gather x1, blocking collectives, body(): lax.all_gather(jnp.exp(log_total / view_count), 'view', axis=0, tiled=True)  15.7 us
    all_to_all x1, waiting for transfers between devices, body(): arrived_logs = lax.all_to_all(outgoing, ('view', 'dom'), 0, 0, tiled=True)  13.8 us
    all_to_all x1, waiting for transfers between devices, body(): lax.all_to_all(outgoing, 'dom', split_axis=0, concat_axis=0, tiled=True)  7.33 us
    all_to_all x1, starting transfers between devices, body(): arrived_logs = lax.all_to_all(outgoing, ('view', 'dom'), 0, 0, tiled=True)  5.74 us
    all_to_all x1, starting transfers between devices, body(): lax.all_to_all(outgoing, 'dom', split_axis=0, concat_axis=0, tiled=True)  4.37 us
    add x2, other arithmetic, taps_along(): total = total + taps[offset][:, None, None] * piece  3.95 us
    gather x1, local copies, waits for them, and re-layouts, body(): outgoing = jnp.take(flat_blocks, send_index, axis=0, mode='clip')  2.66 us
    ppermute x1, starting transfers between devices, extended_2(): before = lax.ppermute(last, axis, up)  2.42 us
  transfers between devices with their start and end apart: 4, of which 2 were waited for; matrix products, arithmetic and copies ran while one was open for 12% of the time, Pallas kernels for 0%

profile of v22, /device:TPU:0, one launch (start us, length us, event | category | flops | bytes accessed | tf_op | source)
XLA Modules:
  0.0 69.3 jit_solution(2390471931347457309)
XLA Ops:
  0.0 0.8 %select_reduce_fusion.3 = s32[16]{0:T(128)S(1)} fusion(s32[4,16]{1,0:T(4,128)} %param.8, pred[4]{0:T(512)(128)(4,1)S(1)} %iota_compare_fusion.5), kind=kLoop, calls=%fused_computation.220 | loop fusion | flops 112 | bytes 324 | tf_op jit(solution)/shard_map/reduce_sum | solution.py:55
  0.8 0.1 fusion.151
  0.9 0.1 slice_bitcast_fusion.63
  0.9 0.1 stack_reshape.3
  1.0 0.1 slice.524
  1.1 0.1 slice.526
  1.2 0.2 fusion.139
  1.4 0.1 select_add_fusion
  1.4 0.1 reshape.569
  1.5 2.7 %gather_fusion = f32[128,8,256]{2,1,0:T(8,128)} fusion(f32[64,8,256]{2,1,0:T(8,128)} %bitcast.172, s32[1024]{0:T(1024)S(1)} %pad_clamp_fusion.2), kind=kCustom, calls=%fused_computation | custom fusion | bytes 2097664 | tf_op jit(solution)/shard_map/jit(_take)/gather | solution.py:89
  4.2 4.4 %all-to-all-start = ((f32[128,8,256]{2,1,0:T(8,128)}), f32[128,8,256]{2,1,0:T(8,128)S(1)}, u32[]{:S(2)}, u32[]{:S(2)}) async-start(f32[128,8,256]{2,1,0:T(8,128)} %gather_fusion), calls=%async_computation | async-start | bytes 2097152 | tf_op jit(solution)/shard_map/all_to_all | solution.py:91
  8.6 2.4 %collective-permute-start = (f32[4,32,256]{2,1,0:T(8,128)S(1)}, f32[4,32,256]{2,1,0:T(8,128)S(1)}, u32[]{:S(2)}, u32[]{:S(2)}) collective-permute-start(f32[4,32,256]{2,1,0:T(8,128)S(1)} %get-tuple-element.5), channel_id=1, source_target_pairs={{0,4},{4,8},{8,12},{1,5},{5,9},{9,13},{2,6},{6,10},{10,14},{3,7},{... | collective-permute-start | bytes 393224 | tf_op jit(solution)/shard_map/ppermute | solution.py:19
  11.0 1.3 %collective-permute-start.1 = (f32[4,32,256]{2,1,0:T(8,128)S(1)}, f32[4,32,256]{2,1,0:T(8,128)S(1)}, u32[]{:S(2)}, u32[]{:S(2)}) collective-permute-start(f32[4,32,256]{2,1,0:T(8,128)S(1)} %get-tuple-element.6), channel_id=1, source_target_pairs={{4,0},{8,4},{12,8},{5,1},{9,5},{13,9},{6,2},{10,6},{14,10},{7,3},{... | collective-permute-start | bytes 393224 | tf_op jit(solution)/shard_map/ppermute | solution.py:20
  12.3 0.1 reshape.562
  12.4 0.6 fusion.150
  13.1 0.6 reshape.560
  13.7 0.6 reshape.561
  14.4 0.1 pad_add_fusion.1
  14.4 0.1 dynamic_slice.13
  14.5 0.1 copy.15
  14.6 0.1 select_reduce_fusion
  14.8 0.1 select_reduce_fusion.2
  14.9 0.1 iota_add_fusion.1
  15.0 0.1 slice_bitcast_fusion.58
  15.1 0.1 iota_add_fusion
  15.1 0.1 slice_select_fusion.8
  15.3 0.1 reshape.577
  15.4 0.1 add.307
  15.5 0.1 slice_bitcast_fusion.48
  15.6 0.1 fusion.132
  15.7 7.3 %all-to-all-done = f32[128,8,256]{2,1,0:T(8,128)S(1)} async-done(((f32[128,8,256]{2,1,0:T(8,128)}), f32[128,8,256]{2,1,0:T(8,128)S(1)}, u32[]{:S(2)}, u32[]{:S(2)}) %all-to-all-start) | async-done | bytes 1048608 | tf_op jit(solution)/shard_map/all_to_all | solution.py:91
  23.0 0.8 %gather_fusion.1 = f32[128,8,256]{2,1,0:T(8,128)S(1)} fusion(f32[128,8,256]{2,1,0:T(8,128)S(1)} %all-to-all-done, s32[1024]{0:T(1024)S(1)} %pad_clamp_fusion.1), kind=kCustom, calls=%fused_computation.1 | custom fusion | bytes 2097664 | tf_op jit(solution)/shard_map/jit(_take)/gather | solution.py:99
  23.8 2.7 %fusion.24 = f32[32,32,256]{2,1,0:T(8,128)S(1)} fusion(f32[32,32,256]{2,1,0:T(8,128)S(1)} %bitcast.173, f32[32]{0:T(128)S(1)} %get-tuple-element.19, f32[32]{0:T(128)S(1)} %get-tuple-element.20, f32[32]{0:T(128)S(1)} %get-tuple-element.21, f32[32]{0:T(128)S(1)} %get-tuple-element.22, f32[32]{0:T(128)S(1)} %get-tuple-element.23, f32[32]{0:T(128)S(1)} %get-tuple-element.24, ...), kind=kLoop, calls=%fused_computation.51 | loop fusion | flops 4456448 | bytes 2098304 | tf_op jit(solution)/shard_map/add | solution.py:36
  26.4 1.3 %fusion.8 = f32[32,32,256]{2,1,0:T(8,128)S(1)} fusion(f32[32,32,256]{2,1,0:T(8,128)S(1)} %fusion.24, f32[32]{0:T(128)S(1)} %get-tuple-element.11, f32[32]{0:T(128)S(1)} %get-tuple-element.12, f32[32]{0:T(128)S(1)} %get-tuple-element.13, f32[32]{0:T(128)S(1)} %get-tuple-element.14, f32[32]{0:T(128)S(1)} %get-tuple-element.15, f32[32]{0:T(128)S(1)} %get-tuple-element.16, ...), kind=kLoop, calls=%fused_computation.35 | loop fusion | flops 4456448 | bytes 2098304 | tf_op jit(solution)/shard_map/add | solution.py:36
  27.8 0.9 %fusion.34 = f32[24,32,256]{2,1,0:T(8,128)S(1)} fusion(f32[32,32,256]{2,1,0:T(8,128)S(1)} %fusion.8, f32[4,32,256]{2,1,0:T(8,128)S(1)} %collective-permute-done.1, f32[16,32,256]{2,1,0:T(8,128)S(1)} %bitcast.175, f32[4,32,256]{2,1,0:T(8,128)S(1)} %collective-permute-done, f32[24]{0:T(128)S(1)} %get-tuple-element.29, f32[24]{0:T(128)S(1)} %get-tuple-element.30, ...), kind=kLoop, calls=%fused_computation.62 | loop fusion | flops 4128768 | bytes 8651640 | tf_op jit(solution)/shard_map/jit(_where)/select_n | solution.py:121
  28.7 1.2 %fusion.60 = f32[16,32,256]{2,1,0:T(8,128)S(1)} fusion(f32[24,32,256]{2,1,0:T(8,128)S(1)} %fusion.34, f32[16]{0:T(128)S(1)} %get-tuple-element.56, f32[16]{0:T(128)S(1)} %get-tuple-element.57, f32[16]{0:T(128)S(1)} %get-tuple-element.58, f32[16]{0:T(128)S(1)} %get-tuple-element.59, f32[16]{0:T(128)S(1)} %get-tuple-element.60, f32[16]{0:T(128)S(1)} %get-tuple-element.61, ...), kind=kOutput, calls=%fused_computation.97 | convolution fusion | flops 52838400 | bytes 5288960 | tf_op jit(solution)/shard_map/pri,pix->prx/dot_general | solution.py:136
  29.9 1.3 %fusion.51 = f32[16,32,256]{2,1,0:T(8,128)S(1)} fusion(f32[16,32,256]{2,1,0:T(8,128)S(1)} %fusion.60, f32[16]{0:T(128)S(1)} %get-tuple-element.38, f32[16]{0:T(128)S(1)} %get-tuple-element.39, f32[16]{0:T(128)S(1)} %get-tuple-element.40, f32[16]{0:T(128)S(1)} %get-tuple-element.41, f32[16]{0:T(128)S(1)} %get-tuple-element.42, f32[16]{0:T(128)S(1)} %get-tuple-element.43, ...), kind=kLoop, calls=%fused_computation.87 | loop fusion | flops 2228224 | bytes 1049152 | tf_op jit(solution)/shard_map/log | solution.py:139
  31.2 0.8 %copy.16 = f32[4,4,4,8,256]{4,3,1,2,0:T(8,128)} copy(f32[4,4,4,8,256]{4,3,2,1,0:T(8,128)S(1)} %bitcast.174) | data formatting | bytes 1048576 | tf_op jit(solution)/shard_map/reshape | solution.py:139
  32.1 5.7 %all-to-all-start.1 = ((f32[16,4,8,256]{3,2,1,0:T(8,128)}), f32[16,4,8,256]{3,2,1,0:T(8,128)S(1)}, u32[]{:S(2)}, u32[]{:S(2)}) async-start(f32[16,4,8,256]{3,2,1,0:T(8,128)} %bitcast.78), calls=%async_computation.1 | async-start | bytes 1048576 | tf_op jit(solution)/shard_map/all_to_all | solution.py:141
  37.8 0.1 reshape.566
  37.9 0.2 fusion.135
  38.1 0.1 select_reduce_fusion.1
  38.2 0.1 broadcast_add_fusion
  38.2 0.1 reshape.585
  38.3 13.8 %all-to-all-done.1 = f32[16,4,8,256]{3,2,1,0:T(8,128)S(1)} async-done(((f32[16,4,8,256]{3,2,1,0:T(8,128)}), f32[16,4,8,256]{3,2,1,0:T(8,128)S(1)}, u32[]{:S(2)}, u32[]{:S(2)}) %all-to-all-start.1) | async-done | bytes 524320 | tf_op jit(solution)/shard_map/all_to_all | solution.py:141
  52.1 0.6 gather_fusion.2
  52.7 15.7 %all_gather.3 = f32[16,32,256]{2,1,0:T(8,128)S(1)} all-gather(f32[4,32,256]{2,1,0:T(8,128)S(1)} %copy_bitcast_fusion), channel_id=1, replica_groups=mesh['tile'=2,'dom'=4,'view'=4] {'view'}, dimensions={0}, use_global_device_ids=true | all-gather | bytes 655360 | tf_op jit(solution)/shard_map/all_gather | solution.py:156
  68.4 0.9 %mul.612 = f32[16,32,256]{2,1,0:T(8,128)} multiply(f32[16,32,256]{2,1,0:T(8,128)S(1)} %copy-done, f32[16,32,256]{2,1,0:T(8,128)S(1)} %all_gather.3) | non-fusion elementwise | flops 131072 | bytes 1572864 | tf_op jit(solution)/shard_map/mul | solution.py:157
  (31 shorter events, 0.2 us)
Async XLA Ops:
  4.2 4.4 %copy-start.1 = (f32[1,16,32,256]{3,2,1,0:T(8,128)S(1)}, f32[1,16,32,256]{3,2,1,0:T(8,128)}, u32[]{:S(2)}) copy-start(f32[1,16,32,256]{3,2,1,0:T(8,128)} %param.6) | copy-start | bytes 1572868
  4.2 8.2 %copy-start.4 = (s32[1,64]{1,0:T(1,128)S(1)}, s32[1,64]{1,0:T(1,128)}, u32[]{:S(2)}) copy-start(s32[1,64]{1,0:T(1,128)} %param.9) | copy-start | bytes 772
  4.2 10.3 %copy-start.3 = (f32[1,4,3,9]{3,1,2,0:T(4,128)S(1)}, f32[1,4,3,9]{3,1,2,0:T(4,128)}, u32[]{:S(2)}) copy-start(f32[1,4,3,9]{3,1,2,0:T(4,128)} %param.7) | copy-start | bytes 1300
  4.2 18.8 %all-to-all-start = ((f32[128,8,256]{2,1,0:T(8,128)}), f32[128,8,256]{2,1,0:T(8,128)S(1)}, u32[]{:S(2)}, u32[]{:S(2)}) async-start(f32[128,8,256]{2,1,0:T(8,128)} %gather_fusion), calls=%async_computation | async-start | bytes 2097152 | tf_op jit(solution)/shard_map/all_to_all | solution.py:91
  8.6 19.1 %collective-permute-start = (f32[4,32,256]{2,1,0:T(8,128)S(1)}, f32[4,32,256]{2,1,0:T(8,128)S(1)}, u32[]{:S(2)}, u32[]{:S(2)}) collective-permute-start(f32[4,32,256]{2,1,0:T(8,128)S(1)} %get-tuple-element.5), channel_id=1, source_target_pairs={{0,4},{4,8},{8,12},{1,5},{5,9},{9,13},{2,6},{6,10},{10,14},{3,7},{... | collective-permute-start | bytes 393224 | tf_op jit(solution)/shard_map/ppermute | solution.py:19
  11.0 16.7 %collective-permute-start.1 = (f32[4,32,256]{2,1,0:T(8,128)S(1)}, f32[4,32,256]{2,1,0:T(8,128)S(1)}, u32[]{:S(2)}, u32[]{:S(2)}) collective-permute-start(f32[4,32,256]{2,1,0:T(8,128)S(1)} %get-tuple-element.6), channel_id=1, source_target_pairs={{4,0},{8,4},{12,8},{5,1},{9,5},{13,9},{6,2},{10,6},{14,10},{7,3},{... | collective-permute-start | bytes 393224 | tf_op jit(solution)/shard_map/ppermute | solution.py:20
  31.2 6.6 %copy-start.2 = (s32[4,16]{1,0:T(4,128)S(1)}, s32[4,16]{1,0:T(4,128)}, u32[]{:S(2)}) copy-start(s32[4,16]{1,0:T(4,128)} %param.8) | copy-start | bytes 772
  32.1 20.0 %all-to-all-start.1 = ((f32[16,4,8,256]{3,2,1,0:T(8,128)}), f32[16,4,8,256]{3,2,1,0:T(8,128)S(1)}, u32[]{:S(2)}, u32[]{:S(2)}) async-start(f32[16,4,8,256]{3,2,1,0:T(8,128)} %bitcast.78), calls=%async_computation.1 | async-start | bytes 1048576 | tf_op jit(solution)/shard_map/all_to_all | solution.py:141
  38.3 30.1 %copy-start = (f32[16,32,256]{2,1,0:T(8,128)S(1)}, f32[16,32,256]{2,1,0:T(8,128)}, u32[]{:S(2)}) copy-start(f32[16,32,256]{2,1,0:T(8,128)} %param.5) | copy-start | bytes 1572868

commit v23 on v17

--- a/solution.py
+++ b/solution.py
@@ -84,9 +84,13 @@
     source_block = jnp.where(
         in_top[:, None], above[None, :], jnp.where(in_bottom[:, None], below[None, :], send_slot[None, :])
     )
-    send_index = (source_plane[None, :] * block_count + source_block.T).reshape(-1)
+    main_index = (jnp.arange(plane_count, dtype=jnp.int32)[None, :] * block_count + send_slot[:, None]).reshape(-1)
     flat_blocks = estimate.reshape(plane_count * block_count, block_rows, lane_count)
-    outgoing = jnp.take(flat_blocks, send_index, axis=0, mode="clip")
+    main = jnp.take(flat_blocks, main_index, axis=0, mode="clip")
+    main = main.reshape(block_count, plane_count, block_rows, lane_count)
+    prev_main = jnp.concatenate([main[:1], main[:-1]], axis=0)
+    next_main = jnp.concatenate([main[1:], main[-1:]], axis=0)
+    outgoing = jnp.concatenate([prev_main[:, plane_count - wide :], main, next_main[:, :wide]], axis=1)
     outgoing = outgoing.reshape(block_count * wide_count, block_rows, lane_count)
     arrived = lax.all_to_all(outgoing, "dom", split_axis=0, concat_axis=0, tiled=True)
     my_sources = lax.dynamic_index_in_dim(source_dev, dom_index, 0, keepdims=False)

time: 69.7 us -> 69.8 us (level)
  other arithmetic: 9.17 us -> 10.2 us
  local copies, waits for them, and re-layouts: 8.08 us -> 7.09 us
    concatenate x0 -> x1, other arithmetic: none -> 1.04 us  [body(): jnp.concatenate([prev_main[:, plane_count - wide:], main, next_main[:, :w...]
    gather x1, local copies, waits for them, and re-layouts: 2.66 us -> 1.64 us  [body(): main = jnp.take(flat_blocks, main_index, axis=0, mode='clip')]
where the time goes in v23:
time: 69.8 us; the launch traced here: 69.4 us
  waiting for transfers between devices  21.1 us (30%)
  blocking collectives  15.7 us (22%)
  starting transfers between devices  13.8 us (20%)
  other arithmetic  10.2 us (15%)
  local copies, waits for them, and re-layouts  7.09 us (10%)
  matrix products  1.21 us (2%)
    all_gather x1, blocking collectives, body(): log_joined = lax.all_gather(log_total, 'view', axis=0, tiled=True)  15.7 us
    all_to_all x1, waiting for transfers between devices, body(): arrived_logs = lax.all_to_all(outgoing, ('view', 'dom'), 0, 0, tiled=True)  13.8 us
    all_to_all x1, waiting for transfers between devices, body(): lax.all_to_all(outgoing, 'dom', split_axis=0, concat_axis=0, tiled=True)  7.38 us
    all_to_all x1, starting transfers between devices, body(): arrived_logs = lax.all_to_all(outgoing, ('view', 'dom'), 0, 0, tiled=True)  5.74 us
    all_to_all x1, starting transfers between devices, body(): lax.all_to_all(outgoing, 'dom', split_axis=0, concat_axis=0, tiled=True)  4.37 us
    add x2, other arithmetic, taps_along(): total = total + taps[offset][:, None, None] * piece  3.95 us
    ppermute x1, starting transfers between devices, extended_2(): before = lax.ppermute(last, axis, up)  2.42 us
    gather x1, local copies, waits for them, and re-layouts, body(): main = jnp.take(flat_blocks, main_index, axis=0, mode='clip')  1.64 us
  transfers between devices with their start and end apart: 4, of which 2 were waited for; matrix products, arithmetic and copies ran while one was open for 12% of the time, Pallas kernels for 0%

profile of v23, /device:TPU:0, one launch (start us, length us, event | category | flops | bytes accessed | tf_op | source)
XLA Modules:
  0.0 69.4 jit_solution(13880474734969462398)
XLA Ops:
  0.0 0.8 %select_reduce_fusion.3 = s32[16]{0:T(128)S(1)} fusion(s32[4,16]{1,0:T(4,128)} %param.8, pred[4]{0:T(512)(128)(4,1)S(1)} %iota_compare_fusion.5), kind=kLoop, calls=%fused_computation.224 | loop fusion | flops 112 | bytes 324 | tf_op jit(solution)/shard_map/reduce_sum | solution.py:55
  0.8 0.1 fusion.149
  0.9 0.1 stack_reshape.3
  1.0 0.1 slice.548
  1.1 0.1 slice.550
  1.2 0.2 fusion.139
  1.4 0.1 broadcast_add_fusion.1
  1.4 0.1 reshape.525
  1.5 1.6 %gather_fusion = f32[64,8,256]{2,1,0:T(8,128)S(1)} fusion(f32[64,8,256]{2,1,0:T(8,128)} %bitcast.178, s32[1024]{0:T(1024)S(1)} %pad_clamp_fusion.2), kind=kCustom, calls=%fused_computation | custom fusion | bytes 1048832 | tf_op jit(solution)/shard_map/jit(_take)/gather | solution.py:89
  3.3 1.0 %fusion.32 = f32[4,32,8,256]{3,2,1,0:T(8,128)} fusion(f32[1,16,8,256]{3,2,1,0:T(8,128)S(1)} %get-tuple-element.8, f32[3,16,8,256]{3,2,1,0:T(8,128)S(1)} %bitcast.181, f32[3,16,8,256]{3,2,1,0:T(8,128)S(1)} %bitcast.180, f32[1,16,8,256]{3,2,1,0:T(8,128)S(1)} %get-tuple-element.7, f32[4,16,8,256]{3,2,1,0:T(8,128)S(1)} %bitcast.176), kind=kLoop, calls=%fused_computation.60 | loop fusion | flops 1048576 | bytes 2621440 | tf_op jit(solution)/shard_map/concatenate | solution.py:93
  4.3 4.4 %all-to-all-start = ((f32[128,8,256]{2,1,0:T(8,128)}), f32[128,8,256]{2,1,0:T(8,128)S(1)}, u32[]{:S(2)}, u32[]{:S(2)}) async-start(f32[128,8,256]{2,1,0:T(8,128)} %bitcast.36), calls=%async_computation | async-start | bytes 2097152 | tf_op jit(solution)/shard_map/all_to_all | solution.py:95
  8.7 2.4 %collective-permute-start = (f32[4,32,256]{2,1,0:T(8,128)S(1)}, f32[4,32,256]{2,1,0:T(8,128)S(1)}, u32[]{:S(2)}, u32[]{:S(2)}) collective-permute-start(f32[4,32,256]{2,1,0:T(8,128)S(1)} %get-tuple-element.5), channel_id=1, source_target_pairs={{0,4},{4,8},{8,12},{1,5},{5,9},{9,13},{2,6},{6,10},{10,14},{3,7},{... | collective-permute-start | bytes 393224 | tf_op jit(solution)/shard_map/ppermute | solution.py:19
  11.1 1.3 %collective-permute-start.1 = (f32[4,32,256]{2,1,0:T(8,128)S(1)}, f32[4,32,256]{2,1,0:T(8,128)S(1)}, u32[]{:S(2)}, u32[]{:S(2)}) collective-permute-start(f32[4,32,256]{2,1,0:T(8,128)S(1)} %get-tuple-element.6), channel_id=1, source_target_pairs={{4,0},{8,4},{12,8},{5,1},{9,5},{13,9},{6,2},{10,6},{14,10},{7,3},{... | collective-permute-start | bytes 393224 | tf_op jit(solution)/shard_map/ppermute | solution.py:20
  12.4 0.1 reshape.515
  12.5 0.6 fusion.148
  13.1 0.6 reshape.513
  13.8 0.6 reshape.514
  14.4 0.1 pad_add_fusion.1
  14.5 0.1 dynamic_slice.13
  14.6 0.1 copy.15
  14.7 0.1 select_reduce_fusion
  14.9 0.1 select_reduce_fusion.2
  15.0 0.1 iota_add_fusion.1
  15.1 0.1 slice_bitcast_fusion.60
  15.1 0.1 slice_select_fusion.8
  15.2 0.1 iota_add_fusion
  15.3 0.1 reshape.533
  15.4 0.1 add.293
  15.5 0.1 slice_bitcast_fusion.50
  15.6 0.1 fusion.132
  15.7 7.4 %all-to-all-done = f32[128,8,256]{2,1,0:T(8,128)S(1)} async-done(((f32[128,8,256]{2,1,0:T(8,128)}), f32[128,8,256]{2,1,0:T(8,128)S(1)}, u32[]{:S(2)}, u32[]{:S(2)}) %all-to-all-start) | async-done | bytes 1048608 | tf_op jit(solution)/shard_map/all_to_all | solution.py:95
  23.1 0.8 %gather_fusion.1 = f32[128,8,256]{2,1,0:T(8,128)S(1)} fusion(f32[128,8,256]{2,1,0:T(8,128)S(1)} %all-to-all-done, s32[1024]{0:T(1024)S(1)} %pad_clamp_fusion.1), kind=kCustom, calls=%fused_computation.1 | custom fusion | bytes 2097664 | tf_op jit(solution)/shard_map/jit(_take)/gather | solution.py:103
  23.9 2.7 %fusion.24 = f32[32,32,256]{2,1,0:T(8,128)S(1)} fusion(f32[32,32,256]{2,1,0:T(8,128)S(1)} %bitcast.177, f32[32]{0:T(128)S(1)} %get-tuple-element.23, f32[32]{0:T(128)S(1)} %get-tuple-element.24, f32[32]{0:T(128)S(1)} %get-tuple-element.25, f32[32]{0:T(128)S(1)} %get-tuple-element.26, f32[32]{0:T(128)S(1)} %get-tuple-element.27, f32[32]{0:T(128)S(1)} %get-tuple-element.28, ...), kind=kLoop, calls=%fused_computation.51 | loop fusion | flops 4456448 | bytes 2098304 | tf_op jit(solution)/shard_map/add | solution.py:36
  26.5 1.3 %fusion.8 = f32[32,32,256]{2,1,0:T(8,128)S(1)} fusion(f32[32,32,256]{2,1,0:T(8,128)S(1)} %fusion.24, f32[32]{0:T(128)S(1)} %get-tuple-element.15, f32[32]{0:T(128)S(1)} %get-tuple-element.16, f32[32]{0:T(128)S(1)} %get-tuple-element.17, f32[32]{0:T(128)S(1)} %get-tuple-element.18, f32[32]{0:T(128)S(1)} %get-tuple-element.19, f32[32]{0:T(128)S(1)} %get-tuple-element.20, ...), kind=kLoop, calls=%fused_computation.35 | loop fusion | flops 4456448 | bytes 2098304 | tf_op jit(solution)/shard_map/add | solution.py:36
  27.9 0.9 %fusion.36 = f32[24,32,256]{2,1,0:T(8,128)S(1)} fusion(f32[32,32,256]{2,1,0:T(8,128)S(1)} %fusion.8, f32[4,32,256]{2,1,0:T(8,128)S(1)} %collective-permute-done.1, f32[16,32,256]{2,1,0:T(8,128)S(1)} %bitcast.182, f32[4,32,256]{2,1,0:T(8,128)S(1)} %collective-permute-done, f32[24]{0:T(128)S(1)} %get-tuple-element.33, f32[24]{0:T(128)S(1)} %get-tuple-element.34, ...), kind=kLoop, calls=%fused_computation.66 | loop fusion | flops 4128768 | bytes 8651640 | tf_op jit(solution)/shard_map/jit(_where)/select_n | solution.py:125
  28.8 1.2 %fusion.62 = f32[16,32,256]{2,1,0:T(8,128)S(1)} fusion(f32[24,32,256]{2,1,0:T(8,128)S(1)} %fusion.36, f32[16]{0:T(128)S(1)} %get-tuple-element.60, f32[16]{0:T(128)S(1)} %get-tuple-element.61, f32[16]{0:T(128)S(1)} %get-tuple-element.62, f32[16]{0:T(128)S(1)} %get-tuple-element.63, f32[16]{0:T(128)S(1)} %get-tuple-element.64, ...), kind=kOutput, calls=%fused_computation.101 | convolution fusion | flops 52838400 | bytes 5288960 | tf_op jit(solution)/shard_map/pri,pix->prx/dot_general | solution.py:140
  30.0 1.3 %fusion.53 = f32[16,32,256]{2,1,0:T(8,128)S(1)} fusion(f32[16,32,256]{2,1,0:T(8,128)S(1)} %fusion.62, f32[16]{0:T(128)S(1)} %get-tuple-element.42, f32[16]{0:T(128)S(1)} %get-tuple-element.43, f32[16]{0:T(128)S(1)} %get-tuple-element.44, f32[16]{0:T(128)S(1)} %get-tuple-element.45, f32[16]{0:T(128)S(1)} %get-tuple-element.46, f32[16]{0:T(128)S(1)} %get-tuple-element.47, ...), kind=kLoop, calls=%fused_computation.91 | loop fusion | flops 2228224 | bytes 1049152 | tf_op jit(solution)/shard_map/log | solution.py:143
  31.3 0.8 %copy.16 = f32[4,4,4,8,256]{4,3,1,2,0:T(8,128)} copy(f32[4,4,4,8,256]{4,3,2,1,0:T(8,128)S(1)} %bitcast.179) | data formatting | bytes 1048576 | tf_op jit(solution)/shard_map/reshape | solution.py:143
  32.2 5.7 %all-to-all-start.1 = ((f32[16,4,8,256]{3,2,1,0:T(8,128)}), f32[16,4,8,256]{3,2,1,0:T(8,128)S(1)}, u32[]{:S(2)}, u32[]{:S(2)}) async-start(f32[16,4,8,256]{3,2,1,0:T(8,128)} %bitcast.82), calls=%async_computation.1 | async-start | bytes 1048576 | tf_op jit(solution)/shard_map/all_to_all | solution.py:145
  37.9 0.1 reshape.521
  38.0 0.2 fusion.135
  38.2 0.1 select_reduce_fusion.1
  38.3 0.1 broadcast_add_fusion
  38.4 0.1 reshape.541
  38.4 13.8 %all-to-all-done.1 = f32[16,4,8,256]{3,2,1,0:T(8,128)S(1)} async-done(((f32[16,4,8,256]{3,2,1,0:T(8,128)}), f32[16,4,8,256]{3,2,1,0:T(8,128)S(1)}, u32[]{:S(2)}, u32[]{:S(2)}) %all-to-all-start.1) | async-done | bytes 524320 | tf_op jit(solution)/shard_map/all_to_all | solution.py:145
  52.2 0.6 gather_fusion.2
  52.8 15.7 %all_gather.3 = f32[16,32,256]{2,1,0:T(8,128)S(1)} all-gather(f32[4,32,256]{2,1,0:T(8,128)S(1)} %copy_bitcast_fusion), channel_id=1, replica_groups=mesh['tile'=2,'dom'=4,'view'=4] {'view'}, dimensions={0}, use_global_device_ids=true | all-gather | bytes 655360 | tf_op jit(solution)/shard_map/all_gather | solution.py:160
  68.5 0.9 %exponential_multiply_fusion = f32[16,32,256]{2,1,0:T(8,128)} fusion(f32[16,32,256]{2,1,0:T(8,128)S(1)} %copy-done, f32[16,32,256]{2,1,0:T(8,128)S(1)} %all_gather.3), kind=kLoop, calls=%fused_computation.117 | loop fusion | flops 262144 | bytes 1572864 | tf_op jit(solution)/shard_map/mul | solution.py:161
  (34 shorter events, 0.3 us)
Async XLA Ops:
  4.3 4.4 %copy-start.1 = (f32[1,16,32,256]{3,2,1,0:T(8,128)S(1)}, f32[1,16,32,256]{3,2,1,0:T(8,128)}, u32[]{:S(2)}) copy-start(f32[1,16,32,256]{3,2,1,0:T(8,128)} %param.6) | copy-start | bytes 1572868
  4.3 8.2 %copy-start.4 = (s32[1,64]{1,0:T(1,128)S(1)}, s32[1,64]{1,0:T(1,128)}, u32[]{:S(2)}) copy-start(s32[1,64]{1,0:T(1,128)} %param.9) | copy-start | bytes 772
  4.3 10.3 %copy-start.3 = (f32[1,4,3,9]{3,1,2,0:T(4,128)S(1)}, f32[1,4,3,9]{3,1,2,0:T(4,128)}, u32[]{:S(2)}) copy-start(f32[1,4,3,9]{3,1,2,0:T(4,128)} %param.7) | copy-start | bytes 1300
  4.3 18.8 %all-to-all-start = ((f32[128,8,256]{2,1,0:T(8,128)}), f32[128,8,256]{2,1,0:T(8,128)S(1)}, u32[]{:S(2)}, u32[]{:S(2)}) async-start(f32[128,8,256]{2,1,0:T(8,128)} %bitcast.36), calls=%async_computation | async-start | bytes 2097152 | tf_op jit(solution)/shard_map/all_to_all | solution.py:95
  8.7 19.1 %collective-permute-start = (f32[4,32,256]{2,1,0:T(8,128)S(1)}, f32[4,32,256]{2,1,0:T(8,128)S(1)}, u32[]{:S(2)}, u32[]{:S(2)}) collective-permute-start(f32[4,32,256]{2,1,0:T(8,128)S(1)} %get-tuple-element.5), channel_id=1, source_target_pairs={{0,4},{4,8},{8,12},{1,5},{5,9},{9,13},{2,6},{6,10},{10,14},{3,7},{... | collective-permute-start | bytes 393224 | tf_op jit(solution)/shard_map/ppermute | solution.py:19
  11.1 16.7 %collective-permute-start.1 = (f32[4,32,256]{2,1,0:T(8,128)S(1)}, f32[4,32,256]{2,1,0:T(8,128)S(1)}, u32[]{:S(2)}, u32[]{:S(2)}) collective-permute-start(f32[4,32,256]{2,1,0:T(8,128)S(1)} %get-tuple-element.6), channel_id=1, source_target_pairs={{4,0},{8,4},{12,8},{5,1},{9,5},{13,9},{6,2},{10,6},{14,10},{7,3},{... | collective-permute-start | bytes 393224 | tf_op jit(solution)/shard_map/ppermute | solution.py:20
  31.3 6.6 %copy-start.2 = (s32[4,16]{1,0:T(4,128)S(1)}, s32[4,16]{1,0:T(4,128)}, u32[]{:S(2)}) copy-start(s32[4,16]{1,0:T(4,128)} %param.8) | copy-start | bytes 772
  32.2 20.0 %all-to-all-start.1 = ((f32[16,4,8,256]{3,2,1,0:T(8,128)}), f32[16,4,8,256]{3,2,1,0:T(8,128)S(1)}, u32[]{:S(2)}, u32[]{:S(2)}) async-start(f32[16,4,8,256]{3,2,1,0:T(8,128)} %bitcast.82), calls=%async_computation.1 | async-start | bytes 1048576 | tf_op jit(solution)/shard_map/all_to_all | solution.py:145
  38.4 30.1 %copy-start = (f32[16,32,256]{2,1,0:T(8,128)S(1)}, f32[16,32,256]{2,1,0:T(8,128)}, u32[]{:S(2)}) copy-start(f32[16,32,256]{2,1,0:T(8,128)} %param.5) | copy-start | bytes 1572868

commit v24 on v23

--- a/solution.py
+++ b/solution.py
@@ -91,6 +91,15 @@
     prev_main = jnp.concatenate([main[:1], main[:-1]], axis=0)
     next_main = jnp.concatenate([main[1:], main[-1:]], axis=0)
     outgoing = jnp.concatenate([prev_main[:, plane_count - wide :], main, next_main[:, :wide]], axis=1)
+    send_planes = (jnp.arange(block_count, dtype=jnp.int32)[:, None] * plane_count
+                   + jnp.arange(plane_count + 2 * wide, dtype=jnp.int32)[None, :])
+    send_band = jnp.take(jnp.pad(band_all, wide, mode="edge"), send_planes, mode="clip")
+    send_in_band = send_band[None] == jnp.arange(kernels.shape[0], dtype=jnp.int32)[:, None, None]
+    send_x = jnp.sum(jnp.where(send_in_band[:, None], kernels[:, 2, :, None, None], 0.0), axis=0)
+    lane_pad = jnp.pad(outgoing, [(0, 0), (0, 0), (0, 0), (reach, reach)])
+    outgoing = jnp.zeros(outgoing.shape, jnp.float32)
+    for tap in range(2 * reach + 1):
+        outgoing = outgoing + send_x[tap][:, :, None, None] * lane_pad[..., tap : tap + lane_count]
     outgoing = outgoing.reshape(block_count * wide_count, block_rows, lane_count)
     arrived = lax.all_to_all(outgoing, "dom", split_axis=0, concat_axis=0, tiled=True)
     my_sources = lax.dynamic_index_in_dim(source_dev, dom_index, 0, keepdims=False)
@@ -112,7 +121,7 @@
     tables = jnp.sum(jnp.where(in_band[:, None, None, :], kernels[:, :, :, None], 0.0), axis=0)
     x_wide = tables[2]
     y_wide = tables[1]
-    lateral_ext = lateral_fwd(camera_ext, x_wide, y_wide)
+    lateral_ext = taps_along(camera_ext, y_wide, 1, False)
     ext_count = plane_count + 2 * reach
     ext_planes = plane_start - reach + jnp.arange(ext_count, dtype=jnp.int32)
     ext_inside = (ext_planes >= 0) & (ext_planes < total_planes)

time: 69.8 us -> 74.9 us (1.073)
  local copies, waits for them, and re-layouts: 7.09 us -> 9.17 us
  waiting for transfers between devices: 21.1 us -> 23.1 us
  other arithmetic: 10.2 us -> 11.2 us
    add x0 -> x2, other arithmetic: none -> 4.49 us  [the longest x1 4.42 us: body(): outgoing + send_x[tap][:, :, None, None] * lane_pad[..., tap:tap + lane_c...]
    add x2 -> x1, other arithmetic: 3.95 us -> 1.28 us  [taps_along(): total = total + taps[offset][:, None, None] * piece]
    all_to_all x1, waiting for transfers between devices: 7.38 us -> 9.34 us  [body(): lax.all_to_all(outgoing, 'dom', split_axis=0, concat_axis=0, tiled=True)]
    gather x0 -> x2, local copies, waits for them, and re-layouts: none -> 1.31 us  [body(): jnp.take(jnp.pad(band_all, wide, mode='edge'), send_planes, mode='clip')]
    concatenate x1, other arithmetic: 1.04 us -> 0.07 us  [body(): jnp.concatenate([prev_main[:, plane_count - wide:], main, next_main[:, :w...]
  transfers between devices with their start and end apart: 4 -> 4, of which waited for: 2 -> 2; matrix products, arithmetic and copies ran while one was open for 12% -> 5% of each run, Pallas kernels for 0% -> 0%
where the time goes in v24:
time: 74.9 us; the launch traced here: 74.5 us
  waiting for transfers between devices  23.1 us (31%)
  blocking collectives  15.7 us (21%)
  starting transfers between devices  13.8 us (18%)
  other arithmetic  11.2 us (15%)
  local copies, waits for them, and re-layouts  9.17 us (12%)
  matrix products  1.21 us (2%)
    all_gather x1, blocking collectives, body(): log_joined = lax.all_gather(log_total, 'view', axis=0, tiled=True)  15.7 us
    all_to_all x1, waiting for transfers between devices, body(): arrived_logs = lax.all_to_all(outgoing, ('view', 'dom'), 0, 0, tiled=True)  13.8 us
    all_to_all x1, waiting for transfers between devices, body(): lax.all_to_all(outgoing, 'dom', split_axis=0, concat_axis=0, tiled=True)  9.34 us
    all_to_all x1, starting transfers between devices, body(): arrived_logs = lax.all_to_all(outgoing, ('view', 'dom'), 0, 0, tiled=True)  5.73 us
    add x1, other arithmetic, body(): outgoing + send_x[tap][:, :, None, None] * lane_pad[..., tap:tap + lane_c...  4.42 us
    all_to_all x1, starting transfers between devices, body(): lax.all_to_all(outgoing, 'dom', split_axis=0, concat_axis=0, tiled=True)  4.37 us
    ppermute x1, starting transfers between devices, extended_2(): before = lax.ppermute(last, axis, up)  2.42 us
    gather x1, local copies, waits for them, and re-layouts, body(): main = jnp.take(flat_blocks, main_index, axis=0, mode='clip')  1.64 us
  transfers between devices with their start and end apart: 4, of which 2 were waited for; matrix products, arithmetic and copies ran while one was open for 5% of the time, Pallas kernels for 0%

profile of v24, /device:TPU:0, one launch (start us, length us, event | category | flops | bytes accessed | tf_op | source)
XLA Modules:
  0.0 74.5 jit_solution(16769264839244266462)
XLA Ops:
  0.0 0.8 %select_reduce_fusion.4 = s32[16]{0:T(128)S(1)} fusion(s32[4,16]{1,0:T(4,128)} %param.8, pred[4]{0:T(512)(128)(4,1)S(1)} %iota_compare_fusion.6), kind=kLoop, calls=%fused_computation.239 | loop fusion | flops 112 | bytes 324 | tf_op jit(solution)/shard_map/reduce_sum | solution.py:55
  0.8 0.1 fusion.149
  0.9 0.1 stack_reshape.3
  1.0 0.1 slice.535
  1.1 0.1 slice.537
  1.2 0.2 fusion.139
  1.4 0.1 reshape.557
  1.5 1.6 %gather_fusion.1 = f32[64,8,256]{2,1,0:T(8,128)S(1)} fusion(f32[64,8,256]{2,1,0:T(8,128)} %bitcast.182, s32[1024]{0:T(1024)S(1)} %pad_clamp_fusion.2), kind=kCustom, calls=%fused_computation.1 | custom fusion | bytes 1048832 | tf_op jit(solution)/shard_map/jit(_take)/gather | solution.py:89
  3.3 0.5 copy-done.4
  3.8 0.7 fusion.148
  4.6 0.1 reshape.549
  4.7 0.6 reshape.537
  5.3 0.7 reshape.538
  6.0 0.1 pad_add_fusion.1
  6.1 1.2 %gather_fusion = s32[128]{0:T(128)S(1)} fusion(s32[80]{0:T(128)S(1)} %pad_add_fusion.1, s32[1024]{0:T(1024)S(1)} %pad_clamp_fusion.3), kind=kCustom, calls=%fused_computation | custom fusion | bytes 1536 | tf_op jit(solution)/shard_map/jit(_take)/gather | solution.py:96
  7.3 0.1 reshape.548
  7.4 0.1 select_reduce_fusion
  7.6 4.4 %fusion.24 = f32[4,32,8,256]{3,2,1,0:T(8,128)} fusion(f32[4,32,8,256]{3,2,1,0:T(8,128)S(1)} %fusion.32, f32[4,32]{1,0:T(4,128)S(1)} %get-tuple-element.24, f32[4,32]{1,0:T(4,128)S(1)} %get-tuple-element.25, f32[4,32]{1,0:T(4,128)S(1)} %get-tuple-element.26, f32[4,32]{1,0:T(4,128)S(1)} %get-tuple-element.27, f32[4,32]{1,0:T(4,128)S(1)} %get-tuple-element.28, ...), kind=kLoop, calls=%fused_computation.52 | loop fusion | flops 4456448 | bytes 2101760 | tf_op jit(solution)/shard_map/add | solution.py:102
  12.1 4.4 %all-to-all-start = ((f32[128,8,256]{2,1,0:T(8,128)}), f32[128,8,256]{2,1,0:T(8,128)S(1)}, u32[]{:S(2)}, u32[]{:S(2)}) async-start(f32[128,8,256]{2,1,0:T(8,128)} %bitcast.45), calls=%async_computation | async-start | bytes 2097152 | tf_op jit(solution)/shard_map/all_to_all | solution.py:104
  16.5 2.4 %collective-permute-start = (f32[4,32,256]{2,1,0:T(8,128)S(1)}, f32[4,32,256]{2,1,0:T(8,128)S(1)}, u32[]{:S(2)}, u32[]{:S(2)}) collective-permute-start(f32[4,32,256]{2,1,0:T(8,128)S(1)} %get-tuple-element.5), channel_id=1, source_target_pairs={{0,4},{4,8},{8,12},{1,5},{5,9},{9,13},{2,6},{6,10},{10,14},{3,7},{... | collective-permute-start | bytes 393224 | tf_op jit(solution)/shard_map/ppermute | solution.py:19
  18.9 1.3 %collective-permute-start.1 = (f32[4,32,256]{2,1,0:T(8,128)S(1)}, f32[4,32,256]{2,1,0:T(8,128)S(1)}, u32[]{:S(2)}, u32[]{:S(2)}) collective-permute-start(f32[4,32,256]{2,1,0:T(8,128)S(1)} %get-tuple-element.6), channel_id=1, source_target_pairs={{4,0},{8,4},{12,8},{5,1},{9,5},{13,9},{6,2},{10,6},{14,10},{7,3},{... | collective-permute-start | bytes 393224 | tf_op jit(solution)/shard_map/ppermute | solution.py:20
  20.2 0.1 reshape.539
  20.3 0.1 copy.15
  20.5 0.1 select_reduce_fusion.1
  20.7 0.1 select_reduce_fusion.3
  20.9 0.1 slice_bitcast_fusion.61
  20.9 0.1 iota_add_fusion
  21.0 0.1 reshape.565
  21.1 0.1 add.313
  21.2 0.1 slice_select_fusion.8
  21.3 0.1 slice_bitcast_fusion.51
  21.4 0.1 fusion.132
  21.5 9.3 %all-to-all-done = f32[128,8,256]{2,1,0:T(8,128)S(1)} async-done(((f32[128,8,256]{2,1,0:T(8,128)}), f32[128,8,256]{2,1,0:T(8,128)S(1)}, u32[]{:S(2)}, u32[]{:S(2)}) %all-to-all-start) | async-done | bytes 1048608 | tf_op jit(solution)/shard_map/all_to_all | solution.py:104
  30.9 0.8 %gather_fusion.2 = f32[128,8,256]{2,1,0:T(8,128)S(1)} fusion(f32[128,8,256]{2,1,0:T(8,128)S(1)} %all-to-all-done, s32[1024]{0:T(1024)S(1)} %pad_clamp_fusion.1), kind=kCustom, calls=%fused_computation.2 | custom fusion | bytes 2097664 | tf_op jit(solution)/shard_map/jit(_take)/gather | solution.py:112
  31.6 1.3 %fusion.8 = f32[32,32,256]{2,1,0:T(8,128)S(1)} fusion(f32[32,32,256]{2,1,0:T(8,128)S(1)} %bitcast.181, f32[32]{0:T(128)S(1)} %get-tuple-element.15, f32[32]{0:T(128)S(1)} %get-tuple-element.16, f32[32]{0:T(128)S(1)} %get-tuple-element.17, f32[32]{0:T(128)S(1)} %get-tuple-element.18, f32[32]{0:T(128)S(1)} %get-tuple-element.19, f32[32]{0:T(128)S(1)} %get-tuple-element.20, ...), kind=kLoop, calls=%fused_computation.36 | loop fusion | flops 4456448 | bytes 2098304 | tf_op jit(solution)/shard_map/add | solution.py:36
  32.9 0.9 %fusion.36 = f32[24,32,256]{2,1,0:T(8,128)S(1)} fusion(f32[32,32,256]{2,1,0:T(8,128)S(1)} %fusion.8, f32[4,32,256]{2,1,0:T(8,128)S(1)} %collective-permute-done.1, f32[16,32,256]{2,1,0:T(8,128)S(1)} %bitcast.186, f32[4,32,256]{2,1,0:T(8,128)S(1)} %collective-permute-done, f32[24]{0:T(128)S(1)} %get-tuple-element.33, f32[24]{0:T(128)S(1)} %get-tuple-element.34, ...), kind=kLoop, calls=%fused_computation.67 | loop fusion | flops 4128768 | bytes 8651640 | tf_op jit(solution)/shard_map/jit(_where)/select_n | solution.py:134
  33.8 1.2 %fusion.62 = f32[16,32,256]{2,1,0:T(8,128)S(1)} fusion(f32[24,32,256]{2,1,0:T(8,128)S(1)} %fusion.36, f32[16]{0:T(128)S(1)} %get-tuple-element.60, f32[16]{0:T(128)S(1)} %get-tuple-element.61, f32[16]{0:T(128)S(1)} %get-tuple-element.62, f32[16]{0:T(128)S(1)} %get-tuple-element.63, f32[16]{0:T(128)S(1)} %get-tuple-element.64, ...), kind=kOutput, calls=%fused_computation.102 | convolution fusion | flops 52838400 | bytes 5288960 | tf_op jit(solution)/shard_map/pri,pix->prx/dot_general | solution.py:149
  35.1 1.3 %fusion.53 = f32[16,32,256]{2,1,0:T(8,128)S(1)} fusion(f32[16,32,256]{2,1,0:T(8,128)S(1)} %fusion.62, f32[16]{0:T(128)S(1)} %get-tuple-element.42, f32[16]{0:T(128)S(1)} %get-tuple-element.43, f32[16]{0:T(128)S(1)} %get-tuple-element.44, f32[16]{0:T(128)S(1)} %get-tuple-element.45, f32[16]{0:T(128)S(1)} %get-tuple-element.46, f32[16]{0:T(128)S(1)} %get-tuple-element.47, ...), kind=kLoop, calls=%fused_computation.92 | loop fusion | flops 2228224 | bytes 1049152 | tf_op jit(solution)/shard_map/log | solution.py:152
  36.4 0.8 %copy.16 = f32[4,4,4,8,256]{4,3,1,2,0:T(8,128)} copy(f32[4,4,4,8,256]{4,3,2,1,0:T(8,128)S(1)} %bitcast.183) | data formatting | bytes 1048576 | tf_op jit(solution)/shard_map/reshape | solution.py:152
  37.3 5.7 %all-to-all-start.1 = ((f32[16,4,8,256]{3,2,1,0:T(8,128)}), f32[16,4,8,256]{3,2,1,0:T(8,128)S(1)}, u32[]{:S(2)}, u32[]{:S(2)}) async-start(f32[16,4,8,256]{3,2,1,0:T(8,128)} %bitcast.83), calls=%async_computation.1 | async-start | bytes 1048576 | tf_op jit(solution)/shard_map/all_to_all | solution.py:154
  43.0 0.1 reshape.545
  43.1 0.2 fusion.135
  43.3 0.1 select_reduce_fusion.2
  43.4 0.1 reshape.573
  43.5 13.8 %all-to-all-done.1 = f32[16,4,8,256]{3,2,1,0:T(8,128)S(1)} async-done(((f32[16,4,8,256]{3,2,1,0:T(8,128)}), f32[16,4,8,256]{3,2,1,0:T(8,128)S(1)}, u32[]{:S(2)}, u32[]{:S(2)}) %all-to-all-start.1) | async-done | bytes 524320 | tf_op jit(solution)/shard_map/all_to_all | solution.py:154
  57.3 0.6 gather_fusion.3
  57.9 15.7 %all_gather.3 = f32[16,32,256]{2,1,0:T(8,128)S(1)} all-gather(f32[4,32,256]{2,1,0:T(8,128)S(1)} %copy_bitcast_fusion), channel_id=1, replica_groups=mesh['tile'=2,'dom'=4,'view'=4] {'view'}, dimensions={0}, use_global_device_ids=true | all-gather | bytes 655360 | tf_op jit(solution)/shard_map/all_gather | solution.py:169
  73.6 0.9 %exponential_multiply_fusion = f32[16,32,256]{2,1,0:T(8,128)} fusion(f32[16,32,256]{2,1,0:T(8,128)S(1)} %copy-done, f32[16,32,256]{2,1,0:T(8,128)S(1)} %all_gather.3), kind=kLoop, calls=%fused_computation.118 | loop fusion | flops 262144 | bytes 1572864 | tf_op jit(solution)/shard_map/mul | solution.py:170
  (44 shorter events, 0.8 us)
Async XLA Ops:
  3.2 0.7 copy-start.4
  6.1 1.3 %copy-start.2 = (f32[1,4,3,9]{3,1,2,0:T(4,128)S(1)}, f32[1,4,3,9]{3,1,2,0:T(4,128)}, u32[]{:S(2)}) copy-start(f32[1,4,3,9]{3,1,2,0:T(4,128)} %param.7) | copy-start | bytes 1300
  12.1 4.4 %copy-start.1 = (f32[1,16,32,256]{3,2,1,0:T(8,128)S(1)}, f32[1,16,32,256]{3,2,1,0:T(8,128)}, u32[]{:S(2)}) copy-start(f32[1,16,32,256]{3,2,1,0:T(8,128)} %param.6) | copy-start | bytes 1572868
  12.1 18.8 %all-to-all-start = ((f32[128,8,256]{2,1,0:T(8,128)}), f32[128,8,256]{2,1,0:T(8,128)S(1)}, u32[]{:S(2)}, u32[]{:S(2)}) async-start(f32[128,8,256]{2,1,0:T(8,128)} %bitcast.45), calls=%async_computation | async-start | bytes 2097152 | tf_op jit(solution)/shard_map/all_to_all | solution.py:104
  16.5 16.5 %collective-permute-start = (f32[4,32,256]{2,1,0:T(8,128)S(1)}, f32[4,32,256]{2,1,0:T(8,128)S(1)}, u32[]{:S(2)}, u32[]{:S(2)}) collective-permute-start(f32[4,32,256]{2,1,0:T(8,128)S(1)} %get-tuple-element.5), channel_id=1, source_target_pairs={{0,4},{4,8},{8,12},{1,5},{5,9},{9,13},{2,6},{6,10},{10,14},{3,7},{... | collective-permute-start | bytes 393224 | tf_op jit(solution)/shard_map/ppermute | solution.py:19
  18.9 14.0 %collective-permute-start.1 = (f32[4,32,256]{2,1,0:T(8,128)S(1)}, f32[4,32,256]{2,1,0:T(8,128)S(1)}, u32[]{:S(2)}, u32[]{:S(2)}) collective-permute-start(f32[4,32,256]{2,1,0:T(8,128)S(1)} %get-tuple-element.6), channel_id=1, source_target_pairs={{4,0},{8,4},{12,8},{5,1},{9,5},{13,9},{6,2},{10,6},{14,10},{7,3},{... | collective-permute-start | bytes 393224 | tf_op jit(solution)/shard_map/ppermute | solution.py:20
  36.4 6.6 %copy-start.3 = (s32[4,16]{1,0:T(4,128)S(1)}, s32[4,16]{1,0:T(4,128)}, u32[]{:S(2)}) copy-start(s32[4,16]{1,0:T(4,128)} %param.8) | copy-start | bytes 772
  37.3 20.0 %all-to-all-start.1 = ((f32[16,4,8,256]{3,2,1,0:T(8,128)}), f32[16,4,8,256]{3,2,1,0:T(8,128)S(1)}, u32[]{:S(2)}, u32[]{:S(2)}) async-start(f32[16,4,8,256]{3,2,1,0:T(8,128)} %bitcast.83), calls=%async_computation.1 | async-start | bytes 1048576 | tf_op jit(solution)/shard_map/all_to_all | solution.py:154
  43.5 30.1 %copy-start = (f32[16,32,256]{2,1,0:T(8,128)S(1)}, f32[16,32,256]{2,1,0:T(8,128)}, u32[]{:S(2)}) copy-start(f32[16,32,256]{2,1,0:T(8,128)} %param.5) | copy-start | bytes 1572868
